TPU v7x, 32 devices: a whole 2x2x4 slice. The times are simulated.
32 devices in a mesh: groups: 2 (over x), ctx: 16 (over z, y, core).
Axes of the slice: x: 2, y: 2, z: 4, core: 2. Of those that a mesh axis runs over, the one named last changes fastest.
Arguments:
- queries: bfloat16 [8192, 4096], P(('groups', 'ctx')), parts along dimension 0, may hold values from -24 to 24
- key_rows: bfloat16 [8192, 1024], P(('groups', 'ctx')), parts along dimension 0, may hold values from -6 to 6
- value_rows: bfloat16 [8192, 1024], P(('groups', 'ctx')), parts along dimension 0, may hold values from -6 to 6
- pattern: int32 [32, 11], replicated, may hold values from 0 to 31, as said below
Outputs:
- attended: bfloat16 [8192, 4096], P(('groups', 'ctx')), parts along dimension 0
There are 2 independent parts, one for each index of `groups`. A program takes and returns all parts, laid end to end along the dimension named above; an argument that names none is the same for every part. Nothing has to cross between parts.
Inputs may be any that keep to these rules, and one draw needn't show every extreme that they name: `pattern`: entry j < 8 of block b's list is max(b - j, 0); the other 3 entries are multiples of 32 no larger than b, the first of them exactly (b // 32) * 32.
All inputs are finite; a program needn't handle non-finite values.
Results may differ from a plain program's by a relative error of at most 0.0036.
Values may be sent and summed in bfloat16 or wider, within the bound.
No kernel may reach another device: no remote copies, remote signals or barrier semaphores. Data moves between devices by JAX's collectives and lax.ppermute only.
A program may use at most 128 MiB of HBM per device.

v0:
```python
import jax
import jax.numpy as jnp
from jax import lax
from jax.sharding import PartitionSpec as P

H = 32
KVH = 8
HD = 128
BLK = 128
WIN = 8
STRIDE = 32
LIST = 11


def passed_along(shard, axis, by):
    size = lax.axis_size(axis)
    pairs = [(i, i + by) for i in range(size) if 0 <= i + by < size]
    return lax.ppermute(shard, axis, pairs)


def broadcast(block, axis, source):
    block = jnp.where(lax.axis_index(axis) == source, block, jnp.zeros_like(block))
    return lax.psum(block, axis)


def attend_block(query_block, key_block, value_block, entries, block):
    group_size = H // KVH
    query = query_block.reshape(BLK, KVH, group_size, HD)
    keys_b = key_block.reshape(LIST * BLK, KVH, HD)
    values_b = value_block.reshape(LIST * BLK, KVH, HD)
    scores = jnp.einsum(
        "qkgd,skd->kgqs", query, keys_b, preferred_element_type=jnp.float32
    ) * HD ** (-0.5)
    query_pos = jnp.arange(BLK, dtype=jnp.int32)
    key_pos = jnp.tile(jnp.arange(BLK, dtype=jnp.int32), LIST)
    on_diagonal = jnp.repeat(entries == block, BLK)
    allowed = jnp.logical_not(on_diagonal)[None, :] | (key_pos[None, :] <= query_pos[:, None])
    scores = jnp.where(allowed[None, None], scores, -jnp.inf)
    row_max = jnp.max(scores, axis=-1, keepdims=True)
    powers = jnp.exp(scores - row_max)
    denominator = jnp.sum(powers, axis=-1)
    weights_bf = powers.astype(jnp.bfloat16)
    weighted = jnp.einsum(
        "kgqs,skd->qkgd", weights_bf, values_b, preferred_element_type=jnp.float32
    )
    result = weighted / jnp.transpose(denominator, (2, 0, 1))[..., None]
    return result.astype(jnp.bfloat16).reshape(BLK, H * HD)


def window_tail(key_rows, value_rows, need_rows, offset):
    return passed_along((key_rows[-need_rows:], value_rows[-need_rows:]), "ctx", offset)


def per_device(queries, key_rows, value_rows, pattern):
    tok_rows = queries.shape[0]
    kv_width = key_rows.shape[1]
    blocks_here = tok_rows // BLK
    ctx_count = lax.axis_size("ctx")
    own_index = lax.axis_index("ctx")
    reach_rows = (WIN - 1) * BLK
    hops_back = (reach_rows + tok_rows - 1) // tok_rows
    early_keys = []
    early_values = []
    for offset in range(hops_back, 0, -1):
        need_rows = min(tok_rows, reach_rows - (offset - 1) * tok_rows)
        received = window_tail(key_rows, value_rows, need_rows, offset)
        early_keys.append(received[0])
        early_values.append(received[1])
    window_keys = jnp.concatenate(early_keys + [key_rows], axis=0)
    window_values = jnp.concatenate(early_values + [value_rows], axis=0)
    columns = blocks_here * ctx_count // STRIDE
    spread = STRIDE // blocks_here

    def fetch(column, buffers):
        received = (
            broadcast(key_rows[:BLK], "ctx", column * spread),
            broadcast(value_rows[:BLK], "ctx", column * spread),
        )
        return (
            lax.dynamic_update_slice_in_dim(buffers[0], received[0], column * BLK, 0),
            lax.dynamic_update_slice_in_dim(buffers[1], received[1], column * BLK, 0),
        )

    empty = jnp.zeros((columns * BLK, kv_width), jnp.bfloat16)
    column_keys, column_values = lax.fori_loop(0, columns, fetch, (empty, empty))
    buffer_blocks = columns + WIN - 1 + blocks_here
    key_buffer = jnp.concatenate([column_keys, window_keys], axis=0).reshape(
        buffer_blocks, BLK, kv_width
    )
    value_buffer = jnp.concatenate([column_values, window_values], axis=0).reshape(
        buffer_blocks, BLK, kv_width
    )
    first_block = own_index * blocks_here - (WIN - 1)
    rows_pattern = lax.dynamic_slice_in_dim(pattern, own_index * blocks_here, blocks_here, 0)
    in_window = jnp.arange(LIST, dtype=jnp.int32) < WIN

    def attend_one(local):
        entries = rows_pattern[local]
        block = own_index * blocks_here + local
        source = jnp.where(in_window, columns + entries - first_block, entries // STRIDE)
        key_block = key_buffer[source].reshape(LIST * BLK, kv_width)
        value_block = value_buffer[source].reshape(LIST * BLK, kv_width)
        query_block = lax.dynamic_slice_in_dim(queries, local * BLK, BLK, 0)
        return attend_block(query_block, key_block, value_block, entries, block)

    outputs = lax.map(attend_one, jnp.arange(blocks_here, dtype=jnp.int32))
    return outputs.reshape(tok_rows, H * HD)


def solution(mesh):
    placed = (
        P(("groups", "ctx"), None),
        P(("groups", "ctx"), None),
        P(("groups", "ctx"), None),
        P(),
    )
    return jax.shard_map(
        per_device,
        mesh=mesh,
        in_specs=placed,
        out_specs=P(("groups", "ctx"), None),
        check_vma=False,
    )
```

profile of v0, /device:TPU:16, one launch (start us, length us, event | category | flops | bytes accessed | tf_op | source)
XLA Modules:
  0.0 245.6 jit_solution(16278251806183512577)
XLA Ops:
  6.6 1.9 fusion.19
  8.5 1.8 fusion.18
  10.3 2.9 %collective-permute-start.1 = (bf16[256,1024]{1,0:T(8,128)(2,1)S(1)}, bf16[256,1024]{1,0:T(8,128)(2,1)S(1)}, u32[]{:S(2)}, u32[]{:S(2)}) collective-permute-start(bf16[256,1024]{1,0:T(8,128)(2,1)S(1)} %copy-done.3), channel_id=1, source_target_pairs={{0,3},{1,4},{2,5},{3,6},{4,7},{5,8},{6,9},{7,10},{8,11},{9,12},{10... | collective-permute-start | bytes 1572872 | tf_op jit(solution)/shard_map/ppermute | solution.py:18
  13.2 3.4 %collective-permute-start.2 = (bf16[256,1024]{1,0:T(8,128)(2,1)S(1)}, bf16[256,1024]{1,0:T(8,128)(2,1)S(1)}, u32[]{:S(2)}, u32[]{:S(2)}) collective-permute-start(bf16[256,1024]{1,0:T(8,128)(2,1)S(1)} %copy-done.3), channel_id=1, source_target_pairs={{0,2},{1,3},{2,4},{3,5},{4,6},{5,7},{6,8},{7,9},{8,10},{9,11},{10,... | collective-permute-start | bytes 1572872 | tf_op jit(solution)/shard_map/ppermute | solution.py:18
  16.6 2.4 collective-permute-start.3
  19.0 1.9 collective-permute-start
  20.9 1.9 collective-permute-start.4
  23.0 80.8 %all-reduce.3.cloned.1.call-done = (bf16[128,1024]{1,0:T(8,128)(2,1)}, bf16[128,1024]{1,0:T(8,128)(2,1)}) async-done(((bf16[128,1024]{1,0:T(8,128)(2,1)}, bf16[128,1024]{1,0:T(8,128)(2,1)}), (bf16[128,1024]{1,0:T(8,128)(2,1)}, bf16[128,1024]{1,0:T(8,128)(2,1)})) %all-reduce.3.cloned.1.call-update) | async-done | bytes 524304 | tf_op jit(solution)/shard_map/while/body/eval_jaxpr/psum | solution.py:23
  105.8 1.9 collective-permute-start.5
  107.8 3.4 %collective-permute-start.6 = (bf16[256,1024]{1,0:T(8,128)(2,1)S(1)}, bf16[256,1024]{1,0:T(8,128)(2,1)S(1)}, u32[]{:S(2)}, u32[]{:S(2)}) collective-permute-start(bf16[256,1024]{1,0:T(8,128)(2,1)S(1)} %copy-done.4), channel_id=1, source_target_pairs={{0,2},{1,3},{2,4},{3,5},{4,6},{5,7},{6,8},{7,9},{8,10},{9,11},{10,... | collective-permute-start | bytes 1572872 | tf_op jit(solution)/shard_map/ppermute | solution.py:18
  111.2 2.3 collective-permute-start.7
  113.7 3.2 %collective-permute-done.5 = bf16[256,1024]{1,0:T(8,128)(2,1)S(1)} collective-permute-done((bf16[256,1024]{1,0:T(8,128)(2,1)S(1)}, bf16[256,1024]{1,0:T(8,128)(2,1)S(1)}, u32[]{:S(2)}, u32[]{:S(2)}) %collective-permute-start.5) | collective-permute-done | bytes 524320 | tf_op jit(solution)/shard_map/ppermute | solution.py:18
  116.9 15.6 %collective-permute-done.6 = bf16[256,1024]{1,0:T(8,128)(2,1)S(1)} collective-permute-done((bf16[256,1024]{1,0:T(8,128)(2,1)S(1)}, bf16[256,1024]{1,0:T(8,128)(2,1)S(1)}, u32[]{:S(2)}, u32[]{:S(2)}) %collective-permute-start.6) | collective-permute-done | bytes 524320 | tf_op jit(solution)/shard_map/ppermute | solution.py:18
  132.5 6.4 %collective-permute-done.7 = bf16[256,1024]{1,0:T(8,128)(2,1)S(1)} collective-permute-done((bf16[256,1024]{1,0:T(8,128)(2,1)S(1)}, bf16[256,1024]{1,0:T(8,128)(2,1)S(1)}, u32[]{:S(2)}, u32[]{:S(2)}) %collective-permute-start.7) | collective-permute-done | bytes 524320 | tf_op jit(solution)/shard_map/ppermute | solution.py:18
  139.0 1.5 copy-done.1
  140.5 98.3 %while.9 = (s32[]{:T(128)}, bf16[2,128,4096]{2,1,0:T(8,128)(2,1)}, s32[2]{0:T(128)S(1)}, s32[2,11]{1,0:T(2,128)S(1)}, s32[]{:T(128)}, /*index=5*/bf16[10,128,102...) while((s32[]{:T(128)}, bf16[2,128,4096]{2,1,0:T(8,128)(2,1)}, ...), condition=%wide.region_5.6_spmd.clone, body=%wide.region_2.5_spmd.clone.sunk | while | flops 2994562304 | bytes 108988712 | solution.py:106
  141.7 1.3 constant_dynamic-slice_fusion.4
  143.0 1.3 copy.47
  146.0 2.5 %gather_fusion = bf16[11,128,1024]{2,1,0:T(8,128)(2,1)S(1)} fusion(bf16[10,128,1024]{2,1,0:T(8,128)(2,1)} %get-tuple-element.301, s32[1024]{0:T(1024)S(1)} %pad_clamp_fusion.2), kind=kCustom, calls=%fused_computation.1.clone.clone.1 | custom fusion | bytes 5767212 | tf_op jit(solution)/shard_map/while/body/eval_jaxpr/gather | solution.py:101
  148.5 2.4 copy.48
  152.5 12.9 %fusion.34 = (f32[8,4,128]{2,1,0:T(4,128)S(1)}, f32[8,4,128,1408]{2,3,1,0:T(8,128)}) fusion(bf16[128,8,4,128]{0,3,2,1:T(8,128)(2,1)} %bitcast.94, bf16[1408,8,128,1]{2,1,0,3:T(8,128)(2,1)} %bitcast.93, pred[128,1408]{0,1:T(8,128)(4,1)S(1)} %fusion.33), kind=kOutput, calls=%fused_computation.47.clone.1 | convolution fusion | flops 1493692416 | bytes 27197440 | tf_op jit(solution)/shard_map/while/body/eval_jaxpr/qkgd,skd->kgqs/dot_general | solution.py:31
  165.5 2.5 %gather_fusion.1 = bf16[11,128,1024]{2,1,0:T(8,128)(2,1)S(1)} fusion(bf16[10,128,1024]{2,1,0:T(8,128)(2,1)} %get-tuple-element.299, s32[1024]{0:T(1024)S(1)} %pad_clamp_fusion.2), kind=kCustom, calls=%fused_computation.clone.clone.1 | custom fusion | bytes 5767212 | tf_op jit(solution)/shard_map/while/body/eval_jaxpr/gather | solution.py:102
  168.7 9.6 %fusion.35 = f32[8,4,128]{2,1,0:T(4,128)S(1)} fusion(f32[8,4,128,1408]{2,3,1,0:T(8,128)} %get-tuple-element.264, f32[8,4,128]{2,1,0:T(4,128)S(1)} %get-tuple-element.265), kind=kLoop, calls=%fused_computation.5.clone.1 | loop fusion | flops 11530240 | bytes 23101440 | tf_op jit(solution)/shard_map/while/body/eval_jaxpr/reduce_sum | solution.py:41
  178.3 9.8 %fusion.36 = bf16[128,8,4,128]{0,3,2,1:T(8,128)(2,1)S(1)} fusion(f32[8,4,128,1408]{2,3,1,0:T(8,128)} %get-tuple-element.264, f32[8,4,128]{2,1,0:T(4,128)S(1)} %get-tuple-element.265, bf16[1408,8,128,1]{2,1,0,3:T(8,128)(2,1)S(1)} %bitcast.87, f32[128,8,4]{0,2,1:T(4,128)S(1)} %bitcast.95), kind=kOutput, calls=%fused_computation.12.clone.1 | convolution fusion | flops 1488977920 | bytes 27033600 | tf_op jit(solution)/shard_map/while/body/eval_jaxpr/kgqs,skd->qkgd/dot_general | solution.py:43
  190.8 1.3 constant_dynamic-slice_fusion.4
  192.1 1.3 copy.47
  195.2 2.5 %gather_fusion = bf16[11,128,1024]{2,1,0:T(8,128)(2,1)S(1)} fusion(bf16[10,128,1024]{2,1,0:T(8,128)(2,1)} %get-tuple-element.301, s32[1024]{0:T(1024)S(1)} %pad_clamp_fusion.2), kind=kCustom, calls=%fused_computation.1.clone.clone.1 | custom fusion | bytes 5767212 | tf_op jit(solution)/shard_map/while/body/eval_jaxpr/gather | solution.py:101
  197.6 2.4 copy.48
  201.7 12.9 %fusion.34 = (f32[8,4,128]{2,1,0:T(4,128)S(1)}, f32[8,4,128,1408]{2,3,1,0:T(8,128)}) fusion(bf16[128,8,4,128]{0,3,2,1:T(8,128)(2,1)} %bitcast.94, bf16[1408,8,128,1]{2,1,0,3:T(8,128)(2,1)} %bitcast.93, pred[128,1408]{0,1:T(8,128)(4,1)S(1)} %fusion.33), kind=kOutput, calls=%fused_computation.47.clone.1 | convolution fusion | flops 1493692416 | bytes 27197440 | tf_op jit(solution)/shard_map/while/body/eval_jaxpr/qkgd,skd->kgqs/dot_general | solution.py:31
  214.6 2.5 %gather_fusion.1 = bf16[11,128,1024]{2,1,0:T(8,128)(2,1)S(1)} fusion(bf16[10,128,1024]{2,1,0:T(8,128)(2,1)} %get-tuple-element.299, s32[1024]{0:T(1024)S(1)} %pad_clamp_fusion.2), kind=kCustom, calls=%fused_computation.clone.clone.1 | custom fusion | bytes 5767212 | tf_op jit(solution)/shard_map/while/body/eval_jaxpr/gather | solution.py:102
  217.8 9.6 %fusion.35 = f32[8,4,128]{2,1,0:T(4,128)S(1)} fusion(f32[8,4,128,1408]{2,3,1,0:T(8,128)} %get-tuple-element.264, f32[8,4,128]{2,1,0:T(4,128)S(1)} %get-tuple-element.265), kind=kLoop, calls=%fused_computation.5.clone.1 | loop fusion | flops 11530240 | bytes 23101440 | tf_op jit(solution)/shard_map/while/body/eval_jaxpr/reduce_sum | solution.py:41
  227.4 9.8 %fusion.36 = bf16[128,8,4,128]{0,3,2,1:T(8,128)(2,1)S(1)} fusion(f32[8,4,128,1408]{2,3,1,0:T(8,128)} %get-tuple-element.264, f32[8,4,128]{2,1,0:T(4,128)S(1)} %get-tuple-element.265, bf16[1408,8,128,1]{2,1,0,3:T(8,128)(2,1)S(1)} %bitcast.87, f32[128,8,4]{0,2,1:T(4,128)S(1)} %bitcast.95), kind=kOutput, calls=%fused_computation.12.clone.1 | convolution fusion | flops 1488977920 | bytes 27033600 | tf_op jit(solution)/shard_map/while/body/eval_jaxpr/kgqs,skd->qkgd/dot_general | solution.py:43
  (52 shorter events, 10.5 us)
Async XLA Ops:
  6.5 16.3 %copy-start = (s32[32,11]{0,1:T(8,128)S(1)}, s32[32,11]{0,1:T(8,128)}, u32[]{:S(2)}) copy-start(s32[32,11]{0,1:T(8,128)} %param.9) | copy-start | bytes 4228
  6.5 3.8 %copy-start.3 = (bf16[256,1024]{1,0:T(8,128)(2,1)S(1)}, bf16[256,1024]{1,0:T(8,128)(2,1)}, u32[]{:S(2)}) copy-start(bf16[256,1024]{1,0:T(8,128)(2,1)} %param.8) | copy-start | bytes 1572868
  6.5 99.3 %copy-start.4 = (bf16[256,1024]{1,0:T(8,128)(2,1)S(1)}, bf16[256,1024]{1,0:T(8,128)(2,1)}, u32[]{:S(2)}) copy-start(bf16[256,1024]{1,0:T(8,128)(2,1)} %param.7) | copy-start | bytes 1572868
  6.5 97.3 %all-reduce.3.cloned.1.call-start = ((), (), s32[]{:S(2)}) async-start(), calls=%async_computation | async-start | bytes 1048576 | tf_op jit(solution)/shard_map/while/body/eval_jaxpr/psum | solution.py:23
  10.3 100.9 %collective-permute-start.1 = (bf16[256,1024]{1,0:T(8,128)(2,1)S(1)}, bf16[256,1024]{1,0:T(8,128)(2,1)S(1)}, u32[]{:S(2)}, u32[]{:S(2)}) collective-permute-start(bf16[256,1024]{1,0:T(8,128)(2,1)S(1)} %copy-done.3), channel_id=1, source_target_pairs={{0,3},{1,4},{2,5},{3,6},{4,7},{5,8},{6,9},{7,10},{8,11},{9,12},{10... | collective-permute-start | bytes 1572872 | tf_op jit(solution)/shard_map/ppermute | solution.py:18
  13.2 100.3 %collective-permute-start.2 = (bf16[256,1024]{1,0:T(8,128)(2,1)S(1)}, bf16[256,1024]{1,0:T(8,128)(2,1)S(1)}, u32[]{:S(2)}, u32[]{:S(2)}) collective-permute-start(bf16[256,1024]{1,0:T(8,128)(2,1)S(1)} %copy-done.3), channel_id=1, source_target_pairs={{0,2},{1,3},{2,4},{3,5},{4,6},{5,7},{6,8},{7,9},{8,10},{9,11},{10,... | collective-permute-start | bytes 1572872 | tf_op jit(solution)/shard_map/ppermute | solution.py:18
  16.6 96.9 %collective-permute-start.3 = (bf16[256,1024]{1,0:T(8,128)(2,1)S(1)}, bf16[256,1024]{1,0:T(8,128)(2,1)S(1)}, u32[]{:S(2)}, u32[]{:S(2)}) collective-permute-start(bf16[256,1024]{1,0:T(8,128)(2,1)S(1)} %copy-done.3), channel_id=1, source_target_pairs={{0,1},{1,2},{2,3},{3,4},{4,5},{5,6},{6,7},{7,8},{8,9},{9,10},{10,1... | collective-permute-start | bytes 1572872 | tf_op jit(solution)/shard_map/ppermute | solution.py:18
  19.0 86.8 %collective-permute-start = (bf16[128,1024]{1,0:T(8,128)(2,1)}, bf16[128,1024]{1,0:T(8,128)(2,1)S(1)}, u32[]{:S(2)}, u32[]{:S(2)}) collective-permute-start(bf16[128,1024]{1,0:T(8,128)(2,1)} %get-tuple-element.205), channel_id=1, source_target_pairs={{0,4},{1,5},{2,6},{3,7},{4,8},{5,9},{6,10},{7,11},{8,12},{9,13},{1... | collective-permute-start | bytes 786440 | tf_op jit(solution)/shard_map/ppermute | solution.py:18
  20.9 86.8 %collective-permute-start.4 = (bf16[128,1024]{1,0:T(8,128)(2,1)S(1)}, bf16[128,1024]{1,0:T(8,128)(2,1)S(1)}, u32[]{:S(2)}, u32[]{:S(2)}) collective-permute-start(bf16[128,1024]{1,0:T(8,128)(2,1)S(1)} %get-tuple-element.203), channel_id=1, source_target_pairs={{0,4},{1,5},{2,6},{3,7},{4,8},{5,9},{6,10},{7,11},{8,12},{9,13},{1... | collective-permute-start | bytes 786440 | tf_op jit(solution)/shard_map/ppermute | solution.py:18
  105.8 11.1 %collective-permute-start.5 = (bf16[256,1024]{1,0:T(8,128)(2,1)S(1)}, bf16[256,1024]{1,0:T(8,128)(2,1)S(1)}, u32[]{:S(2)}, u32[]{:S(2)}) collective-permute-start(bf16[256,1024]{1,0:T(8,128)(2,1)S(1)} %copy-done.4), channel_id=1, source_target_pairs={{0,3},{1,4},{2,5},{3,6},{4,7},{5,8},{6,9},{7,10},{8,11},{9,12},{10... | collective-permute-start | bytes 1572872 | tf_op jit(solution)/shard_map/ppermute | solution.py:18
  107.8 24.7 %collective-permute-start.6 = (bf16[256,1024]{1,0:T(8,128)(2,1)S(1)}, bf16[256,1024]{1,0:T(8,128)(2,1)S(1)}, u32[]{:S(2)}, u32[]{:S(2)}) collective-permute-start(bf16[256,1024]{1,0:T(8,128)(2,1)S(1)} %copy-done.4), channel_id=1, source_target_pairs={{0,2},{1,3},{2,4},{3,5},{4,6},{5,7},{6,8},{7,9},{8,10},{9,11},{10,... | collective-permute-start | bytes 1572872 | tf_op jit(solution)/shard_map/ppermute | solution.py:18
  111.2 27.7 %collective-permute-start.7 = (bf16[256,1024]{1,0:T(8,128)(2,1)S(1)}, bf16[256,1024]{1,0:T(8,128)(2,1)S(1)}, u32[]{:S(2)}, u32[]{:S(2)}) collective-permute-start(bf16[256,1024]{1,0:T(8,128)(2,1)S(1)} %copy-done.4), channel_id=1, source_target_pairs={{0,1},{1,2},{2,3},{3,4},{4,5},{5,6},{6,7},{7,8},{8,9},{9,10},{10,1... | collective-permute-start | bytes 1572872 | tf_op jit(solution)/shard_map/ppermute | solution.py:18
  113.7 25.3 %copy-start.2 = (bf16[1280,1024]{1,0:T(8,128)(2,1)}, bf16[1280,1024]{1,0:T(8,128)(2,1)S(1)}, u32[]{:S(2)}) copy-start(bf16[1280,1024]{1,0:T(8,128)(2,1)S(1)} %constant_dynamic-update-slice_fusion.1) | copy-start | bytes 7864324
  139.0 1.6 copy-start.1
Sparse Core Ops, SparseCore 0:
  10.8 92.9 all-reduce.2
where the time goes:
time: 246 us
  waiting for transfers between devices  106 us (43%)
  matrix products  45.4 us (18%)
  local copies, waits for them, and re-layouts  29.8 us (12%)
  other arithmetic  24.9 us (10%)
  starting transfers between devices  20.1 us (8%)
  between operations  13.6 us (6%)
  loops' own time  5.81 us (2%)
    psum x1, waiting for transfers between devices, broadcast(): return lax.psum(block, axis)  80.8 us
    dot_general x2, matrix products, attend_block(): jnp.einsum('qkgd,skd->kgqs', query, keys_b, preferred_element_type=jnp.fl...  25.9 us
    ppermute x8, waiting for transfers between devices, passed_along(): return lax.ppermute(shard, axis, pairs)  25.1 us
    ppermute x8, starting transfers between devices, passed_along(): return lax.ppermute(shard, axis, pairs)  20.1 us
    dot_general x2, matrix products, attend_block(): jnp.einsum('kgqs,skd->qkgd', weights_bf, values_b, preferred_element_type...  19.6 us
    reduce_sum x2, other arithmetic, attend_block(): denominator = jnp.sum(powers, axis=-1)  19.1 us
    while x4, local copies, waits for them, and re-layouts  6.23 us
    another operation x1, loops' own time, per_device(): outputs = lax.map(attend_one, jnp.arange(blocks_here, dtype=jnp.int32))  5.81 us
  transfers between devices with their start and end apart: 9, of which 4 were waited for; matrix products, arithmetic and copies ran while one was open for 1% of the time, Pallas kernels for 0%

commit v1 on v0

v1 whole, which is shorter than its diff:
```python
import functools

import jax
import jax.numpy as jnp
from jax import lax
from jax.experimental import pallas as pl
from jax.experimental.pallas import tpu as pltpu
from jax.sharding import PartitionSpec as P

H = 32
KVH = 8
HD = 128
BLK = 128
WIN = 8
STRIDE = 32
LIST = 11
GROUP = H // KVH


def passed_along(shard, axis, by):
    size = lax.axis_size(axis)
    pairs = [(i, i + by) for i in range(size) if 0 <= i + by < size]
    return lax.ppermute(shard, axis, pairs)


def tree_broadcast(block, axis, source, size):
    index = lax.axis_index(axis)
    span = size - source
    held = block
    dist = 1
    while dist < span:
        dist *= 2
    dist //= 2
    while dist >= 1:
        pairs = [
            (source + j, source + j + dist)
            for j in range(0, span, 2 * dist)
            if j + dist < span
        ]
        got = lax.ppermute(held, axis, pairs)
        rel = index - source
        takes = (rel >= 0) & (rel % (2 * dist) == dist)
        held = jnp.where(takes, got, held)
        dist //= 2
    return held


def attend_kernel(slot_ref, diag_ref, q_ref, k_ref, v_ref, o_ref, score_sc):
    local = pl.program_id(1)
    scale = HD ** (-0.5)
    q = q_ref[...]
    stacked = jnp.concatenate([q[:, j * HD:(j + 1) * HD] for j in range(GROUP)], axis=0)
    row = lax.broadcasted_iota(jnp.int32, (GROUP * BLK, BLK), 0) % BLK
    col = lax.broadcasted_iota(jnp.int32, (GROUP * BLK, BLK), 1)
    future = col > row
    run_max = jnp.full((GROUP * BLK, BLK), -jnp.inf, jnp.float32)
    for s in range(LIST):
        key = k_ref[0, slot_ref[local, s]]
        sc = lax.dot_general(
            stacked, key, (((1,), (1,)), ((), ())), preferred_element_type=jnp.float32
        ) * scale
        masked = jnp.logical_and(future, diag_ref[local, s] != 0)
        sc = jnp.where(masked, -jnp.inf, sc)
        score_sc[s] = sc
        run_max = jnp.maximum(run_max, sc)
    row_max = jnp.max(run_max, axis=1, keepdims=True)
    total = jnp.zeros((GROUP * BLK, BLK), jnp.float32)
    acc = jnp.zeros((GROUP * BLK, HD), jnp.float32)
    for s in range(LIST):
        powers = jnp.exp(score_sc[s] - row_max)
        total = total + powers
        value = v_ref[0, slot_ref[local, s]]
        acc = acc + jnp.dot(
            powers.astype(jnp.bfloat16), value, preferred_element_type=jnp.float32
        )
    denominator = jnp.sum(total, axis=1, keepdims=True)
    result = (acc / denominator).astype(jnp.bfloat16)
    o_ref[...] = jnp.concatenate(
        [result[j * BLK:(j + 1) * BLK] for j in range(GROUP)], axis=1
    )


def attend(slots, diag, queries, kv_buffer):
    blocks_here = queries.shape[0] // BLK
    buffer_blocks = kv_buffer.shape[1]
    flops = 4 * blocks_here * H * BLK * LIST * BLK * HD
    grid_spec = pltpu.PrefetchScalarGridSpec(
        num_scalar_prefetch=2,
        grid=(KVH, blocks_here),
        in_specs=[
            pl.BlockSpec((BLK, GROUP * HD), lambda g, b, *_: (b, g)),
            pl.BlockSpec((1, buffer_blocks, BLK, HD), lambda g, b, *_: (0, 0, 0, g)),
            pl.BlockSpec((1, buffer_blocks, BLK, HD), lambda g, b, *_: (1, 0, 0, g)),
        ],
        out_specs=pl.BlockSpec((BLK, GROUP * HD), lambda g, b, *_: (b, g)),
        scratch_shapes=[pltpu.VMEM((LIST, GROUP * BLK, BLK), jnp.float32)],
    )
    return pl.pallas_call(
        attend_kernel,
        out_shape=jax.ShapeDtypeStruct(queries.shape, jnp.bfloat16),
        grid_spec=grid_spec,
        compiler_params=pltpu.CompilerParams(
            dimension_semantics=("arbitrary", "arbitrary"),
        ),
        cost_estimate=pl.CostEstimate(
            flops=flops,
            transcendentals=blocks_here * H * BLK * LIST * BLK,
            bytes_accessed=2 * queries.size * 2 + kv_buffer.size * 2,
        ),
    )(slots, diag, queries, kv_buffer, kv_buffer)


def per_device(queries, key_rows, value_rows, pattern):
    tok_rows = queries.shape[0]
    blocks_here = tok_rows // BLK
    ctx_count = lax.axis_size("ctx")
    own_index = lax.axis_index("ctx")
    kv = jnp.stack([key_rows, value_rows])
    reach_rows = (WIN - 1) * BLK
    hops_back = (reach_rows + tok_rows - 1) // tok_rows
    early = []
    for offset in range(hops_back, 0, -1):
        need_rows = min(tok_rows, reach_rows - (offset - 1) * tok_rows)
        early.append(passed_along(kv[:, tok_rows - need_rows:], "ctx", offset))
    columns = blocks_here * ctx_count // STRIDE
    spread = STRIDE // blocks_here
    column_blocks = [
        tree_broadcast(kv[:, :BLK], "ctx", column * spread, ctx_count)
        for column in range(columns)
    ]
    buffer_blocks = columns + WIN - 1 + blocks_here
    kv_buffer = jnp.concatenate(column_blocks + early + [kv], axis=1).reshape(
        2, buffer_blocks, BLK, kv.shape[2]
    )
    first_block = own_index * blocks_here - (WIN - 1)
    rows_pattern = lax.dynamic_slice_in_dim(pattern, own_index * blocks_here, blocks_here, 0)
    in_window = jnp.arange(LIST, dtype=jnp.int32) < WIN
    slots = jnp.where(
        in_window[None, :],
        columns + rows_pattern - first_block,
        rows_pattern // STRIDE,
    )
    slots = jnp.clip(slots, 0, buffer_blocks - 1).astype(jnp.int32)
    blocks = own_index * blocks_here + jnp.arange(blocks_here, dtype=jnp.int32)
    diag = (rows_pattern == blocks[:, None]).astype(jnp.int32)
    return attend(slots, diag, queries, kv_buffer)


def solution(mesh):
    placed = (
        P(("groups", "ctx"), None),
        P(("groups", "ctx"), None),
        P(("groups", "ctx"), None),
        P(),
    )
    return jax.shard_map(
        per_device,
        mesh=mesh,
        in_specs=placed,
        out_specs=P(("groups", "ctx"), None),
        check_vma=False,
    )
```

time: 246 us -> 125 us (0.51)
  the two profiles are of different devices: /device:TPU:16 before, /device:TPU:15 now
where the time goes in v1:
time: 125 us; the launch traced here: 124 us
  Pallas kernels  39.3 us (31%)
  waiting for transfers between devices  38.4 us (31%)
  starting transfers between devices  34.9 us (28%)
  local copies, waits for them, and re-layouts  7.44 us (6%)
  other arithmetic  3.93 us (3%)
    pallas_call x1, Pallas kernels, attend(): pl.pallas_call(attend_kernel, out_shape=jax.ShapeDtypeStruct(queries.shap...  39.3 us
    ppermute x4, waiting for transfers between devices, passed_along(): return lax.ppermute(shard, axis, pairs)  36.5 us
    ppermute x4, starting transfers between devices, passed_along(): return lax.ppermute(shard, axis, pairs)  30.8 us
    unnamed x13, local copies, waits for them, and re-layouts  7.36 us
    ppermute x4, starting transfers between devices, tree_broadcast(): got = lax.ppermute(held, axis, pairs)  4.15 us
  transfers between devices with their start and end apart: 8, of which 2 were waited for; matrix products, arithmetic and copies ran while one was open for 4% of the time, Pallas kernels for 0%

profile of v1, /device:TPU:15, one launch (start us, length us, event | category | flops | bytes accessed | tf_op | source)
XLA Modules:
  0.0 124.3 jit_solution(13026155005826409347)
XLA Ops:
  0.0 2.2 %fusion.1 = (bf16[2,128,1024]{2,1,0:T(8,128)(2,1)}, bf16[2,128,1024]{2,1,0:T(8,128)(2,1)S(1)}) fusion(bf16[1,256,1024]{2,1,0:T(8,128)(2,1)} %bitcast.3, bf16[1,256,1024]{2,1,0:T(8,128)(2,1)} %bitcast.6), kind=kLoop, calls=%fused_computation.6 | loop fusion | flops 524288 | bytes 2097152 | tf_op jit(solution)/shard_map/stack | solution.py:118
  2.2 0.7 collective-permute-start
  2.9 0.0 collective-permute-done
  2.9 0.1 broadcast_select_fusion
  3.0 0.7 collective-permute-start.1
  3.7 0.0 collective-permute-done.1
  3.7 0.1 broadcast_select_fusion.1
  3.7 1.5 %collective-permute-start.2 = (bf16[2,128,1024]{2,1,0:T(8,128)(2,1)S(1)}, bf16[2,128,1024]{2,1,0:T(8,128)(2,1)}, u32[]{:S(2)}, u32[]{:S(2)}) collective-permute-start(bf16[2,128,1024]{2,1,0:T(8,128)(2,1)S(1)} %broadcast_select_fusion.1), channel_id=1, source_target_pairs={{0,2},{4,6},{8,10},{12,14},{16,18},{20,22},{24,26},{28,30}} | collective-permute-start | bytes 1572872 | tf_op jit(solution)/shard_map/ppermute | solution.py:40
  5.2 0.1 pad_maximum_fusion
  5.3 3.6 %collective-permute-start.5 = (bf16[2,256,1024]{2,1,0:T(8,128)(2,1)S(1)}, bf16[2,256,1024]{2,1,0:T(8,128)(2,1)}, u32[]{:S(2)}, u32[]{:S(2)}) collective-permute-start(bf16[2,256,1024]{2,1,0:T(8,128)(2,1)S(1)} %pad_maximum_fusion), channel_id=1, source_target_pairs={{0,3},{1,4},{2,5},{3,6},{4,7},{5,8},{6,9},{7,10},{8,11},{9,12},{10... | collective-permute-start | bytes 3145736 | tf_op jit(solution)/shard_map/ppermute | solution.py:23
  8.9 23.3 %collective-permute-start.6 = (bf16[2,256,1024]{2,1,0:T(8,128)(2,1)S(1)}, bf16[2,256,1024]{2,1,0:T(8,128)(2,1)}, u32[]{:S(2)}, u32[]{:S(2)}) collective-permute-start(bf16[2,256,1024]{2,1,0:T(8,128)(2,1)S(1)} %pad_maximum_fusion), channel_id=1, source_target_pairs={{0,2},{1,3},{2,4},{3,5},{4,6},{5,7},{6,8},{7,9},{8,10},{9,11},{10,... | collective-permute-start | bytes 3145736 | tf_op jit(solution)/shard_map/ppermute | solution.py:23
  32.3 1.9 %collective-permute-start.7 = (bf16[2,256,1024]{2,1,0:T(8,128)(2,1)S(1)}, bf16[2,256,1024]{2,1,0:T(8,128)(2,1)}, u32[]{:S(2)}, u32[]{:S(2)}) collective-permute-start(bf16[2,256,1024]{2,1,0:T(8,128)(2,1)S(1)} %pad_maximum_fusion), channel_id=1, source_target_pairs={{0,1},{1,2},{2,3},{3,4},{4,5},{5,6},{6,7},{7,8},{8,9},{9,10},{10,1... | collective-permute-start | bytes 3145736 | tf_op jit(solution)/shard_map/ppermute | solution.py:23
  34.2 1.9 %collective-permute-start.4 = (bf16[2,128,1024]{2,1,0:T(8,128)(2,1)}, bf16[2,128,1024]{2,1,0:T(8,128)(2,1)}, u32[]{:S(2)}, u32[]{:S(2)}) collective-permute-start(bf16[2,128,1024]{2,1,0:T(8,128)(2,1)} %get-tuple-element.5), channel_id=1, source_target_pairs={{0,4},{1,5},{2,6},{3,7},{4,8},{5,9},{6,10},{7,11},{8,12},{9,13},{1... | collective-permute-start | bytes 1572872 | tf_op jit(solution)/shard_map/ppermute | solution.py:23
  36.2 0.1 constant_dynamic-slice_fusion
  36.3 0.1 copy.6
  36.4 0.1 broadcast_select_fusion.2
  36.4 1.3 %collective-permute-start.3 = (bf16[2,128,1024]{2,1,0:T(8,128)(2,1)S(1)}, bf16[2,128,1024]{2,1,0:T(8,128)(2,1)S(1)}, u32[]{:S(2)}, u32[]{:S(2)}) collective-permute-start(bf16[2,128,1024]{2,1,0:T(8,128)(2,1)S(1)} %broadcast_select_fusion.2), channel_id=1, source_target_pairs={{0,1},{2,3},{4,5},{6,7},{8,9},{10,11},{12,13},{14,15},{16,17},{18,... | collective-permute-start | bytes 1572872 | tf_op jit(solution)/shard_map/ppermute | solution.py:40
  37.7 0.6 compare_convert_fusion.diag_ref
  38.4 0.6 select_clamp_fusion.slot_ref
  39.0 1.9 %collective-permute-done.3 = bf16[2,128,1024]{2,1,0:T(8,128)(2,1)S(1)} collective-permute-done((bf16[2,128,1024]{2,1,0:T(8,128)(2,1)S(1)}, bf16[2,128,1024]{2,1,0:T(8,128)(2,1)S(1)}, u32[]{:S(2)}, u32[]{:S(2)}) %collective-permute-start.3) | collective-permute-done | bytes 524320 | tf_op jit(solution)/shard_map/ppermute | solution.py:40
  40.8 0.2 select_dynamic-update-slice_fusion
  41.0 36.5 %collective-permute-done.4 = bf16[2,128,1024]{2,1,0:T(8,128)(2,1)} collective-permute-done((bf16[2,128,1024]{2,1,0:T(8,128)(2,1)}, bf16[2,128,1024]{2,1,0:T(8,128)(2,1)}, u32[]{:S(2)}, u32[]{:S(2)}) %collective-permute-start.4) | collective-permute-done | bytes 524320 | tf_op jit(solution)/shard_map/ppermute | solution.py:23
  77.6 1.1 constant_dynamic-update-slice_fusion.4
  78.6 0.0 collective-permute-done.5
  78.7 1.3 %constant_dynamic-update-slice_fusion.3 = bf16[2,1280,1024]{2,1,0:T(8,128)(2,1)S(1)} fusion(bf16[2,1280,1024]{2,1,0:T(8,128)(2,1)S(1)} %constant_dynamic-update-slice_fusion.4, bf16[2,256,1024]{2,1,0:T(8,128)(2,1)} %collective-permute-done.5), kind=kLoop, calls=%fused_computation.14 | loop fusion | bytes 2097152
  79.9 0.0 collective-permute-done.6
  80.0 1.3 %constant_dynamic-update-slice_fusion.2 = bf16[2,1280,1024]{2,1,0:T(8,128)(2,1)S(1)} fusion(bf16[2,1280,1024]{2,1,0:T(8,128)(2,1)S(1)} %constant_dynamic-update-slice_fusion.3, bf16[2,256,1024]{2,1,0:T(8,128)(2,1)} %collective-permute-done.6), kind=kLoop, calls=%fused_computation.13 | loop fusion | bytes 2097152
  81.3 0.0 collective-permute-done.7
  81.3 1.3 %constant_dynamic-update-slice_fusion.1 = bf16[2,1280,1024]{2,1,0:T(8,128)(2,1)S(1)} fusion(bf16[2,1280,1024]{2,1,0:T(8,128)(2,1)S(1)} %constant_dynamic-update-slice_fusion.2, bf16[2,256,1024]{2,1,0:T(8,128)(2,1)} %collective-permute-done.7), kind=kLoop, calls=%fused_computation.12 | loop fusion | bytes 2097152
  82.6 0.1 constant_dynamic-update-slice_fusion
  82.7 2.3 %copy-done.3 = bf16[2,1280,1024]{2,1,0:T(8,128)(2,1)} copy-done((bf16[2,1280,1024]{2,1,0:T(8,128)(2,1)}, bf16[2,1280,1024]{2,1,0:T(8,128)(2,1)S(1)}, u32[]{:S(2)}) %copy-start.3) | copy-done | bytes 5242904
  84.9 39.3 %shard_map.46 = bf16[256,4096]{1,0:T(8,128)(2,1)} custom-call(s32[2,11]{1,0:T(2,128)} %select_clamp_fusion.slot_ref, s32[2,11]{1,0:T(2,128)} %compare_convert_fusion.diag_ref, bf16[256,4096]{1,0:T(8,128)(2,1)} %q_ref.1, bf16[2,10,128,1024]{3,2,1,0:T(8,128)(2,1)} %bitcast.9, bf16[2,10,128,1024]{3,2,1,0:T(8,128)(2,1)} %bitcast.10), custom_call_target="tpu_custom_call" | custom-call | flops 5905580032 | bytes 9437184 | tf_op jit(solution)/shard_map/pallas_call | solution.py:98
  (10 shorter events, 0.0 us)
Async XLA Ops:
  0.0 36.2 %copy-start = (s32[32,11]{0,1:T(8,128)S(1)}, s32[32,11]{0,1:T(8,128)}, u32[]{:S(2)}) copy-start(s32[32,11]{0,1:T(8,128)} %param.7) | copy-start | bytes 4228
  0.0 5.2 %copy-start.1 = (bf16[256,1024]{1,0:T(8,128)(2,1)S(1)}, bf16[256,1024]{1,0:T(8,128)(2,1)}, u32[]{:S(2)}) copy-start(bf16[256,1024]{1,0:T(8,128)(2,1)} %param.5) | copy-start | bytes 1572868
  0.0 5.2 %copy-start.2 = (bf16[256,1024]{1,0:T(8,128)(2,1)S(1)}, bf16[256,1024]{1,0:T(8,128)(2,1)}, u32[]{:S(2)}) copy-start(bf16[256,1024]{1,0:T(8,128)(2,1)} %param.6) | copy-start | bytes 1572868
  2.2 0.7 collective-permute-start
  3.0 0.7 collective-permute-start.1
  3.7 32.6 %collective-permute-start.2 = (bf16[2,128,1024]{2,1,0:T(8,128)(2,1)S(1)}, bf16[2,128,1024]{2,1,0:T(8,128)(2,1)}, u32[]{:S(2)}, u32[]{:S(2)}) collective-permute-start(bf16[2,128,1024]{2,1,0:T(8,128)(2,1)S(1)} %broadcast_select_fusion.1), channel_id=1, source_target_pairs={{0,2},{4,6},{8,10},{12,14},{16,18},{20,22},{24,26},{28,30}} | collective-permute-start | bytes 1572872 | tf_op jit(solution)/shard_map/ppermute | solution.py:40
  5.3 73.3 %collective-permute-start.5 = (bf16[2,256,1024]{2,1,0:T(8,128)(2,1)S(1)}, bf16[2,256,1024]{2,1,0:T(8,128)(2,1)}, u32[]{:S(2)}, u32[]{:S(2)}) collective-permute-start(bf16[2,256,1024]{2,1,0:T(8,128)(2,1)S(1)} %pad_maximum_fusion), channel_id=1, source_target_pairs={{0,3},{1,4},{2,5},{3,6},{4,7},{5,8},{6,9},{7,10},{8,11},{9,12},{10... | collective-permute-start | bytes 3145736 | tf_op jit(solution)/shard_map/ppermute | solution.py:23
  8.9 71.0 %collective-permute-start.6 = (bf16[2,256,1024]{2,1,0:T(8,128)(2,1)S(1)}, bf16[2,256,1024]{2,1,0:T(8,128)(2,1)}, u32[]{:S(2)}, u32[]{:S(2)}) collective-permute-start(bf16[2,256,1024]{2,1,0:T(8,128)(2,1)S(1)} %pad_maximum_fusion), channel_id=1, source_target_pairs={{0,2},{1,3},{2,4},{3,5},{4,6},{5,7},{6,8},{7,9},{8,10},{9,11},{10,... | collective-permute-start | bytes 3145736 | tf_op jit(solution)/shard_map/ppermute | solution.py:23
  32.3 49.0 %collective-permute-start.7 = (bf16[2,256,1024]{2,1,0:T(8,128)(2,1)S(1)}, bf16[2,256,1024]{2,1,0:T(8,128)(2,1)}, u32[]{:S(2)}, u32[]{:S(2)}) collective-permute-start(bf16[2,256,1024]{2,1,0:T(8,128)(2,1)S(1)} %pad_maximum_fusion), channel_id=1, source_target_pairs={{0,1},{1,2},{2,3},{3,4},{4,5},{5,6},{6,7},{7,8},{8,9},{9,10},{10,1... | collective-permute-start | bytes 3145736 | tf_op jit(solution)/shard_map/ppermute | solution.py:23
  34.2 43.3 %collective-permute-start.4 = (bf16[2,128,1024]{2,1,0:T(8,128)(2,1)}, bf16[2,128,1024]{2,1,0:T(8,128)(2,1)}, u32[]{:S(2)}, u32[]{:S(2)}) collective-permute-start(bf16[2,128,1024]{2,1,0:T(8,128)(2,1)} %get-tuple-element.5), channel_id=1, source_target_pairs={{0,4},{1,5},{2,6},{3,7},{4,8},{5,9},{6,10},{7,11},{8,12},{9,13},{1... | collective-permute-start | bytes 1572872 | tf_op jit(solution)/shard_map/ppermute | solution.py:23
  36.4 4.4 %collective-permute-start.3 = (bf16[2,128,1024]{2,1,0:T(8,128)(2,1)S(1)}, bf16[2,128,1024]{2,1,0:T(8,128)(2,1)S(1)}, u32[]{:S(2)}, u32[]{:S(2)}) collective-permute-start(bf16[2,128,1024]{2,1,0:T(8,128)(2,1)S(1)} %broadcast_select_fusion.2), channel_id=1, source_target_pairs={{0,1},{2,3},{4,5},{6,7},{8,9},{10,11},{12,13},{14,15},{16,17},{18,... | collective-permute-start | bytes 1572872 | tf_op jit(solution)/shard_map/ppermute | solution.py:40
  82.6 2.3 %copy-start.3 = (bf16[2,1280,1024]{2,1,0:T(8,128)(2,1)}, bf16[2,1280,1024]{2,1,0:T(8,128)(2,1)S(1)}, u32[]{:S(2)}) copy-start(bf16[2,1280,1024]{2,1,0:T(8,128)(2,1)S(1)} %constant_dynamic-update-slice_fusion) | copy-start | bytes 15728644

commit v2 on v1

--- a/solution.py
+++ b/solution.py
@@ -17,10 +17,28 @@
 GROUP = H // KVH
 
 
-def passed_along(shard, axis, by):
+def shifted(shard, axis, by, sends):
     size = lax.axis_size(axis)
-    pairs = [(i, i + by) for i in range(size) if 0 <= i + by < size]
+    pairs = [(i, i + by) for i in range(size) if sends(i) and 0 <= i + by < size]
     return lax.ppermute(shard, axis, pairs)
+
+
+def window_blocks(kv, axis):
+    index = lax.axis_index(axis)
+    y_low = (index // 2) % 2 == 0
+    core0 = index % 2 == 0
+    back4 = shifted(kv, axis, 4, lambda i: True)
+    up_y = shifted(kv, axis, 2, lambda i: (i // 2) % 2 == 0)
+    next_core = shifted(kv, axis, 1, lambda i: i % 2 == 0)
+    down_y = shifted(back4, axis, -2, lambda i: (i // 2) % 2 == 1)
+    back2 = jnp.where(y_low, down_y, up_y)
+    partner_back4 = shifted(back4, axis, -1, lambda i: i % 2 == 1)
+    size = lax.axis_size(axis)
+    swap_pairs = [(i, i ^ 1) for i in range(size)]
+    partner_back2 = lax.ppermute(back2, axis, swap_pairs)
+    back3 = jnp.where(core0, partner_back4, partner_back2)
+    back1 = jnp.where(core0, partner_back2, next_core)
+    return [back4, back3, back2, back1]
 
 
 def tree_broadcast(block, axis, source, size):
@@ -116,27 +134,22 @@
     ctx_count = lax.axis_size("ctx")
     own_index = lax.axis_index("ctx")
     kv = jnp.stack([key_rows, value_rows])
-    reach_rows = (WIN - 1) * BLK
-    hops_back = (reach_rows + tok_rows - 1) // tok_rows
-    early = []
-    for offset in range(hops_back, 0, -1):
-        need_rows = min(tok_rows, reach_rows - (offset - 1) * tok_rows)
-        early.append(passed_along(kv[:, tok_rows - need_rows:], "ctx", offset))
+    assert blocks_here == 2 and ctx_count % 4 == 0
+    early = window_blocks(kv, "ctx")
     columns = blocks_here * ctx_count // STRIDE
     spread = STRIDE // blocks_here
     column_blocks = [
         tree_broadcast(kv[:, :BLK], "ctx", column * spread, ctx_count)
         for column in range(columns)
     ]
-    buffer_blocks = columns + WIN - 1 + blocks_here
+    buffer_blocks = columns + 4 * blocks_here + blocks_here
     kv_buffer = jnp.concatenate(column_blocks + early + [kv], axis=1).reshape(
         2, buffer_blocks, BLK, kv.shape[2]
     )
-    first_block = own_index * blocks_here - (WIN - 1)
+    first_block = own_index * blocks_here - 4 * blocks_here
     rows_pattern = lax.dynamic_slice_in_dim(pattern, own_index * blocks_here, blocks_here, 0)
-    in_window = jnp.arange(LIST, dtype=jnp.int32) < WIN
     slots = jnp.where(
-        in_window[None, :],
+        rows_pattern >= first_block,
         columns + rows_pattern - first_block,
         rows_pattern // STRIDE,
     )

time: 125 us -> 105 us (0.84)
  the two profiles are of different devices: /device:TPU:15 before, /device:TPU:19 now
where the time goes in v2:
time: 105 us; the launch traced here: 104 us
  Pallas kernels  39.3 us (37%)
  starting transfers between devices  35.5 us (34%)
  waiting for transfers between devices  18.1 us (17%)
  other arithmetic  8.49 us (8%)
  local copies, waits for them, and re-layouts  2.8 us (3%)
    pallas_call x1, Pallas kernels, attend(): pl.pallas_call(attend_kernel, out_shape=jax.ShapeDtypeStruct(queries.shap...  39.3 us
    ppermute x5, starting transfers between devices, shifted(): return lax.ppermute(shard, axis, pairs)  27.1 us
    ppermute x5, waiting for transfers between devices, shifted(): return lax.ppermute(shard, axis, pairs)  16.8 us
    ppermute x4, starting transfers between devices, tree_broadcast(): got = lax.ppermute(held, axis, pairs)  4.94 us
    ppermute x1, starting transfers between devices, window_blocks(): partner_back2 = lax.ppermute(back2, axis, swap_pairs)  3.46 us
    unnamed x11, local copies, waits for them, and re-layouts  2.72 us
    another operation x2, other arithmetic, per_device(): kv = jnp.stack([key_rows, value_rows])  2.38 us
    unnamed x3, other arithmetic  2.24 us
  transfers between devices with their start and end apart: 10, of which 2 were waited for; matrix products, arithmetic and copies ran while one was open for 6% of the time, Pallas kernels for 0%

profile of v2, /device:TPU:19, one launch (start us, length us, event | category | flops | bytes accessed | tf_op | source)
XLA Modules:
  0.0 104.4 jit_solution(1333554428562364972)
XLA Ops:
  0.0 1.3 %pad_maximum_fusion = bf16[2,256,1024]{2,1,0:T(8,128)(2,1)S(1)} fusion(bf16[1,256,1024]{2,1,0:T(8,128)(2,1)} %bitcast.7, bf16[1,256,1024]{2,1,0:T(8,128)(2,1)} %bitcast.3), kind=kLoop, calls=%fused_computation.1 | loop fusion | flops 524288 | bytes 2097152 | tf_op jit(solution)/shard_map/stack | solution.py:136
  1.3 3.2 %collective-permute-start.4 = (bf16[2,256,1024]{2,1,0:T(8,128)(2,1)S(1)}, bf16[2,256,1024]{2,1,0:T(8,128)(2,1)S(1)}, u32[]{:S(2)}, u32[]{:S(2)}) collective-permute-start(bf16[2,256,1024]{2,1,0:T(8,128)(2,1)S(1)} %pad_maximum_fusion), channel_id=1, source_target_pairs={{0,4},{1,5},{2,6},{3,7},{4,8},{5,9},{6,10},{7,11},{8,12},{9,13},{1... | collective-permute-start | bytes 3145736 | tf_op jit(solution)/shard_map/ppermute | solution.py:23
  4.5 1.1 %fusion = bf16[2,128,1024]{2,1,0:T(8,128)(2,1)S(1)} fusion(bf16[1,256,1024]{2,1,0:T(8,128)(2,1)} %bitcast.4, bf16[1,256,1024]{2,1,0:T(8,128)(2,1)} %bitcast.8), kind=kLoop, calls=%fused_computation.6 | loop fusion | flops 262144 | bytes 1572864 | tf_op jit(solution)/shard_map/stack | solution.py:136
  5.6 0.7 collective-permute-start
  6.3 4.2 %collective-permute-start.7 = (bf16[2,256,1024]{2,1,0:T(8,128)(2,1)S(1)}, bf16[2,256,1024]{2,1,0:T(8,128)(2,1)}, u32[]{:S(2)}, u32[]{:S(2)}) collective-permute-start(bf16[2,256,1024]{2,1,0:T(8,128)(2,1)S(1)} %pad_maximum_fusion), channel_id=1, source_target_pairs={{0,2},{1,3},{4,6},{5,7},{8,10},{9,11},{12,14},{13,15},{16,18},{17,... | collective-permute-start | bytes 3145736 | tf_op jit(solution)/shard_map/ppermute | solution.py:23
  10.5 16.8 %collective-permute-done.4 = bf16[2,256,1024]{2,1,0:T(8,128)(2,1)S(1)} collective-permute-done((bf16[2,256,1024]{2,1,0:T(8,128)(2,1)S(1)}, bf16[2,256,1024]{2,1,0:T(8,128)(2,1)S(1)}, u32[]{:S(2)}, u32[]{:S(2)}) %collective-permute-start.4) | collective-permute-done | bytes 1048608 | tf_op jit(solution)/shard_map/ppermute | solution.py:23
  27.2 1.3 %collective-permute-start.6 = (bf16[2,256,1024]{2,1,0:T(8,128)(2,1)S(1)}, bf16[2,256,1024]{2,1,0:T(8,128)(2,1)}, u32[]{:S(2)}, u32[]{:S(2)}) collective-permute-start(bf16[2,256,1024]{2,1,0:T(8,128)(2,1)S(1)} %collective-permute-done.4), channel_id=1, source_target_pairs={{2,0},{3,1},{6,4},{7,5},{10,8},{11,9},{14,12},{15,13},{18,16},{19,... | collective-permute-start | bytes 3145736 | tf_op jit(solution)/shard_map/ppermute | solution.py:23
  28.5 1.1 %broadcast_select_fusion.1 = bf16[2,128,1024]{2,1,0:T(8,128)(2,1)S(1)} fusion(bf16[2,128,1024]{2,1,0:T(8,128)(2,1)S(1)} %collective-permute-done, pred[]{:T(512)S(6)} %and.53, bf16[1,256,1024]{2,1,0:T(8,128)(2,1)} %bitcast.9, bf16[1,256,1024]{2,1,0:T(8,128)(2,1)} %bitcast.5), kind=kLoop, calls=%fused_computation.8 | loop fusion | flops 524288 | bytes 2097153 | tf_op jit(solution)/shard_map/jit(_where)/select_n | solution.py:61
  29.6 1.5 %collective-permute-start.1 = (bf16[2,128,1024]{2,1,0:T(8,128)(2,1)S(1)}, bf16[2,128,1024]{2,1,0:T(8,128)(2,1)}, u32[]{:S(2)}, u32[]{:S(2)}) collective-permute-start(bf16[2,128,1024]{2,1,0:T(8,128)(2,1)S(1)} %broadcast_select_fusion.1), channel_id=1, source_target_pairs={{0,4},{8,12},{16,20},{24,28}} | collective-permute-start | bytes 1572872 | tf_op jit(solution)/shard_map/ppermute | solution.py:58
  31.1 0.0 collective-permute-done.1
  31.1 0.1 broadcast_select_fusion.2
  31.2 1.5 %collective-permute-start.2 = (bf16[2,128,1024]{2,1,0:T(8,128)(2,1)S(1)}, bf16[2,128,1024]{2,1,0:T(8,128)(2,1)}, u32[]{:S(2)}, u32[]{:S(2)}) collective-permute-start(bf16[2,128,1024]{2,1,0:T(8,128)(2,1)S(1)} %broadcast_select_fusion.2), channel_id=1, source_target_pairs={{0,2},{4,6},{8,10},{12,14},{16,18},{20,22},{24,26},{28,30}} | collective-permute-start | bytes 1572872 | tf_op jit(solution)/shard_map/ppermute | solution.py:58
  32.7 1.3 %collective-permute-start.9 = (bf16[2,256,1024]{2,1,0:T(8,128)(2,1)S(1)}, bf16[2,256,1024]{2,1,0:T(8,128)(2,1)}, u32[]{:S(2)}, u32[]{:S(2)}) collective-permute-start(bf16[2,256,1024]{2,1,0:T(8,128)(2,1)S(1)} %pad_maximum_fusion), channel_id=1, source_target_pairs={{0,1},{2,3},{4,5},{6,7},{8,9},{10,11},{12,13},{14,15},{16,17},{18,... | collective-permute-start | bytes 3145736 | tf_op jit(solution)/shard_map/ppermute | solution.py:23
  34.0 0.1 constant_dynamic-slice_fusion
  34.1 0.1 copy.6
  34.2 17.2 %collective-permute-start.5 = (bf16[2,256,1024]{2,1,0:T(8,128)(2,1)S(1)}, bf16[2,256,1024]{2,1,0:T(8,128)(2,1)S(1)}, u32[]{:S(2)}, u32[]{:S(2)}) collective-permute-start(bf16[2,256,1024]{2,1,0:T(8,128)(2,1)S(1)} %collective-permute-done.4), channel_id=1, source_target_pairs={{1,0},{3,2},{5,4},{7,6},{9,8},{11,10},{13,12},{15,14},{17,16},{19,... | collective-permute-start | bytes 3145736 | tf_op jit(solution)/shard_map/ppermute | solution.py:23
  51.4 0.0 collective-permute-done.7
  51.4 1.3 %broadcast_select_fusion = bf16[2,256,1024]{2,1,0:T(8,128)(2,1)S(1)} fusion(bf16[2,256,1024]{2,1,0:T(8,128)(2,1)} %collective-permute-done.6, bf16[2,256,1024]{2,1,0:T(8,128)(2,1)} %collective-permute-done.7, pred[]{:T(512)S(6)} %eq.40), kind=kLoop, calls=%fused_computation.5 | loop fusion | flops 524288 | bytes 3145729 | tf_op jit(solution)/shard_map/jit(_where)/select_n | solution.py:34
  52.7 3.5 %collective-permute-start.8 = (bf16[2,256,1024]{2,1,0:T(8,128)(2,1)S(1)}, bf16[2,256,1024]{2,1,0:T(8,128)(2,1)S(1)}, u32[]{:S(2)}, u32[]{:S(2)}) collective-permute-start(bf16[2,256,1024]{2,1,0:T(8,128)(2,1)S(1)} %broadcast_select_fusion), channel_id=1, source_target_pairs={{0,1},{1,0},{2,3},{3,2},{4,5},{5,4},{6,7},{7,6},{8,9},{9,8},{10,11... | collective-permute-start | bytes 3145736 | tf_op jit(solution)/shard_map/ppermute | solution.py:38
  56.2 0.1 broadcast_select_fusion.3
  56.3 1.3 %collective-permute-start.3 = (bf16[2,128,1024]{2,1,0:T(8,128)(2,1)S(1)}, bf16[2,128,1024]{2,1,0:T(8,128)(2,1)S(1)}, u32[]{:S(2)}, u32[]{:S(2)}) collective-permute-start(bf16[2,128,1024]{2,1,0:T(8,128)(2,1)S(1)} %broadcast_select_fusion.3), channel_id=1, source_target_pairs={{0,1},{2,3},{4,5},{6,7},{8,9},{10,11},{12,13},{14,15},{16,17},{18,... | collective-permute-start | bytes 1572872 | tf_op jit(solution)/shard_map/ppermute | solution.py:58
  57.6 0.6 compare_convert_fusion.diag_ref
  58.2 0.6 fusion.1.slot_ref
  58.8 1.3 %collective-permute-done.3 = bf16[2,128,1024]{2,1,0:T(8,128)(2,1)S(1)} collective-permute-done((bf16[2,128,1024]{2,1,0:T(8,128)(2,1)S(1)}, bf16[2,128,1024]{2,1,0:T(8,128)(2,1)S(1)}, u32[]{:S(2)}, u32[]{:S(2)}) %collective-permute-start.3) | collective-permute-done | bytes 524320 | tf_op jit(solution)/shard_map/ppermute | solution.py:58
  60.1 0.2 select_dynamic-update-slice_fusion.2
  60.3 0.1 constant_dynamic-update-slice_fusion.2
  60.4 0.4 select_dynamic-update-slice_fusion.1
  60.8 0.1 constant_dynamic-update-slice_fusion.1
  60.9 1.6 %select_dynamic-update-slice_fusion = bf16[2,1408,1024]{2,1,0:T(8,128)(2,1)S(1)} fusion(bf16[2,1408,1024]{2,1,0:T(8,128)(2,1)S(1)} %constant_dynamic-update-slice_fusion.1, bf16[2,256,1024]{2,1,0:T(8,128)(2,1)S(1)} %collective-permute-done.8, bf16[2,256,1024]{2,1,0:T(8,128)(2,1)} %collective-permute-done.9, pred[]{:T(512)S(6)} %eq.39), kind=kLoop, calls=%fused_computation.3 | loop fusion | flops 524288 | bytes 3145729
  62.5 0.1 constant_dynamic-update-slice_fusion
  62.6 2.5 %copy-done.3 = bf16[2,1408,1024]{2,1,0:T(8,128)(2,1)} copy-done((bf16[2,1408,1024]{2,1,0:T(8,128)(2,1)}, bf16[2,1408,1024]{2,1,0:T(8,128)(2,1)S(1)}, u32[]{:S(2)}) %copy-start.3) | copy-done | bytes 5767192
  65.1 39.3 %shard_map.46 = bf16[256,4096]{1,0:T(8,128)(2,1)} custom-call(s32[2,11]{1,0:T(2,128)} %fusion.1.slot_ref, s32[2,11]{1,0:T(2,128)} %compare_convert_fusion.diag_ref, bf16[256,4096]{1,0:T(8,128)(2,1)} %q_ref.1, bf16[2,11,128,1024]{3,2,1,0:T(8,128)(2,1)} %bitcast.11, bf16[2,11,128,1024]{3,2,1,0:T(8,128)(2,1)} %bitcast.12), custom_call_target="tpu_custom_call" | custom-call | flops 5905580032 | bytes 9961472 | tf_op jit(solution)/shard_map/pallas_call | solution.py:116
  (14 shorter events, 0.0 us)
Async XLA Ops:
  0.0 34.0 %copy-start = (s32[32,11]{0,1:T(8,128)S(1)}, s32[32,11]{0,1:T(8,128)}, u32[]{:S(2)}) copy-start(s32[32,11]{0,1:T(8,128)} %param.7) | copy-start | bytes 4228
  1.3 25.9 %collective-permute-start.4 = (bf16[2,256,1024]{2,1,0:T(8,128)(2,1)S(1)}, bf16[2,256,1024]{2,1,0:T(8,128)(2,1)S(1)}, u32[]{:S(2)}, u32[]{:S(2)}) collective-permute-start(bf16[2,256,1024]{2,1,0:T(8,128)(2,1)S(1)} %pad_maximum_fusion), channel_id=1, source_target_pairs={{0,4},{1,5},{2,6},{3,7},{4,8},{5,9},{6,10},{7,11},{8,12},{9,13},{1... | collective-permute-start | bytes 3145736 | tf_op jit(solution)/shard_map/ppermute | solution.py:23
  5.6 22.9 %collective-permute-start = (bf16[2,128,1024]{2,1,0:T(8,128)(2,1)S(1)}, bf16[2,128,1024]{2,1,0:T(8,128)(2,1)S(1)}, u32[]{:S(2)}, u32[]{:S(2)}) collective-permute-start(bf16[2,128,1024]{2,1,0:T(8,128)(2,1)S(1)} %fusion), channel_id=1, source_target_pairs={{0,8},{16,24}} | collective-permute-start | bytes 1572872 | tf_op jit(solution)/shard_map/ppermute | solution.py:58
  6.3 45.1 %collective-permute-start.7 = (bf16[2,256,1024]{2,1,0:T(8,128)(2,1)S(1)}, bf16[2,256,1024]{2,1,0:T(8,128)(2,1)}, u32[]{:S(2)}, u32[]{:S(2)}) collective-permute-start(bf16[2,256,1024]{2,1,0:T(8,128)(2,1)S(1)} %pad_maximum_fusion), channel_id=1, source_target_pairs={{0,2},{1,3},{4,6},{5,7},{8,10},{9,11},{12,14},{13,15},{16,18},{17,... | collective-permute-start | bytes 3145736 | tf_op jit(solution)/shard_map/ppermute | solution.py:23
  27.2 24.2 %collective-permute-start.6 = (bf16[2,256,1024]{2,1,0:T(8,128)(2,1)S(1)}, bf16[2,256,1024]{2,1,0:T(8,128)(2,1)}, u32[]{:S(2)}, u32[]{:S(2)}) collective-permute-start(bf16[2,256,1024]{2,1,0:T(8,128)(2,1)S(1)} %collective-permute-done.4), channel_id=1, source_target_pairs={{2,0},{3,1},{6,4},{7,5},{10,8},{11,9},{14,12},{15,13},{18,16},{19,... | collective-permute-start | bytes 3145736 | tf_op jit(solution)/shard_map/ppermute | solution.py:23
  29.6 1.5 %collective-permute-start.1 = (bf16[2,128,1024]{2,1,0:T(8,128)(2,1)S(1)}, bf16[2,128,1024]{2,1,0:T(8,128)(2,1)}, u32[]{:S(2)}, u32[]{:S(2)}) collective-permute-start(bf16[2,128,1024]{2,1,0:T(8,128)(2,1)S(1)} %broadcast_select_fusion.1), channel_id=1, source_target_pairs={{0,4},{8,12},{16,20},{24,28}} | collective-permute-start | bytes 1572872 | tf_op jit(solution)/shard_map/ppermute | solution.py:58
  31.2 25.0 %collective-permute-start.2 = (bf16[2,128,1024]{2,1,0:T(8,128)(2,1)S(1)}, bf16[2,128,1024]{2,1,0:T(8,128)(2,1)}, u32[]{:S(2)}, u32[]{:S(2)}) collective-permute-start(bf16[2,128,1024]{2,1,0:T(8,128)(2,1)S(1)} %broadcast_select_fusion.2), channel_id=1, source_target_pairs={{0,2},{4,6},{8,10},{12,14},{16,18},{20,22},{24,26},{28,30}} | collective-permute-start | bytes 1572872 | tf_op jit(solution)/shard_map/ppermute | solution.py:58
  32.7 28.2 %collective-permute-start.9 = (bf16[2,256,1024]{2,1,0:T(8,128)(2,1)S(1)}, bf16[2,256,1024]{2,1,0:T(8,128)(2,1)}, u32[]{:S(2)}, u32[]{:S(2)}) collective-permute-start(bf16[2,256,1024]{2,1,0:T(8,128)(2,1)S(1)} %pad_maximum_fusion), channel_id=1, source_target_pairs={{0,1},{2,3},{4,5},{6,7},{8,9},{10,11},{12,13},{14,15},{16,17},{18,... | collective-permute-start | bytes 3145736 | tf_op jit(solution)/shard_map/ppermute | solution.py:23
  34.2 26.2 %collective-permute-start.5 = (bf16[2,256,1024]{2,1,0:T(8,128)(2,1)S(1)}, bf16[2,256,1024]{2,1,0:T(8,128)(2,1)S(1)}, u32[]{:S(2)}, u32[]{:S(2)}) collective-permute-start(bf16[2,256,1024]{2,1,0:T(8,128)(2,1)S(1)} %collective-permute-done.4), channel_id=1, source_target_pairs={{1,0},{3,2},{5,4},{7,6},{9,8},{11,10},{13,12},{15,14},{17,16},{19,... | collective-permute-start | bytes 3145736 | tf_op jit(solution)/shard_map/ppermute | solution.py:23
  52.7 7.6 %collective-permute-start.8 = (bf16[2,256,1024]{2,1,0:T(8,128)(2,1)S(1)}, bf16[2,256,1024]{2,1,0:T(8,128)(2,1)S(1)}, u32[]{:S(2)}, u32[]{:S(2)}) collective-permute-start(bf16[2,256,1024]{2,1,0:T(8,128)(2,1)S(1)} %broadcast_select_fusion), channel_id=1, source_target_pairs={{0,1},{1,0},{2,3},{3,2},{4,5},{5,4},{6,7},{7,6},{8,9},{9,8},{10,11... | collective-permute-start | bytes 3145736 | tf_op jit(solution)/shard_map/ppermute | solution.py:38
  56.3 3.8 %collective-permute-start.3 = (bf16[2,128,1024]{2,1,0:T(8,128)(2,1)S(1)}, bf16[2,128,1024]{2,1,0:T(8,128)(2,1)S(1)}, u32[]{:S(2)}, u32[]{:S(2)}) collective-permute-start(bf16[2,128,1024]{2,1,0:T(8,128)(2,1)S(1)} %broadcast_select_fusion.3), channel_id=1, source_target_pairs={{0,1},{2,3},{4,5},{6,7},{8,9},{10,11},{12,13},{14,15},{16,17},{18,... | collective-permute-start | bytes 1572872 | tf_op jit(solution)/shard_map/ppermute | solution.py:58
  58.8 3.7 %copy-start.1 = (bf16[256,1024]{1,0:T(8,128)(2,1)S(1)}, bf16[256,1024]{1,0:T(8,128)(2,1)}, u32[]{:S(2)}) copy-start(bf16[256,1024]{1,0:T(8,128)(2,1)} %param.5) | copy-start | bytes 1572868
  58.8 3.7 %copy-start.2 = (bf16[256,1024]{1,0:T(8,128)(2,1)S(1)}, bf16[256,1024]{1,0:T(8,128)(2,1)}, u32[]{:S(2)}) copy-start(bf16[256,1024]{1,0:T(8,128)(2,1)} %param.6) | copy-start | bytes 1572868
  62.6 2.5 %copy-start.3 = (bf16[2,1408,1024]{2,1,0:T(8,128)(2,1)}, bf16[2,1408,1024]{2,1,0:T(8,128)(2,1)S(1)}, u32[]{:S(2)}) copy-start(bf16[2,1408,1024]{2,1,0:T(8,128)(2,1)S(1)} %constant_dynamic-update-slice_fusion) | copy-start | bytes 17301508

commit v3 on v2

--- a/solution.py
+++ b/solution.py
@@ -25,20 +25,27 @@
 
 def window_blocks(kv, axis):
     index = lax.axis_index(axis)
+    size = lax.axis_size(axis)
     y_low = (index // 2) % 2 == 0
     core0 = index % 2 == 0
-    back4 = shifted(kv, axis, 4, lambda i: True)
+    swap_pairs = [(i, i ^ 1) for i in range(size)]
     up_y = shifted(kv, axis, 2, lambda i: (i // 2) % 2 == 0)
-    next_core = shifted(kv, axis, 1, lambda i: i % 2 == 0)
-    down_y = shifted(back4, axis, -2, lambda i: (i // 2) % 2 == 1)
-    back2 = jnp.where(y_low, down_y, up_y)
-    partner_back4 = shifted(back4, axis, -1, lambda i: i % 2 == 1)
-    size = lax.axis_size(axis)
-    swap_pairs = [(i, i ^ 1) for i in range(size)]
-    partner_back2 = lax.ppermute(back2, axis, swap_pairs)
-    back3 = jnp.where(core0, partner_back4, partner_back2)
-    back1 = jnp.where(core0, partner_back2, next_core)
-    return [back4, back3, back2, back1]
+    later = kv[:, BLK:]
+    pieces = {"back4": [], "back3": [], "back2": [], "back1": []}
+    for half in range(2):
+        own = kv[:, half * BLK:(half + 1) * BLK]
+        if half == 1:
+            own, pieces["back4"][0] = lax.optimization_barrier((later, pieces["back4"][0]))
+        back4 = shifted(own, axis, 4, lambda i: True)
+        down_y = shifted(back4, axis, -2, lambda i: (i // 2) % 2 == 1)
+        back2 = jnp.where(y_low, down_y, up_y[:, half * BLK:(half + 1) * BLK])
+        sent = jnp.stack([jnp.where(core0, own, back4), back2])
+        got = lax.ppermute(sent, axis, swap_pairs)
+        pieces["back4"].append(back4)
+        pieces["back3"].append(jnp.where(core0, got[0], got[1]))
+        pieces["back2"].append(back2)
+        pieces["back1"].append(jnp.where(core0, got[1], got[0]))
+    return pieces["back4"] + pieces["back3"] + pieces["back2"] + pieces["back1"]
 
 
 def tree_broadcast(block, axis, source, size):
@@ -77,8 +84,12 @@
         sc = lax.dot_general(
             stacked, key, (((1,), (1,)), ((), ())), preferred_element_type=jnp.float32
         ) * scale
-        masked = jnp.logical_and(future, diag_ref[local, s] != 0)
-        sc = jnp.where(masked, -jnp.inf, sc)
+        sc = lax.cond(
+            diag_ref[local, s] != 0,
+            lambda x: jnp.where(future, -jnp.inf, x),
+            lambda x: x,
+            sc,
+        )
         score_sc[s] = sc
         run_max = jnp.maximum(run_max, sc)
     row_max = jnp.max(run_max, axis=1, keepdims=True)

time: 105 us -> 151 us (1.44); the launches traced: 104 us -> 148 us
  Pallas kernels: 39.3 us -> 66.4 us
  other arithmetic: 8.49 us -> 26.6 us
  waiting for transfers between devices: 18.1 us -> 30.7 us
  starting transfers between devices: 35.5 us -> 23.5 us
  local copies, waits for them, and re-layouts: 2.8 us -> 1.01 us
    pallas_call x1, Pallas kernels: 39.3 us -> 66.4 us  [attend(): pl.pallas_call(attend_kernel, out_shape=jax.ShapeDtypeStruct(queries.shap...]
    ppermute x5, starting transfers between devices: 27.1 us -> 12.2 us  [shifted(): return lax.ppermute(shard, axis, pairs)]
    ppermute x5, waiting for transfers between devices: 16.8 us -> 30 us  [shifted(): return lax.ppermute(shard, axis, pairs)]
    unnamed x3 -> x7, other arithmetic: 2.24 us -> 12.5 us
    another operation x0 -> x5, other arithmetic: none -> 5.51 us  [window_blocks(): sent = jnp.stack([jnp.where(core0, own, back4), back2])]
    ppermute x1 -> x2, starting transfers between devices: 3.46 us -> 6.46 us  [window_blocks(): got = lax.ppermute(sent, axis, swap_pairs)]
    unnamed x11 -> x10, local copies, waits for them, and re-layouts: 2.72 us -> 0.94 us
    select_n x3 -> x2, other arithmetic: 1.25 us -> 2.8 us  [tree_broadcast(): held = jnp.where(takes, got, held)]
  transfers between devices with their start and end apart: 10 -> 11, of which waited for: 2 -> 4; matrix products, arithmetic and copies ran while one was open for 6% -> 11% of each run, Pallas kernels for 0% -> 0%
where the time goes in v3:
time: 151 us; the launch traced here: 148 us
  Pallas kernels  66.4 us (44%)
  waiting for transfers between devices  30.7 us (20%)
  other arithmetic  26.6 us (18%)
  starting transfers between devices  23.5 us (16%)
    pallas_call x1, Pallas kernels, attend(): pl.pallas_call(attend_kernel, out_shape=jax.ShapeDtypeStruct(queries.shap...  66.4 us
    ppermute x5, waiting for transfers between devices, shifted(): return lax.ppermute(shard, axis, pairs)  30 us
    unnamed x7, other arithmetic  12.5 us
    ppermute x5, starting transfers between devices, shifted(): return lax.ppermute(shard, axis, pairs)  12.2 us
    ppermute x2, starting transfers between devices, window_blocks(): got = lax.ppermute(sent, axis, swap_pairs)  6.46 us
    another operation x5, other arithmetic, window_blocks(): sent = jnp.stack([jnp.where(core0, own, back4), back2])  5.51 us
    ppermute x4, starting transfers between devices, tree_broadcast(): got = lax.ppermute(held, axis, pairs)  4.9 us
    another operation x2, other arithmetic, per_device(): kv = jnp.stack([key_rows, value_rows])  3.54 us
  transfers between devices with their start and end apart: 11, of which 4 were waited for; matrix products, arithmetic and copies ran while one was open for 11% of the time, Pallas kernels for 0%

profile of v3, /device:TPU:19, one launch (start us, length us, event | category | flops | bytes accessed | tf_op | source)
XLA Modules:
  0.0 148.5 jit_solution(3895028374195080296)
XLA Ops:
  0.0 1.3 fusion.1
  1.3 3.2 %collective-permute-start.4 = (bf16[2,128,1024]{2,1,0:T(8,128)(2,1)S(1)}, bf16[2,128,1024]{2,1,0:T(8,128)(2,1)S(1)}, u32[]{:S(2)}, u32[]{:S(2)}) collective-permute-start(bf16[2,128,1024]{2,1,0:T(8,128)(2,1)S(1)} %get-tuple-element.12), channel_id=1, source_target_pairs={{0,4},{1,5},{2,6},{3,7},{4,8},{5,9},{6,10},{7,11},{8,12},{9,13},{1... | collective-permute-start | bytes 1572872 | tf_op jit(solution)/shard_map/ppermute | solution.py:23
  4.5 0.7 collective-permute-start
  5.2 10.7 %collective-permute-done.4 = bf16[2,128,1024]{2,1,0:T(8,128)(2,1)S(1)} collective-permute-done((bf16[2,128,1024]{2,1,0:T(8,128)(2,1)S(1)}, bf16[2,128,1024]{2,1,0:T(8,128)(2,1)S(1)}, u32[]{:S(2)}, u32[]{:S(2)}) %collective-permute-start.4) | collective-permute-done | bytes 524320 | tf_op jit(solution)/shard_map/ppermute | solution.py:23
  16.1 1.5 collective-permute-start.1
  17.5 2.3 %pad_maximum_fusion = bf16[2,256,1024]{2,1,0:T(8,128)(2,1)} fusion(bf16[1,256,1024]{2,1,0:T(8,128)(2,1)} %bitcast.23, bf16[1,256,1024]{2,1,0:T(8,128)(2,1)} %bitcast.20), kind=kLoop, calls=%fused_computation.2 | loop fusion | flops 524288 | bytes 2097152 | tf_op jit(solution)/shard_map/stack | solution.py:147
  19.8 3.2 %collective-permute-start.7 = (bf16[2,256,1024]{2,1,0:T(8,128)(2,1)}, bf16[2,256,1024]{2,1,0:T(8,128)(2,1)S(1)}, u32[]{:S(2)}, u32[]{:S(2)}) collective-permute-start(bf16[2,256,1024]{2,1,0:T(8,128)(2,1)} %pad_maximum_fusion), channel_id=1, source_target_pairs={{0,2},{1,3},{4,6},{5,7},{8,10},{9,11},{12,14},{13,15},{16,18},{17,... | collective-permute-start | bytes 3145736 | tf_op jit(solution)/shard_map/ppermute | solution.py:23
  23.0 3.2 %collective-permute-start.5 = (bf16[2,128,1024]{2,1,0:T(8,128)(2,1)S(1)}, bf16[2,128,1024]{2,1,0:T(8,128)(2,1)}, u32[]{:S(2)}, u32[]{:S(2)}) collective-permute-start(bf16[2,128,1024]{2,1,0:T(8,128)(2,1)S(1)} %get-tuple-element.8), channel_id=1, source_target_pairs={{0,4},{1,5},{2,6},{3,7},{4,8},{5,9},{6,10},{7,11},{8,12},{9,13},{1... | collective-permute-start | bytes 1572872 | tf_op jit(solution)/shard_map/ppermute | solution.py:23
  26.3 0.9 broadcast_select_fusion.1
  27.1 1.4 collective-permute-start.2
  28.6 1.3 collective-permute-start.6
  29.9 8.1 %collective-permute-done.5 = bf16[2,128,1024]{2,1,0:T(8,128)(2,1)} collective-permute-done((bf16[2,128,1024]{2,1,0:T(8,128)(2,1)S(1)}, bf16[2,128,1024]{2,1,0:T(8,128)(2,1)}, u32[]{:S(2)}, u32[]{:S(2)}) %collective-permute-start.5) | collective-permute-done | bytes 524320 | tf_op jit(solution)/shard_map/ppermute | solution.py:23
  38.0 1.3 collective-permute-start.9
  39.3 1.9 %broadcast_select_fusion.2 = bf16[2,128,1024]{2,1,0:T(8,128)(2,1)} fusion(bf16[2,128,1024]{2,1,0:T(8,128)(2,1)} %collective-permute-done.2, bf16[2,128,1024]{2,1,0:T(8,128)(2,1)} %broadcast_select_fusion.1, pred[]{:T(512)S(6)} %and.49), kind=kLoop, calls=%fused_computation.20 | loop fusion | flops 262144 | bytes 1572865 | tf_op jit(solution)/shard_map/jit(_where)/select_n | solution.py:68
  41.2 1.3 collective-permute-start.3
  42.6 11.1 %collective-permute-done.9 = bf16[2,128,1024]{2,1,0:T(8,128)(2,1)} collective-permute-done((bf16[2,128,1024]{2,1,0:T(8,128)(2,1)}, bf16[2,128,1024]{2,1,0:T(8,128)(2,1)}, u32[]{:S(2)}, u32[]{:S(2)}) %collective-permute-start.9) | collective-permute-done | bytes 524320 | tf_op jit(solution)/shard_map/ppermute | solution.py:23
  53.7 1.2 fusion.5
  54.9 1.1 pad_maximum_fusion.1
  56.0 6.5 %collective-permute-start.8 = (bf16[2,2,128,1024]{3,2,1,0:T(8,128)(2,1)}, bf16[2,2,128,1024]{3,2,1,0:T(8,128)(2,1)S(1)}, u32[]{:S(2)}, u32[]{:S(2)}) collective-permute-start(bf16[2,2,128,1024]{3,2,1,0:T(8,128)(2,1)} %pad_maximum_fusion.1), channel_id=1, source_target_pairs={{0,1},{1,0},{2,3},{3,2},{4,5},{5,4},{6,7},{7,6},{8,9},{9,8},{10,11... | collective-permute-start | bytes 3145736 | tf_op jit(solution)/shard_map/ppermute | solution.py:43
  62.5 2.0 %select_dynamic-update-slice_fusion = bf16[2,1408,1024]{2,1,0:T(8,128)(2,1)} fusion(bf16[2,128,1024]{2,1,0:T(8,128)(2,1)} %collective-permute-done.3, bf16[2,128,1024]{2,1,0:T(8,128)(2,1)} %broadcast_select_fusion.2, pred[]{:T(512)S(6)} %and.47), kind=kLoop, calls=%fused_computation.17 | loop fusion | flops 262143 | bytes 1572865
  64.5 0.8 constant_dynamic-update-slice_fusion.2
  65.3 2.1 %select_bitcast_fusion = (bf16[1,2,128,1024]{3,2,1,0:T(8,128)(2,1)S(1)}, bf16[2,1408,1024]{2,1,0:T(8,128)(2,1)}) fusion(bf16[2,128,1024]{2,1,0:T(8,128)(2,1)S(1)} %get-tuple-element.8, bf16[2,128,1024]{2,1,0:T(8,128)(2,1)} %collective-permute-done.5, pred[]{:T(512)S(6)} %eq.39, bf16[2,1408,1024]{2,1,0:T(8,128)(2,1)} %constant_dynamic-update-slice_fusion.2), kind=kLoop, calls=%fused_computation.15 | loop fusion | flops 262144 | bytes 2097153 | tf_op jit(solution)/shard_map/stack | solution.py:42
  67.4 1.1 pad_maximum_fusion.2
  69.8 1.0 bitcast_dynamic-update-slice_fusion.3
  70.8 0.7 collective-permute-done.10
  71.5 2.2 %bitcast_dynamic-update-slice_fusion.2 = bf16[2,1408,1024]{2,1,0:T(8,128)(2,1)} fusion(bf16[2,1408,1024]{2,1,0:T(8,128)(2,1)} %bitcast_dynamic-update-slice_fusion.3, pred[]{:T(512)S(6)} %eq.39, bf16[2,2,128,1024]{3,2,1,0:T(8,128)(2,1)} %collective-permute-done.10), kind=kLoop, calls=%fused_computation.13 | loop fusion | flops 262144 | bytes 1572865
  73.7 2.1 %fusion.2 = bf16[2,1408,1024]{2,1,0:T(8,128)(2,1)} fusion(bf16[2,1408,1024]{2,1,0:T(8,128)(2,1)} %bitcast_dynamic-update-slice_fusion.2, bf16[2,128,1024]{2,1,0:T(8,128)(2,1)} %copy-done.3, bf16[2,256,1024]{2,1,0:T(8,128)(2,1)S(1)} %collective-permute-done.7, pred[]{:T(512)S(6)} %eq.40), kind=kLoop, calls=%fused_computation.21 | loop fusion | flops 262144 | bytes 1572865
  75.8 2.0 %fusion.4 = bf16[2,1408,1024]{2,1,0:T(8,128)(2,1)} fusion(bf16[2,1408,1024]{2,1,0:T(8,128)(2,1)} %fusion.2, bf16[2,128,1024]{2,1,0:T(8,128)(2,1)} %collective-permute-done.9, bf16[2,256,1024]{2,1,0:T(8,128)(2,1)S(1)} %collective-permute-done.7, pred[]{:T(512)S(6)} %eq.40), kind=kLoop, calls=%fused_computation.23 | loop fusion | flops 262144 | bytes 1572865
  77.8 1.0 bitcast_dynamic-update-slice_fusion.1
  78.8 2.2 %bitcast_dynamic-update-slice_fusion = bf16[2,1408,1024]{2,1,0:T(8,128)(2,1)} fusion(bf16[2,1408,1024]{2,1,0:T(8,128)(2,1)} %bitcast_dynamic-update-slice_fusion.1, pred[]{:T(512)S(6)} %eq.39, bf16[2,2,128,1024]{3,2,1,0:T(8,128)(2,1)} %collective-permute-done.10), kind=kLoop, calls=%fused_computation.11 | loop fusion | flops 262144 | bytes 1572865
  81.0 1.1 constant_dynamic-update-slice_fusion
  82.1 66.4 %shard_map.46 = bf16[256,4096]{1,0:T(8,128)(2,1)} custom-call(s32[2,11]{1,0:T(2,128)} %fusion.6.slot_ref, s32[2,11]{1,0:T(2,128)} %compare_convert_fusion.diag_ref, bf16[256,4096]{1,0:T(8,128)(2,1)} %q_ref.1, bf16[2,11,128,1024]{3,2,1,0:T(8,128)(2,1)} %bitcast.25, bf16[2,11,128,1024]{3,2,1,0:T(8,128)(2,1)} %bitcast.26), custom_call_target="tpu_custom_call" | custom-call | flops 5905580032 | bytes 9961472 | tf_op jit(solution)/shard_map/pallas_call | solution.py:127
  (22 shorter events, 1.4 us)
Async XLA Ops:
  0.0 68.5 %copy-start = (s32[32,11]{0,1:T(8,128)S(1)}, s32[32,11]{0,1:T(8,128)}, u32[]{:S(2)}) copy-start(s32[32,11]{0,1:T(8,128)} %param.7) | copy-start | bytes 4228
  1.3 14.7 %collective-permute-start.4 = (bf16[2,128,1024]{2,1,0:T(8,128)(2,1)S(1)}, bf16[2,128,1024]{2,1,0:T(8,128)(2,1)S(1)}, u32[]{:S(2)}, u32[]{:S(2)}) collective-permute-start(bf16[2,128,1024]{2,1,0:T(8,128)(2,1)S(1)} %get-tuple-element.12), channel_id=1, source_target_pairs={{0,4},{1,5},{2,6},{3,7},{4,8},{5,9},{6,10},{7,11},{8,12},{9,13},{1... | collective-permute-start | bytes 1572872 | tf_op jit(solution)/shard_map/ppermute | solution.py:23
  4.5 11.5 %collective-permute-start = (bf16[2,128,1024]{2,1,0:T(8,128)(2,1)S(1)}, bf16[2,128,1024]{2,1,0:T(8,128)(2,1)S(1)}, u32[]{:S(2)}, u32[]{:S(2)}) collective-permute-start(bf16[2,128,1024]{2,1,0:T(8,128)(2,1)S(1)} %get-tuple-element.12), channel_id=1, source_target_pairs={{0,8},{16,24}} | collective-permute-start | bytes 1572872 | tf_op jit(solution)/shard_map/ppermute | solution.py:65
  16.1 10.2 %collective-permute-start.1 = (bf16[2,128,1024]{2,1,0:T(8,128)(2,1)S(1)}, bf16[2,128,1024]{2,1,0:T(8,128)(2,1)}, u32[]{:S(2)}, u32[]{:S(2)}) collective-permute-start(bf16[2,128,1024]{2,1,0:T(8,128)(2,1)S(1)} %get-tuple-element.16), channel_id=1, source_target_pairs={{0,4},{8,12},{16,20},{24,28}} | collective-permute-start | bytes 1572872 | tf_op jit(solution)/shard_map/ppermute | solution.py:65
  19.8 22.8 %collective-permute-start.7 = (bf16[2,256,1024]{2,1,0:T(8,128)(2,1)}, bf16[2,256,1024]{2,1,0:T(8,128)(2,1)S(1)}, u32[]{:S(2)}, u32[]{:S(2)}) collective-permute-start(bf16[2,256,1024]{2,1,0:T(8,128)(2,1)} %pad_maximum_fusion), channel_id=1, source_target_pairs={{0,2},{1,3},{4,6},{5,7},{8,10},{9,11},{12,14},{13,15},{16,18},{17,... | collective-permute-start | bytes 3145736 | tf_op jit(solution)/shard_map/ppermute | solution.py:23
  23.0 15.0 %collective-permute-start.5 = (bf16[2,128,1024]{2,1,0:T(8,128)(2,1)S(1)}, bf16[2,128,1024]{2,1,0:T(8,128)(2,1)}, u32[]{:S(2)}, u32[]{:S(2)}) collective-permute-start(bf16[2,128,1024]{2,1,0:T(8,128)(2,1)S(1)} %get-tuple-element.8), channel_id=1, source_target_pairs={{0,4},{1,5},{2,6},{3,7},{4,8},{5,9},{6,10},{7,11},{8,12},{9,13},{1... | collective-permute-start | bytes 1572872 | tf_op jit(solution)/shard_map/ppermute | solution.py:23
  27.1 12.2 %collective-permute-start.2 = (bf16[2,128,1024]{2,1,0:T(8,128)(2,1)}, bf16[2,128,1024]{2,1,0:T(8,128)(2,1)}, u32[]{:S(2)}, u32[]{:S(2)}) collective-permute-start(bf16[2,128,1024]{2,1,0:T(8,128)(2,1)} %broadcast_select_fusion.1), channel_id=1, source_target_pairs={{0,2},{4,6},{8,10},{12,14},{16,18},{20,22},{24,26},{28,30}} | collective-permute-start | bytes 1572872 | tf_op jit(solution)/shard_map/ppermute | solution.py:65
  28.6 14.0 %collective-permute-start.6 = (bf16[2,128,1024]{2,1,0:T(8,128)(2,1)S(1)}, bf16[2,128,1024]{2,1,0:T(8,128)(2,1)S(1)}, u32[]{:S(2)}, u32[]{:S(2)}) collective-permute-start(bf16[2,128,1024]{2,1,0:T(8,128)(2,1)S(1)} %collective-permute-done.4), channel_id=1, source_target_pairs={{2,0},{3,1},{6,4},{7,5},{10,8},{11,9},{14,12},{15,13},{18,16},{19,... | collective-permute-start | bytes 1572872 | tf_op jit(solution)/shard_map/ppermute | solution.py:23
  38.0 15.7 %collective-permute-start.9 = (bf16[2,128,1024]{2,1,0:T(8,128)(2,1)}, bf16[2,128,1024]{2,1,0:T(8,128)(2,1)}, u32[]{:S(2)}, u32[]{:S(2)}) collective-permute-start(bf16[2,128,1024]{2,1,0:T(8,128)(2,1)} %collective-permute-done.5), channel_id=1, source_target_pairs={{2,0},{3,1},{6,4},{7,5},{10,8},{11,9},{14,12},{15,13},{18,16},{19,... | collective-permute-start | bytes 1572872 | tf_op jit(solution)/shard_map/ppermute | solution.py:23
  41.2 21.2 %collective-permute-start.3 = (bf16[2,128,1024]{2,1,0:T(8,128)(2,1)}, bf16[2,128,1024]{2,1,0:T(8,128)(2,1)}, u32[]{:S(2)}, u32[]{:S(2)}) collective-permute-start(bf16[2,128,1024]{2,1,0:T(8,128)(2,1)} %broadcast_select_fusion.2), channel_id=1, source_target_pairs={{0,1},{2,3},{4,5},{6,7},{8,9},{10,11},{12,13},{14,15},{16,17},{18,... | collective-permute-start | bytes 1572872 | tf_op jit(solution)/shard_map/ppermute | solution.py:65
  42.6 12.4 %copy-start.3 = (bf16[2,128,1024]{2,1,0:T(8,128)(2,1)}, bf16[2,128,1024]{2,1,0:T(8,128)(2,1)S(1)}, u32[]{:S(2)}) copy-start(bf16[2,128,1024]{2,1,0:T(8,128)(2,1)S(1)} %collective-permute-done.6) | copy-start | bytes 1572868
  56.0 13.8 %collective-permute-start.8 = (bf16[2,2,128,1024]{3,2,1,0:T(8,128)(2,1)}, bf16[2,2,128,1024]{3,2,1,0:T(8,128)(2,1)S(1)}, u32[]{:S(2)}, u32[]{:S(2)}) collective-permute-start(bf16[2,2,128,1024]{3,2,1,0:T(8,128)(2,1)} %pad_maximum_fusion.1), channel_id=1, source_target_pairs={{0,1},{1,0},{2,3},{3,2},{4,5},{5,4},{6,7},{7,6},{8,9},{9,8},{10,11... | collective-permute-start | bytes 3145736 | tf_op jit(solution)/shard_map/ppermute | solution.py:43
  67.4 13.6 %copy-start.1 = (bf16[256,1024]{1,0:T(8,128)(2,1)S(1)}, bf16[256,1024]{1,0:T(8,128)(2,1)}, u32[]{:S(2)}) copy-start(bf16[256,1024]{1,0:T(8,128)(2,1)} %param.5) | copy-start | bytes 1572868
  67.4 13.6 %copy-start.2 = (bf16[256,1024]{1,0:T(8,128)(2,1)S(1)}, bf16[256,1024]{1,0:T(8,128)(2,1)}, u32[]{:S(2)}) copy-start(bf16[256,1024]{1,0:T(8,128)(2,1)} %param.6) | copy-start | bytes 1572868
  68.5 3.0 %collective-permute-start.10 = (bf16[2,2,128,1024]{3,2,1,0:T(8,128)(2,1)}, bf16[2,2,128,1024]{3,2,1,0:T(8,128)(2,1)}, u32[]{:S(2)}, u32[]{:S(2)}) collective-permute-start(bf16[2,2,128,1024]{3,2,1,0:T(8,128)(2,1)} %pad_maximum_fusion.2), channel_id=1, source_target_pairs={{0,1},{1,0},{2,3},{3,2},{4,5},{5,4},{6,7},{7,6},{8,9},{9,8},{10,11... | collective-permute-start | bytes 3145736 | tf_op jit(solution)/shard_map/ppermute | solution.py:43

commit v4 on v2

--- a/solution.py
+++ b/solution.py
@@ -63,29 +63,28 @@
     return held
 
 
-def attend_kernel(slot_ref, diag_ref, q_ref, k_ref, v_ref, o_ref, score_sc):
+def attend_kernel(slot_ref, diag_ref, q_ref, k_ref, v_ref, o_ref, score_sc, bias_sc):
     local = pl.program_id(1)
-    scale = HD ** (-0.5)
+    exp2_scale = (HD ** (-0.5)) * 1.4426950408889634
     q = q_ref[...]
     stacked = jnp.concatenate([q[:, j * HD:(j + 1) * HD] for j in range(GROUP)], axis=0)
     row = lax.broadcasted_iota(jnp.int32, (GROUP * BLK, BLK), 0) % BLK
     col = lax.broadcasted_iota(jnp.int32, (GROUP * BLK, BLK), 1)
-    future = col > row
+    bias_sc[0] = jnp.zeros((GROUP * BLK, BLK), jnp.float32)
+    bias_sc[1] = jnp.where(col > row, -jnp.inf, 0.0).astype(jnp.float32)
     run_max = jnp.full((GROUP * BLK, BLK), -jnp.inf, jnp.float32)
     for s in range(LIST):
         key = k_ref[0, slot_ref[local, s]]
         sc = lax.dot_general(
             stacked, key, (((1,), (1,)), ((), ())), preferred_element_type=jnp.float32
-        ) * scale
-        masked = jnp.logical_and(future, diag_ref[local, s] != 0)
-        sc = jnp.where(masked, -jnp.inf, sc)
+        ) + bias_sc[diag_ref[local, s]]
         score_sc[s] = sc
         run_max = jnp.maximum(run_max, sc)
     row_max = jnp.max(run_max, axis=1, keepdims=True)
     total = jnp.zeros((GROUP * BLK, BLK), jnp.float32)
     acc = jnp.zeros((GROUP * BLK, HD), jnp.float32)
     for s in range(LIST):
-        powers = jnp.exp(score_sc[s] - row_max)
+        powers = jnp.exp2((score_sc[s] - row_max) * exp2_scale)
         total = total + powers
         value = v_ref[0, slot_ref[local, s]]
         acc = acc + jnp.dot(
@@ -111,7 +110,10 @@
             pl.BlockSpec((1, buffer_blocks, BLK, HD), lambda g, b, *_: (1, 0, 0, g)),
         ],
         out_specs=pl.BlockSpec((BLK, GROUP * HD), lambda g, b, *_: (b, g)),
-        scratch_shapes=[pltpu.VMEM((LIST, GROUP * BLK, BLK), jnp.float32)],
+        scratch_shapes=[
+            pltpu.VMEM((LIST, GROUP * BLK, BLK), jnp.float32),
+            pltpu.VMEM((2, GROUP * BLK, BLK), jnp.float32),
+        ],
     )
     return pl.pallas_call(
         attend_kernel,

time: 105 us -> 104 us (level)
  no operation moved by 1% of the time
where the time goes in v4:
time: 104 us; the launch traced here: 103 us
  Pallas kernels  38.4 us (37%)
  starting transfers between devices  35.5 us (34%)
  waiting for transfers between devices  18.1 us (17%)
  other arithmetic  8.49 us (8%)
  local copies, waits for them, and re-layouts  2.8 us (3%)
    pallas_call x1, Pallas kernels, attend(): pl.pallas_call(attend_kernel, out_shape=jax.ShapeDtypeStruct(queries.shap...  38.4 us
    ppermute x5, starting transfers between devices, shifted(): return lax.ppermute(shard, axis, pairs)  27.1 us
    ppermute x5, waiting for transfers between devices, shifted(): return lax.ppermute(shard, axis, pairs)  16.8 us
    ppermute x4, starting transfers between devices, tree_broadcast(): got = lax.ppermute(held, axis, pairs)  4.94 us
    ppermute x1, starting transfers between devices, window_blocks(): partner_back2 = lax.ppermute(back2, axis, swap_pairs)  3.46 us
    unnamed x11, local copies, waits for them, and re-layouts  2.72 us
    another operation x2, other arithmetic, per_device(): kv = jnp.stack([key_rows, value_rows])  2.38 us
    unnamed x3, other arithmetic  2.24 us
  transfers between devices with their start and end apart: 10, of which 2 were waited for; matrix products, arithmetic and copies ran while one was open for 6% of the time, Pallas kernels for 0%

profile of v4, /device:TPU:19, one launch (start us, length us, event | category | flops | bytes accessed | tf_op | source)
XLA Modules:
  0.0 103.5 jit_solution(14852885857248846869)
XLA Ops:
  0.0 1.3 %pad_maximum_fusion = bf16[2,256,1024]{2,1,0:T(8,128)(2,1)S(1)} fusion(bf16[1,256,1024]{2,1,0:T(8,128)(2,1)} %bitcast.7, bf16[1,256,1024]{2,1,0:T(8,128)(2,1)} %bitcast.3), kind=kLoop, calls=%fused_computation.1 | loop fusion | flops 524288 | bytes 2097152 | tf_op jit(solution)/shard_map/stack | solution.py:138
  1.3 3.2 %collective-permute-start.4 = (bf16[2,256,1024]{2,1,0:T(8,128)(2,1)S(1)}, bf16[2,256,1024]{2,1,0:T(8,128)(2,1)S(1)}, u32[]{:S(2)}, u32[]{:S(2)}) collective-permute-start(bf16[2,256,1024]{2,1,0:T(8,128)(2,1)S(1)} %pad_maximum_fusion), channel_id=1, source_target_pairs={{0,4},{1,5},{2,6},{3,7},{4,8},{5,9},{6,10},{7,11},{8,12},{9,13},{1... | collective-permute-start | bytes 3145736 | tf_op jit(solution)/shard_map/ppermute | solution.py:23
  4.5 1.1 %fusion = bf16[2,128,1024]{2,1,0:T(8,128)(2,1)S(1)} fusion(bf16[1,256,1024]{2,1,0:T(8,128)(2,1)} %bitcast.4, bf16[1,256,1024]{2,1,0:T(8,128)(2,1)} %bitcast.8), kind=kLoop, calls=%fused_computation.6 | loop fusion | flops 262144 | bytes 1572864 | tf_op jit(solution)/shard_map/stack | solution.py:138
  5.6 0.7 collective-permute-start
  6.3 4.2 %collective-permute-start.7 = (bf16[2,256,1024]{2,1,0:T(8,128)(2,1)S(1)}, bf16[2,256,1024]{2,1,0:T(8,128)(2,1)}, u32[]{:S(2)}, u32[]{:S(2)}) collective-permute-start(bf16[2,256,1024]{2,1,0:T(8,128)(2,1)S(1)} %pad_maximum_fusion), channel_id=1, source_target_pairs={{0,2},{1,3},{4,6},{5,7},{8,10},{9,11},{12,14},{13,15},{16,18},{17,... | collective-permute-start | bytes 3145736 | tf_op jit(solution)/shard_map/ppermute | solution.py:23
  10.5 16.8 %collective-permute-done.4 = bf16[2,256,1024]{2,1,0:T(8,128)(2,1)S(1)} collective-permute-done((bf16[2,256,1024]{2,1,0:T(8,128)(2,1)S(1)}, bf16[2,256,1024]{2,1,0:T(8,128)(2,1)S(1)}, u32[]{:S(2)}, u32[]{:S(2)}) %collective-permute-start.4) | collective-permute-done | bytes 1048608 | tf_op jit(solution)/shard_map/ppermute | solution.py:23
  27.2 1.3 %collective-permute-start.6 = (bf16[2,256,1024]{2,1,0:T(8,128)(2,1)S(1)}, bf16[2,256,1024]{2,1,0:T(8,128)(2,1)}, u32[]{:S(2)}, u32[]{:S(2)}) collective-permute-start(bf16[2,256,1024]{2,1,0:T(8,128)(2,1)S(1)} %collective-permute-done.4), channel_id=1, source_target_pairs={{2,0},{3,1},{6,4},{7,5},{10,8},{11,9},{14,12},{15,13},{18,16},{19,... | collective-permute-start | bytes 3145736 | tf_op jit(solution)/shard_map/ppermute | solution.py:23
  28.5 0.0 collective-permute-done
  28.5 1.1 %broadcast_select_fusion.1 = bf16[2,128,1024]{2,1,0:T(8,128)(2,1)S(1)} fusion(bf16[2,128,1024]{2,1,0:T(8,128)(2,1)S(1)} %collective-permute-done, pred[]{:T(512)S(6)} %and.53, bf16[1,256,1024]{2,1,0:T(8,128)(2,1)} %bitcast.9, bf16[1,256,1024]{2,1,0:T(8,128)(2,1)} %bitcast.5), kind=kLoop, calls=%fused_computation.8 | loop fusion | flops 524288 | bytes 2097153 | tf_op jit(solution)/shard_map/jit(_where)/select_n | solution.py:61
  29.6 1.5 %collective-permute-start.1 = (bf16[2,128,1024]{2,1,0:T(8,128)(2,1)S(1)}, bf16[2,128,1024]{2,1,0:T(8,128)(2,1)}, u32[]{:S(2)}, u32[]{:S(2)}) collective-permute-start(bf16[2,128,1024]{2,1,0:T(8,128)(2,1)S(1)} %broadcast_select_fusion.1), channel_id=1, source_target_pairs={{0,4},{8,12},{16,20},{24,28}} | collective-permute-start | bytes 1572872 | tf_op jit(solution)/shard_map/ppermute | solution.py:58
  31.1 0.0 collective-permute-done.1
  31.1 0.1 broadcast_select_fusion.2
  31.2 1.5 %collective-permute-start.2 = (bf16[2,128,1024]{2,1,0:T(8,128)(2,1)S(1)}, bf16[2,128,1024]{2,1,0:T(8,128)(2,1)}, u32[]{:S(2)}, u32[]{:S(2)}) collective-permute-start(bf16[2,128,1024]{2,1,0:T(8,128)(2,1)S(1)} %broadcast_select_fusion.2), channel_id=1, source_target_pairs={{0,2},{4,6},{8,10},{12,14},{16,18},{20,22},{24,26},{28,30}} | collective-permute-start | bytes 1572872 | tf_op jit(solution)/shard_map/ppermute | solution.py:58
  32.7 1.3 %collective-permute-start.9 = (bf16[2,256,1024]{2,1,0:T(8,128)(2,1)S(1)}, bf16[2,256,1024]{2,1,0:T(8,128)(2,1)}, u32[]{:S(2)}, u32[]{:S(2)}) collective-permute-start(bf16[2,256,1024]{2,1,0:T(8,128)(2,1)S(1)} %pad_maximum_fusion), channel_id=1, source_target_pairs={{0,1},{2,3},{4,5},{6,7},{8,9},{10,11},{12,13},{14,15},{16,17},{18,... | collective-permute-start | bytes 3145736 | tf_op jit(solution)/shard_map/ppermute | solution.py:23
  34.0 0.1 constant_dynamic-slice_fusion
  34.1 0.1 copy.6
  34.2 17.2 %collective-permute-start.5 = (bf16[2,256,1024]{2,1,0:T(8,128)(2,1)S(1)}, bf16[2,256,1024]{2,1,0:T(8,128)(2,1)S(1)}, u32[]{:S(2)}, u32[]{:S(2)}) collective-permute-start(bf16[2,256,1024]{2,1,0:T(8,128)(2,1)S(1)} %collective-permute-done.4), channel_id=1, source_target_pairs={{1,0},{3,2},{5,4},{7,6},{9,8},{11,10},{13,12},{15,14},{17,16},{19,... | collective-permute-start | bytes 3145736 | tf_op jit(solution)/shard_map/ppermute | solution.py:23
  51.4 1.3 %broadcast_select_fusion = bf16[2,256,1024]{2,1,0:T(8,128)(2,1)S(1)} fusion(bf16[2,256,1024]{2,1,0:T(8,128)(2,1)} %collective-permute-done.6, bf16[2,256,1024]{2,1,0:T(8,128)(2,1)} %collective-permute-done.7, pred[]{:T(512)S(6)} %eq.40), kind=kLoop, calls=%fused_computation.5 | loop fusion | flops 524288 | bytes 3145729 | tf_op jit(solution)/shard_map/jit(_where)/select_n | solution.py:34
  52.7 3.5 %collective-permute-start.8 = (bf16[2,256,1024]{2,1,0:T(8,128)(2,1)S(1)}, bf16[2,256,1024]{2,1,0:T(8,128)(2,1)S(1)}, u32[]{:S(2)}, u32[]{:S(2)}) collective-permute-start(bf16[2,256,1024]{2,1,0:T(8,128)(2,1)S(1)} %broadcast_select_fusion), channel_id=1, source_target_pairs={{0,1},{1,0},{2,3},{3,2},{4,5},{5,4},{6,7},{7,6},{8,9},{9,8},{10,11... | collective-permute-start | bytes 3145736 | tf_op jit(solution)/shard_map/ppermute | solution.py:38
  56.2 0.1 broadcast_select_fusion.3
  56.3 1.3 %collective-permute-start.3 = (bf16[2,128,1024]{2,1,0:T(8,128)(2,1)S(1)}, bf16[2,128,1024]{2,1,0:T(8,128)(2,1)S(1)}, u32[]{:S(2)}, u32[]{:S(2)}) collective-permute-start(bf16[2,128,1024]{2,1,0:T(8,128)(2,1)S(1)} %broadcast_select_fusion.3), channel_id=1, source_target_pairs={{0,1},{2,3},{4,5},{6,7},{8,9},{10,11},{12,13},{14,15},{16,17},{18,... | collective-permute-start | bytes 1572872 | tf_op jit(solution)/shard_map/ppermute | solution.py:58
  57.6 0.6 compare_convert_fusion.diag_ref
  58.2 0.6 fusion.1.slot_ref
  58.8 1.3 %collective-permute-done.3 = bf16[2,128,1024]{2,1,0:T(8,128)(2,1)S(1)} collective-permute-done((bf16[2,128,1024]{2,1,0:T(8,128)(2,1)S(1)}, bf16[2,128,1024]{2,1,0:T(8,128)(2,1)S(1)}, u32[]{:S(2)}, u32[]{:S(2)}) %collective-permute-start.3) | collective-permute-done | bytes 524320 | tf_op jit(solution)/shard_map/ppermute | solution.py:58
  60.1 0.2 select_dynamic-update-slice_fusion.2
  60.3 0.1 constant_dynamic-update-slice_fusion.2
  60.4 0.4 select_dynamic-update-slice_fusion.1
  60.8 0.1 constant_dynamic-update-slice_fusion.1
  60.9 1.6 %select_dynamic-update-slice_fusion = bf16[2,1408,1024]{2,1,0:T(8,128)(2,1)S(1)} fusion(bf16[2,1408,1024]{2,1,0:T(8,128)(2,1)S(1)} %constant_dynamic-update-slice_fusion.1, bf16[2,256,1024]{2,1,0:T(8,128)(2,1)S(1)} %collective-permute-done.8, bf16[2,256,1024]{2,1,0:T(8,128)(2,1)} %collective-permute-done.9, pred[]{:T(512)S(6)} %eq.39), kind=kLoop, calls=%fused_computation.3 | loop fusion | flops 524288 | bytes 3145729
  62.5 0.1 constant_dynamic-update-slice_fusion
  62.6 2.5 %copy-done.3 = bf16[2,1408,1024]{2,1,0:T(8,128)(2,1)} copy-done((bf16[2,1408,1024]{2,1,0:T(8,128)(2,1)}, bf16[2,1408,1024]{2,1,0:T(8,128)(2,1)S(1)}, u32[]{:S(2)}) %copy-start.3) | copy-done | bytes 5767192
  65.1 38.4 %shard_map.46 = bf16[256,4096]{1,0:T(8,128)(2,1)} custom-call(s32[2,11]{1,0:T(2,128)} %fusion.1.slot_ref, s32[2,11]{1,0:T(2,128)} %compare_convert_fusion.diag_ref, bf16[256,4096]{1,0:T(8,128)(2,1)} %q_ref.1, bf16[2,11,128,1024]{3,2,1,0:T(8,128)(2,1)} %bitcast.11, bf16[2,11,128,1024]{3,2,1,0:T(8,128)(2,1)} %bitcast.12), custom_call_target="tpu_custom_call" | custom-call | flops 5905580032 | bytes 9961472 | tf_op jit(solution)/shard_map/pallas_call | solution.py:118
  (14 shorter events, 0.0 us)
Async XLA Ops:
  0.0 34.0 %copy-start = (s32[32,11]{0,1:T(8,128)S(1)}, s32[32,11]{0,1:T(8,128)}, u32[]{:S(2)}) copy-start(s32[32,11]{0,1:T(8,128)} %param.7) | copy-start | bytes 4228
  1.3 25.9 %collective-permute-start.4 = (bf16[2,256,1024]{2,1,0:T(8,128)(2,1)S(1)}, bf16[2,256,1024]{2,1,0:T(8,128)(2,1)S(1)}, u32[]{:S(2)}, u32[]{:S(2)}) collective-permute-start(bf16[2,256,1024]{2,1,0:T(8,128)(2,1)S(1)} %pad_maximum_fusion), channel_id=1, source_target_pairs={{0,4},{1,5},{2,6},{3,7},{4,8},{5,9},{6,10},{7,11},{8,12},{9,13},{1... | collective-permute-start | bytes 3145736 | tf_op jit(solution)/shard_map/ppermute | solution.py:23
  5.6 22.9 %collective-permute-start = (bf16[2,128,1024]{2,1,0:T(8,128)(2,1)S(1)}, bf16[2,128,1024]{2,1,0:T(8,128)(2,1)S(1)}, u32[]{:S(2)}, u32[]{:S(2)}) collective-permute-start(bf16[2,128,1024]{2,1,0:T(8,128)(2,1)S(1)} %fusion), channel_id=1, source_target_pairs={{0,8},{16,24}} | collective-permute-start | bytes 1572872 | tf_op jit(solution)/shard_map/ppermute | solution.py:58
  6.3 45.1 %collective-permute-start.7 = (bf16[2,256,1024]{2,1,0:T(8,128)(2,1)S(1)}, bf16[2,256,1024]{2,1,0:T(8,128)(2,1)}, u32[]{:S(2)}, u32[]{:S(2)}) collective-permute-start(bf16[2,256,1024]{2,1,0:T(8,128)(2,1)S(1)} %pad_maximum_fusion), channel_id=1, source_target_pairs={{0,2},{1,3},{4,6},{5,7},{8,10},{9,11},{12,14},{13,15},{16,18},{17,... | collective-permute-start | bytes 3145736 | tf_op jit(solution)/shard_map/ppermute | solution.py:23
  27.2 24.2 %collective-permute-start.6 = (bf16[2,256,1024]{2,1,0:T(8,128)(2,1)S(1)}, bf16[2,256,1024]{2,1,0:T(8,128)(2,1)}, u32[]{:S(2)}, u32[]{:S(2)}) collective-permute-start(bf16[2,256,1024]{2,1,0:T(8,128)(2,1)S(1)} %collective-permute-done.4), channel_id=1, source_target_pairs={{2,0},{3,1},{6,4},{7,5},{10,8},{11,9},{14,12},{15,13},{18,16},{19,... | collective-permute-start | bytes 3145736 | tf_op jit(solution)/shard_map/ppermute | solution.py:23
  29.6 1.5 %collective-permute-start.1 = (bf16[2,128,1024]{2,1,0:T(8,128)(2,1)S(1)}, bf16[2,128,1024]{2,1,0:T(8,128)(2,1)}, u32[]{:S(2)}, u32[]{:S(2)}) collective-permute-start(bf16[2,128,1024]{2,1,0:T(8,128)(2,1)S(1)} %broadcast_select_fusion.1), channel_id=1, source_target_pairs={{0,4},{8,12},{16,20},{24,28}} | collective-permute-start | bytes 1572872 | tf_op jit(solution)/shard_map/ppermute | solution.py:58
  31.2 25.0 %collective-permute-start.2 = (bf16[2,128,1024]{2,1,0:T(8,128)(2,1)S(1)}, bf16[2,128,1024]{2,1,0:T(8,128)(2,1)}, u32[]{:S(2)}, u32[]{:S(2)}) collective-permute-start(bf16[2,128,1024]{2,1,0:T(8,128)(2,1)S(1)} %broadcast_select_fusion.2), channel_id=1, source_target_pairs={{0,2},{4,6},{8,10},{12,14},{16,18},{20,22},{24,26},{28,30}} | collective-permute-start | bytes 1572872 | tf_op jit(solution)/shard_map/ppermute | solution.py:58
  32.7 28.2 %collective-permute-start.9 = (bf16[2,256,1024]{2,1,0:T(8,128)(2,1)S(1)}, bf16[2,256,1024]{2,1,0:T(8,128)(2,1)}, u32[]{:S(2)}, u32[]{:S(2)}) collective-permute-start(bf16[2,256,1024]{2,1,0:T(8,128)(2,1)S(1)} %pad_maximum_fusion), channel_id=1, source_target_pairs={{0,1},{2,3},{4,5},{6,7},{8,9},{10,11},{12,13},{14,15},{16,17},{18,... | collective-permute-start | bytes 3145736 | tf_op jit(solution)/shard_map/ppermute | solution.py:23
  34.2 26.2 %collective-permute-start.5 = (bf16[2,256,1024]{2,1,0:T(8,128)(2,1)S(1)}, bf16[2,256,1024]{2,1,0:T(8,128)(2,1)S(1)}, u32[]{:S(2)}, u32[]{:S(2)}) collective-permute-start(bf16[2,256,1024]{2,1,0:T(8,128)(2,1)S(1)} %collective-permute-done.4), channel_id=1, source_target_pairs={{1,0},{3,2},{5,4},{7,6},{9,8},{11,10},{13,12},{15,14},{17,16},{19,... | collective-permute-start | bytes 3145736 | tf_op jit(solution)/shard_map/ppermute | solution.py:23
  52.7 7.6 %collective-permute-start.8 = (bf16[2,256,1024]{2,1,0:T(8,128)(2,1)S(1)}, bf16[2,256,1024]{2,1,0:T(8,128)(2,1)S(1)}, u32[]{:S(2)}, u32[]{:S(2)}) collective-permute-start(bf16[2,256,1024]{2,1,0:T(8,128)(2,1)S(1)} %broadcast_select_fusion), channel_id=1, source_target_pairs={{0,1},{1,0},{2,3},{3,2},{4,5},{5,4},{6,7},{7,6},{8,9},{9,8},{10,11... | collective-permute-start | bytes 3145736 | tf_op jit(solution)/shard_map/ppermute | solution.py:38
  56.3 3.8 %collective-permute-start.3 = (bf16[2,128,1024]{2,1,0:T(8,128)(2,1)S(1)}, bf16[2,128,1024]{2,1,0:T(8,128)(2,1)S(1)}, u32[]{:S(2)}, u32[]{:S(2)}) collective-permute-start(bf16[2,128,1024]{2,1,0:T(8,128)(2,1)S(1)} %broadcast_select_fusion.3), channel_id=1, source_target_pairs={{0,1},{2,3},{4,5},{6,7},{8,9},{10,11},{12,13},{14,15},{16,17},{18,... | collective-permute-start | bytes 1572872 | tf_op jit(solution)/shard_map/ppermute | solution.py:58
  58.8 3.7 %copy-start.1 = (bf16[256,1024]{1,0:T(8,128)(2,1)S(1)}, bf16[256,1024]{1,0:T(8,128)(2,1)}, u32[]{:S(2)}) copy-start(bf16[256,1024]{1,0:T(8,128)(2,1)} %param.5) | copy-start | bytes 1572868
  58.8 3.7 %copy-start.2 = (bf16[256,1024]{1,0:T(8,128)(2,1)S(1)}, bf16[256,1024]{1,0:T(8,128)(2,1)}, u32[]{:S(2)}) copy-start(bf16[256,1024]{1,0:T(8,128)(2,1)} %param.6) | copy-start | bytes 1572868
  62.6 2.5 %copy-start.3 = (bf16[2,1408,1024]{2,1,0:T(8,128)(2,1)}, bf16[2,1408,1024]{2,1,0:T(8,128)(2,1)S(1)}, u32[]{:S(2)}) copy-start(bf16[2,1408,1024]{2,1,0:T(8,128)(2,1)S(1)} %constant_dynamic-update-slice_fusion) | copy-start | bytes 17301508

commit v5 on v4

--- a/solution.py
+++ b/solution.py
@@ -25,20 +25,28 @@
 
 def window_blocks(kv, axis):
     index = lax.axis_index(axis)
+    size = lax.axis_size(axis)
     y_low = (index // 2) % 2 == 0
     core0 = index % 2 == 0
-    back4 = shifted(kv, axis, 4, lambda i: True)
-    up_y = shifted(kv, axis, 2, lambda i: (i // 2) % 2 == 0)
-    next_core = shifted(kv, axis, 1, lambda i: i % 2 == 0)
-    down_y = shifted(back4, axis, -2, lambda i: (i // 2) % 2 == 1)
-    back2 = jnp.where(y_low, down_y, up_y)
-    partner_back4 = shifted(back4, axis, -1, lambda i: i % 2 == 1)
-    size = lax.axis_size(axis)
-    swap_pairs = [(i, i ^ 1) for i in range(size)]
-    partner_back2 = lax.ppermute(back2, axis, swap_pairs)
-    back3 = jnp.where(core0, partner_back4, partner_back2)
-    back1 = jnp.where(core0, partner_back2, next_core)
-    return [back4, back3, back2, back1]
+    is_y_low = lambda i: (i // 2) % 2 == 0
+    is_core0 = lambda i: i % 2 == 0
+    back4_c0 = shifted(kv[:, BLK:], axis, 4, is_core0)
+    back4_c1 = shifted(kv, axis, 4, lambda i: not is_core0(i))
+    up_y = shifted(kv, axis, 2, is_y_low)
+    down_first = shifted(kv, axis, -2, lambda i: is_core0(i) and not is_y_low(i))
+    down_then_z = shifted(down_first, axis, 4, lambda i: is_core0(i) and is_y_low(i))
+    z_then_down = shifted(back4_c1, axis, -2, lambda i: not is_core0(i) and not is_y_low(i))
+    from_c0 = jnp.where(y_low, down_then_z, up_y)
+    from_c1 = jnp.where(y_low, z_then_down, up_y)
+    sent = jnp.where(
+        core0, jnp.stack([from_c0, kv]), jnp.stack([back4_c1, from_c1])
+    )
+    got = lax.ppermute(sent, axis, [(i, i ^ 1) for i in range(size)])
+    back4 = jnp.concatenate(
+        [back4_c1[:, :BLK], jnp.where(core0, back4_c0, back4_c1[:, BLK:])], axis=1
+    )
+    back2 = jnp.where(core0, from_c0, from_c1)
+    return [back4, got[0], back2, got[1]]
 
 
 def tree_broadcast(block, axis, source, size):
@@ -151,7 +159,7 @@
     first_block = own_index * blocks_here - 4 * blocks_here
     rows_pattern = lax.dynamic_slice_in_dim(pattern, own_index * blocks_here, blocks_here, 0)
     slots = jnp.where(
-        rows_pattern >= first_block,
+        rows_pattern > first_block,
         columns + rows_pattern - first_block,
         rows_pattern // STRIDE,
     )

time: 104 us -> 109 us (1.048)
  the two profiles are of different devices: /device:TPU:19 before, /device:TPU:0 now
where the time goes in v5:
time: 109 us; the launch traced here: 108 us
  Pallas kernels  38.4 us (35%)
  starting transfers between devices  29.3 us (27%)
  waiting for transfers between devices  18 us (17%)
  other arithmetic  16.9 us (16%)
  local copies, waits for them, and re-layouts  5.3 us (5%)
    pallas_call x1, Pallas kernels, attend(): pl.pallas_call(attend_kernel, out_shape=jax.ShapeDtypeStruct(queries.shap...  38.4 us
    ppermute x6, starting transfers between devices, shifted(): return lax.ppermute(shard, axis, pairs)  15 us
    ppermute x4, starting transfers between devices, tree_broadcast(): got = lax.ppermute(held, axis, pairs)  14.3 us
    ppermute x4, waiting for transfers between devices, tree_broadcast(): got = lax.ppermute(held, axis, pairs)  12 us
    ppermute x6, waiting for transfers between devices, shifted(): return lax.ppermute(shard, axis, pairs)  5.97 us
    unnamed x12, local copies, waits for them, and re-layouts  5.23 us
    select_n x3, other arithmetic, tree_broadcast(): held = jnp.where(takes, got, held)  4.92 us
    unnamed x3, other arithmetic  2.57 us
  transfers between devices with their start and end apart: 11, of which 3 were waited for; matrix products, arithmetic and copies ran while one was open for 12% of the time, Pallas kernels for 0%

profile of v5, /device:TPU:0, one launch (start us, length us, event | category | flops | bytes accessed | tf_op | source)
XLA Modules:
  0.0 108.0 jit_solution(7648944572296236168)
XLA Ops:
  0.0 2.3 %fusion.8 = (bf16[1,2,256,1024]{3,2,1,0:T(8,128)(2,1)S(1)}, bf16[2,256,1024]{2,1,0:T(8,128)(2,1)}) fusion(bf16[1,256,1024]{2,1,0:T(8,128)(2,1)} %bitcast.21, bf16[1,256,1024]{2,1,0:T(8,128)(2,1)} %bitcast.18), kind=kLoop, calls=%fused_computation.34 | loop fusion | flops 524288 | bytes 3145728 | tf_op jit(solution)/shard_map/stack | solution.py:42
  2.3 0.7 collective-permute-start.4
  3.0 1.3 %collective-permute-start.6 = (bf16[2,256,1024]{2,1,0:T(8,128)(2,1)}, bf16[2,256,1024]{2,1,0:T(8,128)(2,1)}, u32[]{:S(2)}, u32[]{:S(2)}) collective-permute-start(bf16[2,256,1024]{2,1,0:T(8,128)(2,1)} %get-tuple-element.8), channel_id=1, source_target_pairs={{2,0},{6,4},{10,8},{14,12},{18,16},{22,20},{26,24},{30,28}} | collective-permute-start | bytes 3145736 | tf_op jit(solution)/shard_map/ppermute | solution.py:23
  4.3 2.3 %fusion.3 = (bf16[2,128,1024]{2,1,0:T(8,128)(2,1)}, bf16[2,128,1024]{2,1,0:T(8,128)(2,1)}) fusion(bf16[1,256,1024]{2,1,0:T(8,128)(2,1)} %bitcast.19, bf16[1,256,1024]{2,1,0:T(8,128)(2,1)} %bitcast.22), kind=kLoop, calls=%fused_computation.14 | loop fusion | flops 524288 | bytes 2097152 | tf_op jit(solution)/shard_map/stack | solution.py:146
  6.7 6.8 %collective-permute-start = (bf16[2,128,1024]{2,1,0:T(8,128)(2,1)}, bf16[2,128,1024]{2,1,0:T(8,128)(2,1)}, u32[]{:S(2)}, u32[]{:S(2)}) collective-permute-start(bf16[2,128,1024]{2,1,0:T(8,128)(2,1)} %get-tuple-element.10), channel_id=1, source_target_pairs={{0,8},{16,24}} | collective-permute-start | bytes 1572872 | tf_op jit(solution)/shard_map/ppermute | solution.py:66
  13.4 1.3 %collective-permute-start.8 = (bf16[2,256,1024]{2,1,0:T(8,128)(2,1)}, bf16[2,256,1024]{2,1,0:T(8,128)(2,1)S(1)}, u32[]{:S(2)}, u32[]{:S(2)}) collective-permute-start(bf16[2,256,1024]{2,1,0:T(8,128)(2,1)} %get-tuple-element.8), channel_id=1, source_target_pairs={{0,2},{1,3},{4,6},{5,7},{8,10},{9,11},{12,14},{13,15},{16,18},{17,... | collective-permute-start | bytes 3145736 | tf_op jit(solution)/shard_map/ppermute | solution.py:23
  14.8 1.6 %collective-permute-start.9 = (bf16[2,256,1024]{2,1,0:T(8,128)(2,1)S(1)}, bf16[2,256,1024]{2,1,0:T(8,128)(2,1)}, u32[]{:S(2)}, u32[]{:S(2)}) collective-permute-start(bf16[2,256,1024]{2,1,0:T(8,128)(2,1)S(1)} %collective-permute-done.4), channel_id=1, source_target_pairs={{3,1},{7,5},{11,9},{15,13},{19,17},{23,21},{27,25},{31,29}} | collective-permute-start | bytes 3145736 | tf_op jit(solution)/shard_map/ppermute | solution.py:23
  16.4 3.9 %collective-permute-done.6 = bf16[2,256,1024]{2,1,0:T(8,128)(2,1)} collective-permute-done((bf16[2,256,1024]{2,1,0:T(8,128)(2,1)}, bf16[2,256,1024]{2,1,0:T(8,128)(2,1)}, u32[]{:S(2)}, u32[]{:S(2)}) %collective-permute-start.6) | collective-permute-done | bytes 1048608 | tf_op jit(solution)/shard_map/ppermute | solution.py:23
  20.4 5.6 %collective-permute-start.7 = (bf16[2,256,1024]{2,1,0:T(8,128)(2,1)}, bf16[2,256,1024]{2,1,0:T(8,128)(2,1)}, u32[]{:S(2)}, u32[]{:S(2)}) collective-permute-start(bf16[2,256,1024]{2,1,0:T(8,128)(2,1)} %collective-permute-done.6), channel_id=1, source_target_pairs={{0,4},{4,8},{8,12},{16,20},{20,24},{24,28}} | collective-permute-start | bytes 3145736 | tf_op jit(solution)/shard_map/ppermute | solution.py:23
  26.0 1.9 %broadcast_select_fusion.2 = bf16[2,128,1024]{2,1,0:T(8,128)(2,1)} fusion(bf16[2,128,1024]{2,1,0:T(8,128)(2,1)} %collective-permute-done, bf16[2,128,1024]{2,1,0:T(8,128)(2,1)} %get-tuple-element.10, pred[]{:T(512)S(6)} %and.53), kind=kLoop, calls=%fused_computation.19 | loop fusion | flops 262144 | bytes 1572865 | tf_op jit(solution)/shard_map/jit(_where)/select_n | solution.py:69
  27.9 3.3 %collective-permute-start.1 = (bf16[2,128,1024]{2,1,0:T(8,128)(2,1)}, bf16[2,128,1024]{2,1,0:T(8,128)(2,1)}, u32[]{:S(2)}, u32[]{:S(2)}) collective-permute-start(bf16[2,128,1024]{2,1,0:T(8,128)(2,1)} %broadcast_select_fusion.2), channel_id=1, source_target_pairs={{0,4},{8,12},{16,20},{24,28}} | collective-permute-start | bytes 1572872 | tf_op jit(solution)/shard_map/ppermute | solution.py:66
  31.2 12.0 %collective-permute-done.1 = bf16[2,128,1024]{2,1,0:T(8,128)(2,1)} collective-permute-done((bf16[2,128,1024]{2,1,0:T(8,128)(2,1)}, bf16[2,128,1024]{2,1,0:T(8,128)(2,1)}, u32[]{:S(2)}, u32[]{:S(2)}) %collective-permute-start.1) | collective-permute-done | bytes 524320 | tf_op jit(solution)/shard_map/ppermute | solution.py:66
  43.2 1.9 %broadcast_select_fusion.3 = bf16[2,128,1024]{2,1,0:T(8,128)(2,1)} fusion(bf16[2,128,1024]{2,1,0:T(8,128)(2,1)} %collective-permute-done.1, bf16[2,128,1024]{2,1,0:T(8,128)(2,1)} %broadcast_select_fusion.2, pred[]{:T(512)S(6)} %and.51), kind=kLoop, calls=%fused_computation.20 | loop fusion | flops 262144 | bytes 1572865 | tf_op jit(solution)/shard_map/jit(_where)/select_n | solution.py:69
  45.1 2.1 %collective-permute-start.2 = (bf16[2,128,1024]{2,1,0:T(8,128)(2,1)}, bf16[2,128,1024]{2,1,0:T(8,128)(2,1)}, u32[]{:S(2)}, u32[]{:S(2)}) collective-permute-start(bf16[2,128,1024]{2,1,0:T(8,128)(2,1)} %broadcast_select_fusion.3), channel_id=1, source_target_pairs={{0,2},{4,6},{8,10},{12,14},{16,18},{20,22},{24,26},{28,30}} | collective-permute-start | bytes 1572872 | tf_op jit(solution)/shard_map/ppermute | solution.py:66
  47.2 1.7 %fusion.6 = (bf16[1,2,256,1024]{3,2,1,0:T(8,128)(2,1)S(1)}, bf16[1,2,256,1024]{3,2,1,0:T(8,128)(2,1)S(1)}) fusion(bf16[2,256,1024]{2,1,0:T(8,128)(2,1)} %collective-permute-done.9, bf16[2,256,1024]{2,1,0:T(8,128)(2,1)S(1)} %collective-permute-done.8, pred[]{:T(512)S(6)} %eq.40, bf16[2,256,1024]{2,1,0:T(8,128)(2,1)} %collective-permute-done.7), kind=kLoop, calls=%fused_computation.23 | loop fusion | flops 1048576 | bytes 5242881 | tf_op jit(solution)/shard_map/stack | solution.py:42
  49.0 1.7 %maximum_select_fusion = bf16[2,2,256,1024]{3,2,1,0:T(8,128)(2,1)} fusion(bf16[1,2,256,1024]{3,2,1,0:T(8,128)(2,1)S(1)} %get-tuple-element.7, bf16[1,2,256,1024]{3,2,1,0:T(8,128)(2,1)S(1)} %get-tuple-element.6, bf16[1,2,256,1024]{3,2,1,0:T(8,128)(2,1)S(1)} %get-tuple-element.5, bf16[1,2,256,1024]{3,2,1,0:T(8,128)(2,1)S(1)} %bitcast.24, pred[]{:T(512)S(6)} %eq.39), kind=kLoop, calls=%fused_computation | loop fusion | flops 3145728 | bytes 6291457 | tf_op jit(solution)/shard_map/jit(_where)/select_n | solution.py:41
  50.7 4.4 %collective-permute-start.5 = (bf16[2,128,1024]{2,1,0:T(8,128)(2,1)}, bf16[2,128,1024]{2,1,0:T(8,128)(2,1)S(1)}, u32[]{:S(2)}, u32[]{:S(2)}) collective-permute-start(bf16[2,128,1024]{2,1,0:T(8,128)(2,1)} %get-tuple-element.9), channel_id=1, source_target_pairs={{0,4},{2,6},{4,8},{6,10},{8,12},{10,14},{16,20},{18,22},{20,24},{2... | collective-permute-start | bytes 1572872 | tf_op jit(solution)/shard_map/ppermute | solution.py:23
  55.1 0.1 constant_dynamic-slice_fusion
  55.2 0.1 copy.6
  55.3 1.1 %broadcast_select_fusion.4 = bf16[2,128,1024]{2,1,0:T(8,128)(2,1)S(1)} fusion(bf16[2,128,1024]{2,1,0:T(8,128)(2,1)} %collective-permute-done.2, bf16[2,128,1024]{2,1,0:T(8,128)(2,1)} %broadcast_select_fusion.3, pred[]{:T(512)S(6)} %and.49), kind=kLoop, calls=%fused_computation.21 | loop fusion | flops 262144 | bytes 1572865 | tf_op jit(solution)/shard_map/jit(_where)/select_n | solution.py:69
  56.4 2.1 %collective-permute-start.3 = (bf16[2,128,1024]{2,1,0:T(8,128)(2,1)S(1)}, bf16[2,128,1024]{2,1,0:T(8,128)(2,1)}, u32[]{:S(2)}, u32[]{:S(2)}) collective-permute-start(bf16[2,128,1024]{2,1,0:T(8,128)(2,1)S(1)} %broadcast_select_fusion.4), channel_id=1, source_target_pairs={{0,1},{2,3},{4,5},{6,7},{8,9},{10,11},{12,13},{14,15},{16,17},{18,... | collective-permute-start | bytes 1572872 | tf_op jit(solution)/shard_map/ppermute | solution.py:66
  58.5 0.7 compare_convert_fusion.diag_ref
  59.1 0.6 fusion.7.slot_ref
  59.8 0.2 select_dynamic-update-slice_fusion.1
  60.0 2.0 %collective-permute-done.5 = bf16[2,128,1024]{2,1,0:T(8,128)(2,1)S(1)} collective-permute-done((bf16[2,128,1024]{2,1,0:T(8,128)(2,1)}, bf16[2,128,1024]{2,1,0:T(8,128)(2,1)S(1)}, u32[]{:S(2)}, u32[]{:S(2)}) %collective-permute-start.5) | collective-permute-done | bytes 524320 | tf_op jit(solution)/shard_map/ppermute | solution.py:23
  62.0 0.2 fusion.4
  62.2 1.3 %fusion.1 = bf16[2,1408,1024]{2,1,0:T(8,128)(2,1)S(1)} fusion(bf16[2,1408,1024]{2,1,0:T(8,128)(2,1)S(1)} %fusion.4, bf16[2,2,256,1024]{3,2,1,0:T(8,128)(2,1)} %collective-permute-done.10), kind=kLoop, calls=%fused_computation.9 | loop fusion | bytes 2097152
  63.5 2.2 %select_dynamic-update-slice_fusion = bf16[2,1408,1024]{2,1,0:T(8,128)(2,1)S(1)} fusion(bf16[2,1408,1024]{2,1,0:T(8,128)(2,1)S(1)} %fusion.1, pred[]{:T(512)S(6)} %eq.39, bf16[2,256,1024]{2,1,0:T(8,128)(2,1)} %collective-permute-done.7, bf16[2,256,1024]{2,1,0:T(8,128)(2,1)S(1)} %collective-permute-done.8, pred[]{:T(512)S(6)} %eq.40, ...), kind=kLoop, calls=%fused_computation.10 | loop fusion | flops 1572864 | bytes 4194306
  65.7 1.3 %fusion = bf16[2,1408,1024]{2,1,0:T(8,128)(2,1)S(1)} fusion(bf16[2,1408,1024]{2,1,0:T(8,128)(2,1)S(1)} %select_dynamic-update-slice_fusion, bf16[2,2,256,1024]{3,2,1,0:T(8,128)(2,1)} %collective-permute-done.10), kind=kLoop, calls=%fused_computation.7 | loop fusion | bytes 2097152
  67.1 0.1 constant_dynamic-update-slice_fusion
  67.1 2.5 %copy-done.3 = bf16[2,1408,1024]{2,1,0:T(8,128)(2,1)} copy-done((bf16[2,1408,1024]{2,1,0:T(8,128)(2,1)}, bf16[2,1408,1024]{2,1,0:T(8,128)(2,1)S(1)}, u32[]{:S(2)}) %copy-start.3) | copy-done | bytes 5767192
  69.6 38.4 %shard_map.46 = bf16[256,4096]{1,0:T(8,128)(2,1)} custom-call(s32[2,11]{1,0:T(2,128)} %fusion.7.slot_ref, s32[2,11]{1,0:T(2,128)} %compare_convert_fusion.diag_ref, bf16[256,4096]{1,0:T(8,128)(2,1)} %q_ref.1, bf16[2,11,128,1024]{3,2,1,0:T(8,128)(2,1)} %bitcast.25, bf16[2,11,128,1024]{3,2,1,0:T(8,128)(2,1)} %bitcast.26), custom_call_target="tpu_custom_call" | custom-call | flops 5905580032 | bytes 9961472 | tf_op jit(solution)/shard_map/pallas_call | solution.py:126
  (18 shorter events, 0.1 us)
Async XLA Ops:
  0.0 55.1 %copy-start = (s32[32,11]{0,1:T(8,128)S(1)}, s32[32,11]{0,1:T(8,128)}, u32[]{:S(2)}) copy-start(s32[32,11]{0,1:T(8,128)} %param.7) | copy-start | bytes 4228
  2.3 12.5 %collective-permute-start.4 = (bf16[2,256,1024]{2,1,0:T(8,128)(2,1)}, bf16[2,256,1024]{2,1,0:T(8,128)(2,1)S(1)}, u32[]{:S(2)}, u32[]{:S(2)}) collective-permute-start(bf16[2,256,1024]{2,1,0:T(8,128)(2,1)} %get-tuple-element.8), channel_id=1, source_target_pairs={{1,5},{3,7},{5,9},{7,11},{9,13},{11,15},{17,21},{19,23},{21,25},{2... | collective-permute-start | bytes 3145736 | tf_op jit(solution)/shard_map/ppermute | solution.py:23
  3.0 17.3 %collective-permute-start.6 = (bf16[2,256,1024]{2,1,0:T(8,128)(2,1)}, bf16[2,256,1024]{2,1,0:T(8,128)(2,1)}, u32[]{:S(2)}, u32[]{:S(2)}) collective-permute-start(bf16[2,256,1024]{2,1,0:T(8,128)(2,1)} %get-tuple-element.8), channel_id=1, source_target_pairs={{2,0},{6,4},{10,8},{14,12},{18,16},{22,20},{26,24},{30,28}} | collective-permute-start | bytes 3145736 | tf_op jit(solution)/shard_map/ppermute | solution.py:23
  6.7 19.3 %collective-permute-start = (bf16[2,128,1024]{2,1,0:T(8,128)(2,1)}, bf16[2,128,1024]{2,1,0:T(8,128)(2,1)}, u32[]{:S(2)}, u32[]{:S(2)}) collective-permute-start(bf16[2,128,1024]{2,1,0:T(8,128)(2,1)} %get-tuple-element.10), channel_id=1, source_target_pairs={{0,8},{16,24}} | collective-permute-start | bytes 1572872 | tf_op jit(solution)/shard_map/ppermute | solution.py:66
  13.4 33.8 %collective-permute-start.8 = (bf16[2,256,1024]{2,1,0:T(8,128)(2,1)}, bf16[2,256,1024]{2,1,0:T(8,128)(2,1)S(1)}, u32[]{:S(2)}, u32[]{:S(2)}) collective-permute-start(bf16[2,256,1024]{2,1,0:T(8,128)(2,1)} %get-tuple-element.8), channel_id=1, source_target_pairs={{0,2},{1,3},{4,6},{5,7},{8,10},{9,11},{12,14},{13,15},{16,18},{17,... | collective-permute-start | bytes 3145736 | tf_op jit(solution)/shard_map/ppermute | solution.py:23
  14.8 32.4 %collective-permute-start.9 = (bf16[2,256,1024]{2,1,0:T(8,128)(2,1)S(1)}, bf16[2,256,1024]{2,1,0:T(8,128)(2,1)}, u32[]{:S(2)}, u32[]{:S(2)}) collective-permute-start(bf16[2,256,1024]{2,1,0:T(8,128)(2,1)S(1)} %collective-permute-done.4), channel_id=1, source_target_pairs={{3,1},{7,5},{11,9},{15,13},{19,17},{23,21},{27,25},{31,29}} | collective-permute-start | bytes 3145736 | tf_op jit(solution)/shard_map/ppermute | solution.py:23
  20.4 26.9 %collective-permute-start.7 = (bf16[2,256,1024]{2,1,0:T(8,128)(2,1)}, bf16[2,256,1024]{2,1,0:T(8,128)(2,1)}, u32[]{:S(2)}, u32[]{:S(2)}) collective-permute-start(bf16[2,256,1024]{2,1,0:T(8,128)(2,1)} %collective-permute-done.6), channel_id=1, source_target_pairs={{0,4},{4,8},{8,12},{16,20},{20,24},{24,28}} | collective-permute-start | bytes 3145736 | tf_op jit(solution)/shard_map/ppermute | solution.py:23
  27.9 15.3 %collective-permute-start.1 = (bf16[2,128,1024]{2,1,0:T(8,128)(2,1)}, bf16[2,128,1024]{2,1,0:T(8,128)(2,1)}, u32[]{:S(2)}, u32[]{:S(2)}) collective-permute-start(bf16[2,128,1024]{2,1,0:T(8,128)(2,1)} %broadcast_select_fusion.2), channel_id=1, source_target_pairs={{0,4},{8,12},{16,20},{24,28}} | collective-permute-start | bytes 1572872 | tf_op jit(solution)/shard_map/ppermute | solution.py:66
  45.1 10.2 %collective-permute-start.2 = (bf16[2,128,1024]{2,1,0:T(8,128)(2,1)}, bf16[2,128,1024]{2,1,0:T(8,128)(2,1)}, u32[]{:S(2)}, u32[]{:S(2)}) collective-permute-start(bf16[2,128,1024]{2,1,0:T(8,128)(2,1)} %broadcast_select_fusion.3), channel_id=1, source_target_pairs={{0,2},{4,6},{8,10},{12,14},{16,18},{20,22},{24,26},{28,30}} | collective-permute-start | bytes 1572872 | tf_op jit(solution)/shard_map/ppermute | solution.py:66
  50.7 11.6 %collective-permute-start.10 = (bf16[2,2,256,1024]{3,2,1,0:T(8,128)(2,1)}, bf16[2,2,256,1024]{3,2,1,0:T(8,128)(2,1)}, u32[]{:S(2)}, u32[]{:S(2)}) collective-permute-start(bf16[2,2,256,1024]{3,2,1,0:T(8,128)(2,1)} %maximum_select_fusion), channel_id=1, source_target_pairs={{0,1},{1,0},{2,3},{3,2},{4,5},{5,4},{6,7},{7,6},{8,9},{9,8},{10,11... | collective-permute-start | bytes 6291464 | tf_op jit(solution)/shard_map/ppermute | solution.py:44
  50.7 11.4 %collective-permute-start.5 = (bf16[2,128,1024]{2,1,0:T(8,128)(2,1)}, bf16[2,128,1024]{2,1,0:T(8,128)(2,1)S(1)}, u32[]{:S(2)}, u32[]{:S(2)}) collective-permute-start(bf16[2,128,1024]{2,1,0:T(8,128)(2,1)} %get-tuple-element.9), channel_id=1, source_target_pairs={{0,4},{2,6},{4,8},{6,10},{8,12},{10,14},{16,20},{18,22},{20,24},{2... | collective-permute-start | bytes 1572872 | tf_op jit(solution)/shard_map/ppermute | solution.py:23
  56.4 3.4 %collective-permute-start.3 = (bf16[2,128,1024]{2,1,0:T(8,128)(2,1)S(1)}, bf16[2,128,1024]{2,1,0:T(8,128)(2,1)}, u32[]{:S(2)}, u32[]{:S(2)}) collective-permute-start(bf16[2,128,1024]{2,1,0:T(8,128)(2,1)S(1)} %broadcast_select_fusion.4), channel_id=1, source_target_pairs={{0,1},{2,3},{4,5},{6,7},{8,9},{10,11},{12,13},{14,15},{16,17},{18,... | collective-permute-start | bytes 1572872 | tf_op jit(solution)/shard_map/ppermute | solution.py:66
  59.9 7.1 %copy-start.1 = (bf16[256,1024]{1,0:T(8,128)(2,1)S(1)}, bf16[256,1024]{1,0:T(8,128)(2,1)}, u32[]{:S(2)}) copy-start(bf16[256,1024]{1,0:T(8,128)(2,1)} %param.5) | copy-start | bytes 1572868
  60.0 7.1 %copy-start.2 = (bf16[256,1024]{1,0:T(8,128)(2,1)S(1)}, bf16[256,1024]{1,0:T(8,128)(2,1)}, u32[]{:S(2)}) copy-start(bf16[256,1024]{1,0:T(8,128)(2,1)} %param.6) | copy-start | bytes 1572868
  67.1 2.5 %copy-start.3 = (bf16[2,1408,1024]{2,1,0:T(8,128)(2,1)}, bf16[2,1408,1024]{2,1,0:T(8,128)(2,1)S(1)}, u32[]{:S(2)}) copy-start(bf16[2,1408,1024]{2,1,0:T(8,128)(2,1)S(1)} %constant_dynamic-update-slice_fusion) | copy-start | bytes 17301508

commit v6 on v4

--- a/solution.py
+++ b/solution.py
@@ -121,6 +121,7 @@
         grid_spec=grid_spec,
         compiler_params=pltpu.CompilerParams(
             dimension_semantics=("arbitrary", "arbitrary"),
+            vmem_limit_bytes=24 * 1024 * 1024,
         ),
         cost_estimate=pl.CostEstimate(
             flops=flops,

time: 104 us -> 102 us (0.981)
  local copies, waits for them, and re-layouts: 2.8 us -> 0.33 us
  waiting for transfers between devices: 18.1 us -> 19.2 us
  other arithmetic: 8.49 us -> 7.44 us
    unnamed x11, local copies, waits for them, and re-layouts: 2.72 us -> 0.26 us
    ppermute x4, waiting for transfers between devices: 1.29 us -> 2.39 us  [tree_broadcast(): got = lax.ppermute(held, axis, pairs)]
  transfers between devices with their start and end apart: 10 -> 10, of which waited for: 2 -> 2; matrix products, arithmetic and copies ran while one was open for 6% -> 5% of each run, Pallas kernels for 0% -> 0%
where the time goes in v6:
time: 102 us; the launch traced here: 101 us
  Pallas kernels  38.6 us (38%)
  starting transfers between devices  35.5 us (35%)
  waiting for transfers between devices  19.2 us (19%)
  other arithmetic  7.44 us (7%)
    pallas_call x1, Pallas kernels, attend(): pl.pallas_call(attend_kernel, out_shape=jax.ShapeDtypeStruct(queries.shap...  38.6 us
    ppermute x5, starting transfers between devices, shifted(): return lax.ppermute(shard, axis, pairs)  27.1 us
    ppermute x5, waiting for transfers between devices, shifted(): return lax.ppermute(shard, axis, pairs)  16.8 us
    ppermute x4, starting transfers between devices, tree_broadcast(): got = lax.ppermute(held, axis, pairs)  4.94 us
    ppermute x1, starting transfers between devices, window_blocks(): partner_back2 = lax.ppermute(back2, axis, swap_pairs)  3.46 us
    ppermute x4, waiting for transfers between devices, tree_broadcast(): got = lax.ppermute(held, axis, pairs)  2.39 us
    another operation x2, other arithmetic, per_device(): kv = jnp.stack([key_rows, value_rows])  2.38 us
    unnamed x3, other arithmetic  2.31 us
  transfers between devices with their start and end apart: 10, of which 2 were waited for; matrix products, arithmetic and copies ran while one was open for 5% of the time, Pallas kernels for 0%

profile of v6, /device:TPU:19, one launch (start us, length us, event | category | flops | bytes accessed | tf_op | source)
XLA Modules:
  0.0 101.3 jit_solution(1468679016492915284)
XLA Ops:
  0.0 1.3 %pad_maximum_fusion = bf16[2,256,1024]{2,1,0:T(8,128)(2,1)S(1)} fusion(bf16[1,256,1024]{2,1,0:T(8,128)(2,1)} %bitcast.9, bf16[1,256,1024]{2,1,0:T(8,128)(2,1)} %bitcast.5), kind=kLoop, calls=%fused_computation.1 | loop fusion | flops 524288 | bytes 2097152 | tf_op jit(solution)/shard_map/stack | solution.py:139
  1.3 3.2 %collective-permute-start.4 = (bf16[2,256,1024]{2,1,0:T(8,128)(2,1)S(1)}, bf16[2,256,1024]{2,1,0:T(8,128)(2,1)S(1)}, u32[]{:S(2)}, u32[]{:S(2)}) collective-permute-start(bf16[2,256,1024]{2,1,0:T(8,128)(2,1)S(1)} %pad_maximum_fusion), channel_id=1, source_target_pairs={{0,4},{1,5},{2,6},{3,7},{4,8},{5,9},{6,10},{7,11},{8,12},{9,13},{1... | collective-permute-start | bytes 3145736 | tf_op jit(solution)/shard_map/ppermute | solution.py:23
  4.5 1.1 %fusion = bf16[2,128,1024]{2,1,0:T(8,128)(2,1)S(1)} fusion(bf16[1,256,1024]{2,1,0:T(8,128)(2,1)} %bitcast.6, bf16[1,256,1024]{2,1,0:T(8,128)(2,1)} %bitcast.10), kind=kLoop, calls=%fused_computation.6 | loop fusion | flops 262144 | bytes 1572864 | tf_op jit(solution)/shard_map/stack | solution.py:139
  5.6 0.7 collective-permute-start
  6.3 4.2 %collective-permute-start.7 = (bf16[2,256,1024]{2,1,0:T(8,128)(2,1)S(1)}, bf16[2,256,1024]{2,1,0:T(8,128)(2,1)}, u32[]{:S(2)}, u32[]{:S(2)}) collective-permute-start(bf16[2,256,1024]{2,1,0:T(8,128)(2,1)S(1)} %pad_maximum_fusion), channel_id=1, source_target_pairs={{0,2},{1,3},{4,6},{5,7},{8,10},{9,11},{12,14},{13,15},{16,18},{17,... | collective-permute-start | bytes 3145736 | tf_op jit(solution)/shard_map/ppermute | solution.py:23
  10.5 16.8 %collective-permute-done.4 = bf16[2,256,1024]{2,1,0:T(8,128)(2,1)S(1)} collective-permute-done((bf16[2,256,1024]{2,1,0:T(8,128)(2,1)S(1)}, bf16[2,256,1024]{2,1,0:T(8,128)(2,1)S(1)}, u32[]{:S(2)}, u32[]{:S(2)}) %collective-permute-start.4) | collective-permute-done | bytes 1048608 | tf_op jit(solution)/shard_map/ppermute | solution.py:23
  27.2 1.3 %collective-permute-start.6 = (bf16[2,256,1024]{2,1,0:T(8,128)(2,1)S(1)}, bf16[2,256,1024]{2,1,0:T(8,128)(2,1)}, u32[]{:S(2)}, u32[]{:S(2)}) collective-permute-start(bf16[2,256,1024]{2,1,0:T(8,128)(2,1)S(1)} %collective-permute-done.4), channel_id=1, source_target_pairs={{2,0},{3,1},{6,4},{7,5},{10,8},{11,9},{14,12},{15,13},{18,16},{19,... | collective-permute-start | bytes 3145736 | tf_op jit(solution)/shard_map/ppermute | solution.py:23
  28.5 0.0 collective-permute-done
  28.5 1.1 %broadcast_select_fusion.1 = bf16[2,128,1024]{2,1,0:T(8,128)(2,1)S(1)} fusion(bf16[2,128,1024]{2,1,0:T(8,128)(2,1)S(1)} %collective-permute-done, pred[]{:T(512)S(6)} %and.53, bf16[1,256,1024]{2,1,0:T(8,128)(2,1)} %bitcast.11, bf16[1,256,1024]{2,1,0:T(8,128)(2,1)} %bitcast.7), kind=kLoop, calls=%fused_computation.8 | loop fusion | flops 524288 | bytes 2097153 | tf_op jit(solution)/shard_map/jit(_where)/select_n | solution.py:61
  29.6 1.5 %collective-permute-start.1 = (bf16[2,128,1024]{2,1,0:T(8,128)(2,1)S(1)}, bf16[2,128,1024]{2,1,0:T(8,128)(2,1)}, u32[]{:S(2)}, u32[]{:S(2)}) collective-permute-start(bf16[2,128,1024]{2,1,0:T(8,128)(2,1)S(1)} %broadcast_select_fusion.1), channel_id=1, source_target_pairs={{0,4},{8,12},{16,20},{24,28}} | collective-permute-start | bytes 1572872 | tf_op jit(solution)/shard_map/ppermute | solution.py:58
  31.1 0.1 broadcast_select_fusion.2
  31.2 1.5 %collective-permute-start.2 = (bf16[2,128,1024]{2,1,0:T(8,128)(2,1)S(1)}, bf16[2,128,1024]{2,1,0:T(8,128)(2,1)}, u32[]{:S(2)}, u32[]{:S(2)}) collective-permute-start(bf16[2,128,1024]{2,1,0:T(8,128)(2,1)S(1)} %broadcast_select_fusion.2), channel_id=1, source_target_pairs={{0,2},{4,6},{8,10},{12,14},{16,18},{20,22},{24,26},{28,30}} | collective-permute-start | bytes 1572872 | tf_op jit(solution)/shard_map/ppermute | solution.py:58
  32.7 1.3 %collective-permute-start.9 = (bf16[2,256,1024]{2,1,0:T(8,128)(2,1)S(1)}, bf16[2,256,1024]{2,1,0:T(8,128)(2,1)}, u32[]{:S(2)}, u32[]{:S(2)}) collective-permute-start(bf16[2,256,1024]{2,1,0:T(8,128)(2,1)S(1)} %pad_maximum_fusion), channel_id=1, source_target_pairs={{0,1},{2,3},{4,5},{6,7},{8,9},{10,11},{12,13},{14,15},{16,17},{18,... | collective-permute-start | bytes 3145736 | tf_op jit(solution)/shard_map/ppermute | solution.py:23
  34.0 0.1 constant_dynamic-slice_fusion
  34.1 0.1 copy.6
  34.2 17.2 %collective-permute-start.5 = (bf16[2,256,1024]{2,1,0:T(8,128)(2,1)S(1)}, bf16[2,256,1024]{2,1,0:T(8,128)(2,1)S(1)}, u32[]{:S(2)}, u32[]{:S(2)}) collective-permute-start(bf16[2,256,1024]{2,1,0:T(8,128)(2,1)S(1)} %collective-permute-done.4), channel_id=1, source_target_pairs={{1,0},{3,2},{5,4},{7,6},{9,8},{11,10},{13,12},{15,14},{17,16},{19,... | collective-permute-start | bytes 3145736 | tf_op jit(solution)/shard_map/ppermute | solution.py:23
  51.4 1.3 %broadcast_select_fusion = bf16[2,256,1024]{2,1,0:T(8,128)(2,1)S(1)} fusion(bf16[2,256,1024]{2,1,0:T(8,128)(2,1)} %collective-permute-done.6, bf16[2,256,1024]{2,1,0:T(8,128)(2,1)} %collective-permute-done.7, pred[]{:T(512)S(6)} %eq.40), kind=kLoop, calls=%fused_computation.5 | loop fusion | flops 524288 | bytes 3145729 | tf_op jit(solution)/shard_map/jit(_where)/select_n | solution.py:34
  52.7 3.5 %collective-permute-start.8 = (bf16[2,256,1024]{2,1,0:T(8,128)(2,1)S(1)}, bf16[2,256,1024]{2,1,0:T(8,128)(2,1)S(1)}, u32[]{:S(2)}, u32[]{:S(2)}) collective-permute-start(bf16[2,256,1024]{2,1,0:T(8,128)(2,1)S(1)} %broadcast_select_fusion), channel_id=1, source_target_pairs={{0,1},{1,0},{2,3},{3,2},{4,5},{5,4},{6,7},{7,6},{8,9},{9,8},{10,11... | collective-permute-start | bytes 3145736 | tf_op jit(solution)/shard_map/ppermute | solution.py:38
  56.2 0.1 broadcast_select_fusion.3
  56.3 1.3 %collective-permute-start.3 = (bf16[2,128,1024]{2,1,0:T(8,128)(2,1)S(1)}, bf16[2,128,1024]{2,1,0:T(8,128)(2,1)S(1)}, u32[]{:S(2)}, u32[]{:S(2)}) collective-permute-start(bf16[2,128,1024]{2,1,0:T(8,128)(2,1)S(1)} %broadcast_select_fusion.3), channel_id=1, source_target_pairs={{0,1},{2,3},{4,5},{6,7},{8,9},{10,11},{12,13},{14,15},{16,17},{18,... | collective-permute-start | bytes 1572872 | tf_op jit(solution)/shard_map/ppermute | solution.py:58
  57.6 0.1 compare_convert_fusion.diag_ref
  57.7 0.0 copy-start.2
  57.7 0.0 copy-start.3
  57.7 2.4 %collective-permute-done.3 = bf16[2,128,1024]{2,1,0:T(8,128)(2,1)S(1)} collective-permute-done((bf16[2,128,1024]{2,1,0:T(8,128)(2,1)S(1)}, bf16[2,128,1024]{2,1,0:T(8,128)(2,1)S(1)}, u32[]{:S(2)}, u32[]{:S(2)}) %collective-permute-start.3) | collective-permute-done | bytes 524320 | tf_op jit(solution)/shard_map/ppermute | solution.py:58
  60.1 0.2 select_dynamic-update-slice_fusion.2
  60.3 0.1 constant_dynamic-update-slice_fusion.2
  60.4 0.0 copy-start.1
  60.4 0.4 select_dynamic-update-slice_fusion.1
  60.8 0.1 constant_dynamic-update-slice_fusion.1
  60.9 1.7 %select_dynamic-update-slice_fusion = bf16[2,1408,1024]{2,1,0:T(8,128)(2,1)S(1)} fusion(bf16[2,1408,1024]{2,1,0:T(8,128)(2,1)S(1)} %constant_dynamic-update-slice_fusion.1, bf16[2,256,1024]{2,1,0:T(8,128)(2,1)S(1)} %collective-permute-done.8, bf16[2,256,1024]{2,1,0:T(8,128)(2,1)} %collective-permute-done.9, pred[]{:T(512)S(6)} %eq.39), kind=kLoop, calls=%fused_computation.3 | loop fusion | flops 524288 | bytes 3145729
  62.6 0.1 constant_dynamic-update-slice_fusion
  62.7 38.6 %shard_map.46 = bf16[256,4096]{1,0:T(8,128)(2,1)} custom-call(s32[2,11]{1,0:T(2,128)S(1)} %fusion.1.slot_ref, s32[2,11]{1,0:T(2,128)S(1)} %compare_convert_fusion.diag_ref, bf16[256,4096]{1,0:T(8,128)(2,1)S(1)} %copy-done.1, bf16[2,11,128,1024]{3,2,1,0:T(8,128)(2,1)S(1)} %bitcast.3, bf16[2,11,128,1024]{3,2,1,0:T(8,128)(2,1)S(1)} %bitcast.4), custom_call_target="tpu_custom_call" | custom-call | flops 5905580032 | bytes 9961472 | tf_op jit(solution)/shard_map/pallas_call | solution.py:118
  (14 shorter events, 0.0 us)
Async XLA Ops:
  0.0 34.0 %copy-start = (s32[32,11]{0,1:T(8,128)S(1)}, s32[32,11]{0,1:T(8,128)}, u32[]{:S(2)}) copy-start(s32[32,11]{0,1:T(8,128)} %param.7) | copy-start | bytes 4228
  1.3 25.9 %collective-permute-start.4 = (bf16[2,256,1024]{2,1,0:T(8,128)(2,1)S(1)}, bf16[2,256,1024]{2,1,0:T(8,128)(2,1)S(1)}, u32[]{:S(2)}, u32[]{:S(2)}) collective-permute-start(bf16[2,256,1024]{2,1,0:T(8,128)(2,1)S(1)} %pad_maximum_fusion), channel_id=1, source_target_pairs={{0,4},{1,5},{2,6},{3,7},{4,8},{5,9},{6,10},{7,11},{8,12},{9,13},{1... | collective-permute-start | bytes 3145736 | tf_op jit(solution)/shard_map/ppermute | solution.py:23
  5.6 22.9 %collective-permute-start = (bf16[2,128,1024]{2,1,0:T(8,128)(2,1)S(1)}, bf16[2,128,1024]{2,1,0:T(8,128)(2,1)S(1)}, u32[]{:S(2)}, u32[]{:S(2)}) collective-permute-start(bf16[2,128,1024]{2,1,0:T(8,128)(2,1)S(1)} %fusion), channel_id=1, source_target_pairs={{0,8},{16,24}} | collective-permute-start | bytes 1572872 | tf_op jit(solution)/shard_map/ppermute | solution.py:58
  6.3 45.1 %collective-permute-start.7 = (bf16[2,256,1024]{2,1,0:T(8,128)(2,1)S(1)}, bf16[2,256,1024]{2,1,0:T(8,128)(2,1)}, u32[]{:S(2)}, u32[]{:S(2)}) collective-permute-start(bf16[2,256,1024]{2,1,0:T(8,128)(2,1)S(1)} %pad_maximum_fusion), channel_id=1, source_target_pairs={{0,2},{1,3},{4,6},{5,7},{8,10},{9,11},{12,14},{13,15},{16,18},{17,... | collective-permute-start | bytes 3145736 | tf_op jit(solution)/shard_map/ppermute | solution.py:23
  27.2 24.2 %collective-permute-start.6 = (bf16[2,256,1024]{2,1,0:T(8,128)(2,1)S(1)}, bf16[2,256,1024]{2,1,0:T(8,128)(2,1)}, u32[]{:S(2)}, u32[]{:S(2)}) collective-permute-start(bf16[2,256,1024]{2,1,0:T(8,128)(2,1)S(1)} %collective-permute-done.4), channel_id=1, source_target_pairs={{2,0},{3,1},{6,4},{7,5},{10,8},{11,9},{14,12},{15,13},{18,16},{19,... | collective-permute-start | bytes 3145736 | tf_op jit(solution)/shard_map/ppermute | solution.py:23
  29.6 1.5 %collective-permute-start.1 = (bf16[2,128,1024]{2,1,0:T(8,128)(2,1)S(1)}, bf16[2,128,1024]{2,1,0:T(8,128)(2,1)}, u32[]{:S(2)}, u32[]{:S(2)}) collective-permute-start(bf16[2,128,1024]{2,1,0:T(8,128)(2,1)S(1)} %broadcast_select_fusion.1), channel_id=1, source_target_pairs={{0,4},{8,12},{16,20},{24,28}} | collective-permute-start | bytes 1572872 | tf_op jit(solution)/shard_map/ppermute | solution.py:58
  31.2 25.0 %collective-permute-start.2 = (bf16[2,128,1024]{2,1,0:T(8,128)(2,1)S(1)}, bf16[2,128,1024]{2,1,0:T(8,128)(2,1)}, u32[]{:S(2)}, u32[]{:S(2)}) collective-permute-start(bf16[2,128,1024]{2,1,0:T(8,128)(2,1)S(1)} %broadcast_select_fusion.2), channel_id=1, source_target_pairs={{0,2},{4,6},{8,10},{12,14},{16,18},{20,22},{24,26},{28,30}} | collective-permute-start | bytes 1572872 | tf_op jit(solution)/shard_map/ppermute | solution.py:58
  32.7 28.2 %collective-permute-start.9 = (bf16[2,256,1024]{2,1,0:T(8,128)(2,1)S(1)}, bf16[2,256,1024]{2,1,0:T(8,128)(2,1)}, u32[]{:S(2)}, u32[]{:S(2)}) collective-permute-start(bf16[2,256,1024]{2,1,0:T(8,128)(2,1)S(1)} %pad_maximum_fusion), channel_id=1, source_target_pairs={{0,1},{2,3},{4,5},{6,7},{8,9},{10,11},{12,13},{14,15},{16,17},{18,... | collective-permute-start | bytes 3145736 | tf_op jit(solution)/shard_map/ppermute | solution.py:23
  34.2 26.2 %collective-permute-start.5 = (bf16[2,256,1024]{2,1,0:T(8,128)(2,1)S(1)}, bf16[2,256,1024]{2,1,0:T(8,128)(2,1)S(1)}, u32[]{:S(2)}, u32[]{:S(2)}) collective-permute-start(bf16[2,256,1024]{2,1,0:T(8,128)(2,1)S(1)} %collective-permute-done.4), channel_id=1, source_target_pairs={{1,0},{3,2},{5,4},{7,6},{9,8},{11,10},{13,12},{15,14},{17,16},{19,... | collective-permute-start | bytes 3145736 | tf_op jit(solution)/shard_map/ppermute | solution.py:23
  52.7 7.6 %collective-permute-start.8 = (bf16[2,256,1024]{2,1,0:T(8,128)(2,1)S(1)}, bf16[2,256,1024]{2,1,0:T(8,128)(2,1)S(1)}, u32[]{:S(2)}, u32[]{:S(2)}) collective-permute-start(bf16[2,256,1024]{2,1,0:T(8,128)(2,1)S(1)} %broadcast_select_fusion), channel_id=1, source_target_pairs={{0,1},{1,0},{2,3},{3,2},{4,5},{5,4},{6,7},{7,6},{8,9},{9,8},{10,11... | collective-permute-start | bytes 3145736 | tf_op jit(solution)/shard_map/ppermute | solution.py:38
  56.3 3.8 %collective-permute-start.3 = (bf16[2,128,1024]{2,1,0:T(8,128)(2,1)S(1)}, bf16[2,128,1024]{2,1,0:T(8,128)(2,1)S(1)}, u32[]{:S(2)}, u32[]{:S(2)}) collective-permute-start(bf16[2,128,1024]{2,1,0:T(8,128)(2,1)S(1)} %broadcast_select_fusion.3), channel_id=1, source_target_pairs={{0,1},{2,3},{4,5},{6,7},{8,9},{10,11},{12,13},{14,15},{16,17},{18,... | collective-permute-start | bytes 1572872 | tf_op jit(solution)/shard_map/ppermute | solution.py:58
  57.7 4.9 %copy-start.2 = (bf16[256,1024]{1,0:T(8,128)(2,1)S(1)}, bf16[256,1024]{1,0:T(8,128)(2,1)}, u32[]{:S(2)}) copy-start(bf16[256,1024]{1,0:T(8,128)(2,1)} %param.5) | copy-start | bytes 1572868
  57.7 4.9 %copy-start.3 = (bf16[256,1024]{1,0:T(8,128)(2,1)S(1)}, bf16[256,1024]{1,0:T(8,128)(2,1)}, u32[]{:S(2)}) copy-start(bf16[256,1024]{1,0:T(8,128)(2,1)} %param.6) | copy-start | bytes 1572868
  60.4 2.4 %copy-start.1 = (bf16[256,4096]{1,0:T(8,128)(2,1)S(1)}, bf16[256,4096]{1,0:T(8,128)(2,1)}, u32[]{:S(2)}) copy-start(bf16[256,4096]{1,0:T(8,128)(2,1)} %q_ref.1) | copy-start | bytes 6291460

commit v7 on v6

--- a/solution.py
+++ b/solution.py
@@ -23,22 +23,31 @@
     return lax.ppermute(shard, axis, pairs)
 
 
-def window_blocks(kv, axis):
-    index = lax.axis_index(axis)
-    y_low = (index // 2) % 2 == 0
-    core0 = index % 2 == 0
+def window_start(kv, axis, gate=None):
+    if gate is not None:
+        kv, gate = lax.optimization_barrier((kv, gate))
     back4 = shifted(kv, axis, 4, lambda i: True)
     up_y = shifted(kv, axis, 2, lambda i: (i // 2) % 2 == 0)
     next_core = shifted(kv, axis, 1, lambda i: i % 2 == 0)
     down_y = shifted(back4, axis, -2, lambda i: (i // 2) % 2 == 1)
+    partner_back4 = shifted(back4, axis, -1, lambda i: i % 2 == 1)
+    return back4, up_y, next_core, down_y, partner_back4
+
+
+def window_finish(started, axis, hold=None):
+    back4, up_y, next_core, down_y, partner_back4 = started
+    index = lax.axis_index(axis)
+    size = lax.axis_size(axis)
+    y_low = (index // 2) % 2 == 0
+    core0 = index % 2 == 0
+    if hold is not None:
+        down_y, hold = lax.optimization_barrier((down_y, hold))
     back2 = jnp.where(y_low, down_y, up_y)
-    partner_back4 = shifted(back4, axis, -1, lambda i: i % 2 == 1)
-    size = lax.axis_size(axis)
     swap_pairs = [(i, i ^ 1) for i in range(size)]
     partner_back2 = lax.ppermute(back2, axis, swap_pairs)
     back3 = jnp.where(core0, partner_back4, partner_back2)
     back1 = jnp.where(core0, partner_back2, next_core)
-    return [back4, back3, back2, back1]
+    return [back4, back3, back2, back1], hold
 
 
 def tree_broadcast(block, axis, source, size):
@@ -97,38 +106,53 @@
     )
 
 
-def attend(slots, diag, queries, kv_buffer):
+def attend(slots, diag, queries, kv_buffer, first_head, into=None):
     blocks_here = queries.shape[0] // BLK
     buffer_blocks = kv_buffer.shape[1]
-    flops = 4 * blocks_here * H * BLK * LIST * BLK * HD
+    heads = kv_buffer.shape[3] // HD
+    flops = 4 * blocks_here * heads * GROUP * BLK * LIST * BLK * HD
+    head_block = first_head
+    in_specs = [
+        pl.BlockSpec((BLK, GROUP * HD), lambda g, b, *_: (b, g + head_block)),
+        pl.BlockSpec((1, buffer_blocks, BLK, HD), lambda g, b, *_: (0, 0, 0, g)),
+        pl.BlockSpec((1, buffer_blocks, BLK, HD), lambda g, b, *_: (1, 0, 0, g)),
+    ]
+    operands = [slots, diag, queries, kv_buffer, kv_buffer]
+    aliases = {}
+    if into is not None:
+        in_specs.append(pl.BlockSpec(memory_space=pl.ANY))
+        operands.append(into)
+        aliases = {len(operands) - 1: 0}
     grid_spec = pltpu.PrefetchScalarGridSpec(
         num_scalar_prefetch=2,
-        grid=(KVH, blocks_here),
-        in_specs=[
-            pl.BlockSpec((BLK, GROUP * HD), lambda g, b, *_: (b, g)),
-            pl.BlockSpec((1, buffer_blocks, BLK, HD), lambda g, b, *_: (0, 0, 0, g)),
-            pl.BlockSpec((1, buffer_blocks, BLK, HD), lambda g, b, *_: (1, 0, 0, g)),
-        ],
-        out_specs=pl.BlockSpec((BLK, GROUP * HD), lambda g, b, *_: (b, g)),
+        grid=(heads, blocks_here),
+        in_specs=in_specs,
+        out_specs=pl.BlockSpec((BLK, GROUP * HD), lambda g, b, *_: (b, g + head_block)),
         scratch_shapes=[
             pltpu.VMEM((LIST, GROUP * BLK, BLK), jnp.float32),
             pltpu.VMEM((2, GROUP * BLK, BLK), jnp.float32),
         ],
     )
+    kernel = attend_kernel if into is None else aliased_kernel
     return pl.pallas_call(
-        attend_kernel,
+        kernel,
         out_shape=jax.ShapeDtypeStruct(queries.shape, jnp.bfloat16),
         grid_spec=grid_spec,
+        input_output_aliases=aliases,
         compiler_params=pltpu.CompilerParams(
             dimension_semantics=("arbitrary", "arbitrary"),
             vmem_limit_bytes=24 * 1024 * 1024,
         ),
         cost_estimate=pl.CostEstimate(
             flops=flops,
-            transcendentals=blocks_here * H * BLK * LIST * BLK,
-            bytes_accessed=2 * queries.size * 2 + kv_buffer.size * 2,
+            transcendentals=blocks_here * heads * GROUP * BLK * LIST * BLK,
+            bytes_accessed=2 * queries.size * heads // KVH * 2 + kv_buffer.size * 2,
         ),
-    )(slots, diag, queries, kv_buffer, kv_buffer)
+    )(*operands)
+
+
+def aliased_kernel(slot_ref, diag_ref, q_ref, k_ref, v_ref, into_ref, o_ref, score_sc, bias_sc):
+    attend_kernel(slot_ref, diag_ref, q_ref, k_ref, v_ref, o_ref, score_sc, bias_sc)
 
 
 def per_device(queries, key_rows, value_rows, pattern):
@@ -138,7 +162,6 @@
     own_index = lax.axis_index("ctx")
     kv = jnp.stack([key_rows, value_rows])
     assert blocks_here == 2 and ctx_count % 4 == 0
-    early = window_blocks(kv, "ctx")
     columns = blocks_here * ctx_count // STRIDE
     spread = STRIDE // blocks_here
     column_blocks = [
@@ -146,9 +169,18 @@
         for column in range(columns)
     ]
     buffer_blocks = columns + 4 * blocks_here + blocks_here
-    kv_buffer = jnp.concatenate(column_blocks + early + [kv], axis=1).reshape(
-        2, buffer_blocks, BLK, kv.shape[2]
-    )
+    half = kv.shape[2] // 2
+    chunks = [kv[:, :, :half], kv[:, :, half:]]
+    first_started = window_start(chunks[0], "ctx")
+    second_started = window_start(chunks[1], "ctx", gate=first_started[0])
+    first, _ = window_finish(first_started, "ctx")
+
+    def slab(pieces, part):
+        cols = [c[:, :, part * half:(part + 1) * half] for c in column_blocks]
+        return jnp.concatenate(cols + pieces + [chunks[part]], axis=1).reshape(
+            2, buffer_blocks, BLK, half
+        )
+
     first_block = own_index * blocks_here - 4 * blocks_here
     rows_pattern = lax.dynamic_slice_in_dim(pattern, own_index * blocks_here, blocks_here, 0)
     slots = jnp.where(
@@ -159,7 +191,10 @@
     slots = jnp.clip(slots, 0, buffer_blocks - 1).astype(jnp.int32)
     blocks = own_index * blocks_here + jnp.arange(blocks_here, dtype=jnp.int32)
     diag = (rows_pattern == blocks[:, None]).astype(jnp.int32)
-    return attend(slots, diag, queries, kv_buffer)
+    slab_first, _ = lax.optimization_barrier((slab(first, 0), second_started[0]))
+    out = attend(slots, diag, queries, slab_first, 0)
+    second, out = window_finish(second_started, "ctx", hold=out)
+    return attend(slots, diag, queries, slab(second, 1), KVH // 2, into=out)
 
 
 def solution(mesh):

time: 102 us -> 109 us (1.069)
  starting transfers between devices: 35.5 us -> 52.7 us
  waiting for transfers between devices: 19.2 us -> 8.25 us
  other arithmetic: 7.44 us -> 4.41 us
  local copies, waits for them, and re-layouts: 0.33 us -> 2.53 us
    ppermute x5 -> x10, starting transfers between devices: 27.1 us -> 47.7 us  [shifted(): return lax.ppermute(shard, axis, pairs)]
    ppermute x5 -> x10, waiting for transfers between devices: 16.8 us -> 8.23 us  [shifted(): return lax.ppermute(shard, axis, pairs)]
    ppermute x1 -> x2, starting transfers between devices: 3.46 us -> 0.14 us  [window_finish(): partner_back2 = lax.ppermute(back2, axis, swap_pairs)]
    ppermute x4, waiting for transfers between devices: 2.39 us -> 0.01 us  [tree_broadcast(): got = lax.ppermute(held, axis, pairs)]
    unnamed x11 -> x14, local copies, waits for them, and re-layouts: 0.26 us -> 2.38 us
    unnamed x3 -> x4, other arithmetic: 2.31 us -> 0.57 us
    another operation x2, other arithmetic: 2.38 us -> 1.26 us  [per_device(): kv = jnp.stack([key_rows, value_rows])]
    pallas_call x1 -> x2, Pallas kernels: 38.6 us -> 39.3 us  [attend(): pl.pallas_call(kernel, out_shape=jax.ShapeDtypeStruct(queries.shape, jnp....]
  transfers between devices with their start and end apart: 10 -> 16, of which waited for: 2 -> 3; matrix products, arithmetic and copies ran while one was open for 5% -> 4% of each run, Pallas kernels for 0% -> 18%
where the time goes in v7:
time: 109 us; the launch traced here: 108 us
  starting transfers between devices  52.7 us (48%)
  Pallas kernels  39.3 us (36%)
  waiting for transfers between devices  8.25 us (8%)
  other arithmetic  4.41 us (4%)
  local copies, waits for them, and re-layouts  2.53 us (2%)
    ppermute x10, starting transfers between devices, shifted(): return lax.ppermute(shard, axis, pairs)  47.7 us
    pallas_call x2, Pallas kernels, attend(): pl.pallas_call(kernel, out_shape=jax.ShapeDtypeStruct(queries.shape, jnp....  39.3 us
    ppermute x10, waiting for transfers between devices, shifted(): return lax.ppermute(shard, axis, pairs)  8.23 us
    ppermute x4, starting transfers between devices, tree_broadcast(): got = lax.ppermute(held, axis, pairs)  4.91 us
    unnamed x14, local copies, waits for them, and re-layouts  2.38 us
  transfers between devices with their start and end apart: 16, of which 3 were waited for; matrix products, arithmetic and copies ran while one was open for 4% of the time, Pallas kernels for 18%

profile of v7, /device:TPU:19, one launch (start us, length us, event | category | flops | bytes accessed | tf_op | source)
XLA Modules:
  0.0 107.6 jit_solution(11467885020162533513)
XLA Ops:
  0.0 1.2 %fusion.1 = bf16[2,128,1024]{2,1,0:T(8,128)(2,1)S(1)} fusion(bf16[1,256,1024]{2,1,0:T(8,128)(2,1)} %bitcast.8, bf16[1,256,1024]{2,1,0:T(8,128)(2,1)} %bitcast.11), kind=kLoop, calls=%fused_computation.5 | loop fusion | flops 262144 | bytes 1572864 | tf_op jit(solution)/shard_map/stack | solution.py:163
  1.2 0.7 collective-permute-start
  1.9 1.1 %broadcast_select_fusion.2 = bf16[2,128,1024]{2,1,0:T(8,128)(2,1)S(1)} fusion(bf16[2,128,1024]{2,1,0:T(8,128)(2,1)S(1)} %collective-permute-done, pred[]{:T(512)S(6)} %and.56, bf16[1,256,1024]{2,1,0:T(8,128)(2,1)} %bitcast.12, bf16[1,256,1024]{2,1,0:T(8,128)(2,1)} %bitcast.9), kind=kLoop, calls=%fused_computation.13 | loop fusion | flops 524288 | bytes 2097153 | tf_op jit(solution)/shard_map/jit(_where)/select_n | solution.py:70
  3.0 1.5 %collective-permute-start.1 = (bf16[2,128,1024]{2,1,0:T(8,128)(2,1)S(1)}, bf16[2,128,1024]{2,1,0:T(8,128)(2,1)}, u32[]{:S(2)}, u32[]{:S(2)}) collective-permute-start(bf16[2,128,1024]{2,1,0:T(8,128)(2,1)S(1)} %broadcast_select_fusion.2), channel_id=1, source_target_pairs={{0,4},{8,12},{16,20},{24,28}} | collective-permute-start | bytes 1572872 | tf_op jit(solution)/shard_map/ppermute | solution.py:67
  4.5 0.1 pad_maximum_fusion
  4.6 3.2 %collective-permute-start.4 = (bf16[2,256,512]{2,1,0:T(8,128)(2,1)S(1)}, bf16[2,256,512]{2,1,0:T(8,128)(2,1)}, u32[]{:S(2)}, u32[]{:S(2)}) collective-permute-start(bf16[2,256,512]{2,1,0:T(8,128)(2,1)S(1)} %get-tuple-element.13), channel_id=1, source_target_pairs={{0,4},{1,5},{2,6},{3,7},{4,8},{5,9},{6,10},{7,11},{8,12},{9,13},{1... | collective-permute-start | bytes 1572872 | tf_op jit(solution)/shard_map/ppermute | solution.py:23
  7.8 0.1 broadcast_select_fusion.3
  7.9 1.5 %collective-permute-start.2 = (bf16[2,128,1024]{2,1,0:T(8,128)(2,1)S(1)}, bf16[2,128,1024]{2,1,0:T(8,128)(2,1)}, u32[]{:S(2)}, u32[]{:S(2)}) collective-permute-start(bf16[2,128,1024]{2,1,0:T(8,128)(2,1)S(1)} %broadcast_select_fusion.3), channel_id=1, source_target_pairs={{0,2},{4,6},{8,10},{12,14},{16,18},{20,22},{24,26},{28,30}} | collective-permute-start | bytes 1572872 | tf_op jit(solution)/shard_map/ppermute | solution.py:67
  9.4 4.0 %collective-permute-start.10 = (bf16[2,256,512]{2,1,0:T(8,128)(2,1)S(1)}, bf16[2,256,512]{2,1,0:T(8,128)(2,1)}, u32[]{:S(2)}, u32[]{:S(2)}) collective-permute-start(bf16[2,256,512]{2,1,0:T(8,128)(2,1)S(1)} %get-tuple-element.13), channel_id=1, source_target_pairs={{0,2},{1,3},{4,6},{5,7},{8,10},{9,11},{12,14},{13,15},{16,18},{17,... | collective-permute-start | bytes 1572872 | tf_op jit(solution)/shard_map/ppermute | solution.py:23
  13.3 1.3 %collective-permute-start.12 = (bf16[2,256,512]{2,1,0:T(8,128)(2,1)S(1)}, bf16[2,256,512]{2,1,0:T(8,128)(2,1)S(1)}, u32[]{:S(2)}, u32[]{:S(2)}) collective-permute-start(bf16[2,256,512]{2,1,0:T(8,128)(2,1)S(1)} %get-tuple-element.13), channel_id=1, source_target_pairs={{0,1},{2,3},{4,5},{6,7},{8,9},{10,11},{12,13},{14,15},{16,17},{18,... | collective-permute-start | bytes 1572872 | tf_op jit(solution)/shard_map/ppermute | solution.py:23
  14.7 0.1 copy.7
  14.8 4.1 %collective-permute-done.4 = bf16[2,256,512]{2,1,0:T(8,128)(2,1)} collective-permute-done((bf16[2,256,512]{2,1,0:T(8,128)(2,1)S(1)}, bf16[2,256,512]{2,1,0:T(8,128)(2,1)}, u32[]{:S(2)}, u32[]{:S(2)}) %collective-permute-start.4) | collective-permute-done | bytes 524320 | tf_op jit(solution)/shard_map/ppermute | solution.py:23
  18.9 1.9 %collective-permute-start.5 = (bf16[2,256,512]{2,1,0:T(8,128)(2,1)S(1)}, bf16[2,256,512]{2,1,0:T(8,128)(2,1)}, u32[]{:S(2)}, u32[]{:S(2)}) collective-permute-start(bf16[2,256,512]{2,1,0:T(8,128)(2,1)S(1)} %get-tuple-element.9), channel_id=1, source_target_pairs={{0,4},{1,5},{2,6},{3,7},{4,8},{5,9},{6,10},{7,11},{8,12},{9,13},{1... | collective-permute-start | bytes 1572872 | tf_op jit(solution)/shard_map/ppermute | solution.py:23
  20.8 1.3 %collective-permute-start.9 = (bf16[2,256,512]{2,1,0:T(8,128)(2,1)}, bf16[2,256,512]{2,1,0:T(8,128)(2,1)}, u32[]{:S(2)}, u32[]{:S(2)}) collective-permute-start(bf16[2,256,512]{2,1,0:T(8,128)(2,1)} %collective-permute-done.4), channel_id=1, source_target_pairs={{2,0},{3,1},{6,4},{7,5},{10,8},{11,9},{14,12},{15,13},{18,16},{19,... | collective-permute-start | bytes 1572872 | tf_op jit(solution)/shard_map/ppermute | solution.py:23
  22.1 0.1 broadcast_select_fusion.4
  22.2 1.3 %collective-permute-start.3 = (bf16[2,128,1024]{2,1,0:T(8,128)(2,1)S(1)}, bf16[2,128,1024]{2,1,0:T(8,128)(2,1)S(1)}, u32[]{:S(2)}, u32[]{:S(2)}) collective-permute-start(bf16[2,128,1024]{2,1,0:T(8,128)(2,1)S(1)} %broadcast_select_fusion.4), channel_id=1, source_target_pairs={{0,1},{2,3},{4,5},{6,7},{8,9},{10,11},{12,13},{14,15},{16,17},{18,... | collective-permute-start | bytes 1572872 | tf_op jit(solution)/shard_map/ppermute | solution.py:67
  23.6 5.7 %collective-permute-start.13 = (bf16[2,256,512]{2,1,0:T(8,128)(2,1)S(1)}, bf16[2,256,512]{2,1,0:T(8,128)(2,1)S(1)}, u32[]{:S(2)}, u32[]{:S(2)}) collective-permute-start(bf16[2,256,512]{2,1,0:T(8,128)(2,1)S(1)} %get-tuple-element.9), channel_id=1, source_target_pairs={{0,2},{1,3},{4,6},{5,7},{8,10},{9,11},{12,14},{13,15},{16,18},{17,... | collective-permute-start | bytes 1572872 | tf_op jit(solution)/shard_map/ppermute | solution.py:23
  29.3 2.9 %collective-permute-done.9 = bf16[2,256,512]{2,1,0:T(8,128)(2,1)} collective-permute-done((bf16[2,256,512]{2,1,0:T(8,128)(2,1)}, bf16[2,256,512]{2,1,0:T(8,128)(2,1)}, u32[]{:S(2)}, u32[]{:S(2)}) %collective-permute-start.9) | collective-permute-done | bytes 524320 | tf_op jit(solution)/shard_map/ppermute | solution.py:23
  32.3 25.2 %collective-permute-start.8 = (bf16[2,256,512]{2,1,0:T(8,128)(2,1)}, bf16[2,256,512]{2,1,0:T(8,128)(2,1)S(1)}, u32[]{:S(2)}, u32[]{:S(2)}) collective-permute-start(bf16[2,256,512]{2,1,0:T(8,128)(2,1)} %collective-permute-done.4), channel_id=1, source_target_pairs={{1,0},{3,2},{5,4},{7,6},{9,8},{11,10},{13,12},{15,14},{17,16},{19,... | collective-permute-start | bytes 1572872 | tf_op jit(solution)/shard_map/ppermute | solution.py:23
  57.5 1.1 %broadcast_select_fusion.1 = bf16[2,256,512]{2,1,0:T(8,128)(2,1)S(1)} fusion(bf16[2,256,512]{2,1,0:T(8,128)(2,1)} %collective-permute-done.9, bf16[2,256,512]{2,1,0:T(8,128)(2,1)} %collective-permute-done.10, pred[]{:T(512)S(6)} %eq.44), kind=kLoop, calls=%fused_computation.12 | loop fusion | flops 262144 | bytes 1572865 | tf_op jit(solution)/shard_map/jit(_where)/select_n | solution.py:45
  58.7 1.3 %collective-permute-start.7 = (bf16[2,256,512]{2,1,0:T(8,128)(2,1)}, bf16[2,256,512]{2,1,0:T(8,128)(2,1)S(1)}, u32[]{:S(2)}, u32[]{:S(2)}) collective-permute-start(bf16[2,256,512]{2,1,0:T(8,128)(2,1)} %collective-permute-done.5), channel_id=1, source_target_pairs={{2,0},{3,1},{6,4},{7,5},{10,8},{11,9},{14,12},{15,13},{18,16},{19,... | collective-permute-start | bytes 1572872 | tf_op jit(solution)/shard_map/ppermute | solution.py:23
  60.1 1.1 %constant_dynamic-update-slice_fusion.2 = bf16[2,1408,512]{2,1,0:T(8,128)(2,1)S(1)} fusion(bf16[2,1408,512]{2,1,0:T(8,128)(2,1)S(1)} %get-tuple-element.15, bf16[2,256,512]{2,1,0:T(8,128)(2,1)} %collective-permute-done.4), kind=kLoop, calls=%fused_computation.21 | loop fusion | bytes 1048576
  61.2 2.5 %collective-permute-start.6 = (bf16[2,256,512]{2,1,0:T(8,128)(2,1)}, bf16[2,256,512]{2,1,0:T(8,128)(2,1)S(1)}, u32[]{:S(2)}, u32[]{:S(2)}) collective-permute-start(bf16[2,256,512]{2,1,0:T(8,128)(2,1)} %collective-permute-done.5), channel_id=1, source_target_pairs={{1,0},{3,2},{5,4},{7,6},{9,8},{11,10},{13,12},{15,14},{17,16},{19,... | collective-permute-start | bytes 1572872 | tf_op jit(solution)/shard_map/ppermute | solution.py:23
  63.8 0.1 select_dynamic-update-slice_fusion.3
  64.0 0.1 select_dynamic-update-slice_fusion.2
  64.2 19.7 %shard_map.46.into_ref = bf16[256,4096]{1,0:T(8,128)(2,1)} custom-call(s32[2,11]{1,0:T(2,128)S(1)} %fusion.2.slot_ref, s32[2,11]{1,0:T(2,128)S(1)} %compare_convert_fusion.diag_ref, bf16[256,4096]{1,0:T(8,128)(2,1)S(1)} %copy-done.1, bf16[2,11,128,512]{3,2,1,0:T(8,128)(2,1)S(1)} %bitcast.6, bf16[2,11,128,512]{3,2,1,0:T(8,128)(2,1)S(1)} %bitcast.7), custom_call_target="tpu_custom_call" | custom-call | flops 2952790016 | bytes 4980736 | tf_op jit(solution)/shard_map/pallas_call | solution.py:137
  84.0 1.3 %collective-permute-start.15 = (bf16[2,256,512]{2,1,0:T(8,128)(2,1)S(1)}, bf16[2,256,512]{2,1,0:T(8,128)(2,1)S(1)}, u32[]{:S(2)}, u32[]{:S(2)}) collective-permute-start(bf16[2,256,512]{2,1,0:T(8,128)(2,1)S(1)} %get-tuple-element.9), channel_id=1, source_target_pairs={{0,1},{2,3},{4,5},{6,7},{8,9},{10,11},{12,13},{14,15},{16,17},{18,... | collective-permute-start | bytes 1572872 | tf_op jit(solution)/shard_map/ppermute | solution.py:23
  85.3 1.1 %constant_dynamic-update-slice_fusion.5 = bf16[2,1408,512]{2,1,0:T(8,128)(2,1)S(1)} fusion(bf16[2,1408,512]{2,1,0:T(8,128)(2,1)S(1)} %get-tuple-element.16, bf16[2,256,512]{2,1,0:T(8,128)(2,1)} %collective-permute-done.5), kind=kLoop, calls=%fused_computation.24 | loop fusion | bytes 1048576
  86.4 0.1 select_dynamic-update-slice_fusion.1
  86.6 1.2 %collective-permute-done.15 = bf16[2,256,512]{2,1,0:T(8,128)(2,1)S(1)} collective-permute-done((bf16[2,256,512]{2,1,0:T(8,128)(2,1)S(1)}, bf16[2,256,512]{2,1,0:T(8,128)(2,1)S(1)}, u32[]{:S(2)}, u32[]{:S(2)}) %collective-permute-start.15) | collective-permute-done | bytes 524320 | tf_op jit(solution)/shard_map/ppermute | solution.py:23
  87.8 0.1 select_dynamic-update-slice_fusion
  88.0 19.7 %shard_map.47 = bf16[256,4096]{1,0:T(8,128)(2,1)} custom-call(s32[2,11]{1,0:T(2,128)S(1)} %fusion.2.slot_ref, s32[2,11]{1,0:T(2,128)S(1)} %compare_convert_fusion.diag_ref, bf16[256,4096]{1,0:T(8,128)(2,1)S(1)} %copy-done.1, bf16[2,11,128,512]{3,2,1,0:T(8,128)(2,1)S(1)} %bitcast.4, ...), custom_call_target="tpu_custom_call", output_to_operand_aliasing={{}: (5, {})} | custom-call | flops 2952790016 | bytes 4980736 | tf_op jit(solution)/shard_map/pallas_call | solution.py:137
  (34 shorter events, 0.7 us)
Async XLA Ops:
  0.0 14.6 %copy-start = (s32[32,11]{0,1:T(8,128)S(1)}, s32[32,11]{0,1:T(8,128)}, u32[]{:S(2)}) copy-start(s32[32,11]{0,1:T(8,128)} %param.7) | copy-start | bytes 4228
  0.0 4.5 %copy-start.2 = (bf16[256,1024]{1,0:T(8,128)(2,1)S(1)}, bf16[256,1024]{1,0:T(8,128)(2,1)}, u32[]{:S(2)}) copy-start(bf16[256,1024]{1,0:T(8,128)(2,1)} %param.5) | copy-start | bytes 1572868
  0.0 4.5 %copy-start.3 = (bf16[256,1024]{1,0:T(8,128)(2,1)S(1)}, bf16[256,1024]{1,0:T(8,128)(2,1)}, u32[]{:S(2)}) copy-start(bf16[256,1024]{1,0:T(8,128)(2,1)} %param.6) | copy-start | bytes 1572868
  1.2 0.7 collective-permute-start
  3.0 4.8 %collective-permute-start.1 = (bf16[2,128,1024]{2,1,0:T(8,128)(2,1)S(1)}, bf16[2,128,1024]{2,1,0:T(8,128)(2,1)}, u32[]{:S(2)}, u32[]{:S(2)}) collective-permute-start(bf16[2,128,1024]{2,1,0:T(8,128)(2,1)S(1)} %broadcast_select_fusion.2), channel_id=1, source_target_pairs={{0,4},{8,12},{16,20},{24,28}} | collective-permute-start | bytes 1572872 | tf_op jit(solution)/shard_map/ppermute | solution.py:67
  4.6 14.3 %collective-permute-start.4 = (bf16[2,256,512]{2,1,0:T(8,128)(2,1)S(1)}, bf16[2,256,512]{2,1,0:T(8,128)(2,1)}, u32[]{:S(2)}, u32[]{:S(2)}) collective-permute-start(bf16[2,256,512]{2,1,0:T(8,128)(2,1)S(1)} %get-tuple-element.13), channel_id=1, source_target_pairs={{0,4},{1,5},{2,6},{3,7},{4,8},{5,9},{6,10},{7,11},{8,12},{9,13},{1... | collective-permute-start | bytes 1572872 | tf_op jit(solution)/shard_map/ppermute | solution.py:23
  7.9 14.2 %collective-permute-start.2 = (bf16[2,128,1024]{2,1,0:T(8,128)(2,1)S(1)}, bf16[2,128,1024]{2,1,0:T(8,128)(2,1)}, u32[]{:S(2)}, u32[]{:S(2)}) collective-permute-start(bf16[2,128,1024]{2,1,0:T(8,128)(2,1)S(1)} %broadcast_select_fusion.3), channel_id=1, source_target_pairs={{0,2},{4,6},{8,10},{12,14},{16,18},{20,22},{24,26},{28,30}} | collective-permute-start | bytes 1572872 | tf_op jit(solution)/shard_map/ppermute | solution.py:67
  9.4 14.3 %collective-permute-start.10 = (bf16[2,256,512]{2,1,0:T(8,128)(2,1)S(1)}, bf16[2,256,512]{2,1,0:T(8,128)(2,1)}, u32[]{:S(2)}, u32[]{:S(2)}) collective-permute-start(bf16[2,256,512]{2,1,0:T(8,128)(2,1)S(1)} %get-tuple-element.13), channel_id=1, source_target_pairs={{0,2},{1,3},{4,6},{5,7},{8,10},{9,11},{12,14},{13,15},{16,18},{17,... | collective-permute-start | bytes 1572872 | tf_op jit(solution)/shard_map/ppermute | solution.py:23
  13.3 50.6 %collective-permute-start.12 = (bf16[2,256,512]{2,1,0:T(8,128)(2,1)S(1)}, bf16[2,256,512]{2,1,0:T(8,128)(2,1)S(1)}, u32[]{:S(2)}, u32[]{:S(2)}) collective-permute-start(bf16[2,256,512]{2,1,0:T(8,128)(2,1)S(1)} %get-tuple-element.13), channel_id=1, source_target_pairs={{0,1},{2,3},{4,5},{6,7},{8,9},{10,11},{12,13},{14,15},{16,17},{18,... | collective-permute-start | bytes 1572872 | tf_op jit(solution)/shard_map/ppermute | solution.py:23
  18.9 39.7 %collective-permute-start.5 = (bf16[2,256,512]{2,1,0:T(8,128)(2,1)S(1)}, bf16[2,256,512]{2,1,0:T(8,128)(2,1)}, u32[]{:S(2)}, u32[]{:S(2)}) collective-permute-start(bf16[2,256,512]{2,1,0:T(8,128)(2,1)S(1)} %get-tuple-element.9), channel_id=1, source_target_pairs={{0,4},{1,5},{2,6},{3,7},{4,8},{5,9},{6,10},{7,11},{8,12},{9,13},{1... | collective-permute-start | bytes 1572872 | tf_op jit(solution)/shard_map/ppermute | solution.py:23
  20.8 11.4 %collective-permute-start.9 = (bf16[2,256,512]{2,1,0:T(8,128)(2,1)}, bf16[2,256,512]{2,1,0:T(8,128)(2,1)}, u32[]{:S(2)}, u32[]{:S(2)}) collective-permute-start(bf16[2,256,512]{2,1,0:T(8,128)(2,1)} %collective-permute-done.4), channel_id=1, source_target_pairs={{2,0},{3,1},{6,4},{7,5},{10,8},{11,9},{14,12},{15,13},{18,16},{19,... | collective-permute-start | bytes 1572872 | tf_op jit(solution)/shard_map/ppermute | solution.py:23
  22.2 36.5 %collective-permute-start.3 = (bf16[2,128,1024]{2,1,0:T(8,128)(2,1)S(1)}, bf16[2,128,1024]{2,1,0:T(8,128)(2,1)S(1)}, u32[]{:S(2)}, u32[]{:S(2)}) collective-permute-start(bf16[2,128,1024]{2,1,0:T(8,128)(2,1)S(1)} %broadcast_select_fusion.4), channel_id=1, source_target_pairs={{0,1},{2,3},{4,5},{6,7},{8,9},{10,11},{12,13},{14,15},{16,17},{18,... | collective-permute-start | bytes 1572872 | tf_op jit(solution)/shard_map/ppermute | solution.py:67
  23.6 60.2 %collective-permute-start.13 = (bf16[2,256,512]{2,1,0:T(8,128)(2,1)S(1)}, bf16[2,256,512]{2,1,0:T(8,128)(2,1)S(1)}, u32[]{:S(2)}, u32[]{:S(2)}) collective-permute-start(bf16[2,256,512]{2,1,0:T(8,128)(2,1)S(1)} %get-tuple-element.9), channel_id=1, source_target_pairs={{0,2},{1,3},{4,6},{5,7},{8,10},{9,11},{12,14},{13,15},{16,18},{17,... | collective-permute-start | bytes 1572872 | tf_op jit(solution)/shard_map/ppermute | solution.py:23
  32.3 28.9 %collective-permute-start.8 = (bf16[2,256,512]{2,1,0:T(8,128)(2,1)}, bf16[2,256,512]{2,1,0:T(8,128)(2,1)S(1)}, u32[]{:S(2)}, u32[]{:S(2)}) collective-permute-start(bf16[2,256,512]{2,1,0:T(8,128)(2,1)} %collective-permute-done.4), channel_id=1, source_target_pairs={{1,0},{3,2},{5,4},{7,6},{9,8},{11,10},{13,12},{15,14},{17,16},{19,... | collective-permute-start | bytes 1572872 | tf_op jit(solution)/shard_map/ppermute | solution.py:23
  58.6 5.2 %collective-permute-start.11 = (bf16[2,256,512]{2,1,0:T(8,128)(2,1)S(1)}, bf16[2,256,512]{2,1,0:T(8,128)(2,1)S(1)}, u32[]{:S(2)}, u32[]{:S(2)}) collective-permute-start(bf16[2,256,512]{2,1,0:T(8,128)(2,1)S(1)} %broadcast_select_fusion.1), channel_id=1, source_target_pairs={{0,1},{1,0},{2,3},{3,2},{4,5},{5,4},{6,7},{7,6},{8,9},{9,8},{10,11... | collective-permute-start | bytes 1572872 | tf_op jit(solution)/shard_map/ppermute | solution.py:47
  58.7 25.1 %collective-permute-start.7 = (bf16[2,256,512]{2,1,0:T(8,128)(2,1)}, bf16[2,256,512]{2,1,0:T(8,128)(2,1)S(1)}, u32[]{:S(2)}, u32[]{:S(2)}) collective-permute-start(bf16[2,256,512]{2,1,0:T(8,128)(2,1)} %collective-permute-done.5), channel_id=1, source_target_pairs={{2,0},{3,1},{6,4},{7,5},{10,8},{11,9},{14,12},{15,13},{18,16},{19,... | collective-permute-start | bytes 1572872 | tf_op jit(solution)/shard_map/ppermute | solution.py:23
  61.2 3.0 %copy-start.1 = (bf16[256,4096]{1,0:T(8,128)(2,1)S(1)}, bf16[256,4096]{1,0:T(8,128)(2,1)}, u32[]{:S(2)}) copy-start(bf16[256,4096]{1,0:T(8,128)(2,1)} %q_ref.3) | copy-start | bytes 6291460
  61.2 25.2 %collective-permute-start.6 = (bf16[2,256,512]{2,1,0:T(8,128)(2,1)}, bf16[2,256,512]{2,1,0:T(8,128)(2,1)S(1)}, u32[]{:S(2)}, u32[]{:S(2)}) collective-permute-start(bf16[2,256,512]{2,1,0:T(8,128)(2,1)} %collective-permute-done.5), channel_id=1, source_target_pairs={{1,0},{3,2},{5,4},{7,6},{9,8},{11,10},{13,12},{15,14},{17,16},{19,... | collective-permute-start | bytes 1572872 | tf_op jit(solution)/shard_map/ppermute | solution.py:23
  83.9 2.5 %collective-permute-start.14 = (bf16[2,256,512]{2,1,0:T(8,128)(2,1)S(1)}, bf16[2,256,512]{2,1,0:T(8,128)(2,1)S(1)}, u32[]{:S(2)}, u32[]{:S(2)}) collective-permute-start(bf16[2,256,512]{2,1,0:T(8,128)(2,1)S(1)} %broadcast_select_fusion), channel_id=1, source_target_pairs={{0,1},{1,0},{2,3},{3,2},{4,5},{5,4},{6,7},{7,6},{8,9},{9,8},{10,11... | collective-permute-start | bytes 1572872 | tf_op jit(solution)/shard_map/ppermute | solution.py:47
  84.0 3.8 %collective-permute-start.15 = (bf16[2,256,512]{2,1,0:T(8,128)(2,1)S(1)}, bf16[2,256,512]{2,1,0:T(8,128)(2,1)S(1)}, u32[]{:S(2)}, u32[]{:S(2)}) collective-permute-start(bf16[2,256,512]{2,1,0:T(8,128)(2,1)S(1)} %get-tuple-element.9), channel_id=1, source_target_pairs={{0,1},{2,3},{4,5},{6,7},{8,9},{10,11},{12,13},{14,15},{16,17},{18,... | collective-permute-start | bytes 1572872 | tf_op jit(solution)/shard_map/ppermute | solution.py:23

commit v8 on v6

--- a/solution.py
+++ b/solution.py
@@ -23,7 +23,7 @@
     return lax.ppermute(shard, axis, pairs)
 
 
-def window_blocks(kv, axis):
+def window_blocks(kv, axis, extra=()):
     index = lax.axis_index(axis)
     y_low = (index // 2) % 2 == 0
     core0 = index % 2 == 0
@@ -35,13 +35,19 @@
     partner_back4 = shifted(back4, axis, -1, lambda i: i % 2 == 1)
     size = lax.axis_size(axis)
     swap_pairs = [(i, i ^ 1) for i in range(size)]
-    partner_back2 = lax.ppermute(back2, axis, swap_pairs)
+    rows = back2.shape[1]
+    sent = jnp.concatenate([back2] + list(extra), axis=1)
+    got = lax.ppermute(sent, axis, swap_pairs)
+    partner_back2 = got[:, :rows]
+    partner_extra = [
+        got[:, rows + k * BLK:rows + (k + 1) * BLK] for k in range(len(extra))
+    ]
     back3 = jnp.where(core0, partner_back4, partner_back2)
     back1 = jnp.where(core0, partner_back2, next_core)
-    return [back4, back3, back2, back1]
+    return [back4, back3, back2, back1], partner_extra
 
 
-def tree_broadcast(block, axis, source, size):
+def tree_broadcast(block, axis, source, size, last_round=True):
     index = lax.axis_index(axis)
     span = size - source
     held = block
@@ -49,7 +55,7 @@
     while dist < span:
         dist *= 2
     dist //= 2
-    while dist >= 1:
+    while dist >= (1 if last_round else 2):
         pairs = [
             (source + j, source + j + dist)
             for j in range(0, span, 2 * dist)
@@ -138,13 +144,16 @@
     own_index = lax.axis_index("ctx")
     kv = jnp.stack([key_rows, value_rows])
     assert blocks_here == 2 and ctx_count % 4 == 0
-    early = window_blocks(kv, "ctx")
     columns = blocks_here * ctx_count // STRIDE
     spread = STRIDE // blocks_here
-    column_blocks = [
-        tree_broadcast(kv[:, :BLK], "ctx", column * spread, ctx_count)
+    assert spread % 2 == 0
+    held = [
+        tree_broadcast(kv[:, :BLK], "ctx", column * spread, ctx_count, last_round=False)
         for column in range(columns)
     ]
+    early, from_partner = window_blocks(kv, "ctx", extra=held)
+    core0 = own_index % 2 == 0
+    column_blocks = [jnp.where(core0, h, p) for h, p in zip(held, from_partner)]
     buffer_blocks = columns + 4 * blocks_here + blocks_here
     kv_buffer = jnp.concatenate(column_blocks + early + [kv], axis=1).reshape(
         2, buffer_blocks, BLK, kv.shape[2]

time: 102 us -> 116 us (1.14)
  waiting for transfers between devices: 19.2 us -> 44.8 us
  starting transfers between devices: 35.5 us -> 19.2 us
  other arithmetic: 7.44 us -> 9.67 us
  Pallas kernels: 38.6 us -> 40.3 us
  local copies, waits for them, and re-layouts: 0.33 us -> 1.64 us
    ppermute x5, waiting for transfers between devices: 16.8 us -> 44.8 us  [shifted(): return lax.ppermute(shard, axis, pairs)]
    ppermute x5, starting transfers between devices: 27.1 us -> 14.9 us  [shifted(): return lax.ppermute(shard, axis, pairs)]
    ppermute x4 -> x3, starting transfers between devices: 4.94 us -> 2.08 us  [tree_broadcast(): got = lax.ppermute(held, axis, pairs)]
    ppermute x4 -> x3, waiting for transfers between devices: 2.39 us -> 0.01 us  [tree_broadcast(): got = lax.ppermute(held, axis, pairs)]
    pallas_call x1, Pallas kernels: 38.6 us -> 40.3 us  [attend(): pl.pallas_call(attend_kernel, out_shape=jax.ShapeDtypeStruct(queries.shap...]
    unnamed x11 -> x13, local copies, waits for them, and re-layouts: 0.26 us -> 1.57 us
    concatenate x0 -> x1, other arithmetic: none -> 1.26 us  [window_blocks(): sent = jnp.concatenate([back2] + list(extra), axis=1)]
    ppermute x1, starting transfers between devices: 3.46 us -> 2.25 us  [window_blocks(): got = lax.ppermute(sent, axis, swap_pairs)]
  transfers between devices with their start and end apart: 10 -> 9, of which waited for: 2 -> 2; matrix products, arithmetic and copies ran while one was open for 5% -> 5% of each run, Pallas kernels for 0% -> 0%
where the time goes in v8:
time: 116 us
  waiting for transfers between devices  44.8 us (39%)
  Pallas kernels  40.3 us (35%)
  starting transfers between devices  19.2 us (17%)
  other arithmetic  9.67 us (8%)
  local copies, waits for them, and re-layouts  1.64 us (1%)
    ppermute x5, waiting for transfers between devices, shifted(): return lax.ppermute(shard, axis, pairs)  44.8 us
    pallas_call x1, Pallas kernels, attend(): pl.pallas_call(attend_kernel, out_shape=jax.ShapeDtypeStruct(queries.shap...  40.3 us
    ppermute x5, starting transfers between devices, shifted(): return lax.ppermute(shard, axis, pairs)  14.9 us
    another operation x2, other arithmetic, per_device(): kv = jnp.stack([key_rows, value_rows])  3.35 us
  transfers between devices with their start and end apart: 9, of which 2 were waited for; matrix products, arithmetic and copies ran while one was open for 5% of the time, Pallas kernels for 0%

profile of v8, /device:TPU:19, one launch (start us, length us, event | category | flops | bytes accessed | tf_op | source)
XLA Modules:
  0.0 115.9 jit_solution(9435053329407691491)
XLA Ops:
  0.0 1.1 fusion
  1.1 0.7 collective-permute-start
  1.8 2.3 %pad_maximum_fusion.1 = bf16[2,256,1024]{2,1,0:T(8,128)(2,1)} fusion(bf16[1,256,1024]{2,1,0:T(8,128)(2,1)} %bitcast.10, bf16[1,256,1024]{2,1,0:T(8,128)(2,1)} %bitcast.6), kind=kLoop, calls=%fused_computation.2 | loop fusion | flops 524288 | bytes 2097152 | tf_op jit(solution)/shard_map/stack | solution.py:145
  4.1 3.2 %collective-permute-start.3 = (bf16[2,256,1024]{2,1,0:T(8,128)(2,1)}, bf16[2,256,1024]{2,1,0:T(8,128)(2,1)S(1)}, u32[]{:S(2)}, u32[]{:S(2)}) collective-permute-start(bf16[2,256,1024]{2,1,0:T(8,128)(2,1)} %pad_maximum_fusion.1), channel_id=1, source_target_pairs={{0,4},{1,5},{2,6},{3,7},{4,8},{5,9},{6,10},{7,11},{8,12},{9,13},{1... | collective-permute-start | bytes 3145736 | tf_op jit(solution)/shard_map/ppermute | solution.py:23
  7.3 1.1 broadcast_select_fusion.1
  8.4 0.7 collective-permute-start.1
  9.1 4.1 %collective-permute-start.5 = (bf16[2,256,1024]{2,1,0:T(8,128)(2,1)}, bf16[2,256,1024]{2,1,0:T(8,128)(2,1)}, u32[]{:S(2)}, u32[]{:S(2)}) collective-permute-start(bf16[2,256,1024]{2,1,0:T(8,128)(2,1)} %pad_maximum_fusion.1), channel_id=1, source_target_pairs={{0,2},{1,3},{4,6},{5,7},{8,10},{9,11},{12,14},{13,15},{16,18},{17,... | collective-permute-start | bytes 3145736 | tf_op jit(solution)/shard_map/ppermute | solution.py:23
  13.2 21.7 %collective-permute-done.3 = bf16[2,256,1024]{2,1,0:T(8,128)(2,1)S(1)} collective-permute-done((bf16[2,256,1024]{2,1,0:T(8,128)(2,1)}, bf16[2,256,1024]{2,1,0:T(8,128)(2,1)S(1)}, u32[]{:S(2)}, u32[]{:S(2)}) %collective-permute-start.3) | collective-permute-done | bytes 1048608 | tf_op jit(solution)/shard_map/ppermute | solution.py:23
  34.9 1.3 %collective-permute-start.4 = (bf16[2,256,1024]{2,1,0:T(8,128)(2,1)S(1)}, bf16[2,256,1024]{2,1,0:T(8,128)(2,1)}, u32[]{:S(2)}, u32[]{:S(2)}) collective-permute-start(bf16[2,256,1024]{2,1,0:T(8,128)(2,1)S(1)} %collective-permute-done.3), channel_id=1, source_target_pairs={{2,0},{3,1},{6,4},{7,5},{10,8},{11,9},{14,12},{15,13},{18,16},{19,... | collective-permute-start | bytes 3145736 | tf_op jit(solution)/shard_map/ppermute | solution.py:23
  36.2 0.1 broadcast_select_fusion.2
  36.3 0.7 collective-permute-start.2
  37.0 0.0 collective-permute-done.2
  37.1 0.1 broadcast_select_fusion.3
  37.1 23.1 %collective-permute-done.4 = bf16[2,256,1024]{2,1,0:T(8,128)(2,1)} collective-permute-done((bf16[2,256,1024]{2,1,0:T(8,128)(2,1)S(1)}, bf16[2,256,1024]{2,1,0:T(8,128)(2,1)}, u32[]{:S(2)}, u32[]{:S(2)}) %collective-permute-start.4) | collective-permute-done | bytes 1048608 | tf_op jit(solution)/shard_map/ppermute | solution.py:23
  60.2 1.3 %broadcast_select_fusion = bf16[2,256,1024]{2,1,0:T(8,128)(2,1)S(1)} fusion(bf16[2,256,1024]{2,1,0:T(8,128)(2,1)} %collective-permute-done.4, bf16[2,256,1024]{2,1,0:T(8,128)(2,1)} %collective-permute-done.5, pred[]{:T(512)S(6)} %eq.37), kind=kLoop, calls=%fused_computation.6 | loop fusion | flops 524288 | bytes 3145729 | tf_op jit(solution)/shard_map/jit(_where)/select_n | solution.py:34
  61.6 1.3 %pad_maximum_fusion = bf16[2,384,1024]{2,1,0:T(8,128)(2,1)} fusion(bf16[2,128,1024]{2,1,0:T(8,128)(2,1)S(1)} %broadcast_select_fusion.3, bf16[2,256,1024]{2,1,0:T(8,128)(2,1)S(1)} %broadcast_select_fusion), kind=kLoop, calls=%fused_computation | loop fusion | flops 3145728 | bytes 3145728 | tf_op jit(solution)/shard_map/concatenate | solution.py:39
  62.9 2.2 %collective-permute-start.6 = (bf16[2,384,1024]{2,1,0:T(8,128)(2,1)}, bf16[2,384,1024]{2,1,0:T(8,128)(2,1)S(1)}, u32[]{:S(2)}, u32[]{:S(2)}) collective-permute-start(bf16[2,384,1024]{2,1,0:T(8,128)(2,1)} %pad_maximum_fusion), channel_id=1, source_target_pairs={{0,1},{1,0},{2,3},{3,2},{4,5},{5,4},{6,7},{7,6},{8,9},{9,8},{10,11... | collective-permute-start | bytes 4718600 | tf_op jit(solution)/shard_map/ppermute | solution.py:40
  65.1 1.3 %collective-permute-start.8 = (bf16[2,256,1024]{2,1,0:T(8,128)(2,1)}, bf16[2,256,1024]{2,1,0:T(8,128)(2,1)}, u32[]{:S(2)}, u32[]{:S(2)}) collective-permute-start(bf16[2,256,1024]{2,1,0:T(8,128)(2,1)} %pad_maximum_fusion.1), channel_id=1, source_target_pairs={{0,1},{2,3},{4,5},{6,7},{8,9},{10,11},{12,13},{14,15},{16,17},{18,... | collective-permute-start | bytes 3145736 | tf_op jit(solution)/shard_map/ppermute | solution.py:23
  66.4 5.0 %collective-permute-start.7 = (bf16[2,256,1024]{2,1,0:T(8,128)(2,1)}, bf16[2,256,1024]{2,1,0:T(8,128)(2,1)}, u32[]{:S(2)}, u32[]{:S(2)}) collective-permute-start(bf16[2,256,1024]{2,1,0:T(8,128)(2,1)} %copy-done.4), channel_id=1, source_target_pairs={{1,0},{3,2},{5,4},{7,6},{9,8},{11,10},{13,12},{15,14},{17,16},{19,... | collective-permute-start | bytes 3145736 | tf_op jit(solution)/shard_map/ppermute | solution.py:23
  71.4 0.1 constant_dynamic-slice_fusion
  71.5 0.1 copy.6
  71.6 0.1 compare_convert_fusion.diag_ref
  71.6 0.0 copy-start.2
  71.7 0.0 copy-start.3
  71.7 0.2 fusion.1
  71.9 1.4 %constant_dynamic-update-slice_fusion.2 = bf16[2,1408,1024]{2,1,0:T(8,128)(2,1)S(1)} fusion(bf16[2,1408,1024]{2,1,0:T(8,128)(2,1)S(1)} %fusion.1, bf16[2,256,1024]{2,1,0:T(8,128)(2,1)} %copy-done.4), kind=kLoop, calls=%fused_computation.15 | loop fusion | bytes 2097152
  73.3 0.0 copy-start.1
  73.3 0.4 select_dynamic-update-slice_fusion.1
  73.7 0.1 constant_dynamic-update-slice_fusion.1
  73.8 1.7 %select_dynamic-update-slice_fusion = bf16[2,1408,1024]{2,1,0:T(8,128)(2,1)S(1)} fusion(bf16[2,1408,1024]{2,1,0:T(8,128)(2,1)S(1)} %constant_dynamic-update-slice_fusion.1, bf16[2,256,1024]{2,1,0:T(8,128)(2,1)} %collective-permute-done.8, pred[]{:T(512)S(6)} %eq.33, bf16[2,384,1024]{2,1,0:T(8,128)(2,1)S(1)} %collective-permute-done.6), kind=kLoop, calls=%fused_computation.4 | loop fusion | flops 524288 | bytes 3145729
  75.5 0.1 constant_dynamic-update-slice_fusion
  75.6 40.3 %shard_map.46 = bf16[256,4096]{1,0:T(8,128)(2,1)} custom-call(s32[2,11]{1,0:T(2,128)S(1)} %fusion.2.slot_ref, s32[2,11]{1,0:T(2,128)S(1)} %compare_convert_fusion.diag_ref, bf16[256,4096]{1,0:T(8,128)(2,1)S(1)} %copy-done.1, bf16[2,11,128,1024]{3,2,1,0:T(8,128)(2,1)S(1)} %bitcast.3, bf16[2,11,128,1024]{3,2,1,0:T(8,128)(2,1)S(1)} %bitcast.4), custom_call_target="tpu_custom_call" | custom-call | flops 5905580032 | bytes 9961472 | tf_op jit(solution)/shard_map/pallas_call | solution.py:124
  (15 shorter events, 0.0 us)
Async XLA Ops:
  0.0 71.4 %copy-start = (s32[32,11]{0,1:T(8,128)S(1)}, s32[32,11]{0,1:T(8,128)}, u32[]{:S(2)}) copy-start(s32[32,11]{0,1:T(8,128)} %param.7) | copy-start | bytes 4228
  1.1 6.2 %collective-permute-start = (bf16[2,128,1024]{2,1,0:T(8,128)(2,1)S(1)}, bf16[2,128,1024]{2,1,0:T(8,128)(2,1)S(1)}, u32[]{:S(2)}, u32[]{:S(2)}) collective-permute-start(bf16[2,128,1024]{2,1,0:T(8,128)(2,1)S(1)} %fusion), channel_id=1, source_target_pairs={{0,8},{16,24}} | collective-permute-start | bytes 1572872 | tf_op jit(solution)/shard_map/ppermute | solution.py:64
  4.1 30.9 %collective-permute-start.3 = (bf16[2,256,1024]{2,1,0:T(8,128)(2,1)}, bf16[2,256,1024]{2,1,0:T(8,128)(2,1)S(1)}, u32[]{:S(2)}, u32[]{:S(2)}) collective-permute-start(bf16[2,256,1024]{2,1,0:T(8,128)(2,1)} %pad_maximum_fusion.1), channel_id=1, source_target_pairs={{0,4},{1,5},{2,6},{3,7},{4,8},{5,9},{6,10},{7,11},{8,12},{9,13},{1... | collective-permute-start | bytes 3145736 | tf_op jit(solution)/shard_map/ppermute | solution.py:23
  8.4 27.8 %collective-permute-start.1 = (bf16[2,128,1024]{2,1,0:T(8,128)(2,1)S(1)}, bf16[2,128,1024]{2,1,0:T(8,128)(2,1)S(1)}, u32[]{:S(2)}, u32[]{:S(2)}) collective-permute-start(bf16[2,128,1024]{2,1,0:T(8,128)(2,1)S(1)} %broadcast_select_fusion.1), channel_id=1, source_target_pairs={{0,4},{8,12},{16,20},{24,28}} | collective-permute-start | bytes 1572872 | tf_op jit(solution)/shard_map/ppermute | solution.py:64
  9.1 28.0 %collective-permute-start.5 = (bf16[2,256,1024]{2,1,0:T(8,128)(2,1)}, bf16[2,256,1024]{2,1,0:T(8,128)(2,1)}, u32[]{:S(2)}, u32[]{:S(2)}) collective-permute-start(bf16[2,256,1024]{2,1,0:T(8,128)(2,1)} %pad_maximum_fusion.1), channel_id=1, source_target_pairs={{0,2},{1,3},{4,6},{5,7},{8,10},{9,11},{12,14},{13,15},{16,18},{17,... | collective-permute-start | bytes 3145736 | tf_op jit(solution)/shard_map/ppermute | solution.py:23
  34.9 2.2 %copy-start.4 = (bf16[2,256,1024]{2,1,0:T(8,128)(2,1)}, bf16[2,256,1024]{2,1,0:T(8,128)(2,1)S(1)}, u32[]{:S(2)}) copy-start(bf16[2,256,1024]{2,1,0:T(8,128)(2,1)S(1)} %collective-permute-done.3) | copy-start | bytes 3145732
  34.9 25.3 %collective-permute-start.4 = (bf16[2,256,1024]{2,1,0:T(8,128)(2,1)S(1)}, bf16[2,256,1024]{2,1,0:T(8,128)(2,1)}, u32[]{:S(2)}, u32[]{:S(2)}) collective-permute-start(bf16[2,256,1024]{2,1,0:T(8,128)(2,1)S(1)} %collective-permute-done.3), channel_id=1, source_target_pairs={{2,0},{3,1},{6,4},{7,5},{10,8},{11,9},{14,12},{15,13},{18,16},{19,... | collective-permute-start | bytes 3145736 | tf_op jit(solution)/shard_map/ppermute | solution.py:23
  36.3 0.7 collective-permute-start.2
  62.9 8.8 %collective-permute-start.6 = (bf16[2,384,1024]{2,1,0:T(8,128)(2,1)}, bf16[2,384,1024]{2,1,0:T(8,128)(2,1)S(1)}, u32[]{:S(2)}, u32[]{:S(2)}) collective-permute-start(bf16[2,384,1024]{2,1,0:T(8,128)(2,1)} %pad_maximum_fusion), channel_id=1, source_target_pairs={{0,1},{1,0},{2,3},{3,2},{4,5},{5,4},{6,7},{7,6},{8,9},{9,8},{10,11... | collective-permute-start | bytes 4718600 | tf_op jit(solution)/shard_map/ppermute | solution.py:40
  65.1 8.7 %collective-permute-start.8 = (bf16[2,256,1024]{2,1,0:T(8,128)(2,1)}, bf16[2,256,1024]{2,1,0:T(8,128)(2,1)}, u32[]{:S(2)}, u32[]{:S(2)}) collective-permute-start(bf16[2,256,1024]{2,1,0:T(8,128)(2,1)} %pad_maximum_fusion.1), channel_id=1, source_target_pairs={{0,1},{2,3},{4,5},{6,7},{8,9},{10,11},{12,13},{14,15},{16,17},{18,... | collective-permute-start | bytes 3145736 | tf_op jit(solution)/shard_map/ppermute | solution.py:23
  66.4 6.9 %collective-permute-start.7 = (bf16[2,256,1024]{2,1,0:T(8,128)(2,1)}, bf16[2,256,1024]{2,1,0:T(8,128)(2,1)}, u32[]{:S(2)}, u32[]{:S(2)}) collective-permute-start(bf16[2,256,1024]{2,1,0:T(8,128)(2,1)} %copy-done.4), channel_id=1, source_target_pairs={{1,0},{3,2},{5,4},{7,6},{9,8},{11,10},{13,12},{15,14},{17,16},{19,... | collective-permute-start | bytes 3145736 | tf_op jit(solution)/shard_map/ppermute | solution.py:23
  71.6 3.9 %copy-start.2 = (bf16[256,1024]{1,0:T(8,128)(2,1)S(1)}, bf16[256,1024]{1,0:T(8,128)(2,1)}, u32[]{:S(2)}) copy-start(bf16[256,1024]{1,0:T(8,128)(2,1)} %param.5) | copy-start | bytes 1572868
  71.7 3.9 %copy-start.3 = (bf16[256,1024]{1,0:T(8,128)(2,1)S(1)}, bf16[256,1024]{1,0:T(8,128)(2,1)}, u32[]{:S(2)}) copy-start(bf16[256,1024]{1,0:T(8,128)(2,1)} %param.6) | copy-start | bytes 1572868
  73.3 2.4 %copy-start.1 = (bf16[256,4096]{1,0:T(8,128)(2,1)S(1)}, bf16[256,4096]{1,0:T(8,128)(2,1)}, u32[]{:S(2)}) copy-start(bf16[256,4096]{1,0:T(8,128)(2,1)} %q_ref.1) | copy-start | bytes 6291460

commit v9 on v8

--- a/solution.py
+++ b/solution.py
@@ -23,17 +23,22 @@
     return lax.ppermute(shard, axis, pairs)
 
 
-def window_blocks(kv, axis, extra=()):
-    index = lax.axis_index(axis)
-    y_low = (index // 2) % 2 == 0
-    core0 = index % 2 == 0
+def window_start(kv, axis):
     back4 = shifted(kv, axis, 4, lambda i: True)
     up_y = shifted(kv, axis, 2, lambda i: (i // 2) % 2 == 0)
     next_core = shifted(kv, axis, 1, lambda i: i % 2 == 0)
     down_y = shifted(back4, axis, -2, lambda i: (i // 2) % 2 == 1)
+    partner_back4 = shifted(back4, axis, -1, lambda i: i % 2 == 1)
+    return back4, up_y, next_core, down_y, partner_back4
+
+
+def window_finish(started, axis, extra=()):
+    back4, up_y, next_core, down_y, partner_back4 = started
+    index = lax.axis_index(axis)
+    size = lax.axis_size(axis)
+    y_low = (index // 2) % 2 == 0
+    core0 = index % 2 == 0
     back2 = jnp.where(y_low, down_y, up_y)
-    partner_back4 = shifted(back4, axis, -1, lambda i: i % 2 == 1)
-    size = lax.axis_size(axis)
     swap_pairs = [(i, i ^ 1) for i in range(size)]
     rows = back2.shape[1]
     sent = jnp.concatenate([back2] + list(extra), axis=1)
@@ -147,11 +152,13 @@
     columns = blocks_here * ctx_count // STRIDE
     spread = STRIDE // blocks_here
     assert spread % 2 == 0
+    started = window_start(kv, "ctx")
+    first_rows, _, _ = lax.optimization_barrier((kv[:, :BLK], started[0], started[1]))
     held = [
-        tree_broadcast(kv[:, :BLK], "ctx", column * spread, ctx_count, last_round=False)
+        tree_broadcast(first_rows, "ctx", column * spread, ctx_count, last_round=False)
         for column in range(columns)
     ]
-    early, from_partner = window_blocks(kv, "ctx", extra=held)
+    early, from_partner = window_finish(started, "ctx", extra=held)
     core0 = own_index % 2 == 0
     column_blocks = [jnp.where(core0, h, p) for h, p in zip(held, from_partner)]
     buffer_blocks = columns + 4 * blocks_here + blocks_here

time: 116 us -> 114 us (0.983)
  the two profiles are of different devices: /device:TPU:19 before, /device:TPU:29 now
where the time goes in v9:
time: 114 us
  waiting for transfers between devices  41.6 us (36%)
  Pallas kernels  38.6 us (34%)
  starting transfers between devices  23.1 us (20%)
  other arithmetic  8.63 us (8%)
  local copies, waits for them, and re-layouts  1.64 us (1%)
    ppermute x5, waiting for transfers between devices, shifted(): return lax.ppermute(shard, axis, pairs)  41.6 us
    pallas_call x1, Pallas kernels, attend(): pl.pallas_call(attend_kernel, out_shape=jax.ShapeDtypeStruct(queries.shap...  38.6 us
    ppermute x5, starting transfers between devices, shifted(): return lax.ppermute(shard, axis, pairs)  11.1 us
    ppermute x1, starting transfers between devices, window_finish(): got = lax.ppermute(sent, axis, swap_pairs)  9.18 us
    another operation x2, other arithmetic, per_device(): kv = jnp.stack([key_rows, value_rows])  3.35 us
    ppermute x3, starting transfers between devices, tree_broadcast(): got = lax.ppermute(held, axis, pairs)  2.84 us
    unnamed x3, other arithmetic  2.32 us
  transfers between devices with their start and end apart: 9, of which 3 were waited for; matrix products, arithmetic and copies ran while one was open for 4% of the time, Pallas kernels for 0%

profile of v9, /device:TPU:29, one launch (start us, length us, event | category | flops | bytes accessed | tf_op | source)
XLA Modules:
  0.0 113.8 jit_solution(9602499720515569886)
XLA Ops:
  0.0 2.3 %pad_maximum_fusion.1 = bf16[2,256,1024]{2,1,0:T(8,128)(2,1)} fusion(bf16[1,256,1024]{2,1,0:T(8,128)(2,1)} %bitcast.8, bf16[1,256,1024]{2,1,0:T(8,128)(2,1)} %bitcast.5), kind=kLoop, calls=%fused_computation.2 | loop fusion | flops 524288 | bytes 2097152 | tf_op jit(solution)/shard_map/stack | solution.py:150
  2.3 1.3 %collective-permute-start = (bf16[2,256,1024]{2,1,0:T(8,128)(2,1)}, bf16[2,256,1024]{2,1,0:T(8,128)(2,1)S(1)}, u32[]{:S(2)}, u32[]{:S(2)}) collective-permute-start(bf16[2,256,1024]{2,1,0:T(8,128)(2,1)} %pad_maximum_fusion.1), channel_id=1, source_target_pairs={{0,4},{1,5},{2,6},{3,7},{4,8},{5,9},{6,10},{7,11},{8,12},{9,13},{1... | collective-permute-start | bytes 3145736 | tf_op jit(solution)/shard_map/ppermute | solution.py:23
  3.6 1.3 %collective-permute-start.1 = (bf16[2,256,1024]{2,1,0:T(8,128)(2,1)}, bf16[2,256,1024]{2,1,0:T(8,128)(2,1)}, u32[]{:S(2)}, u32[]{:S(2)}) collective-permute-start(bf16[2,256,1024]{2,1,0:T(8,128)(2,1)} %pad_maximum_fusion.1), channel_id=1, source_target_pairs={{0,2},{1,3},{4,6},{5,7},{8,10},{9,11},{12,14},{13,15},{16,18},{17,... | collective-permute-start | bytes 3145736 | tf_op jit(solution)/shard_map/ppermute | solution.py:23
  4.9 1.1 fusion
  5.9 22.6 %collective-permute-done = bf16[2,256,1024]{2,1,0:T(8,128)(2,1)S(1)} collective-permute-done((bf16[2,256,1024]{2,1,0:T(8,128)(2,1)}, bf16[2,256,1024]{2,1,0:T(8,128)(2,1)S(1)}, u32[]{:S(2)}, u32[]{:S(2)}) %collective-permute-start) | collective-permute-done | bytes 1048608 | tf_op jit(solution)/shard_map/ppermute | solution.py:23
  28.5 1.3 %collective-permute-done.1 = bf16[2,256,1024]{2,1,0:T(8,128)(2,1)} collective-permute-done((bf16[2,256,1024]{2,1,0:T(8,128)(2,1)}, bf16[2,256,1024]{2,1,0:T(8,128)(2,1)}, u32[]{:S(2)}, u32[]{:S(2)}) %collective-permute-start.1) | collective-permute-done | bytes 1048608 | tf_op jit(solution)/shard_map/ppermute | solution.py:23
  29.8 0.7 collective-permute-start.2
  30.5 2.3 %collective-permute-start.5 = (bf16[2,256,1024]{2,1,0:T(8,128)(2,1)S(1)}, bf16[2,256,1024]{2,1,0:T(8,128)(2,1)}, u32[]{:S(2)}, u32[]{:S(2)}) collective-permute-start(bf16[2,256,1024]{2,1,0:T(8,128)(2,1)S(1)} %collective-permute-done), channel_id=1, source_target_pairs={{2,0},{3,1},{6,4},{7,5},{10,8},{11,9},{14,12},{15,13},{18,16},{19,... | collective-permute-start | bytes 3145736 | tf_op jit(solution)/shard_map/ppermute | solution.py:23
  32.8 0.1 broadcast_select_fusion.1
  32.9 0.7 collective-permute-start.3
  33.6 0.1 broadcast_select_fusion.2
  33.7 1.5 %collective-permute-start.4 = (bf16[2,128,1024]{2,1,0:T(8,128)(2,1)S(1)}, bf16[2,128,1024]{2,1,0:T(8,128)(2,1)}, u32[]{:S(2)}, u32[]{:S(2)}) collective-permute-start(bf16[2,128,1024]{2,1,0:T(8,128)(2,1)S(1)} %broadcast_select_fusion.2), channel_id=1, source_target_pairs={{0,2},{4,6},{8,10},{12,14},{16,18},{20,22},{24,26},{28,30}} | collective-permute-start | bytes 1572872 | tf_op jit(solution)/shard_map/ppermute | solution.py:69
  35.1 17.7 %collective-permute-done.5 = bf16[2,256,1024]{2,1,0:T(8,128)(2,1)} collective-permute-done((bf16[2,256,1024]{2,1,0:T(8,128)(2,1)S(1)}, bf16[2,256,1024]{2,1,0:T(8,128)(2,1)}, u32[]{:S(2)}, u32[]{:S(2)}) %collective-permute-start.5) | collective-permute-done | bytes 1048608 | tf_op jit(solution)/shard_map/ppermute | solution.py:23
  52.8 1.3 %broadcast_select_fusion = bf16[2,256,1024]{2,1,0:T(8,128)(2,1)S(1)} fusion(bf16[2,256,1024]{2,1,0:T(8,128)(2,1)} %collective-permute-done.5, bf16[2,256,1024]{2,1,0:T(8,128)(2,1)} %collective-permute-done.1, pred[]{:T(512)S(6)} %eq.37), kind=kLoop, calls=%fused_computation.6 | loop fusion | flops 524288 | bytes 3145729 | tf_op jit(solution)/shard_map/jit(_where)/select_n | solution.py:41
  54.2 0.1 broadcast_select_fusion.3
  54.3 1.3 %pad_maximum_fusion = bf16[2,384,1024]{2,1,0:T(8,128)(2,1)} fusion(bf16[2,128,1024]{2,1,0:T(8,128)(2,1)S(1)} %broadcast_select_fusion.3, bf16[2,256,1024]{2,1,0:T(8,128)(2,1)S(1)} %broadcast_select_fusion), kind=kLoop, calls=%fused_computation | loop fusion | flops 3145728 | bytes 3145728 | tf_op jit(solution)/shard_map/concatenate | solution.py:44
  55.5 9.2 %collective-permute-start.6 = (bf16[2,384,1024]{2,1,0:T(8,128)(2,1)}, bf16[2,384,1024]{2,1,0:T(8,128)(2,1)S(1)}, u32[]{:S(2)}, u32[]{:S(2)}) collective-permute-start(bf16[2,384,1024]{2,1,0:T(8,128)(2,1)} %pad_maximum_fusion), channel_id=1, source_target_pairs={{0,1},{1,0},{2,3},{3,2},{4,5},{5,4},{6,7},{7,6},{8,9},{9,8},{10,11... | collective-permute-start | bytes 4718600 | tf_op jit(solution)/shard_map/ppermute | solution.py:45
  64.7 1.3 %collective-permute-start.8 = (bf16[2,256,1024]{2,1,0:T(8,128)(2,1)}, bf16[2,256,1024]{2,1,0:T(8,128)(2,1)}, u32[]{:S(2)}, u32[]{:S(2)}) collective-permute-start(bf16[2,256,1024]{2,1,0:T(8,128)(2,1)} %pad_maximum_fusion.1), channel_id=1, source_target_pairs={{0,1},{2,3},{4,5},{6,7},{8,9},{10,11},{12,13},{14,15},{16,17},{18,... | collective-permute-start | bytes 3145736 | tf_op jit(solution)/shard_map/ppermute | solution.py:23
  66.0 5.0 %collective-permute-start.7 = (bf16[2,256,1024]{2,1,0:T(8,128)(2,1)}, bf16[2,256,1024]{2,1,0:T(8,128)(2,1)}, u32[]{:S(2)}, u32[]{:S(2)}) collective-permute-start(bf16[2,256,1024]{2,1,0:T(8,128)(2,1)} %copy-done.4), channel_id=1, source_target_pairs={{1,0},{3,2},{5,4},{7,6},{9,8},{11,10},{13,12},{15,14},{17,16},{19,... | collective-permute-start | bytes 3145736 | tf_op jit(solution)/shard_map/ppermute | solution.py:23
  71.0 0.1 constant_dynamic-slice_fusion
  71.1 0.1 copy.6
  71.2 0.1 compare_convert_fusion.diag_ref
  71.2 0.0 copy-start.2
  71.3 0.0 copy-start.3
  71.3 0.2 fusion.1
  71.5 1.4 %constant_dynamic-update-slice_fusion.2 = bf16[2,1408,1024]{2,1,0:T(8,128)(2,1)S(1)} fusion(bf16[2,1408,1024]{2,1,0:T(8,128)(2,1)S(1)} %fusion.1, bf16[2,256,1024]{2,1,0:T(8,128)(2,1)} %copy-done.4), kind=kLoop, calls=%fused_computation.15 | loop fusion | bytes 2097152
  72.9 0.0 copy-start.1
  72.9 0.4 select_dynamic-update-slice_fusion.1
  73.3 0.1 constant_dynamic-update-slice_fusion.1
  73.4 1.7 %select_dynamic-update-slice_fusion = bf16[2,1408,1024]{2,1,0:T(8,128)(2,1)S(1)} fusion(bf16[2,1408,1024]{2,1,0:T(8,128)(2,1)S(1)} %constant_dynamic-update-slice_fusion.1, bf16[2,256,1024]{2,1,0:T(8,128)(2,1)} %collective-permute-done.8, pred[]{:T(512)S(6)} %eq.33, bf16[2,384,1024]{2,1,0:T(8,128)(2,1)S(1)} %collective-permute-done.6), kind=kLoop, calls=%fused_computation.4 | loop fusion | flops 524288 | bytes 3145729
  75.1 0.1 constant_dynamic-update-slice_fusion
  75.2 38.6 %shard_map.46 = bf16[256,4096]{1,0:T(8,128)(2,1)} custom-call(s32[2,11]{1,0:T(2,128)S(1)} %fusion.2.slot_ref, s32[2,11]{1,0:T(2,128)S(1)} %compare_convert_fusion.diag_ref, bf16[256,4096]{1,0:T(8,128)(2,1)S(1)} %copy-done.1, bf16[2,11,128,1024]{3,2,1,0:T(8,128)(2,1)S(1)} %bitcast.3, bf16[2,11,128,1024]{3,2,1,0:T(8,128)(2,1)S(1)} %bitcast.4), custom_call_target="tpu_custom_call" | custom-call | flops 5905580032 | bytes 9961472 | tf_op jit(solution)/shard_map/pallas_call | solution.py:129
  (15 shorter events, 0.0 us)
Async XLA Ops:
  0.0 71.0 %copy-start = (s32[32,11]{0,1:T(8,128)S(1)}, s32[32,11]{0,1:T(8,128)}, u32[]{:S(2)}) copy-start(s32[32,11]{0,1:T(8,128)} %param.7) | copy-start | bytes 4228
  2.3 26.2 %collective-permute-start = (bf16[2,256,1024]{2,1,0:T(8,128)(2,1)}, bf16[2,256,1024]{2,1,0:T(8,128)(2,1)S(1)}, u32[]{:S(2)}, u32[]{:S(2)}) collective-permute-start(bf16[2,256,1024]{2,1,0:T(8,128)(2,1)} %pad_maximum_fusion.1), channel_id=1, source_target_pairs={{0,4},{1,5},{2,6},{3,7},{4,8},{5,9},{6,10},{7,11},{8,12},{9,13},{1... | collective-permute-start | bytes 3145736 | tf_op jit(solution)/shard_map/ppermute | solution.py:23
  3.6 26.2 %collective-permute-start.1 = (bf16[2,256,1024]{2,1,0:T(8,128)(2,1)}, bf16[2,256,1024]{2,1,0:T(8,128)(2,1)}, u32[]{:S(2)}, u32[]{:S(2)}) collective-permute-start(bf16[2,256,1024]{2,1,0:T(8,128)(2,1)} %pad_maximum_fusion.1), channel_id=1, source_target_pairs={{0,2},{1,3},{4,6},{5,7},{8,10},{9,11},{12,14},{13,15},{16,18},{17,... | collective-permute-start | bytes 3145736 | tf_op jit(solution)/shard_map/ppermute | solution.py:23
  28.5 25.8 %copy-start.4 = (bf16[2,256,1024]{2,1,0:T(8,128)(2,1)}, bf16[2,256,1024]{2,1,0:T(8,128)(2,1)S(1)}, u32[]{:S(2)}) copy-start(bf16[2,256,1024]{2,1,0:T(8,128)(2,1)S(1)} %collective-permute-done) | copy-start | bytes 3145732
  29.8 3.0 %collective-permute-start.2 = (bf16[2,128,1024]{2,1,0:T(8,128)(2,1)S(1)}, bf16[2,128,1024]{2,1,0:T(8,128)(2,1)S(1)}, u32[]{:S(2)}, u32[]{:S(2)}) collective-permute-start(bf16[2,128,1024]{2,1,0:T(8,128)(2,1)S(1)} %fusion), channel_id=1, source_target_pairs={{0,8},{16,24}} | collective-permute-start | bytes 1572872 | tf_op jit(solution)/shard_map/ppermute | solution.py:69
  30.5 22.3 %collective-permute-start.5 = (bf16[2,256,1024]{2,1,0:T(8,128)(2,1)S(1)}, bf16[2,256,1024]{2,1,0:T(8,128)(2,1)}, u32[]{:S(2)}, u32[]{:S(2)}) collective-permute-start(bf16[2,256,1024]{2,1,0:T(8,128)(2,1)S(1)} %collective-permute-done), channel_id=1, source_target_pairs={{2,0},{3,1},{6,4},{7,5},{10,8},{11,9},{14,12},{15,13},{18,16},{19,... | collective-permute-start | bytes 3145736 | tf_op jit(solution)/shard_map/ppermute | solution.py:23
  32.9 0.7 collective-permute-start.3
  33.7 20.5 %collective-permute-start.4 = (bf16[2,128,1024]{2,1,0:T(8,128)(2,1)S(1)}, bf16[2,128,1024]{2,1,0:T(8,128)(2,1)}, u32[]{:S(2)}, u32[]{:S(2)}) collective-permute-start(bf16[2,128,1024]{2,1,0:T(8,128)(2,1)S(1)} %broadcast_select_fusion.2), channel_id=1, source_target_pairs={{0,2},{4,6},{8,10},{12,14},{16,18},{20,22},{24,26},{28,30}} | collective-permute-start | bytes 1572872 | tf_op jit(solution)/shard_map/ppermute | solution.py:69
  55.5 15.7 %collective-permute-start.6 = (bf16[2,384,1024]{2,1,0:T(8,128)(2,1)}, bf16[2,384,1024]{2,1,0:T(8,128)(2,1)S(1)}, u32[]{:S(2)}, u32[]{:S(2)}) collective-permute-start(bf16[2,384,1024]{2,1,0:T(8,128)(2,1)} %pad_maximum_fusion), channel_id=1, source_target_pairs={{0,1},{1,0},{2,3},{3,2},{4,5},{5,4},{6,7},{7,6},{8,9},{9,8},{10,11... | collective-permute-start | bytes 4718600 | tf_op jit(solution)/shard_map/ppermute | solution.py:45
  64.7 8.7 %collective-permute-start.8 = (bf16[2,256,1024]{2,1,0:T(8,128)(2,1)}, bf16[2,256,1024]{2,1,0:T(8,128)(2,1)}, u32[]{:S(2)}, u32[]{:S(2)}) collective-permute-start(bf16[2,256,1024]{2,1,0:T(8,128)(2,1)} %pad_maximum_fusion.1), channel_id=1, source_target_pairs={{0,1},{2,3},{4,5},{6,7},{8,9},{10,11},{12,13},{14,15},{16,17},{18,... | collective-permute-start | bytes 3145736 | tf_op jit(solution)/shard_map/ppermute | solution.py:23
  66.0 6.9 %collective-permute-start.7 = (bf16[2,256,1024]{2,1,0:T(8,128)(2,1)}, bf16[2,256,1024]{2,1,0:T(8,128)(2,1)}, u32[]{:S(2)}, u32[]{:S(2)}) collective-permute-start(bf16[2,256,1024]{2,1,0:T(8,128)(2,1)} %copy-done.4), channel_id=1, source_target_pairs={{1,0},{3,2},{5,4},{7,6},{9,8},{11,10},{13,12},{15,14},{17,16},{19,... | collective-permute-start | bytes 3145736 | tf_op jit(solution)/shard_map/ppermute | solution.py:23
  71.2 3.9 %copy-start.2 = (bf16[256,1024]{1,0:T(8,128)(2,1)S(1)}, bf16[256,1024]{1,0:T(8,128)(2,1)}, u32[]{:S(2)}) copy-start(bf16[256,1024]{1,0:T(8,128)(2,1)} %param.5) | copy-start | bytes 1572868
  71.3 3.9 %copy-start.3 = (bf16[256,1024]{1,0:T(8,128)(2,1)S(1)}, bf16[256,1024]{1,0:T(8,128)(2,1)}, u32[]{:S(2)}) copy-start(bf16[256,1024]{1,0:T(8,128)(2,1)} %param.6) | copy-start | bytes 1572868
  72.9 2.4 %copy-start.1 = (bf16[256,4096]{1,0:T(8,128)(2,1)S(1)}, bf16[256,4096]{1,0:T(8,128)(2,1)}, u32[]{:S(2)}) copy-start(bf16[256,4096]{1,0:T(8,128)(2,1)} %q_ref.1) | copy-start | bytes 6291460

commit v10 on v6

--- a/solution.py
+++ b/solution.py
@@ -15,6 +15,7 @@
 STRIDE = 32
 LIST = 11
 GROUP = H // KVH
+PAIR = 2
 
 
 def shifted(shard, axis, by, sends):
@@ -66,35 +67,37 @@
 def attend_kernel(slot_ref, diag_ref, q_ref, k_ref, v_ref, o_ref, score_sc, bias_sc):
     local = pl.program_id(1)
     exp2_scale = (HD ** (-0.5)) * 1.4426950408889634
+    rows = PAIR * BLK
+    row = lax.broadcasted_iota(jnp.int32, (rows, BLK), 0) % BLK
+    col = lax.broadcasted_iota(jnp.int32, (rows, BLK), 1)
+    bias_sc[0] = jnp.zeros((rows, BLK), jnp.float32)
+    bias_sc[1] = jnp.where(col > row, -jnp.inf, 0.0).astype(jnp.float32)
     q = q_ref[...]
-    stacked = jnp.concatenate([q[:, j * HD:(j + 1) * HD] for j in range(GROUP)], axis=0)
-    row = lax.broadcasted_iota(jnp.int32, (GROUP * BLK, BLK), 0) % BLK
-    col = lax.broadcasted_iota(jnp.int32, (GROUP * BLK, BLK), 1)
-    bias_sc[0] = jnp.zeros((GROUP * BLK, BLK), jnp.float32)
-    bias_sc[1] = jnp.where(col > row, -jnp.inf, 0.0).astype(jnp.float32)
-    run_max = jnp.full((GROUP * BLK, BLK), -jnp.inf, jnp.float32)
-    for s in range(LIST):
-        key = k_ref[0, slot_ref[local, s]]
-        sc = lax.dot_general(
-            stacked, key, (((1,), (1,)), ((), ())), preferred_element_type=jnp.float32
-        ) + bias_sc[diag_ref[local, s]]
-        score_sc[s] = sc
-        run_max = jnp.maximum(run_max, sc)
-    row_max = jnp.max(run_max, axis=1, keepdims=True)
-    total = jnp.zeros((GROUP * BLK, BLK), jnp.float32)
-    acc = jnp.zeros((GROUP * BLK, HD), jnp.float32)
-    for s in range(LIST):
-        powers = jnp.exp2((score_sc[s] - row_max) * exp2_scale)
-        total = total + powers
-        value = v_ref[0, slot_ref[local, s]]
-        acc = acc + jnp.dot(
-            powers.astype(jnp.bfloat16), value, preferred_element_type=jnp.float32
-        )
-    denominator = jnp.sum(total, axis=1, keepdims=True)
-    result = (acc / denominator).astype(jnp.bfloat16)
-    o_ref[...] = jnp.concatenate(
-        [result[j * BLK:(j + 1) * BLK] for j in range(GROUP)], axis=1
-    )
+    for half in range(GROUP // PAIR):
+        heads = range(half * PAIR, (half + 1) * PAIR)
+        stacked = jnp.concatenate([q[:, j * HD:(j + 1) * HD] for j in heads], axis=0)
+        run_max = jnp.full((rows, BLK), -jnp.inf, jnp.float32)
+        for s in range(LIST):
+            key = k_ref[0, slot_ref[local, s]]
+            sc = lax.dot_general(
+                stacked, key, (((1,), (1,)), ((), ())), preferred_element_type=jnp.float32
+            ) + bias_sc[diag_ref[local, s]]
+            score_sc[half, s] = sc
+            run_max = jnp.maximum(run_max, sc)
+        row_max = jnp.max(run_max, axis=1, keepdims=True)
+        total = jnp.zeros((rows, BLK), jnp.float32)
+        acc = jnp.zeros((rows, HD), jnp.float32)
+        for s in range(LIST):
+            powers = jnp.exp2((score_sc[half, s] - row_max) * exp2_scale)
+            total = total + powers
+            value = v_ref[0, slot_ref[local, s]]
+            acc = acc + jnp.dot(
+                powers.astype(jnp.bfloat16), value, preferred_element_type=jnp.float32
+            )
+        denominator = jnp.sum(total, axis=1, keepdims=True)
+        result = (acc / denominator).astype(jnp.bfloat16)
+        for k, j in enumerate(heads):
+            o_ref[:, j * HD:(j + 1) * HD] = result[k * BLK:(k + 1) * BLK]
 
 
 def attend(slots, diag, queries, kv_buffer):
@@ -111,8 +114,8 @@
         ],
         out_specs=pl.BlockSpec((BLK, GROUP * HD), lambda g, b, *_: (b, g)),
         scratch_shapes=[
-            pltpu.VMEM((LIST, GROUP * BLK, BLK), jnp.float32),
-            pltpu.VMEM((2, GROUP * BLK, BLK), jnp.float32),
+            pltpu.VMEM((GROUP // PAIR, LIST, PAIR * BLK, BLK), jnp.float32),
+            pltpu.VMEM((2, PAIR * BLK, BLK), jnp.float32),
         ],
     )
     return pl.pallas_call(

time: 102 us -> 94.8 us (0.929)
  Pallas kernels: 38.6 us -> 31.7 us
    pallas_call x1, Pallas kernels: 38.6 us -> 31.7 us  [attend(): pl.pallas_call(attend_kernel, out_shape=jax.ShapeDtypeStruct(queries.shap...]
where the time goes in v10:
time: 94.8 us; the launch traced here: 94.4 us
  starting transfers between devices  35.5 us (37%)
  Pallas kernels  31.7 us (33%)
  waiting for transfers between devices  19.2 us (20%)
  other arithmetic  7.44 us (8%)
    pallas_call x1, Pallas kernels, attend(): pl.pallas_call(attend_kernel, out_shape=jax.ShapeDtypeStruct(queries.shap...  31.7 us
    ppermute x5, starting transfers between devices, shifted(): return lax.ppermute(shard, axis, pairs)  27.1 us
    ppermute x5, waiting for transfers between devices, shifted(): return lax.ppermute(shard, axis, pairs)  16.8 us
    ppermute x4, starting transfers between devices, tree_broadcast(): got = lax.ppermute(held, axis, pairs)  4.94 us
    ppermute x1, starting transfers between devices, window_blocks(): partner_back2 = lax.ppermute(back2, axis, swap_pairs)  3.46 us
    ppermute x4, waiting for transfers between devices, tree_broadcast(): got = lax.ppermute(held, axis, pairs)  2.39 us
    another operation x2, other arithmetic, per_device(): kv = jnp.stack([key_rows, value_rows])  2.38 us
    unnamed x3, other arithmetic  2.31 us
  transfers between devices with their start and end apart: 10, of which 2 were waited for; matrix products, arithmetic and copies ran while one was open for 5% of the time, Pallas kernels for 0%

profile of v10, /device:TPU:19, one launch (start us, length us, event | category | flops | bytes accessed | tf_op | source)
XLA Modules:
  0.0 94.4 jit_solution(6355693384929204826)
XLA Ops:
  0.0 1.3 %pad_maximum_fusion = bf16[2,256,1024]{2,1,0:T(8,128)(2,1)S(1)} fusion(bf16[1,256,1024]{2,1,0:T(8,128)(2,1)} %bitcast.9, bf16[1,256,1024]{2,1,0:T(8,128)(2,1)} %bitcast.5), kind=kLoop, calls=%fused_computation.1 | loop fusion | flops 524288 | bytes 2097152 | tf_op jit(solution)/shard_map/stack | solution.py:142
  1.3 3.2 %collective-permute-start.4 = (bf16[2,256,1024]{2,1,0:T(8,128)(2,1)S(1)}, bf16[2,256,1024]{2,1,0:T(8,128)(2,1)S(1)}, u32[]{:S(2)}, u32[]{:S(2)}) collective-permute-start(bf16[2,256,1024]{2,1,0:T(8,128)(2,1)S(1)} %pad_maximum_fusion), channel_id=1, source_target_pairs={{0,4},{1,5},{2,6},{3,7},{4,8},{5,9},{6,10},{7,11},{8,12},{9,13},{1... | collective-permute-start | bytes 3145736 | tf_op jit(solution)/shard_map/ppermute | solution.py:24
  4.5 1.1 %fusion = bf16[2,128,1024]{2,1,0:T(8,128)(2,1)S(1)} fusion(bf16[1,256,1024]{2,1,0:T(8,128)(2,1)} %bitcast.6, bf16[1,256,1024]{2,1,0:T(8,128)(2,1)} %bitcast.10), kind=kLoop, calls=%fused_computation.6 | loop fusion | flops 262144 | bytes 1572864 | tf_op jit(solution)/shard_map/stack | solution.py:142
  5.6 0.7 collective-permute-start
  6.3 4.2 %collective-permute-start.7 = (bf16[2,256,1024]{2,1,0:T(8,128)(2,1)S(1)}, bf16[2,256,1024]{2,1,0:T(8,128)(2,1)}, u32[]{:S(2)}, u32[]{:S(2)}) collective-permute-start(bf16[2,256,1024]{2,1,0:T(8,128)(2,1)S(1)} %pad_maximum_fusion), channel_id=1, source_target_pairs={{0,2},{1,3},{4,6},{5,7},{8,10},{9,11},{12,14},{13,15},{16,18},{17,... | collective-permute-start | bytes 3145736 | tf_op jit(solution)/shard_map/ppermute | solution.py:24
  10.5 16.8 %collective-permute-done.4 = bf16[2,256,1024]{2,1,0:T(8,128)(2,1)S(1)} collective-permute-done((bf16[2,256,1024]{2,1,0:T(8,128)(2,1)S(1)}, bf16[2,256,1024]{2,1,0:T(8,128)(2,1)S(1)}, u32[]{:S(2)}, u32[]{:S(2)}) %collective-permute-start.4) | collective-permute-done | bytes 1048608 | tf_op jit(solution)/shard_map/ppermute | solution.py:24
  27.2 1.3 %collective-permute-start.6 = (bf16[2,256,1024]{2,1,0:T(8,128)(2,1)S(1)}, bf16[2,256,1024]{2,1,0:T(8,128)(2,1)}, u32[]{:S(2)}, u32[]{:S(2)}) collective-permute-start(bf16[2,256,1024]{2,1,0:T(8,128)(2,1)S(1)} %collective-permute-done.4), channel_id=1, source_target_pairs={{2,0},{3,1},{6,4},{7,5},{10,8},{11,9},{14,12},{15,13},{18,16},{19,... | collective-permute-start | bytes 3145736 | tf_op jit(solution)/shard_map/ppermute | solution.py:24
  28.5 0.0 collective-permute-done
  28.5 1.1 %broadcast_select_fusion.1 = bf16[2,128,1024]{2,1,0:T(8,128)(2,1)S(1)} fusion(bf16[2,128,1024]{2,1,0:T(8,128)(2,1)S(1)} %collective-permute-done, pred[]{:T(512)S(6)} %and.53, bf16[1,256,1024]{2,1,0:T(8,128)(2,1)} %bitcast.11, bf16[1,256,1024]{2,1,0:T(8,128)(2,1)} %bitcast.7), kind=kLoop, calls=%fused_computation.8 | loop fusion | flops 524288 | bytes 2097153 | tf_op jit(solution)/shard_map/jit(_where)/select_n | solution.py:62
  29.6 1.5 %collective-permute-start.1 = (bf16[2,128,1024]{2,1,0:T(8,128)(2,1)S(1)}, bf16[2,128,1024]{2,1,0:T(8,128)(2,1)}, u32[]{:S(2)}, u32[]{:S(2)}) collective-permute-start(bf16[2,128,1024]{2,1,0:T(8,128)(2,1)S(1)} %broadcast_select_fusion.1), channel_id=1, source_target_pairs={{0,4},{8,12},{16,20},{24,28}} | collective-permute-start | bytes 1572872 | tf_op jit(solution)/shard_map/ppermute | solution.py:59
  31.1 0.1 broadcast_select_fusion.2
  31.2 1.5 %collective-permute-start.2 = (bf16[2,128,1024]{2,1,0:T(8,128)(2,1)S(1)}, bf16[2,128,1024]{2,1,0:T(8,128)(2,1)}, u32[]{:S(2)}, u32[]{:S(2)}) collective-permute-start(bf16[2,128,1024]{2,1,0:T(8,128)(2,1)S(1)} %broadcast_select_fusion.2), channel_id=1, source_target_pairs={{0,2},{4,6},{8,10},{12,14},{16,18},{20,22},{24,26},{28,30}} | collective-permute-start | bytes 1572872 | tf_op jit(solution)/shard_map/ppermute | solution.py:59
  32.7 1.3 %collective-permute-start.9 = (bf16[2,256,1024]{2,1,0:T(8,128)(2,1)S(1)}, bf16[2,256,1024]{2,1,0:T(8,128)(2,1)}, u32[]{:S(2)}, u32[]{:S(2)}) collective-permute-start(bf16[2,256,1024]{2,1,0:T(8,128)(2,1)S(1)} %pad_maximum_fusion), channel_id=1, source_target_pairs={{0,1},{2,3},{4,5},{6,7},{8,9},{10,11},{12,13},{14,15},{16,17},{18,... | collective-permute-start | bytes 3145736 | tf_op jit(solution)/shard_map/ppermute | solution.py:24
  34.0 0.1 constant_dynamic-slice_fusion
  34.1 0.1 copy.6
  34.2 17.2 %collective-permute-start.5 = (bf16[2,256,1024]{2,1,0:T(8,128)(2,1)S(1)}, bf16[2,256,1024]{2,1,0:T(8,128)(2,1)S(1)}, u32[]{:S(2)}, u32[]{:S(2)}) collective-permute-start(bf16[2,256,1024]{2,1,0:T(8,128)(2,1)S(1)} %collective-permute-done.4), channel_id=1, source_target_pairs={{1,0},{3,2},{5,4},{7,6},{9,8},{11,10},{13,12},{15,14},{17,16},{19,... | collective-permute-start | bytes 3145736 | tf_op jit(solution)/shard_map/ppermute | solution.py:24
  51.4 1.3 %broadcast_select_fusion = bf16[2,256,1024]{2,1,0:T(8,128)(2,1)S(1)} fusion(bf16[2,256,1024]{2,1,0:T(8,128)(2,1)} %collective-permute-done.6, bf16[2,256,1024]{2,1,0:T(8,128)(2,1)} %collective-permute-done.7, pred[]{:T(512)S(6)} %eq.40), kind=kLoop, calls=%fused_computation.5 | loop fusion | flops 524288 | bytes 3145729 | tf_op jit(solution)/shard_map/jit(_where)/select_n | solution.py:35
  52.7 3.5 %collective-permute-start.8 = (bf16[2,256,1024]{2,1,0:T(8,128)(2,1)S(1)}, bf16[2,256,1024]{2,1,0:T(8,128)(2,1)S(1)}, u32[]{:S(2)}, u32[]{:S(2)}) collective-permute-start(bf16[2,256,1024]{2,1,0:T(8,128)(2,1)S(1)} %broadcast_select_fusion), channel_id=1, source_target_pairs={{0,1},{1,0},{2,3},{3,2},{4,5},{5,4},{6,7},{7,6},{8,9},{9,8},{10,11... | collective-permute-start | bytes 3145736 | tf_op jit(solution)/shard_map/ppermute | solution.py:39
  56.2 0.1 broadcast_select_fusion.3
  56.3 1.3 %collective-permute-start.3 = (bf16[2,128,1024]{2,1,0:T(8,128)(2,1)S(1)}, bf16[2,128,1024]{2,1,0:T(8,128)(2,1)S(1)}, u32[]{:S(2)}, u32[]{:S(2)}) collective-permute-start(bf16[2,128,1024]{2,1,0:T(8,128)(2,1)S(1)} %broadcast_select_fusion.3), channel_id=1, source_target_pairs={{0,1},{2,3},{4,5},{6,7},{8,9},{10,11},{12,13},{14,15},{16,17},{18,... | collective-permute-start | bytes 1572872 | tf_op jit(solution)/shard_map/ppermute | solution.py:59
  57.6 0.1 compare_convert_fusion.diag_ref
  57.7 0.0 copy-start.2
  57.7 0.0 copy-start.3
  57.7 2.4 %collective-permute-done.3 = bf16[2,128,1024]{2,1,0:T(8,128)(2,1)S(1)} collective-permute-done((bf16[2,128,1024]{2,1,0:T(8,128)(2,1)S(1)}, bf16[2,128,1024]{2,1,0:T(8,128)(2,1)S(1)}, u32[]{:S(2)}, u32[]{:S(2)}) %collective-permute-start.3) | collective-permute-done | bytes 524320 | tf_op jit(solution)/shard_map/ppermute | solution.py:59
  60.1 0.2 select_dynamic-update-slice_fusion.2
  60.3 0.1 constant_dynamic-update-slice_fusion.2
  60.4 0.0 copy-start.1
  60.4 0.4 select_dynamic-update-slice_fusion.1
  60.8 0.1 constant_dynamic-update-slice_fusion.1
  60.9 1.7 %select_dynamic-update-slice_fusion = bf16[2,1408,1024]{2,1,0:T(8,128)(2,1)S(1)} fusion(bf16[2,1408,1024]{2,1,0:T(8,128)(2,1)S(1)} %constant_dynamic-update-slice_fusion.1, bf16[2,256,1024]{2,1,0:T(8,128)(2,1)S(1)} %collective-permute-done.8, bf16[2,256,1024]{2,1,0:T(8,128)(2,1)} %collective-permute-done.9, pred[]{:T(512)S(6)} %eq.39), kind=kLoop, calls=%fused_computation.3 | loop fusion | flops 524288 | bytes 3145729
  62.6 0.1 constant_dynamic-update-slice_fusion
  62.7 31.7 %shard_map.46 = bf16[256,4096]{1,0:T(8,128)(2,1)} custom-call(s32[2,11]{1,0:T(2,128)S(1)} %fusion.1.slot_ref, s32[2,11]{1,0:T(2,128)S(1)} %compare_convert_fusion.diag_ref, bf16[256,4096]{1,0:T(8,128)(2,1)S(1)} %copy-done.1, bf16[2,11,128,1024]{3,2,1,0:T(8,128)(2,1)S(1)} %bitcast.3, bf16[2,11,128,1024]{3,2,1,0:T(8,128)(2,1)S(1)} %bitcast.4), custom_call_target="tpu_custom_call" | custom-call | flops 5905580032 | bytes 9961472 | tf_op jit(solution)/shard_map/pallas_call | solution.py:121
  (14 shorter events, 0.0 us)
Async XLA Ops:
  0.0 34.0 %copy-start = (s32[32,11]{0,1:T(8,128)S(1)}, s32[32,11]{0,1:T(8,128)}, u32[]{:S(2)}) copy-start(s32[32,11]{0,1:T(8,128)} %param.7) | copy-start | bytes 4228
  1.3 25.9 %collective-permute-start.4 = (bf16[2,256,1024]{2,1,0:T(8,128)(2,1)S(1)}, bf16[2,256,1024]{2,1,0:T(8,128)(2,1)S(1)}, u32[]{:S(2)}, u32[]{:S(2)}) collective-permute-start(bf16[2,256,1024]{2,1,0:T(8,128)(2,1)S(1)} %pad_maximum_fusion), channel_id=1, source_target_pairs={{0,4},{1,5},{2,6},{3,7},{4,8},{5,9},{6,10},{7,11},{8,12},{9,13},{1... | collective-permute-start | bytes 3145736 | tf_op jit(solution)/shard_map/ppermute | solution.py:24
  5.6 22.9 %collective-permute-start = (bf16[2,128,1024]{2,1,0:T(8,128)(2,1)S(1)}, bf16[2,128,1024]{2,1,0:T(8,128)(2,1)S(1)}, u32[]{:S(2)}, u32[]{:S(2)}) collective-permute-start(bf16[2,128,1024]{2,1,0:T(8,128)(2,1)S(1)} %fusion), channel_id=1, source_target_pairs={{0,8},{16,24}} | collective-permute-start | bytes 1572872 | tf_op jit(solution)/shard_map/ppermute | solution.py:59
  6.3 45.1 %collective-permute-start.7 = (bf16[2,256,1024]{2,1,0:T(8,128)(2,1)S(1)}, bf16[2,256,1024]{2,1,0:T(8,128)(2,1)}, u32[]{:S(2)}, u32[]{:S(2)}) collective-permute-start(bf16[2,256,1024]{2,1,0:T(8,128)(2,1)S(1)} %pad_maximum_fusion), channel_id=1, source_target_pairs={{0,2},{1,3},{4,6},{5,7},{8,10},{9,11},{12,14},{13,15},{16,18},{17,... | collective-permute-start | bytes 3145736 | tf_op jit(solution)/shard_map/ppermute | solution.py:24
  27.2 24.2 %collective-permute-start.6 = (bf16[2,256,1024]{2,1,0:T(8,128)(2,1)S(1)}, bf16[2,256,1024]{2,1,0:T(8,128)(2,1)}, u32[]{:S(2)}, u32[]{:S(2)}) collective-permute-start(bf16[2,256,1024]{2,1,0:T(8,128)(2,1)S(1)} %collective-permute-done.4), channel_id=1, source_target_pairs={{2,0},{3,1},{6,4},{7,5},{10,8},{11,9},{14,12},{15,13},{18,16},{19,... | collective-permute-start | bytes 3145736 | tf_op jit(solution)/shard_map/ppermute | solution.py:24
  29.6 1.5 %collective-permute-start.1 = (bf16[2,128,1024]{2,1,0:T(8,128)(2,1)S(1)}, bf16[2,128,1024]{2,1,0:T(8,128)(2,1)}, u32[]{:S(2)}, u32[]{:S(2)}) collective-permute-start(bf16[2,128,1024]{2,1,0:T(8,128)(2,1)S(1)} %broadcast_select_fusion.1), channel_id=1, source_target_pairs={{0,4},{8,12},{16,20},{24,28}} | collective-permute-start | bytes 1572872 | tf_op jit(solution)/shard_map/ppermute | solution.py:59
  31.2 25.0 %collective-permute-start.2 = (bf16[2,128,1024]{2,1,0:T(8,128)(2,1)S(1)}, bf16[2,128,1024]{2,1,0:T(8,128)(2,1)}, u32[]{:S(2)}, u32[]{:S(2)}) collective-permute-start(bf16[2,128,1024]{2,1,0:T(8,128)(2,1)S(1)} %broadcast_select_fusion.2), channel_id=1, source_target_pairs={{0,2},{4,6},{8,10},{12,14},{16,18},{20,22},{24,26},{28,30}} | collective-permute-start | bytes 1572872 | tf_op jit(solution)/shard_map/ppermute | solution.py:59
  32.7 28.2 %collective-permute-start.9 = (bf16[2,256,1024]{2,1,0:T(8,128)(2,1)S(1)}, bf16[2,256,1024]{2,1,0:T(8,128)(2,1)}, u32[]{:S(2)}, u32[]{:S(2)}) collective-permute-start(bf16[2,256,1024]{2,1,0:T(8,128)(2,1)S(1)} %pad_maximum_fusion), channel_id=1, source_target_pairs={{0,1},{2,3},{4,5},{6,7},{8,9},{10,11},{12,13},{14,15},{16,17},{18,... | collective-permute-start | bytes 3145736 | tf_op jit(solution)/shard_map/ppermute | solution.py:24
  34.2 26.2 %collective-permute-start.5 = (bf16[2,256,1024]{2,1,0:T(8,128)(2,1)S(1)}, bf16[2,256,1024]{2,1,0:T(8,128)(2,1)S(1)}, u32[]{:S(2)}, u32[]{:S(2)}) collective-permute-start(bf16[2,256,1024]{2,1,0:T(8,128)(2,1)S(1)} %collective-permute-done.4), channel_id=1, source_target_pairs={{1,0},{3,2},{5,4},{7,6},{9,8},{11,10},{13,12},{15,14},{17,16},{19,... | collective-permute-start | bytes 3145736 | tf_op jit(solution)/shard_map/ppermute | solution.py:24
  52.7 7.6 %collective-permute-start.8 = (bf16[2,256,1024]{2,1,0:T(8,128)(2,1)S(1)}, bf16[2,256,1024]{2,1,0:T(8,128)(2,1)S(1)}, u32[]{:S(2)}, u32[]{:S(2)}) collective-permute-start(bf16[2,256,1024]{2,1,0:T(8,128)(2,1)S(1)} %broadcast_select_fusion), channel_id=1, source_target_pairs={{0,1},{1,0},{2,3},{3,2},{4,5},{5,4},{6,7},{7,6},{8,9},{9,8},{10,11... | collective-permute-start | bytes 3145736 | tf_op jit(solution)/shard_map/ppermute | solution.py:39
  56.3 3.8 %collective-permute-start.3 = (bf16[2,128,1024]{2,1,0:T(8,128)(2,1)S(1)}, bf16[2,128,1024]{2,1,0:T(8,128)(2,1)S(1)}, u32[]{:S(2)}, u32[]{:S(2)}) collective-permute-start(bf16[2,128,1024]{2,1,0:T(8,128)(2,1)S(1)} %broadcast_select_fusion.3), channel_id=1, source_target_pairs={{0,1},{2,3},{4,5},{6,7},{8,9},{10,11},{12,13},{14,15},{16,17},{18,... | collective-permute-start | bytes 1572872 | tf_op jit(solution)/shard_map/ppermute | solution.py:59
  57.7 4.9 %copy-start.2 = (bf16[256,1024]{1,0:T(8,128)(2,1)S(1)}, bf16[256,1024]{1,0:T(8,128)(2,1)}, u32[]{:S(2)}) copy-start(bf16[256,1024]{1,0:T(8,128)(2,1)} %param.5) | copy-start | bytes 1572868
  57.7 4.9 %copy-start.3 = (bf16[256,1024]{1,0:T(8,128)(2,1)S(1)}, bf16[256,1024]{1,0:T(8,128)(2,1)}, u32[]{:S(2)}) copy-start(bf16[256,1024]{1,0:T(8,128)(2,1)} %param.6) | copy-start | bytes 1572868
  60.4 2.4 %copy-start.1 = (bf16[256,4096]{1,0:T(8,128)(2,1)S(1)}, bf16[256,4096]{1,0:T(8,128)(2,1)}, u32[]{:S(2)}) copy-start(bf16[256,4096]{1,0:T(8,128)(2,1)} %q_ref.1) | copy-start | bytes 6291460

commit v11 on v10

--- a/solution.py
+++ b/solution.py
@@ -78,9 +78,9 @@
         stacked = jnp.concatenate([q[:, j * HD:(j + 1) * HD] for j in heads], axis=0)
         run_max = jnp.full((rows, BLK), -jnp.inf, jnp.float32)
         for s in range(LIST):
-            key = k_ref[0, slot_ref[local, s]]
-            sc = lax.dot_general(
-                stacked, key, (((1,), (1,)), ((), ())), preferred_element_type=jnp.float32
+            key_t = k_ref[0, slot_ref[local, s], 0]
+            sc = jnp.dot(
+                stacked, key_t, preferred_element_type=jnp.float32
             ) + bias_sc[diag_ref[local, s]]
             score_sc[half, s] = sc
             run_max = jnp.maximum(run_max, sc)
@@ -90,7 +90,7 @@
         for s in range(LIST):
             powers = jnp.exp2((score_sc[half, s] - row_max) * exp2_scale)
             total = total + powers
-            value = v_ref[0, slot_ref[local, s]]
+            value = v_ref[0, slot_ref[local, s], 0]
             acc = acc + jnp.dot(
                 powers.astype(jnp.bfloat16), value, preferred_element_type=jnp.float32
             )
@@ -109,8 +109,8 @@
         grid=(KVH, blocks_here),
         in_specs=[
             pl.BlockSpec((BLK, GROUP * HD), lambda g, b, *_: (b, g)),
-            pl.BlockSpec((1, buffer_blocks, BLK, HD), lambda g, b, *_: (0, 0, 0, g)),
-            pl.BlockSpec((1, buffer_blocks, BLK, HD), lambda g, b, *_: (1, 0, 0, g)),
+            pl.BlockSpec((1, buffer_blocks, 1, HD, BLK), lambda g, b, *_: (0, 0, g, 0, 0)),
+            pl.BlockSpec((1, buffer_blocks, 1, BLK, HD), lambda g, b, *_: (1, 0, g, 0, 0)),
         ],
         out_specs=pl.BlockSpec((BLK, GROUP * HD), lambda g, b, *_: (b, g)),
         scratch_shapes=[
@@ -139,19 +139,19 @@
     blocks_here = tok_rows // BLK
     ctx_count = lax.axis_size("ctx")
     own_index = lax.axis_index("ctx")
-    kv = jnp.stack([key_rows, value_rows])
+    key_tiles = key_rows.reshape(blocks_here, BLK, KVH, HD).transpose(0, 2, 3, 1)
+    value_tiles = value_rows.reshape(blocks_here, BLK, KVH, HD).transpose(0, 2, 1, 3)
+    kv = jnp.stack([key_tiles, value_tiles])
     assert blocks_here == 2 and ctx_count % 4 == 0
     early = window_blocks(kv, "ctx")
     columns = blocks_here * ctx_count // STRIDE
     spread = STRIDE // blocks_here
     column_blocks = [
-        tree_broadcast(kv[:, :BLK], "ctx", column * spread, ctx_count)
+        tree_broadcast(kv[:, :1], "ctx", column * spread, ctx_count)
         for column in range(columns)
     ]
     buffer_blocks = columns + 4 * blocks_here + blocks_here
-    kv_buffer = jnp.concatenate(column_blocks + early + [kv], axis=1).reshape(
-        2, buffer_blocks, BLK, kv.shape[2]
-    )
+    kv_buffer = jnp.concatenate(column_blocks + early + [kv], axis=1)
     first_block = own_index * blocks_here - 4 * blocks_here
     rows_pattern = lax.dynamic_slice_in_dim(pattern, own_index * blocks_here, blocks_here, 0)
     slots = jnp.where(

time: 94.8 us -> 96.8 us (1.021)
  local copies, waits for them, and re-layouts: 0.33 us -> 4.47 us
  other arithmetic: 7.44 us -> 4.21 us
  starting transfers between devices: 35.5 us -> 37.5 us
  Pallas kernels: 31.7 us -> 30.3 us
    unnamed x11 -> x9, local copies, waits for them, and re-layouts: 0.26 us -> 3.92 us
    another operation x2, other arithmetic: 2.38 us -> 0.15 us  [per_device(): kv = jnp.stack([key_tiles, value_tiles])]
    pallas_call x1, Pallas kernels: 31.7 us -> 30.3 us  [attend(): pl.pallas_call(attend_kernel, out_shape=jax.ShapeDtypeStruct(queries.shap...]
    select_n x3, other arithmetic: 1.25 us -> 0.21 us  [tree_broadcast(): held = jnp.where(takes, got, held)]
    ppermute x5, starting transfers between devices: 27.1 us -> 28.1 us  [shifted(): return lax.ppermute(shard, axis, pairs)]
  transfers between devices with their start and end apart: 10 -> 10, of which waited for: 2 -> 2; matrix products, arithmetic and copies ran while one was open for 5% -> 4% of each run, Pallas kernels for 0% -> 0%
where the time goes in v11:
time: 96.8 us; the launch traced here: 96.3 us
  starting transfers between devices  37.5 us (39%)
  Pallas kernels  30.3 us (31%)
  waiting for transfers between devices  19.6 us (20%)
  local copies, waits for them, and re-layouts  4.47 us (5%)
  other arithmetic  4.21 us (4%)
    pallas_call x1, Pallas kernels, attend(): pl.pallas_call(attend_kernel, out_shape=jax.ShapeDtypeStruct(queries.shap...  30.3 us
    ppermute x5, starting transfers between devices, shifted(): return lax.ppermute(shard, axis, pairs)  28.1 us
    ppermute x5, waiting for transfers between devices, shifted(): return lax.ppermute(shard, axis, pairs)  17.1 us
    ppermute x4, starting transfers between devices, tree_broadcast(): got = lax.ppermute(held, axis, pairs)  4.97 us
    ppermute x1, starting transfers between devices, window_blocks(): partner_back2 = lax.ppermute(back2, axis, swap_pairs)  4.4 us
    unnamed x9, local copies, waits for them, and re-layouts  3.92 us
    ppermute x4, waiting for transfers between devices, tree_broadcast(): got = lax.ppermute(held, axis, pairs)  2.42 us
    unnamed x3, other arithmetic  2.28 us
  transfers between devices with their start and end apart: 10, of which 2 were waited for; matrix products, arithmetic and copies ran while one was open for 4% of the time, Pallas kernels for 0%

profile of v11, /device:TPU:19, one launch (start us, length us, event | category | flops | bytes accessed | tf_op | source)
XLA Modules:
  0.0 96.3 jit_solution(6422358003503107903)
XLA Ops:
  0.0 1.1 %copy.10 = bf16[32,8,8,128]{3,2,1,0:T(8,128)(2,1)S(1)} copy(bf16[32,8,8,128]{3,1,2,0:T(8,128)(2,1)} %bitcast.22) | data formatting | bytes 1048576
  1.1 0.4 copy.7
  1.5 1.1 %copy.11 = bf16[32,8,8,128]{3,2,1,0:T(8,128)(2,1)S(1)} copy(bf16[32,8,8,128]{3,1,2,0:T(8,128)(2,1)} %bitcast.23) | data formatting | bytes 1048576
  2.7 0.1 copy.13
  2.8 0.1 pad_maximum_fusion
  2.9 3.2 %collective-permute-start.4 = (bf16[2,2,8,128,128]{4,3,2,1,0:T(8,128)(2,1)S(1)}, bf16[2,2,8,128,128]{4,3,2,1,0:T(8,128)(2,1)}, u32[]{:S(2)}, u32[]{:S(2)}) collective-permute-start(bf16[2,2,8,128,128]{4,3,2,1,0:T(8,128)(2,1)S(1)} %pad_maximum_fusion), channel_id=1, source_target_pairs={{0,4},{1,5},{2,6},{3,7},{4,8},{5,9},{6,10},{7,11},{8,12},{9,13},{1... | collective-permute-start | bytes 3145736 | tf_op jit(solution)/shard_map/ppermute | solution.py:24
  6.1 0.1 fusion
  6.2 1.5 %collective-permute-start = (bf16[2,1,8,128,128]{4,3,2,1,0:T(8,128)(2,1)S(1)}, bf16[2,1,8,128,128]{4,3,2,1,0:T(8,128)(2,1)}, u32[]{:S(2)}, u32[]{:S(2)}) collective-permute-start(bf16[2,1,8,128,128]{4,3,2,1,0:T(8,128)(2,1)S(1)} %fusion), channel_id=1, source_target_pairs={{0,8},{16,24}} | collective-permute-start | bytes 1572872 | tf_op jit(solution)/shard_map/ppermute | solution.py:59
  7.6 4.1 %collective-permute-start.7 = (bf16[2,2,8,128,128]{4,3,2,1,0:T(8,128)(2,1)S(1)}, bf16[2,2,8,128,128]{4,3,2,1,0:T(8,128)(2,1)}, u32[]{:S(2)}, u32[]{:S(2)}) collective-permute-start(bf16[2,2,8,128,128]{4,3,2,1,0:T(8,128)(2,1)S(1)} %pad_maximum_fusion), channel_id=1, source_target_pairs={{0,2},{1,3},{4,6},{5,7},{8,10},{9,11},{12,14},{13,15},{16,18},{17,... | collective-permute-start | bytes 3145736 | tf_op jit(solution)/shard_map/ppermute | solution.py:24
  11.8 17.1 %collective-permute-done.4 = bf16[2,2,8,128,128]{4,3,2,1,0:T(8,128)(2,1)} collective-permute-done((bf16[2,2,8,128,128]{4,3,2,1,0:T(8,128)(2,1)S(1)}, bf16[2,2,8,128,128]{4,3,2,1,0:T(8,128)(2,1)}, u32[]{:S(2)}, u32[]{:S(2)}) %collective-permute-start.4) | collective-permute-done | bytes 1048608 | tf_op jit(solution)/shard_map/ppermute | solution.py:24
  28.9 1.3 %collective-permute-start.6 = (bf16[2,2,8,128,128]{4,3,2,1,0:T(8,128)(2,1)}, bf16[2,2,8,128,128]{4,3,2,1,0:T(8,128)(2,1)}, u32[]{:S(2)}, u32[]{:S(2)}) collective-permute-start(bf16[2,2,8,128,128]{4,3,2,1,0:T(8,128)(2,1)} %collective-permute-done.4), channel_id=1, source_target_pairs={{2,0},{3,1},{6,4},{7,5},{10,8},{11,9},{14,12},{15,13},{18,16},{19,... | collective-permute-start | bytes 3145736 | tf_op jit(solution)/shard_map/ppermute | solution.py:24
  30.2 0.1 broadcast_select_fusion.1
  30.3 1.5 %collective-permute-start.1 = (bf16[2,1,8,128,128]{4,3,2,1,0:T(8,128)(2,1)S(1)}, bf16[2,1,8,128,128]{4,3,2,1,0:T(8,128)(2,1)}, u32[]{:S(2)}, u32[]{:S(2)}) collective-permute-start(bf16[2,1,8,128,128]{4,3,2,1,0:T(8,128)(2,1)S(1)} %broadcast_select_fusion.1), channel_id=1, source_target_pairs={{0,4},{8,12},{16,20},{24,28}} | collective-permute-start | bytes 1572872 | tf_op jit(solution)/shard_map/ppermute | solution.py:59
  31.8 0.1 broadcast_select_fusion.2
  31.9 0.7 collective-permute-start.2
  32.6 1.3 %collective-permute-start.9 = (bf16[2,2,8,128,128]{4,3,2,1,0:T(8,128)(2,1)S(1)}, bf16[2,2,8,128,128]{4,3,2,1,0:T(8,128)(2,1)}, u32[]{:S(2)}, u32[]{:S(2)}) collective-permute-start(bf16[2,2,8,128,128]{4,3,2,1,0:T(8,128)(2,1)S(1)} %pad_maximum_fusion), channel_id=1, source_target_pairs={{0,1},{2,3},{4,5},{6,7},{8,9},{10,11},{12,13},{14,15},{16,17},{18,... | collective-permute-start | bytes 3145736 | tf_op jit(solution)/shard_map/ppermute | solution.py:24
  33.9 0.1 constant_dynamic-slice_fusion
  34.0 0.1 copy.9
  34.1 18.2 %collective-permute-start.5 = (bf16[2,2,8,128,128]{4,3,2,1,0:T(8,128)(2,1)}, bf16[2,2,8,128,128]{4,3,2,1,0:T(8,128)(2,1)S(1)}, u32[]{:S(2)}, u32[]{:S(2)}) collective-permute-start(bf16[2,2,8,128,128]{4,3,2,1,0:T(8,128)(2,1)} %collective-permute-done.4), channel_id=1, source_target_pairs={{1,0},{3,2},{5,4},{7,6},{9,8},{11,10},{13,12},{15,14},{17,16},{19,... | collective-permute-start | bytes 3145736 | tf_op jit(solution)/shard_map/ppermute | solution.py:24
  52.3 1.3 %broadcast_select_fusion = bf16[2,2,8,128,128]{4,3,2,1,0:T(8,128)(2,1)S(1)} fusion(bf16[2,2,8,128,128]{4,3,2,1,0:T(8,128)(2,1)} %collective-permute-done.6, bf16[2,2,8,128,128]{4,3,2,1,0:T(8,128)(2,1)} %collective-permute-done.7, pred[]{:T(512)S(6)} %eq.40), kind=kLoop, calls=%fused_computation.5 | loop fusion | flops 524288 | bytes 3145729 | tf_op jit(solution)/shard_map/jit(_where)/select_n | solution.py:35
  53.7 4.4 %collective-permute-start.8 = (bf16[2,2,8,128,128]{4,3,2,1,0:T(8,128)(2,1)S(1)}, bf16[2,2,8,128,128]{4,3,2,1,0:T(8,128)(2,1)S(1)}, u32[]{:S(2)}, u32[]{:S(2)}) collective-permute-start(bf16[2,2,8,128,128]{4,3,2,1,0:T(8,128)(2,1)S(1)} %broadcast_select_fusion), channel_id=1, source_target_pairs={{0,1},{1,0},{2,3},{3,2},{4,5},{5,4},{6,7},{7,6},{8,9},{9,8},{10,11... | collective-permute-start | bytes 3145736 | tf_op jit(solution)/shard_map/ppermute | solution.py:39
  58.1 0.1 broadcast_select_fusion.3
  58.2 1.3 %collective-permute-start.3 = (bf16[2,1,8,128,128]{4,3,2,1,0:T(8,128)(2,1)S(1)}, bf16[2,1,8,128,128]{4,3,2,1,0:T(8,128)(2,1)S(1)}, u32[]{:S(2)}, u32[]{:S(2)}) collective-permute-start(bf16[2,1,8,128,128]{4,3,2,1,0:T(8,128)(2,1)S(1)} %broadcast_select_fusion.3), channel_id=1, source_target_pairs={{0,1},{2,3},{4,5},{6,7},{8,9},{10,11},{12,13},{14,15},{16,17},{18,... | collective-permute-start | bytes 1572872 | tf_op jit(solution)/shard_map/ppermute | solution.py:59
  59.5 0.1 compare_convert_fusion.diag_ref
  59.6 2.4 %collective-permute-done.3 = bf16[2,1,8,128,128]{4,3,2,1,0:T(8,128)(2,1)S(1)} collective-permute-done((bf16[2,1,8,128,128]{4,3,2,1,0:T(8,128)(2,1)S(1)}, bf16[2,1,8,128,128]{4,3,2,1,0:T(8,128)(2,1)S(1)}, u32[]{:S(2)}, u32[]{:S(2)}) %collective-permute-start.3) | collective-permute-done | bytes 524320 | tf_op jit(solution)/shard_map/ppermute | solution.py:59
  62.0 0.2 select_dynamic-update-slice_fusion.2
  62.1 1.4 %constant_dynamic-update-slice_fusion.2 = bf16[2,11,8,128,128]{4,3,2,1,0:T(8,128)(2,1)S(1)} fusion(bf16[2,11,8,128,128]{4,3,2,1,0:T(8,128)(2,1)S(1)} %select_dynamic-update-slice_fusion.2, bf16[2,2,8,128,128]{4,3,2,1,0:T(8,128)(2,1)} %collective-permute-done.4), kind=kLoop, calls=%fused_computation.14 | loop fusion | bytes 2097152
  63.6 0.4 select_dynamic-update-slice_fusion.1
  64.0 0.1 constant_dynamic-update-slice_fusion.1
  64.2 1.7 %select_dynamic-update-slice_fusion = bf16[2,11,8,128,128]{4,3,2,1,0:T(8,128)(2,1)S(1)} fusion(bf16[2,11,8,128,128]{4,3,2,1,0:T(8,128)(2,1)S(1)} %constant_dynamic-update-slice_fusion.1, bf16[2,2,8,128,128]{4,3,2,1,0:T(8,128)(2,1)S(1)} %collective-permute-done.8, bf16[2,2,8,128,128]{4,3,2,1,0:T(8,128)(2,1)} %collective-permute-done.9, pred[]{:T(512)S(6)} %eq.39), kind=kLoop, calls=%fused_computation.3 | loop fusion | flops 524288 | bytes 3145729
  65.9 0.1 constant_dynamic-update-slice_fusion.k_ref.v_ref
  66.0 30.3 %shard_map.46 = bf16[256,4096]{1,0:T(8,128)(2,1)} custom-call(s32[2,11]{1,0:T(2,128)S(1)} %fusion.1.slot_ref, s32[2,11]{1,0:T(2,128)S(1)} %compare_convert_fusion.diag_ref, bf16[256,4096]{1,0:T(8,128)(2,1)S(1)} %copy-done.1, bf16[2,11,8,128,128]{4,3,2,1,0:T(8,128)(2,1)S(1)} %constant_dynamic-update-slice_fusion.k_ref.v_ref, ...), custom_call_target="tpu_custom_call" | custom-call | flops 5905580032 | bytes 9961472 | tf_op jit(solution)/shard_map/pallas_call | solution.py:121
  (14 shorter events, 0.0 us)
Async XLA Ops:
  0.0 33.9 %copy-start = (s32[32,11]{0,1:T(8,128)S(1)}, s32[32,11]{0,1:T(8,128)}, u32[]{:S(2)}) copy-start(s32[32,11]{0,1:T(8,128)} %param.7) | copy-start | bytes 4228
  2.9 26.0 %collective-permute-start.4 = (bf16[2,2,8,128,128]{4,3,2,1,0:T(8,128)(2,1)S(1)}, bf16[2,2,8,128,128]{4,3,2,1,0:T(8,128)(2,1)}, u32[]{:S(2)}, u32[]{:S(2)}) collective-permute-start(bf16[2,2,8,128,128]{4,3,2,1,0:T(8,128)(2,1)S(1)} %pad_maximum_fusion), channel_id=1, source_target_pairs={{0,4},{1,5},{2,6},{3,7},{4,8},{5,9},{6,10},{7,11},{8,12},{9,13},{1... | collective-permute-start | bytes 3145736 | tf_op jit(solution)/shard_map/ppermute | solution.py:24
  6.2 24.0 %collective-permute-start = (bf16[2,1,8,128,128]{4,3,2,1,0:T(8,128)(2,1)S(1)}, bf16[2,1,8,128,128]{4,3,2,1,0:T(8,128)(2,1)}, u32[]{:S(2)}, u32[]{:S(2)}) collective-permute-start(bf16[2,1,8,128,128]{4,3,2,1,0:T(8,128)(2,1)S(1)} %fusion), channel_id=1, source_target_pairs={{0,8},{16,24}} | collective-permute-start | bytes 1572872 | tf_op jit(solution)/shard_map/ppermute | solution.py:59
  7.6 44.7 %collective-permute-start.7 = (bf16[2,2,8,128,128]{4,3,2,1,0:T(8,128)(2,1)S(1)}, bf16[2,2,8,128,128]{4,3,2,1,0:T(8,128)(2,1)}, u32[]{:S(2)}, u32[]{:S(2)}) collective-permute-start(bf16[2,2,8,128,128]{4,3,2,1,0:T(8,128)(2,1)S(1)} %pad_maximum_fusion), channel_id=1, source_target_pairs={{0,2},{1,3},{4,6},{5,7},{8,10},{9,11},{12,14},{13,15},{16,18},{17,... | collective-permute-start | bytes 3145736 | tf_op jit(solution)/shard_map/ppermute | solution.py:24
  28.9 23.4 %collective-permute-start.6 = (bf16[2,2,8,128,128]{4,3,2,1,0:T(8,128)(2,1)}, bf16[2,2,8,128,128]{4,3,2,1,0:T(8,128)(2,1)}, u32[]{:S(2)}, u32[]{:S(2)}) collective-permute-start(bf16[2,2,8,128,128]{4,3,2,1,0:T(8,128)(2,1)} %collective-permute-done.4), channel_id=1, source_target_pairs={{2,0},{3,1},{6,4},{7,5},{10,8},{11,9},{14,12},{15,13},{18,16},{19,... | collective-permute-start | bytes 3145736 | tf_op jit(solution)/shard_map/ppermute | solution.py:24
  30.3 1.5 %collective-permute-start.1 = (bf16[2,1,8,128,128]{4,3,2,1,0:T(8,128)(2,1)S(1)}, bf16[2,1,8,128,128]{4,3,2,1,0:T(8,128)(2,1)}, u32[]{:S(2)}, u32[]{:S(2)}) collective-permute-start(bf16[2,1,8,128,128]{4,3,2,1,0:T(8,128)(2,1)S(1)} %broadcast_select_fusion.1), channel_id=1, source_target_pairs={{0,4},{8,12},{16,20},{24,28}} | collective-permute-start | bytes 1572872 | tf_op jit(solution)/shard_map/ppermute | solution.py:59
  31.9 26.2 %collective-permute-start.2 = (bf16[2,1,8,128,128]{4,3,2,1,0:T(8,128)(2,1)S(1)}, bf16[2,1,8,128,128]{4,3,2,1,0:T(8,128)(2,1)S(1)}, u32[]{:S(2)}, u32[]{:S(2)}) collective-permute-start(bf16[2,1,8,128,128]{4,3,2,1,0:T(8,128)(2,1)S(1)} %broadcast_select_fusion.2), channel_id=1, source_target_pairs={{0,2},{4,6},{8,10},{12,14},{16,18},{20,22},{24,26},{28,30}} | collective-permute-start | bytes 1572872 | tf_op jit(solution)/shard_map/ppermute | solution.py:59
  32.6 31.6 %collective-permute-start.9 = (bf16[2,2,8,128,128]{4,3,2,1,0:T(8,128)(2,1)S(1)}, bf16[2,2,8,128,128]{4,3,2,1,0:T(8,128)(2,1)}, u32[]{:S(2)}, u32[]{:S(2)}) collective-permute-start(bf16[2,2,8,128,128]{4,3,2,1,0:T(8,128)(2,1)S(1)} %pad_maximum_fusion), channel_id=1, source_target_pairs={{0,1},{2,3},{4,5},{6,7},{8,9},{10,11},{12,13},{14,15},{16,17},{18,... | collective-permute-start | bytes 3145736 | tf_op jit(solution)/shard_map/ppermute | solution.py:24
  34.1 29.4 %collective-permute-start.5 = (bf16[2,2,8,128,128]{4,3,2,1,0:T(8,128)(2,1)}, bf16[2,2,8,128,128]{4,3,2,1,0:T(8,128)(2,1)S(1)}, u32[]{:S(2)}, u32[]{:S(2)}) collective-permute-start(bf16[2,2,8,128,128]{4,3,2,1,0:T(8,128)(2,1)} %collective-permute-done.4), channel_id=1, source_target_pairs={{1,0},{3,2},{5,4},{7,6},{9,8},{11,10},{13,12},{15,14},{17,16},{19,... | collective-permute-start | bytes 3145736 | tf_op jit(solution)/shard_map/ppermute | solution.py:24
  53.7 9.9 %collective-permute-start.8 = (bf16[2,2,8,128,128]{4,3,2,1,0:T(8,128)(2,1)S(1)}, bf16[2,2,8,128,128]{4,3,2,1,0:T(8,128)(2,1)S(1)}, u32[]{:S(2)}, u32[]{:S(2)}) collective-permute-start(bf16[2,2,8,128,128]{4,3,2,1,0:T(8,128)(2,1)S(1)} %broadcast_select_fusion), channel_id=1, source_target_pairs={{0,1},{1,0},{2,3},{3,2},{4,5},{5,4},{6,7},{7,6},{8,9},{9,8},{10,11... | collective-permute-start | bytes 3145736 | tf_op jit(solution)/shard_map/ppermute | solution.py:39
  58.2 3.8 %collective-permute-start.3 = (bf16[2,1,8,128,128]{4,3,2,1,0:T(8,128)(2,1)S(1)}, bf16[2,1,8,128,128]{4,3,2,1,0:T(8,128)(2,1)S(1)}, u32[]{:S(2)}, u32[]{:S(2)}) collective-permute-start(bf16[2,1,8,128,128]{4,3,2,1,0:T(8,128)(2,1)S(1)} %broadcast_select_fusion.3), channel_id=1, source_target_pairs={{0,1},{2,3},{4,5},{6,7},{8,9},{10,11},{12,13},{14,15},{16,17},{18,... | collective-permute-start | bytes 1572872 | tf_op jit(solution)/shard_map/ppermute | solution.py:59
  63.5 2.5 %copy-start.1 = (bf16[256,4096]{1,0:T(8,128)(2,1)S(1)}, bf16[256,4096]{1,0:T(8,128)(2,1)}, u32[]{:S(2)}) copy-start(bf16[256,4096]{1,0:T(8,128)(2,1)} %q_ref.1) | copy-start | bytes 6291460

commit v12 on v10

--- a/solution.py
+++ b/solution.py
@@ -16,6 +16,7 @@
 LIST = 11
 GROUP = H // KVH
 PAIR = 2
+KV_STEP = 2
 
 
 def shifted(shard, axis, by, sends):
@@ -73,31 +74,35 @@
     bias_sc[0] = jnp.zeros((rows, BLK), jnp.float32)
     bias_sc[1] = jnp.where(col > row, -jnp.inf, 0.0).astype(jnp.float32)
     q = q_ref[...]
-    for half in range(GROUP // PAIR):
-        heads = range(half * PAIR, (half + 1) * PAIR)
-        stacked = jnp.concatenate([q[:, j * HD:(j + 1) * HD] for j in heads], axis=0)
-        run_max = jnp.full((rows, BLK), -jnp.inf, jnp.float32)
-        for s in range(LIST):
-            key = k_ref[0, slot_ref[local, s]]
-            sc = lax.dot_general(
-                stacked, key, (((1,), (1,)), ((), ())), preferred_element_type=jnp.float32
-            ) + bias_sc[diag_ref[local, s]]
-            score_sc[half, s] = sc
-            run_max = jnp.maximum(run_max, sc)
-        row_max = jnp.max(run_max, axis=1, keepdims=True)
-        total = jnp.zeros((rows, BLK), jnp.float32)
-        acc = jnp.zeros((rows, HD), jnp.float32)
-        for s in range(LIST):
-            powers = jnp.exp2((score_sc[half, s] - row_max) * exp2_scale)
-            total = total + powers
-            value = v_ref[0, slot_ref[local, s]]
-            acc = acc + jnp.dot(
-                powers.astype(jnp.bfloat16), value, preferred_element_type=jnp.float32
-            )
-        denominator = jnp.sum(total, axis=1, keepdims=True)
-        result = (acc / denominator).astype(jnp.bfloat16)
-        for k, j in enumerate(heads):
-            o_ref[:, j * HD:(j + 1) * HD] = result[k * BLK:(k + 1) * BLK]
+    chain = 0
+    for kv_head in range(KV_STEP):
+        kv_lanes = slice(kv_head * HD, (kv_head + 1) * HD)
+        for half in range(GROUP // PAIR):
+            heads = [kv_head * GROUP + j for j in range(half * PAIR, (half + 1) * PAIR)]
+            stacked = jnp.concatenate([q[:, j * HD:(j + 1) * HD] for j in heads], axis=0)
+            run_max = jnp.full((rows, BLK), -jnp.inf, jnp.float32)
+            for s in range(LIST):
+                key = k_ref[0, slot_ref[local, s], :, kv_lanes]
+                sc = lax.dot_general(
+                    stacked, key, (((1,), (1,)), ((), ())), preferred_element_type=jnp.float32
+                ) + bias_sc[diag_ref[local, s]]
+                score_sc[chain, s] = sc
+                run_max = jnp.maximum(run_max, sc)
+            row_max = jnp.max(run_max, axis=1, keepdims=True)
+            total = jnp.zeros((rows, BLK), jnp.float32)
+            acc = jnp.zeros((rows, HD), jnp.float32)
+            for s in range(LIST):
+                powers = jnp.exp2((score_sc[chain, s] - row_max) * exp2_scale)
+                total = total + powers
+                value = v_ref[0, slot_ref[local, s], :, kv_lanes]
+                acc = acc + jnp.dot(
+                    powers.astype(jnp.bfloat16), value, preferred_element_type=jnp.float32
+                )
+            denominator = jnp.sum(total, axis=1, keepdims=True)
+            result = (acc / denominator).astype(jnp.bfloat16)
+            for k, j in enumerate(heads):
+                o_ref[:, j * HD:(j + 1) * HD] = result[k * BLK:(k + 1) * BLK]
+            chain += 1
 
 
 def attend(slots, diag, queries, kv_buffer):
@@ -106,15 +111,15 @@
     flops = 4 * blocks_here * H * BLK * LIST * BLK * HD
     grid_spec = pltpu.PrefetchScalarGridSpec(
         num_scalar_prefetch=2,
-        grid=(KVH, blocks_here),
+        grid=(KVH // KV_STEP, blocks_here),
         in_specs=[
-            pl.BlockSpec((BLK, GROUP * HD), lambda g, b, *_: (b, g)),
-            pl.BlockSpec((1, buffer_blocks, BLK, HD), lambda g, b, *_: (0, 0, 0, g)),
-            pl.BlockSpec((1, buffer_blocks, BLK, HD), lambda g, b, *_: (1, 0, 0, g)),
+            pl.BlockSpec((BLK, KV_STEP * GROUP * HD), lambda g, b, *_: (b, g)),
+            pl.BlockSpec((1, buffer_blocks, BLK, KV_STEP * HD), lambda g, b, *_: (0, 0, 0, g)),
+            pl.BlockSpec((1, buffer_blocks, BLK, KV_STEP * HD), lambda g, b, *_: (1, 0, 0, g)),
         ],
-        out_specs=pl.BlockSpec((BLK, GROUP * HD), lambda g, b, *_: (b, g)),
+        out_specs=pl.BlockSpec((BLK, KV_STEP * GROUP * HD), lambda g, b, *_: (b, g)),
         scratch_shapes=[
-            pltpu.VMEM((GROUP // PAIR, LIST, PAIR * BLK, BLK), jnp.float32),
+            pltpu.VMEM((KV_STEP * GROUP // PAIR, LIST, PAIR * BLK, BLK), jnp.float32),
             pltpu.VMEM((2, PAIR * BLK, BLK), jnp.float32),
         ],
     )

time: 94.8 us -> 88 us (0.928)
  Pallas kernels: 31.7 us -> 24.9 us
    pallas_call x1, Pallas kernels: 31.7 us -> 24.9 us  [attend(): pl.pallas_call(attend_kernel, out_shape=jax.ShapeDtypeStruct(queries.shap...]
where the time goes in v12:
time: 88 us; the launch traced here: 87.6 us
  starting transfers between devices  35.5 us (40%)
  Pallas kernels  24.9 us (28%)
  waiting for transfers between devices  19.2 us (22%)
  other arithmetic  7.44 us (8%)
    ppermute x5, starting transfers between devices, shifted(): return lax.ppermute(shard, axis, pairs)  27.1 us
    pallas_call x1, Pallas kernels, attend(): pl.pallas_call(attend_kernel, out_shape=jax.ShapeDtypeStruct(queries.shap...  24.9 us
    ppermute x5, waiting for transfers between devices, shifted(): return lax.ppermute(shard, axis, pairs)  16.8 us
    ppermute x4, starting transfers between devices, tree_broadcast(): got = lax.ppermute(held, axis, pairs)  4.94 us
    ppermute x1, starting transfers between devices, window_blocks(): partner_back2 = lax.ppermute(back2, axis, swap_pairs)  3.46 us
    ppermute x4, waiting for transfers between devices, tree_broadcast(): got = lax.ppermute(held, axis, pairs)  2.39 us
    another operation x2, other arithmetic, per_device(): kv = jnp.stack([key_rows, value_rows])  2.38 us
    unnamed x3, other arithmetic  2.31 us
  transfers between devices with their start and end apart: 10, of which 2 were waited for; matrix products, arithmetic and copies ran while one was open for 5% of the time, Pallas kernels for 0%

profile of v12, /device:TPU:19, one launch (start us, length us, event | category | flops | bytes accessed | tf_op | source)
XLA Modules:
  0.0 87.6 jit_solution(6810172595057791549)
XLA Ops:
  0.0 1.3 %pad_maximum_fusion = bf16[2,256,1024]{2,1,0:T(8,128)(2,1)S(1)} fusion(bf16[1,256,1024]{2,1,0:T(8,128)(2,1)} %bitcast.9, bf16[1,256,1024]{2,1,0:T(8,128)(2,1)} %bitcast.5), kind=kLoop, calls=%fused_computation.1 | loop fusion | flops 524288 | bytes 2097152 | tf_op jit(solution)/shard_map/stack | solution.py:147
  1.3 3.2 %collective-permute-start.4 = (bf16[2,256,1024]{2,1,0:T(8,128)(2,1)S(1)}, bf16[2,256,1024]{2,1,0:T(8,128)(2,1)S(1)}, u32[]{:S(2)}, u32[]{:S(2)}) collective-permute-start(bf16[2,256,1024]{2,1,0:T(8,128)(2,1)S(1)} %pad_maximum_fusion), channel_id=1, source_target_pairs={{0,4},{1,5},{2,6},{3,7},{4,8},{5,9},{6,10},{7,11},{8,12},{9,13},{1... | collective-permute-start | bytes 3145736 | tf_op jit(solution)/shard_map/ppermute | solution.py:25
  4.5 1.1 %fusion = bf16[2,128,1024]{2,1,0:T(8,128)(2,1)S(1)} fusion(bf16[1,256,1024]{2,1,0:T(8,128)(2,1)} %bitcast.6, bf16[1,256,1024]{2,1,0:T(8,128)(2,1)} %bitcast.10), kind=kLoop, calls=%fused_computation.6 | loop fusion | flops 262144 | bytes 1572864 | tf_op jit(solution)/shard_map/stack | solution.py:147
  5.6 0.7 collective-permute-start
  6.3 4.2 %collective-permute-start.7 = (bf16[2,256,1024]{2,1,0:T(8,128)(2,1)S(1)}, bf16[2,256,1024]{2,1,0:T(8,128)(2,1)}, u32[]{:S(2)}, u32[]{:S(2)}) collective-permute-start(bf16[2,256,1024]{2,1,0:T(8,128)(2,1)S(1)} %pad_maximum_fusion), channel_id=1, source_target_pairs={{0,2},{1,3},{4,6},{5,7},{8,10},{9,11},{12,14},{13,15},{16,18},{17,... | collective-permute-start | bytes 3145736 | tf_op jit(solution)/shard_map/ppermute | solution.py:25
  10.5 16.8 %collective-permute-done.4 = bf16[2,256,1024]{2,1,0:T(8,128)(2,1)S(1)} collective-permute-done((bf16[2,256,1024]{2,1,0:T(8,128)(2,1)S(1)}, bf16[2,256,1024]{2,1,0:T(8,128)(2,1)S(1)}, u32[]{:S(2)}, u32[]{:S(2)}) %collective-permute-start.4) | collective-permute-done | bytes 1048608 | tf_op jit(solution)/shard_map/ppermute | solution.py:25
  27.2 1.3 %collective-permute-start.6 = (bf16[2,256,1024]{2,1,0:T(8,128)(2,1)S(1)}, bf16[2,256,1024]{2,1,0:T(8,128)(2,1)}, u32[]{:S(2)}, u32[]{:S(2)}) collective-permute-start(bf16[2,256,1024]{2,1,0:T(8,128)(2,1)S(1)} %collective-permute-done.4), channel_id=1, source_target_pairs={{2,0},{3,1},{6,4},{7,5},{10,8},{11,9},{14,12},{15,13},{18,16},{19,... | collective-permute-start | bytes 3145736 | tf_op jit(solution)/shard_map/ppermute | solution.py:25
  28.5 0.0 collective-permute-done
  28.5 1.1 %broadcast_select_fusion.1 = bf16[2,128,1024]{2,1,0:T(8,128)(2,1)S(1)} fusion(bf16[2,128,1024]{2,1,0:T(8,128)(2,1)S(1)} %collective-permute-done, pred[]{:T(512)S(6)} %and.53, bf16[1,256,1024]{2,1,0:T(8,128)(2,1)} %bitcast.11, bf16[1,256,1024]{2,1,0:T(8,128)(2,1)} %bitcast.7), kind=kLoop, calls=%fused_computation.8 | loop fusion | flops 524288 | bytes 2097153 | tf_op jit(solution)/shard_map/jit(_where)/select_n | solution.py:63
  29.6 1.5 %collective-permute-start.1 = (bf16[2,128,1024]{2,1,0:T(8,128)(2,1)S(1)}, bf16[2,128,1024]{2,1,0:T(8,128)(2,1)}, u32[]{:S(2)}, u32[]{:S(2)}) collective-permute-start(bf16[2,128,1024]{2,1,0:T(8,128)(2,1)S(1)} %broadcast_select_fusion.1), channel_id=1, source_target_pairs={{0,4},{8,12},{16,20},{24,28}} | collective-permute-start | bytes 1572872 | tf_op jit(solution)/shard_map/ppermute | solution.py:60
  31.1 0.1 broadcast_select_fusion.2
  31.2 1.5 %collective-permute-start.2 = (bf16[2,128,1024]{2,1,0:T(8,128)(2,1)S(1)}, bf16[2,128,1024]{2,1,0:T(8,128)(2,1)}, u32[]{:S(2)}, u32[]{:S(2)}) collective-permute-start(bf16[2,128,1024]{2,1,0:T(8,128)(2,1)S(1)} %broadcast_select_fusion.2), channel_id=1, source_target_pairs={{0,2},{4,6},{8,10},{12,14},{16,18},{20,22},{24,26},{28,30}} | collective-permute-start | bytes 1572872 | tf_op jit(solution)/shard_map/ppermute | solution.py:60
  32.7 1.3 %collective-permute-start.9 = (bf16[2,256,1024]{2,1,0:T(8,128)(2,1)S(1)}, bf16[2,256,1024]{2,1,0:T(8,128)(2,1)}, u32[]{:S(2)}, u32[]{:S(2)}) collective-permute-start(bf16[2,256,1024]{2,1,0:T(8,128)(2,1)S(1)} %pad_maximum_fusion), channel_id=1, source_target_pairs={{0,1},{2,3},{4,5},{6,7},{8,9},{10,11},{12,13},{14,15},{16,17},{18,... | collective-permute-start | bytes 3145736 | tf_op jit(solution)/shard_map/ppermute | solution.py:25
  34.0 0.1 constant_dynamic-slice_fusion
  34.1 0.1 copy.6
  34.2 17.2 %collective-permute-start.5 = (bf16[2,256,1024]{2,1,0:T(8,128)(2,1)S(1)}, bf16[2,256,1024]{2,1,0:T(8,128)(2,1)S(1)}, u32[]{:S(2)}, u32[]{:S(2)}) collective-permute-start(bf16[2,256,1024]{2,1,0:T(8,128)(2,1)S(1)} %collective-permute-done.4), channel_id=1, source_target_pairs={{1,0},{3,2},{5,4},{7,6},{9,8},{11,10},{13,12},{15,14},{17,16},{19,... | collective-permute-start | bytes 3145736 | tf_op jit(solution)/shard_map/ppermute | solution.py:25
  51.4 1.3 %broadcast_select_fusion = bf16[2,256,1024]{2,1,0:T(8,128)(2,1)S(1)} fusion(bf16[2,256,1024]{2,1,0:T(8,128)(2,1)} %collective-permute-done.6, bf16[2,256,1024]{2,1,0:T(8,128)(2,1)} %collective-permute-done.7, pred[]{:T(512)S(6)} %eq.40), kind=kLoop, calls=%fused_computation.5 | loop fusion | flops 524288 | bytes 3145729 | tf_op jit(solution)/shard_map/jit(_where)/select_n | solution.py:36
  52.7 3.5 %collective-permute-start.8 = (bf16[2,256,1024]{2,1,0:T(8,128)(2,1)S(1)}, bf16[2,256,1024]{2,1,0:T(8,128)(2,1)S(1)}, u32[]{:S(2)}, u32[]{:S(2)}) collective-permute-start(bf16[2,256,1024]{2,1,0:T(8,128)(2,1)S(1)} %broadcast_select_fusion), channel_id=1, source_target_pairs={{0,1},{1,0},{2,3},{3,2},{4,5},{5,4},{6,7},{7,6},{8,9},{9,8},{10,11... | collective-permute-start | bytes 3145736 | tf_op jit(solution)/shard_map/ppermute | solution.py:40
  56.2 0.1 broadcast_select_fusion.3
  56.3 1.3 %collective-permute-start.3 = (bf16[2,128,1024]{2,1,0:T(8,128)(2,1)S(1)}, bf16[2,128,1024]{2,1,0:T(8,128)(2,1)S(1)}, u32[]{:S(2)}, u32[]{:S(2)}) collective-permute-start(bf16[2,128,1024]{2,1,0:T(8,128)(2,1)S(1)} %broadcast_select_fusion.3), channel_id=1, source_target_pairs={{0,1},{2,3},{4,5},{6,7},{8,9},{10,11},{12,13},{14,15},{16,17},{18,... | collective-permute-start | bytes 1572872 | tf_op jit(solution)/shard_map/ppermute | solution.py:60
  57.6 0.1 compare_convert_fusion.diag_ref
  57.7 0.0 copy-start.2
  57.7 0.0 copy-start.3
  57.7 2.4 %collective-permute-done.3 = bf16[2,128,1024]{2,1,0:T(8,128)(2,1)S(1)} collective-permute-done((bf16[2,128,1024]{2,1,0:T(8,128)(2,1)S(1)}, bf16[2,128,1024]{2,1,0:T(8,128)(2,1)S(1)}, u32[]{:S(2)}, u32[]{:S(2)}) %collective-permute-start.3) | collective-permute-done | bytes 524320 | tf_op jit(solution)/shard_map/ppermute | solution.py:60
  60.1 0.2 select_dynamic-update-slice_fusion.2
  60.3 0.1 constant_dynamic-update-slice_fusion.2
  60.4 0.0 copy-start.1
  60.4 0.4 select_dynamic-update-slice_fusion.1
  60.8 0.1 constant_dynamic-update-slice_fusion.1
  60.9 1.7 %select_dynamic-update-slice_fusion = bf16[2,1408,1024]{2,1,0:T(8,128)(2,1)S(1)} fusion(bf16[2,1408,1024]{2,1,0:T(8,128)(2,1)S(1)} %constant_dynamic-update-slice_fusion.1, bf16[2,256,1024]{2,1,0:T(8,128)(2,1)S(1)} %collective-permute-done.8, bf16[2,256,1024]{2,1,0:T(8,128)(2,1)} %collective-permute-done.9, pred[]{:T(512)S(6)} %eq.39), kind=kLoop, calls=%fused_computation.3 | loop fusion | flops 524288 | bytes 3145729
  62.6 0.1 constant_dynamic-update-slice_fusion
  62.7 24.9 %shard_map.46 = bf16[256,4096]{1,0:T(8,128)(2,1)} custom-call(s32[2,11]{1,0:T(2,128)S(1)} %fusion.1.slot_ref, s32[2,11]{1,0:T(2,128)S(1)} %compare_convert_fusion.diag_ref, bf16[256,4096]{1,0:T(8,128)(2,1)S(1)} %copy-done.1, bf16[2,11,128,1024]{3,2,1,0:T(8,128)(2,1)S(1)} %bitcast.3, bf16[2,11,128,1024]{3,2,1,0:T(8,128)(2,1)S(1)} %bitcast.4), custom_call_target="tpu_custom_call" | custom-call | flops 5905580032 | bytes 9961472 | tf_op jit(solution)/shard_map/pallas_call | solution.py:126
  (14 shorter events, 0.0 us)
Async XLA Ops:
  0.0 34.0 %copy-start = (s32[32,11]{0,1:T(8,128)S(1)}, s32[32,11]{0,1:T(8,128)}, u32[]{:S(2)}) copy-start(s32[32,11]{0,1:T(8,128)} %param.7) | copy-start | bytes 4228
  1.3 25.9 %collective-permute-start.4 = (bf16[2,256,1024]{2,1,0:T(8,128)(2,1)S(1)}, bf16[2,256,1024]{2,1,0:T(8,128)(2,1)S(1)}, u32[]{:S(2)}, u32[]{:S(2)}) collective-permute-start(bf16[2,256,1024]{2,1,0:T(8,128)(2,1)S(1)} %pad_maximum_fusion), channel_id=1, source_target_pairs={{0,4},{1,5},{2,6},{3,7},{4,8},{5,9},{6,10},{7,11},{8,12},{9,13},{1... | collective-permute-start | bytes 3145736 | tf_op jit(solution)/shard_map/ppermute | solution.py:25
  5.6 22.9 %collective-permute-start = (bf16[2,128,1024]{2,1,0:T(8,128)(2,1)S(1)}, bf16[2,128,1024]{2,1,0:T(8,128)(2,1)S(1)}, u32[]{:S(2)}, u32[]{:S(2)}) collective-permute-start(bf16[2,128,1024]{2,1,0:T(8,128)(2,1)S(1)} %fusion), channel_id=1, source_target_pairs={{0,8},{16,24}} | collective-permute-start | bytes 1572872 | tf_op jit(solution)/shard_map/ppermute | solution.py:60
  6.3 45.1 %collective-permute-start.7 = (bf16[2,256,1024]{2,1,0:T(8,128)(2,1)S(1)}, bf16[2,256,1024]{2,1,0:T(8,128)(2,1)}, u32[]{:S(2)}, u32[]{:S(2)}) collective-permute-start(bf16[2,256,1024]{2,1,0:T(8,128)(2,1)S(1)} %pad_maximum_fusion), channel_id=1, source_target_pairs={{0,2},{1,3},{4,6},{5,7},{8,10},{9,11},{12,14},{13,15},{16,18},{17,... | collective-permute-start | bytes 3145736 | tf_op jit(solution)/shard_map/ppermute | solution.py:25
  27.2 24.2 %collective-permute-start.6 = (bf16[2,256,1024]{2,1,0:T(8,128)(2,1)S(1)}, bf16[2,256,1024]{2,1,0:T(8,128)(2,1)}, u32[]{:S(2)}, u32[]{:S(2)}) collective-permute-start(bf16[2,256,1024]{2,1,0:T(8,128)(2,1)S(1)} %collective-permute-done.4), channel_id=1, source_target_pairs={{2,0},{3,1},{6,4},{7,5},{10,8},{11,9},{14,12},{15,13},{18,16},{19,... | collective-permute-start | bytes 3145736 | tf_op jit(solution)/shard_map/ppermute | solution.py:25
  29.6 1.5 %collective-permute-start.1 = (bf16[2,128,1024]{2,1,0:T(8,128)(2,1)S(1)}, bf16[2,128,1024]{2,1,0:T(8,128)(2,1)}, u32[]{:S(2)}, u32[]{:S(2)}) collective-permute-start(bf16[2,128,1024]{2,1,0:T(8,128)(2,1)S(1)} %broadcast_select_fusion.1), channel_id=1, source_target_pairs={{0,4},{8,12},{16,20},{24,28}} | collective-permute-start | bytes 1572872 | tf_op jit(solution)/shard_map/ppermute | solution.py:60
  31.2 25.0 %collective-permute-start.2 = (bf16[2,128,1024]{2,1,0:T(8,128)(2,1)S(1)}, bf16[2,128,1024]{2,1,0:T(8,128)(2,1)}, u32[]{:S(2)}, u32[]{:S(2)}) collective-permute-start(bf16[2,128,1024]{2,1,0:T(8,128)(2,1)S(1)} %broadcast_select_fusion.2), channel_id=1, source_target_pairs={{0,2},{4,6},{8,10},{12,14},{16,18},{20,22},{24,26},{28,30}} | collective-permute-start | bytes 1572872 | tf_op jit(solution)/shard_map/ppermute | solution.py:60
  32.7 28.2 %collective-permute-start.9 = (bf16[2,256,1024]{2,1,0:T(8,128)(2,1)S(1)}, bf16[2,256,1024]{2,1,0:T(8,128)(2,1)}, u32[]{:S(2)}, u32[]{:S(2)}) collective-permute-start(bf16[2,256,1024]{2,1,0:T(8,128)(2,1)S(1)} %pad_maximum_fusion), channel_id=1, source_target_pairs={{0,1},{2,3},{4,5},{6,7},{8,9},{10,11},{12,13},{14,15},{16,17},{18,... | collective-permute-start | bytes 3145736 | tf_op jit(solution)/shard_map/ppermute | solution.py:25
  34.2 26.2 %collective-permute-start.5 = (bf16[2,256,1024]{2,1,0:T(8,128)(2,1)S(1)}, bf16[2,256,1024]{2,1,0:T(8,128)(2,1)S(1)}, u32[]{:S(2)}, u32[]{:S(2)}) collective-permute-start(bf16[2,256,1024]{2,1,0:T(8,128)(2,1)S(1)} %collective-permute-done.4), channel_id=1, source_target_pairs={{1,0},{3,2},{5,4},{7,6},{9,8},{11,10},{13,12},{15,14},{17,16},{19,... | collective-permute-start | bytes 3145736 | tf_op jit(solution)/shard_map/ppermute | solution.py:25
  52.7 7.6 %collective-permute-start.8 = (bf16[2,256,1024]{2,1,0:T(8,128)(2,1)S(1)}, bf16[2,256,1024]{2,1,0:T(8,128)(2,1)S(1)}, u32[]{:S(2)}, u32[]{:S(2)}) collective-permute-start(bf16[2,256,1024]{2,1,0:T(8,128)(2,1)S(1)} %broadcast_select_fusion), channel_id=1, source_target_pairs={{0,1},{1,0},{2,3},{3,2},{4,5},{5,4},{6,7},{7,6},{8,9},{9,8},{10,11... | collective-permute-start | bytes 3145736 | tf_op jit(solution)/shard_map/ppermute | solution.py:40
  56.3 3.8 %collective-permute-start.3 = (bf16[2,128,1024]{2,1,0:T(8,128)(2,1)S(1)}, bf16[2,128,1024]{2,1,0:T(8,128)(2,1)S(1)}, u32[]{:S(2)}, u32[]{:S(2)}) collective-permute-start(bf16[2,128,1024]{2,1,0:T(8,128)(2,1)S(1)} %broadcast_select_fusion.3), channel_id=1, source_target_pairs={{0,1},{2,3},{4,5},{6,7},{8,9},{10,11},{12,13},{14,15},{16,17},{18,... | collective-permute-start | bytes 1572872 | tf_op jit(solution)/shard_map/ppermute | solution.py:60
  57.7 4.9 %copy-start.2 = (bf16[256,1024]{1,0:T(8,128)(2,1)S(1)}, bf16[256,1024]{1,0:T(8,128)(2,1)}, u32[]{:S(2)}) copy-start(bf16[256,1024]{1,0:T(8,128)(2,1)} %param.5) | copy-start | bytes 1572868
  57.7 4.9 %copy-start.3 = (bf16[256,1024]{1,0:T(8,128)(2,1)S(1)}, bf16[256,1024]{1,0:T(8,128)(2,1)}, u32[]{:S(2)}) copy-start(bf16[256,1024]{1,0:T(8,128)(2,1)} %param.6) | copy-start | bytes 1572868
  60.4 2.4 %copy-start.1 = (bf16[256,4096]{1,0:T(8,128)(2,1)S(1)}, bf16[256,4096]{1,0:T(8,128)(2,1)}, u32[]{:S(2)}) copy-start(bf16[256,4096]{1,0:T(8,128)(2,1)} %q_ref.1) | copy-start | bytes 6291460

commit v13 on v12

--- a/solution.py
+++ b/solution.py
@@ -16,7 +16,7 @@
 LIST = 11
 GROUP = H // KVH
 PAIR = 2
-KV_STEP = 2
+KV_STEP = 4
 
 
 def shifted(shard, axis, by, sends):
@@ -129,7 +129,7 @@
         grid_spec=grid_spec,
         compiler_params=pltpu.CompilerParams(
             dimension_semantics=("arbitrary", "arbitrary"),
-            vmem_limit_bytes=24 * 1024 * 1024,
+            vmem_limit_bytes=40 * 1024 * 1024,
         ),
         cost_estimate=pl.CostEstimate(
             flops=flops,

time: 88 us -> 84.6 us (0.961)
  Pallas kernels: 24.9 us -> 21.4 us
    pallas_call x1, Pallas kernels: 24.9 us -> 21.4 us  [attend(): pl.pallas_call(attend_kernel, out_shape=jax.ShapeDtypeStruct(queries.shap...]
  transfers between devices with their start and end apart: 10 -> 10, of which waited for: 2 -> 2; matrix products, arithmetic and copies ran while one was open for 5% -> 6% of each run, Pallas kernels for 0% -> 0%
where the time goes in v13:
time: 84.6 us; the launch traced here: 84.2 us
  starting transfers between devices  35.5 us (42%)
  Pallas kernels  21.4 us (25%)
  waiting for transfers between devices  19.2 us (23%)
  other arithmetic  7.44 us (9%)
    ppermute x5, starting transfers between devices, shifted(): return lax.ppermute(shard, axis, pairs)  27.1 us
    pallas_call x1, Pallas kernels, attend(): pl.pallas_call(attend_kernel, out_shape=jax.ShapeDtypeStruct(queries.shap...  21.4 us
    ppermute x5, waiting for transfers between devices, shifted(): return lax.ppermute(shard, axis, pairs)  16.8 us
    ppermute x4, starting transfers between devices, tree_broadcast(): got = lax.ppermute(held, axis, pairs)  4.94 us
    ppermute x1, starting transfers between devices, window_blocks(): partner_back2 = lax.ppermute(back2, axis, swap_pairs)  3.46 us
    ppermute x4, waiting for transfers between devices, tree_broadcast(): got = lax.ppermute(held, axis, pairs)  2.39 us
    another operation x2, other arithmetic, per_device(): kv = jnp.stack([key_rows, value_rows])  2.38 us
    unnamed x3, other arithmetic  2.31 us
  transfers between devices with their start and end apart: 10, of which 2 were waited for; matrix products, arithmetic and copies ran while one was open for 6% of the time, Pallas kernels for 0%

profile of v13, /device:TPU:19, one launch (start us, length us, event | category | flops | bytes accessed | tf_op | source)
XLA Modules:
  0.0 84.2 jit_solution(16046907409137963065)
XLA Ops:
  0.0 1.3 %pad_maximum_fusion = bf16[2,256,1024]{2,1,0:T(8,128)(2,1)S(1)} fusion(bf16[1,256,1024]{2,1,0:T(8,128)(2,1)} %bitcast.9, bf16[1,256,1024]{2,1,0:T(8,128)(2,1)} %bitcast.5), kind=kLoop, calls=%fused_computation.1 | loop fusion | flops 524288 | bytes 2097152 | tf_op jit(solution)/shard_map/stack | solution.py:147
  1.3 3.2 %collective-permute-start.4 = (bf16[2,256,1024]{2,1,0:T(8,128)(2,1)S(1)}, bf16[2,256,1024]{2,1,0:T(8,128)(2,1)S(1)}, u32[]{:S(2)}, u32[]{:S(2)}) collective-permute-start(bf16[2,256,1024]{2,1,0:T(8,128)(2,1)S(1)} %pad_maximum_fusion), channel_id=1, source_target_pairs={{0,4},{1,5},{2,6},{3,7},{4,8},{5,9},{6,10},{7,11},{8,12},{9,13},{1... | collective-permute-start | bytes 3145736 | tf_op jit(solution)/shard_map/ppermute | solution.py:25
  4.5 1.1 %fusion = bf16[2,128,1024]{2,1,0:T(8,128)(2,1)S(1)} fusion(bf16[1,256,1024]{2,1,0:T(8,128)(2,1)} %bitcast.6, bf16[1,256,1024]{2,1,0:T(8,128)(2,1)} %bitcast.10), kind=kLoop, calls=%fused_computation.6 | loop fusion | flops 262144 | bytes 1572864 | tf_op jit(solution)/shard_map/stack | solution.py:147
  5.6 0.7 collective-permute-start
  6.3 4.2 %collective-permute-start.7 = (bf16[2,256,1024]{2,1,0:T(8,128)(2,1)S(1)}, bf16[2,256,1024]{2,1,0:T(8,128)(2,1)}, u32[]{:S(2)}, u32[]{:S(2)}) collective-permute-start(bf16[2,256,1024]{2,1,0:T(8,128)(2,1)S(1)} %pad_maximum_fusion), channel_id=1, source_target_pairs={{0,2},{1,3},{4,6},{5,7},{8,10},{9,11},{12,14},{13,15},{16,18},{17,... | collective-permute-start | bytes 3145736 | tf_op jit(solution)/shard_map/ppermute | solution.py:25
  10.5 16.8 %collective-permute-done.4 = bf16[2,256,1024]{2,1,0:T(8,128)(2,1)S(1)} collective-permute-done((bf16[2,256,1024]{2,1,0:T(8,128)(2,1)S(1)}, bf16[2,256,1024]{2,1,0:T(8,128)(2,1)S(1)}, u32[]{:S(2)}, u32[]{:S(2)}) %collective-permute-start.4) | collective-permute-done | bytes 1048608 | tf_op jit(solution)/shard_map/ppermute | solution.py:25
  27.2 1.3 %collective-permute-start.6 = (bf16[2,256,1024]{2,1,0:T(8,128)(2,1)S(1)}, bf16[2,256,1024]{2,1,0:T(8,128)(2,1)}, u32[]{:S(2)}, u32[]{:S(2)}) collective-permute-start(bf16[2,256,1024]{2,1,0:T(8,128)(2,1)S(1)} %collective-permute-done.4), channel_id=1, source_target_pairs={{2,0},{3,1},{6,4},{7,5},{10,8},{11,9},{14,12},{15,13},{18,16},{19,... | collective-permute-start | bytes 3145736 | tf_op jit(solution)/shard_map/ppermute | solution.py:25
  28.5 0.0 collective-permute-done
  28.5 1.1 %broadcast_select_fusion.1 = bf16[2,128,1024]{2,1,0:T(8,128)(2,1)S(1)} fusion(bf16[2,128,1024]{2,1,0:T(8,128)(2,1)S(1)} %collective-permute-done, pred[]{:T(512)S(6)} %and.53, bf16[1,256,1024]{2,1,0:T(8,128)(2,1)} %bitcast.11, bf16[1,256,1024]{2,1,0:T(8,128)(2,1)} %bitcast.7), kind=kLoop, calls=%fused_computation.8 | loop fusion | flops 524288 | bytes 2097153 | tf_op jit(solution)/shard_map/jit(_where)/select_n | solution.py:63
  29.6 1.5 %collective-permute-start.1 = (bf16[2,128,1024]{2,1,0:T(8,128)(2,1)S(1)}, bf16[2,128,1024]{2,1,0:T(8,128)(2,1)}, u32[]{:S(2)}, u32[]{:S(2)}) collective-permute-start(bf16[2,128,1024]{2,1,0:T(8,128)(2,1)S(1)} %broadcast_select_fusion.1), channel_id=1, source_target_pairs={{0,4},{8,12},{16,20},{24,28}} | collective-permute-start | bytes 1572872 | tf_op jit(solution)/shard_map/ppermute | solution.py:60
  31.1 0.1 broadcast_select_fusion.2
  31.2 1.5 %collective-permute-start.2 = (bf16[2,128,1024]{2,1,0:T(8,128)(2,1)S(1)}, bf16[2,128,1024]{2,1,0:T(8,128)(2,1)}, u32[]{:S(2)}, u32[]{:S(2)}) collective-permute-start(bf16[2,128,1024]{2,1,0:T(8,128)(2,1)S(1)} %broadcast_select_fusion.2), channel_id=1, source_target_pairs={{0,2},{4,6},{8,10},{12,14},{16,18},{20,22},{24,26},{28,30}} | collective-permute-start | bytes 1572872 | tf_op jit(solution)/shard_map/ppermute | solution.py:60
  32.7 1.3 %collective-permute-start.9 = (bf16[2,256,1024]{2,1,0:T(8,128)(2,1)S(1)}, bf16[2,256,1024]{2,1,0:T(8,128)(2,1)}, u32[]{:S(2)}, u32[]{:S(2)}) collective-permute-start(bf16[2,256,1024]{2,1,0:T(8,128)(2,1)S(1)} %pad_maximum_fusion), channel_id=1, source_target_pairs={{0,1},{2,3},{4,5},{6,7},{8,9},{10,11},{12,13},{14,15},{16,17},{18,... | collective-permute-start | bytes 3145736 | tf_op jit(solution)/shard_map/ppermute | solution.py:25
  34.0 0.1 constant_dynamic-slice_fusion
  34.1 0.1 copy.6
  34.2 17.2 %collective-permute-start.5 = (bf16[2,256,1024]{2,1,0:T(8,128)(2,1)S(1)}, bf16[2,256,1024]{2,1,0:T(8,128)(2,1)S(1)}, u32[]{:S(2)}, u32[]{:S(2)}) collective-permute-start(bf16[2,256,1024]{2,1,0:T(8,128)(2,1)S(1)} %collective-permute-done.4), channel_id=1, source_target_pairs={{1,0},{3,2},{5,4},{7,6},{9,8},{11,10},{13,12},{15,14},{17,16},{19,... | collective-permute-start | bytes 3145736 | tf_op jit(solution)/shard_map/ppermute | solution.py:25
  51.4 1.3 %broadcast_select_fusion = bf16[2,256,1024]{2,1,0:T(8,128)(2,1)S(1)} fusion(bf16[2,256,1024]{2,1,0:T(8,128)(2,1)} %collective-permute-done.6, bf16[2,256,1024]{2,1,0:T(8,128)(2,1)} %collective-permute-done.7, pred[]{:T(512)S(6)} %eq.40), kind=kLoop, calls=%fused_computation.5 | loop fusion | flops 524288 | bytes 3145729 | tf_op jit(solution)/shard_map/jit(_where)/select_n | solution.py:36
  52.7 3.5 %collective-permute-start.8 = (bf16[2,256,1024]{2,1,0:T(8,128)(2,1)S(1)}, bf16[2,256,1024]{2,1,0:T(8,128)(2,1)S(1)}, u32[]{:S(2)}, u32[]{:S(2)}) collective-permute-start(bf16[2,256,1024]{2,1,0:T(8,128)(2,1)S(1)} %broadcast_select_fusion), channel_id=1, source_target_pairs={{0,1},{1,0},{2,3},{3,2},{4,5},{5,4},{6,7},{7,6},{8,9},{9,8},{10,11... | collective-permute-start | bytes 3145736 | tf_op jit(solution)/shard_map/ppermute | solution.py:40
  56.2 0.1 broadcast_select_fusion.3
  56.3 1.3 %collective-permute-start.3 = (bf16[2,128,1024]{2,1,0:T(8,128)(2,1)S(1)}, bf16[2,128,1024]{2,1,0:T(8,128)(2,1)S(1)}, u32[]{:S(2)}, u32[]{:S(2)}) collective-permute-start(bf16[2,128,1024]{2,1,0:T(8,128)(2,1)S(1)} %broadcast_select_fusion.3), channel_id=1, source_target_pairs={{0,1},{2,3},{4,5},{6,7},{8,9},{10,11},{12,13},{14,15},{16,17},{18,... | collective-permute-start | bytes 1572872 | tf_op jit(solution)/shard_map/ppermute | solution.py:60
  57.6 0.1 compare_convert_fusion.diag_ref
  57.7 0.0 copy-start.2
  57.7 0.0 copy-start.3
  57.7 2.4 %collective-permute-done.3 = bf16[2,128,1024]{2,1,0:T(8,128)(2,1)S(1)} collective-permute-done((bf16[2,128,1024]{2,1,0:T(8,128)(2,1)S(1)}, bf16[2,128,1024]{2,1,0:T(8,128)(2,1)S(1)}, u32[]{:S(2)}, u32[]{:S(2)}) %collective-permute-start.3) | collective-permute-done | bytes 524320 | tf_op jit(solution)/shard_map/ppermute | solution.py:60
  60.1 0.2 select_dynamic-update-slice_fusion.2
  60.3 0.1 constant_dynamic-update-slice_fusion.2
  60.4 0.0 copy-start.1
  60.4 0.4 select_dynamic-update-slice_fusion.1
  60.8 0.1 constant_dynamic-update-slice_fusion.1
  60.9 1.7 %select_dynamic-update-slice_fusion = bf16[2,1408,1024]{2,1,0:T(8,128)(2,1)S(1)} fusion(bf16[2,1408,1024]{2,1,0:T(8,128)(2,1)S(1)} %constant_dynamic-update-slice_fusion.1, bf16[2,256,1024]{2,1,0:T(8,128)(2,1)S(1)} %collective-permute-done.8, bf16[2,256,1024]{2,1,0:T(8,128)(2,1)} %collective-permute-done.9, pred[]{:T(512)S(6)} %eq.39), kind=kLoop, calls=%fused_computation.3 | loop fusion | flops 524288 | bytes 3145729
  62.6 0.1 constant_dynamic-update-slice_fusion
  62.7 21.4 %shard_map.46 = bf16[256,4096]{1,0:T(8,128)(2,1)} custom-call(s32[2,11]{1,0:T(2,128)S(1)} %fusion.1.slot_ref, s32[2,11]{1,0:T(2,128)S(1)} %compare_convert_fusion.diag_ref, bf16[256,4096]{1,0:T(8,128)(2,1)S(1)} %copy-done.1, bf16[2,11,128,1024]{3,2,1,0:T(8,128)(2,1)S(1)} %bitcast.3, bf16[2,11,128,1024]{3,2,1,0:T(8,128)(2,1)S(1)} %bitcast.4), custom_call_target="tpu_custom_call" | custom-call | flops 5905580032 | bytes 9961472 | tf_op jit(solution)/shard_map/pallas_call | solution.py:126
  (14 shorter events, 0.0 us)
Async XLA Ops:
  0.0 34.0 %copy-start = (s32[32,11]{0,1:T(8,128)S(1)}, s32[32,11]{0,1:T(8,128)}, u32[]{:S(2)}) copy-start(s32[32,11]{0,1:T(8,128)} %param.7) | copy-start | bytes 4228
  1.3 25.9 %collective-permute-start.4 = (bf16[2,256,1024]{2,1,0:T(8,128)(2,1)S(1)}, bf16[2,256,1024]{2,1,0:T(8,128)(2,1)S(1)}, u32[]{:S(2)}, u32[]{:S(2)}) collective-permute-start(bf16[2,256,1024]{2,1,0:T(8,128)(2,1)S(1)} %pad_maximum_fusion), channel_id=1, source_target_pairs={{0,4},{1,5},{2,6},{3,7},{4,8},{5,9},{6,10},{7,11},{8,12},{9,13},{1... | collective-permute-start | bytes 3145736 | tf_op jit(solution)/shard_map/ppermute | solution.py:25
  5.6 22.9 %collective-permute-start = (bf16[2,128,1024]{2,1,0:T(8,128)(2,1)S(1)}, bf16[2,128,1024]{2,1,0:T(8,128)(2,1)S(1)}, u32[]{:S(2)}, u32[]{:S(2)}) collective-permute-start(bf16[2,128,1024]{2,1,0:T(8,128)(2,1)S(1)} %fusion), channel_id=1, source_target_pairs={{0,8},{16,24}} | collective-permute-start | bytes 1572872 | tf_op jit(solution)/shard_map/ppermute | solution.py:60
  6.3 45.1 %collective-permute-start.7 = (bf16[2,256,1024]{2,1,0:T(8,128)(2,1)S(1)}, bf16[2,256,1024]{2,1,0:T(8,128)(2,1)}, u32[]{:S(2)}, u32[]{:S(2)}) collective-permute-start(bf16[2,256,1024]{2,1,0:T(8,128)(2,1)S(1)} %pad_maximum_fusion), channel_id=1, source_target_pairs={{0,2},{1,3},{4,6},{5,7},{8,10},{9,11},{12,14},{13,15},{16,18},{17,... | collective-permute-start | bytes 3145736 | tf_op jit(solution)/shard_map/ppermute | solution.py:25
  27.2 24.2 %collective-permute-start.6 = (bf16[2,256,1024]{2,1,0:T(8,128)(2,1)S(1)}, bf16[2,256,1024]{2,1,0:T(8,128)(2,1)}, u32[]{:S(2)}, u32[]{:S(2)}) collective-permute-start(bf16[2,256,1024]{2,1,0:T(8,128)(2,1)S(1)} %collective-permute-done.4), channel_id=1, source_target_pairs={{2,0},{3,1},{6,4},{7,5},{10,8},{11,9},{14,12},{15,13},{18,16},{19,... | collective-permute-start | bytes 3145736 | tf_op jit(solution)/shard_map/ppermute | solution.py:25
  29.6 1.5 %collective-permute-start.1 = (bf16[2,128,1024]{2,1,0:T(8,128)(2,1)S(1)}, bf16[2,128,1024]{2,1,0:T(8,128)(2,1)}, u32[]{:S(2)}, u32[]{:S(2)}) collective-permute-start(bf16[2,128,1024]{2,1,0:T(8,128)(2,1)S(1)} %broadcast_select_fusion.1), channel_id=1, source_target_pairs={{0,4},{8,12},{16,20},{24,28}} | collective-permute-start | bytes 1572872 | tf_op jit(solution)/shard_map/ppermute | solution.py:60
  31.2 25.0 %collective-permute-start.2 = (bf16[2,128,1024]{2,1,0:T(8,128)(2,1)S(1)}, bf16[2,128,1024]{2,1,0:T(8,128)(2,1)}, u32[]{:S(2)}, u32[]{:S(2)}) collective-permute-start(bf16[2,128,1024]{2,1,0:T(8,128)(2,1)S(1)} %broadcast_select_fusion.2), channel_id=1, source_target_pairs={{0,2},{4,6},{8,10},{12,14},{16,18},{20,22},{24,26},{28,30}} | collective-permute-start | bytes 1572872 | tf_op jit(solution)/shard_map/ppermute | solution.py:60
  32.7 28.2 %collective-permute-start.9 = (bf16[2,256,1024]{2,1,0:T(8,128)(2,1)S(1)}, bf16[2,256,1024]{2,1,0:T(8,128)(2,1)}, u32[]{:S(2)}, u32[]{:S(2)}) collective-permute-start(bf16[2,256,1024]{2,1,0:T(8,128)(2,1)S(1)} %pad_maximum_fusion), channel_id=1, source_target_pairs={{0,1},{2,3},{4,5},{6,7},{8,9},{10,11},{12,13},{14,15},{16,17},{18,... | collective-permute-start | bytes 3145736 | tf_op jit(solution)/shard_map/ppermute | solution.py:25
  34.2 26.2 %collective-permute-start.5 = (bf16[2,256,1024]{2,1,0:T(8,128)(2,1)S(1)}, bf16[2,256,1024]{2,1,0:T(8,128)(2,1)S(1)}, u32[]{:S(2)}, u32[]{:S(2)}) collective-permute-start(bf16[2,256,1024]{2,1,0:T(8,128)(2,1)S(1)} %collective-permute-done.4), channel_id=1, source_target_pairs={{1,0},{3,2},{5,4},{7,6},{9,8},{11,10},{13,12},{15,14},{17,16},{19,... | collective-permute-start | bytes 3145736 | tf_op jit(solution)/shard_map/ppermute | solution.py:25
  52.7 7.6 %collective-permute-start.8 = (bf16[2,256,1024]{2,1,0:T(8,128)(2,1)S(1)}, bf16[2,256,1024]{2,1,0:T(8,128)(2,1)S(1)}, u32[]{:S(2)}, u32[]{:S(2)}) collective-permute-start(bf16[2,256,1024]{2,1,0:T(8,128)(2,1)S(1)} %broadcast_select_fusion), channel_id=1, source_target_pairs={{0,1},{1,0},{2,3},{3,2},{4,5},{5,4},{6,7},{7,6},{8,9},{9,8},{10,11... | collective-permute-start | bytes 3145736 | tf_op jit(solution)/shard_map/ppermute | solution.py:40
  56.3 3.8 %collective-permute-start.3 = (bf16[2,128,1024]{2,1,0:T(8,128)(2,1)S(1)}, bf16[2,128,1024]{2,1,0:T(8,128)(2,1)S(1)}, u32[]{:S(2)}, u32[]{:S(2)}) collective-permute-start(bf16[2,128,1024]{2,1,0:T(8,128)(2,1)S(1)} %broadcast_select_fusion.3), channel_id=1, source_target_pairs={{0,1},{2,3},{4,5},{6,7},{8,9},{10,11},{12,13},{14,15},{16,17},{18,... | collective-permute-start | bytes 1572872 | tf_op jit(solution)/shard_map/ppermute | solution.py:60
  57.7 4.9 %copy-start.2 = (bf16[256,1024]{1,0:T(8,128)(2,1)S(1)}, bf16[256,1024]{1,0:T(8,128)(2,1)}, u32[]{:S(2)}) copy-start(bf16[256,1024]{1,0:T(8,128)(2,1)} %param.5) | copy-start | bytes 1572868
  57.7 4.9 %copy-start.3 = (bf16[256,1024]{1,0:T(8,128)(2,1)S(1)}, bf16[256,1024]{1,0:T(8,128)(2,1)}, u32[]{:S(2)}) copy-start(bf16[256,1024]{1,0:T(8,128)(2,1)} %param.6) | copy-start | bytes 1572868
  60.4 2.4 %copy-start.1 = (bf16[256,4096]{1,0:T(8,128)(2,1)S(1)}, bf16[256,4096]{1,0:T(8,128)(2,1)}, u32[]{:S(2)}) copy-start(bf16[256,4096]{1,0:T(8,128)(2,1)} %q_ref.1) | copy-start | bytes 6291460

commit v14 on v10

--- a/solution.py
+++ b/solution.py
@@ -16,6 +16,7 @@
 LIST = 11
 GROUP = H // KVH
 PAIR = 2
+KV_STEP = 4
 
 
 def shifted(shard, axis, by, sends):
@@ -73,24 +74,30 @@
     bias_sc[0] = jnp.zeros((rows, BLK), jnp.float32)
     bias_sc[1] = jnp.where(col > row, -jnp.inf, 0.0).astype(jnp.float32)
     q = q_ref[...]
-    for half in range(GROUP // PAIR):
-        heads = range(half * PAIR, (half + 1) * PAIR)
+    chains = []
+    for kv_head in range(KV_STEP):
+        for half in range(GROUP // PAIR):
+            heads = [kv_head * GROUP + j for j in range(half * PAIR, (half + 1) * PAIR)]
+            chains.append((slice(kv_head * HD, (kv_head + 1) * HD), heads))
+    row_maxes = []
+    for chain, (kv_lanes, heads) in enumerate(chains):
         stacked = jnp.concatenate([q[:, j * HD:(j + 1) * HD] for j in heads], axis=0)
         run_max = jnp.full((rows, BLK), -jnp.inf, jnp.float32)
         for s in range(LIST):
-            key = k_ref[0, slot_ref[local, s]]
+            key = k_ref[0, slot_ref[local, s], :, kv_lanes]
             sc = lax.dot_general(
                 stacked, key, (((1,), (1,)), ((), ())), preferred_element_type=jnp.float32
             ) + bias_sc[diag_ref[local, s]]
-            score_sc[half, s] = sc
+            score_sc[chain, s] = sc
             run_max = jnp.maximum(run_max, sc)
-        row_max = jnp.max(run_max, axis=1, keepdims=True)
+        row_maxes.append(jnp.max(run_max, axis=1, keepdims=True))
+    for chain, (kv_lanes, heads) in enumerate(chains):
         total = jnp.zeros((rows, BLK), jnp.float32)
         acc = jnp.zeros((rows, HD), jnp.float32)
         for s in range(LIST):
-            powers = jnp.exp2((score_sc[half, s] - row_max) * exp2_scale)
+            powers = jnp.exp2((score_sc[chain, s] - row_maxes[chain]) * exp2_scale)
             total = total + powers
-            value = v_ref[0, slot_ref[local, s]]
+            value = v_ref[0, slot_ref[local, s], :, kv_lanes]
             acc = acc + jnp.dot(
                 powers.astype(jnp.bfloat16), value, preferred_element_type=jnp.float32
             )
@@ -106,15 +113,15 @@
     flops = 4 * blocks_here * H * BLK * LIST * BLK * HD
     grid_spec = pltpu.PrefetchScalarGridSpec(
         num_scalar_prefetch=2,
-        grid=(KVH, blocks_here),
+        grid=(KVH // KV_STEP, blocks_here),
         in_specs=[
-            pl.BlockSpec((BLK, GROUP * HD), lambda g, b, *_: (b, g)),
-            pl.BlockSpec((1, buffer_blocks, BLK, HD), lambda g, b, *_: (0, 0, 0, g)),
-            pl.BlockSpec((1, buffer_blocks, BLK, HD), lambda g, b, *_: (1, 0, 0, g)),
+            pl.BlockSpec((BLK, KV_STEP * GROUP * HD), lambda g, b, *_: (b, g)),
+            pl.BlockSpec((1, buffer_blocks, BLK, KV_STEP * HD), lambda g, b, *_: (0, 0, 0, g)),
+            pl.BlockSpec((1, buffer_blocks, BLK, KV_STEP * HD), lambda g, b, *_: (1, 0, 0, g)),
         ],
-        out_specs=pl.BlockSpec((BLK, GROUP * HD), lambda g, b, *_: (b, g)),
+        out_specs=pl.BlockSpec((BLK, KV_STEP * GROUP * HD), lambda g, b, *_: (b, g)),
         scratch_shapes=[
-            pltpu.VMEM((GROUP // PAIR, LIST, PAIR * BLK, BLK), jnp.float32),
+            pltpu.VMEM((KV_STEP * GROUP // PAIR, LIST, PAIR * BLK, BLK), jnp.float32),
             pltpu.VMEM((2, PAIR * BLK, BLK), jnp.float32),
         ],
     )
@@ -124,7 +131,7 @@
         grid_spec=grid_spec,
         compiler_params=pltpu.CompilerParams(
             dimension_semantics=("arbitrary", "arbitrary"),
-            vmem_limit_bytes=24 * 1024 * 1024,
+            vmem_limit_bytes=40 * 1024 * 1024,
         ),
         cost_estimate=pl.CostEstimate(
             flops=flops,

time: 94.8 us -> 84.6 us (0.89)
  Pallas kernels: 31.7 us -> 21.5 us
    pallas_call x1, Pallas kernels: 31.7 us -> 21.5 us  [attend(): pl.pallas_call(attend_kernel, out_shape=jax.ShapeDtypeStruct(queries.shap...]
  transfers between devices with their start and end apart: 10 -> 10, of which waited for: 2 -> 2; matrix products, arithmetic and copies ran while one was open for 5% -> 6% of each run, Pallas kernels for 0% -> 0%
where the time goes in v14:
time: 84.6 us; the launch traced here: 84.2 us
  starting transfers between devices  35.5 us (42%)
  Pallas kernels  21.5 us (25%)
  waiting for transfers between devices  19.2 us (23%)
  other arithmetic  7.44 us (9%)
    ppermute x5, starting transfers between devices, shifted(): return lax.ppermute(shard, axis, pairs)  27.1 us
    pallas_call x1, Pallas kernels, attend(): pl.pallas_call(attend_kernel, out_shape=jax.ShapeDtypeStruct(queries.shap...  21.5 us
    ppermute x5, waiting for transfers between devices, shifted(): return lax.ppermute(shard, axis, pairs)  16.8 us
    ppermute x4, starting transfers between devices, tree_broadcast(): got = lax.ppermute(held, axis, pairs)  4.94 us
    ppermute x1, starting transfers between devices, window_blocks(): partner_back2 = lax.ppermute(back2, axis, swap_pairs)  3.46 us
    ppermute x4, waiting for transfers between devices, tree_broadcast(): got = lax.ppermute(held, axis, pairs)  2.39 us
    another operation x2, other arithmetic, per_device(): kv = jnp.stack([key_rows, value_rows])  2.38 us
    unnamed x3, other arithmetic  2.31 us
  transfers between devices with their start and end apart: 10, of which 2 were waited for; matrix products, arithmetic and copies ran while one was open for 6% of the time, Pallas kernels for 0%

profile of v14, /device:TPU:19, one launch (start us, length us, event | category | flops | bytes accessed | tf_op | source)
XLA Modules:
  0.0 84.2 jit_solution(11461142945261813745)
XLA Ops:
  0.0 1.3 %pad_maximum_fusion = bf16[2,256,1024]{2,1,0:T(8,128)(2,1)S(1)} fusion(bf16[1,256,1024]{2,1,0:T(8,128)(2,1)} %bitcast.9, bf16[1,256,1024]{2,1,0:T(8,128)(2,1)} %bitcast.5), kind=kLoop, calls=%fused_computation.1 | loop fusion | flops 524288 | bytes 2097152 | tf_op jit(solution)/shard_map/stack | solution.py:149
  1.3 3.2 %collective-permute-start.4 = (bf16[2,256,1024]{2,1,0:T(8,128)(2,1)S(1)}, bf16[2,256,1024]{2,1,0:T(8,128)(2,1)S(1)}, u32[]{:S(2)}, u32[]{:S(2)}) collective-permute-start(bf16[2,256,1024]{2,1,0:T(8,128)(2,1)S(1)} %pad_maximum_fusion), channel_id=1, source_target_pairs={{0,4},{1,5},{2,6},{3,7},{4,8},{5,9},{6,10},{7,11},{8,12},{9,13},{1... | collective-permute-start | bytes 3145736 | tf_op jit(solution)/shard_map/ppermute | solution.py:25
  4.5 1.1 %fusion = bf16[2,128,1024]{2,1,0:T(8,128)(2,1)S(1)} fusion(bf16[1,256,1024]{2,1,0:T(8,128)(2,1)} %bitcast.6, bf16[1,256,1024]{2,1,0:T(8,128)(2,1)} %bitcast.10), kind=kLoop, calls=%fused_computation.6 | loop fusion | flops 262144 | bytes 1572864 | tf_op jit(solution)/shard_map/stack | solution.py:149
  5.6 0.7 collective-permute-start
  6.3 4.2 %collective-permute-start.7 = (bf16[2,256,1024]{2,1,0:T(8,128)(2,1)S(1)}, bf16[2,256,1024]{2,1,0:T(8,128)(2,1)}, u32[]{:S(2)}, u32[]{:S(2)}) collective-permute-start(bf16[2,256,1024]{2,1,0:T(8,128)(2,1)S(1)} %pad_maximum_fusion), channel_id=1, source_target_pairs={{0,2},{1,3},{4,6},{5,7},{8,10},{9,11},{12,14},{13,15},{16,18},{17,... | collective-permute-start | bytes 3145736 | tf_op jit(solution)/shard_map/ppermute | solution.py:25
  10.5 16.8 %collective-permute-done.4 = bf16[2,256,1024]{2,1,0:T(8,128)(2,1)S(1)} collective-permute-done((bf16[2,256,1024]{2,1,0:T(8,128)(2,1)S(1)}, bf16[2,256,1024]{2,1,0:T(8,128)(2,1)S(1)}, u32[]{:S(2)}, u32[]{:S(2)}) %collective-permute-start.4) | collective-permute-done | bytes 1048608 | tf_op jit(solution)/shard_map/ppermute | solution.py:25
  27.2 1.3 %collective-permute-start.6 = (bf16[2,256,1024]{2,1,0:T(8,128)(2,1)S(1)}, bf16[2,256,1024]{2,1,0:T(8,128)(2,1)}, u32[]{:S(2)}, u32[]{:S(2)}) collective-permute-start(bf16[2,256,1024]{2,1,0:T(8,128)(2,1)S(1)} %collective-permute-done.4), channel_id=1, source_target_pairs={{2,0},{3,1},{6,4},{7,5},{10,8},{11,9},{14,12},{15,13},{18,16},{19,... | collective-permute-start | bytes 3145736 | tf_op jit(solution)/shard_map/ppermute | solution.py:25
  28.5 0.0 collective-permute-done
  28.5 1.1 %broadcast_select_fusion.1 = bf16[2,128,1024]{2,1,0:T(8,128)(2,1)S(1)} fusion(bf16[2,128,1024]{2,1,0:T(8,128)(2,1)S(1)} %collective-permute-done, pred[]{:T(512)S(6)} %and.53, bf16[1,256,1024]{2,1,0:T(8,128)(2,1)} %bitcast.11, bf16[1,256,1024]{2,1,0:T(8,128)(2,1)} %bitcast.7), kind=kLoop, calls=%fused_computation.8 | loop fusion | flops 524288 | bytes 2097153 | tf_op jit(solution)/shard_map/jit(_where)/select_n | solution.py:63
  29.6 1.5 %collective-permute-start.1 = (bf16[2,128,1024]{2,1,0:T(8,128)(2,1)S(1)}, bf16[2,128,1024]{2,1,0:T(8,128)(2,1)}, u32[]{:S(2)}, u32[]{:S(2)}) collective-permute-start(bf16[2,128,1024]{2,1,0:T(8,128)(2,1)S(1)} %broadcast_select_fusion.1), channel_id=1, source_target_pairs={{0,4},{8,12},{16,20},{24,28}} | collective-permute-start | bytes 1572872 | tf_op jit(solution)/shard_map/ppermute | solution.py:60
  31.1 0.1 broadcast_select_fusion.2
  31.2 1.5 %collective-permute-start.2 = (bf16[2,128,1024]{2,1,0:T(8,128)(2,1)S(1)}, bf16[2,128,1024]{2,1,0:T(8,128)(2,1)}, u32[]{:S(2)}, u32[]{:S(2)}) collective-permute-start(bf16[2,128,1024]{2,1,0:T(8,128)(2,1)S(1)} %broadcast_select_fusion.2), channel_id=1, source_target_pairs={{0,2},{4,6},{8,10},{12,14},{16,18},{20,22},{24,26},{28,30}} | collective-permute-start | bytes 1572872 | tf_op jit(solution)/shard_map/ppermute | solution.py:60
  32.7 1.3 %collective-permute-start.9 = (bf16[2,256,1024]{2,1,0:T(8,128)(2,1)S(1)}, bf16[2,256,1024]{2,1,0:T(8,128)(2,1)}, u32[]{:S(2)}, u32[]{:S(2)}) collective-permute-start(bf16[2,256,1024]{2,1,0:T(8,128)(2,1)S(1)} %pad_maximum_fusion), channel_id=1, source_target_pairs={{0,1},{2,3},{4,5},{6,7},{8,9},{10,11},{12,13},{14,15},{16,17},{18,... | collective-permute-start | bytes 3145736 | tf_op jit(solution)/shard_map/ppermute | solution.py:25
  34.0 0.1 constant_dynamic-slice_fusion
  34.1 0.1 copy.6
  34.2 17.2 %collective-permute-start.5 = (bf16[2,256,1024]{2,1,0:T(8,128)(2,1)S(1)}, bf16[2,256,1024]{2,1,0:T(8,128)(2,1)S(1)}, u32[]{:S(2)}, u32[]{:S(2)}) collective-permute-start(bf16[2,256,1024]{2,1,0:T(8,128)(2,1)S(1)} %collective-permute-done.4), channel_id=1, source_target_pairs={{1,0},{3,2},{5,4},{7,6},{9,8},{11,10},{13,12},{15,14},{17,16},{19,... | collective-permute-start | bytes 3145736 | tf_op jit(solution)/shard_map/ppermute | solution.py:25
  51.4 1.3 %broadcast_select_fusion = bf16[2,256,1024]{2,1,0:T(8,128)(2,1)S(1)} fusion(bf16[2,256,1024]{2,1,0:T(8,128)(2,1)} %collective-permute-done.6, bf16[2,256,1024]{2,1,0:T(8,128)(2,1)} %collective-permute-done.7, pred[]{:T(512)S(6)} %eq.40), kind=kLoop, calls=%fused_computation.5 | loop fusion | flops 524288 | bytes 3145729 | tf_op jit(solution)/shard_map/jit(_where)/select_n | solution.py:36
  52.7 3.5 %collective-permute-start.8 = (bf16[2,256,1024]{2,1,0:T(8,128)(2,1)S(1)}, bf16[2,256,1024]{2,1,0:T(8,128)(2,1)S(1)}, u32[]{:S(2)}, u32[]{:S(2)}) collective-permute-start(bf16[2,256,1024]{2,1,0:T(8,128)(2,1)S(1)} %broadcast_select_fusion), channel_id=1, source_target_pairs={{0,1},{1,0},{2,3},{3,2},{4,5},{5,4},{6,7},{7,6},{8,9},{9,8},{10,11... | collective-permute-start | bytes 3145736 | tf_op jit(solution)/shard_map/ppermute | solution.py:40
  56.2 0.1 broadcast_select_fusion.3
  56.3 1.3 %collective-permute-start.3 = (bf16[2,128,1024]{2,1,0:T(8,128)(2,1)S(1)}, bf16[2,128,1024]{2,1,0:T(8,128)(2,1)S(1)}, u32[]{:S(2)}, u32[]{:S(2)}) collective-permute-start(bf16[2,128,1024]{2,1,0:T(8,128)(2,1)S(1)} %broadcast_select_fusion.3), channel_id=1, source_target_pairs={{0,1},{2,3},{4,5},{6,7},{8,9},{10,11},{12,13},{14,15},{16,17},{18,... | collective-permute-start | bytes 1572872 | tf_op jit(solution)/shard_map/ppermute | solution.py:60
  57.6 0.1 compare_convert_fusion.diag_ref
  57.7 0.0 copy-start.2
  57.7 0.0 copy-start.3
  57.7 2.4 %collective-permute-done.3 = bf16[2,128,1024]{2,1,0:T(8,128)(2,1)S(1)} collective-permute-done((bf16[2,128,1024]{2,1,0:T(8,128)(2,1)S(1)}, bf16[2,128,1024]{2,1,0:T(8,128)(2,1)S(1)}, u32[]{:S(2)}, u32[]{:S(2)}) %collective-permute-start.3) | collective-permute-done | bytes 524320 | tf_op jit(solution)/shard_map/ppermute | solution.py:60
  60.1 0.2 select_dynamic-update-slice_fusion.2
  60.3 0.1 constant_dynamic-update-slice_fusion.2
  60.4 0.0 copy-start.1
  60.4 0.4 select_dynamic-update-slice_fusion.1
  60.8 0.1 constant_dynamic-update-slice_fusion.1
  60.9 1.7 %select_dynamic-update-slice_fusion = bf16[2,1408,1024]{2,1,0:T(8,128)(2,1)S(1)} fusion(bf16[2,1408,1024]{2,1,0:T(8,128)(2,1)S(1)} %constant_dynamic-update-slice_fusion.1, bf16[2,256,1024]{2,1,0:T(8,128)(2,1)S(1)} %collective-permute-done.8, bf16[2,256,1024]{2,1,0:T(8,128)(2,1)} %collective-permute-done.9, pred[]{:T(512)S(6)} %eq.39), kind=kLoop, calls=%fused_computation.3 | loop fusion | flops 524288 | bytes 3145729
  62.6 0.1 constant_dynamic-update-slice_fusion
  62.7 21.5 %shard_map.46 = bf16[256,4096]{1,0:T(8,128)(2,1)} custom-call(s32[2,11]{1,0:T(2,128)S(1)} %fusion.1.slot_ref, s32[2,11]{1,0:T(2,128)S(1)} %compare_convert_fusion.diag_ref, bf16[256,4096]{1,0:T(8,128)(2,1)S(1)} %copy-done.1, bf16[2,11,128,1024]{3,2,1,0:T(8,128)(2,1)S(1)} %bitcast.3, bf16[2,11,128,1024]{3,2,1,0:T(8,128)(2,1)S(1)} %bitcast.4), custom_call_target="tpu_custom_call" | custom-call | flops 5905580032 | bytes 9961472 | tf_op jit(solution)/shard_map/pallas_call | solution.py:128
  (14 shorter events, 0.0 us)
Async XLA Ops:
  0.0 34.0 %copy-start = (s32[32,11]{0,1:T(8,128)S(1)}, s32[32,11]{0,1:T(8,128)}, u32[]{:S(2)}) copy-start(s32[32,11]{0,1:T(8,128)} %param.7) | copy-start | bytes 4228
  1.3 25.9 %collective-permute-start.4 = (bf16[2,256,1024]{2,1,0:T(8,128)(2,1)S(1)}, bf16[2,256,1024]{2,1,0:T(8,128)(2,1)S(1)}, u32[]{:S(2)}, u32[]{:S(2)}) collective-permute-start(bf16[2,256,1024]{2,1,0:T(8,128)(2,1)S(1)} %pad_maximum_fusion), channel_id=1, source_target_pairs={{0,4},{1,5},{2,6},{3,7},{4,8},{5,9},{6,10},{7,11},{8,12},{9,13},{1... | collective-permute-start | bytes 3145736 | tf_op jit(solution)/shard_map/ppermute | solution.py:25
  5.6 22.9 %collective-permute-start = (bf16[2,128,1024]{2,1,0:T(8,128)(2,1)S(1)}, bf16[2,128,1024]{2,1,0:T(8,128)(2,1)S(1)}, u32[]{:S(2)}, u32[]{:S(2)}) collective-permute-start(bf16[2,128,1024]{2,1,0:T(8,128)(2,1)S(1)} %fusion), channel_id=1, source_target_pairs={{0,8},{16,24}} | collective-permute-start | bytes 1572872 | tf_op jit(solution)/shard_map/ppermute | solution.py:60
  6.3 45.1 %collective-permute-start.7 = (bf16[2,256,1024]{2,1,0:T(8,128)(2,1)S(1)}, bf16[2,256,1024]{2,1,0:T(8,128)(2,1)}, u32[]{:S(2)}, u32[]{:S(2)}) collective-permute-start(bf16[2,256,1024]{2,1,0:T(8,128)(2,1)S(1)} %pad_maximum_fusion), channel_id=1, source_target_pairs={{0,2},{1,3},{4,6},{5,7},{8,10},{9,11},{12,14},{13,15},{16,18},{17,... | collective-permute-start | bytes 3145736 | tf_op jit(solution)/shard_map/ppermute | solution.py:25
  27.2 24.2 %collective-permute-start.6 = (bf16[2,256,1024]{2,1,0:T(8,128)(2,1)S(1)}, bf16[2,256,1024]{2,1,0:T(8,128)(2,1)}, u32[]{:S(2)}, u32[]{:S(2)}) collective-permute-start(bf16[2,256,1024]{2,1,0:T(8,128)(2,1)S(1)} %collective-permute-done.4), channel_id=1, source_target_pairs={{2,0},{3,1},{6,4},{7,5},{10,8},{11,9},{14,12},{15,13},{18,16},{19,... | collective-permute-start | bytes 3145736 | tf_op jit(solution)/shard_map/ppermute | solution.py:25
  29.6 1.5 %collective-permute-start.1 = (bf16[2,128,1024]{2,1,0:T(8,128)(2,1)S(1)}, bf16[2,128,1024]{2,1,0:T(8,128)(2,1)}, u32[]{:S(2)}, u32[]{:S(2)}) collective-permute-start(bf16[2,128,1024]{2,1,0:T(8,128)(2,1)S(1)} %broadcast_select_fusion.1), channel_id=1, source_target_pairs={{0,4},{8,12},{16,20},{24,28}} | collective-permute-start | bytes 1572872 | tf_op jit(solution)/shard_map/ppermute | solution.py:60
  31.2 25.0 %collective-permute-start.2 = (bf16[2,128,1024]{2,1,0:T(8,128)(2,1)S(1)}, bf16[2,128,1024]{2,1,0:T(8,128)(2,1)}, u32[]{:S(2)}, u32[]{:S(2)}) collective-permute-start(bf16[2,128,1024]{2,1,0:T(8,128)(2,1)S(1)} %broadcast_select_fusion.2), channel_id=1, source_target_pairs={{0,2},{4,6},{8,10},{12,14},{16,18},{20,22},{24,26},{28,30}} | collective-permute-start | bytes 1572872 | tf_op jit(solution)/shard_map/ppermute | solution.py:60
  32.7 28.2 %collective-permute-start.9 = (bf16[2,256,1024]{2,1,0:T(8,128)(2,1)S(1)}, bf16[2,256,1024]{2,1,0:T(8,128)(2,1)}, u32[]{:S(2)}, u32[]{:S(2)}) collective-permute-start(bf16[2,256,1024]{2,1,0:T(8,128)(2,1)S(1)} %pad_maximum_fusion), channel_id=1, source_target_pairs={{0,1},{2,3},{4,5},{6,7},{8,9},{10,11},{12,13},{14,15},{16,17},{18,... | collective-permute-start | bytes 3145736 | tf_op jit(solution)/shard_map/ppermute | solution.py:25
  34.2 26.2 %collective-permute-start.5 = (bf16[2,256,1024]{2,1,0:T(8,128)(2,1)S(1)}, bf16[2,256,1024]{2,1,0:T(8,128)(2,1)S(1)}, u32[]{:S(2)}, u32[]{:S(2)}) collective-permute-start(bf16[2,256,1024]{2,1,0:T(8,128)(2,1)S(1)} %collective-permute-done.4), channel_id=1, source_target_pairs={{1,0},{3,2},{5,4},{7,6},{9,8},{11,10},{13,12},{15,14},{17,16},{19,... | collective-permute-start | bytes 3145736 | tf_op jit(solution)/shard_map/ppermute | solution.py:25
  52.7 7.6 %collective-permute-start.8 = (bf16[2,256,1024]{2,1,0:T(8,128)(2,1)S(1)}, bf16[2,256,1024]{2,1,0:T(8,128)(2,1)S(1)}, u32[]{:S(2)}, u32[]{:S(2)}) collective-permute-start(bf16[2,256,1024]{2,1,0:T(8,128)(2,1)S(1)} %broadcast_select_fusion), channel_id=1, source_target_pairs={{0,1},{1,0},{2,3},{3,2},{4,5},{5,4},{6,7},{7,6},{8,9},{9,8},{10,11... | collective-permute-start | bytes 3145736 | tf_op jit(solution)/shard_map/ppermute | solution.py:40
  56.3 3.8 %collective-permute-start.3 = (bf16[2,128,1024]{2,1,0:T(8,128)(2,1)S(1)}, bf16[2,128,1024]{2,1,0:T(8,128)(2,1)S(1)}, u32[]{:S(2)}, u32[]{:S(2)}) collective-permute-start(bf16[2,128,1024]{2,1,0:T(8,128)(2,1)S(1)} %broadcast_select_fusion.3), channel_id=1, source_target_pairs={{0,1},{2,3},{4,5},{6,7},{8,9},{10,11},{12,13},{14,15},{16,17},{18,... | collective-permute-start | bytes 1572872 | tf_op jit(solution)/shard_map/ppermute | solution.py:60
  57.7 4.9 %copy-start.2 = (bf16[256,1024]{1,0:T(8,128)(2,1)S(1)}, bf16[256,1024]{1,0:T(8,128)(2,1)}, u32[]{:S(2)}) copy-start(bf16[256,1024]{1,0:T(8,128)(2,1)} %param.5) | copy-start | bytes 1572868
  57.7 4.9 %copy-start.3 = (bf16[256,1024]{1,0:T(8,128)(2,1)S(1)}, bf16[256,1024]{1,0:T(8,128)(2,1)}, u32[]{:S(2)}) copy-start(bf16[256,1024]{1,0:T(8,128)(2,1)} %param.6) | copy-start | bytes 1572868
  60.4 2.4 %copy-start.1 = (bf16[256,4096]{1,0:T(8,128)(2,1)S(1)}, bf16[256,4096]{1,0:T(8,128)(2,1)}, u32[]{:S(2)}) copy-start(bf16[256,4096]{1,0:T(8,128)(2,1)} %q_ref.1) | copy-start | bytes 6291460

commit v15 on v13

--- a/solution.py
+++ b/solution.py
@@ -16,7 +16,8 @@
 LIST = 11
 GROUP = H // KVH
 PAIR = 2
-KV_STEP = 4
+KV_STEP = 8
+SLOTS = 8
 
 
 def shifted(shard, axis, by, sends):
@@ -86,13 +87,13 @@
                 sc = lax.dot_general(
                     stacked, key, (((1,), (1,)), ((), ())), preferred_element_type=jnp.float32
                 ) + bias_sc[diag_ref[local, s]]
-                score_sc[chain, s] = sc
+                score_sc[chain % SLOTS, s] = sc
                 run_max = jnp.maximum(run_max, sc)
             row_max = jnp.max(run_max, axis=1, keepdims=True)
             total = jnp.zeros((rows, BLK), jnp.float32)
             acc = jnp.zeros((rows, HD), jnp.float32)
             for s in range(LIST):
-                powers = jnp.exp2((score_sc[chain, s] - row_max) * exp2_scale)
+                powers = jnp.exp2((score_sc[chain % SLOTS, s] - row_max) * exp2_scale)
                 total = total + powers
                 value = v_ref[0, slot_ref[local, s], :, kv_lanes]
                 acc = acc + jnp.dot(
@@ -119,7 +120,7 @@
         ],
         out_specs=pl.BlockSpec((BLK, KV_STEP * GROUP * HD), lambda g, b, *_: (b, g)),
         scratch_shapes=[
-            pltpu.VMEM((KV_STEP * GROUP // PAIR, LIST, PAIR * BLK, BLK), jnp.float32),
+            pltpu.VMEM((SLOTS, LIST, PAIR * BLK, BLK), jnp.float32),
             pltpu.VMEM((2, PAIR * BLK, BLK), jnp.float32),
         ],
     )

time: 84.6 us -> 85.1 us (level)
  no operation moved by 1% of the time
where the time goes in v15:
time: 85.1 us; the launch traced here: 84.7 us
  starting transfers between devices  35.5 us (42%)
  Pallas kernels  22 us (26%)
  waiting for transfers between devices  19.2 us (23%)
  other arithmetic  7.44 us (9%)
    ppermute x5, starting transfers between devices, shifted(): return lax.ppermute(shard, axis, pairs)  27.1 us
    pallas_call x1, Pallas kernels, attend(): pl.pallas_call(attend_kernel, out_shape=jax.ShapeDtypeStruct(queries.shap...  22 us
    ppermute x5, waiting for transfers between devices, shifted(): return lax.ppermute(shard, axis, pairs)  16.8 us
    ppermute x4, starting transfers between devices, tree_broadcast(): got = lax.ppermute(held, axis, pairs)  4.94 us
    ppermute x1, starting transfers between devices, window_blocks(): partner_back2 = lax.ppermute(back2, axis, swap_pairs)  3.46 us
    ppermute x4, waiting for transfers between devices, tree_broadcast(): got = lax.ppermute(held, axis, pairs)  2.39 us
    another operation x2, other arithmetic, per_device(): kv = jnp.stack([key_rows, value_rows])  2.38 us
    unnamed x3, other arithmetic  2.31 us
  transfers between devices with their start and end apart: 10, of which 2 were waited for; matrix products, arithmetic and copies ran while one was open for 6% of the time, Pallas kernels for 0%

profile of v15, /device:TPU:19, one launch (start us, length us, event | category | flops | bytes accessed | tf_op | source)
XLA Modules:
  0.0 84.7 jit_solution(10820101030792555485)
XLA Ops:
  0.0 1.3 %pad_maximum_fusion = bf16[2,256,1024]{2,1,0:T(8,128)(2,1)S(1)} fusion(bf16[1,256,1024]{2,1,0:T(8,128)(2,1)} %bitcast.9, bf16[1,256,1024]{2,1,0:T(8,128)(2,1)} %bitcast.5), kind=kLoop, calls=%fused_computation.1 | loop fusion | flops 524288 | bytes 2097152 | tf_op jit(solution)/shard_map/stack | solution.py:148
  1.3 3.2 %collective-permute-start.4 = (bf16[2,256,1024]{2,1,0:T(8,128)(2,1)S(1)}, bf16[2,256,1024]{2,1,0:T(8,128)(2,1)S(1)}, u32[]{:S(2)}, u32[]{:S(2)}) collective-permute-start(bf16[2,256,1024]{2,1,0:T(8,128)(2,1)S(1)} %pad_maximum_fusion), channel_id=1, source_target_pairs={{0,4},{1,5},{2,6},{3,7},{4,8},{5,9},{6,10},{7,11},{8,12},{9,13},{1... | collective-permute-start | bytes 3145736 | tf_op jit(solution)/shard_map/ppermute | solution.py:26
  4.5 1.1 %fusion = bf16[2,128,1024]{2,1,0:T(8,128)(2,1)S(1)} fusion(bf16[1,256,1024]{2,1,0:T(8,128)(2,1)} %bitcast.6, bf16[1,256,1024]{2,1,0:T(8,128)(2,1)} %bitcast.10), kind=kLoop, calls=%fused_computation.6 | loop fusion | flops 262144 | bytes 1572864 | tf_op jit(solution)/shard_map/stack | solution.py:148
  5.6 0.7 collective-permute-start
  6.3 4.2 %collective-permute-start.7 = (bf16[2,256,1024]{2,1,0:T(8,128)(2,1)S(1)}, bf16[2,256,1024]{2,1,0:T(8,128)(2,1)}, u32[]{:S(2)}, u32[]{:S(2)}) collective-permute-start(bf16[2,256,1024]{2,1,0:T(8,128)(2,1)S(1)} %pad_maximum_fusion), channel_id=1, source_target_pairs={{0,2},{1,3},{4,6},{5,7},{8,10},{9,11},{12,14},{13,15},{16,18},{17,... | collective-permute-start | bytes 3145736 | tf_op jit(solution)/shard_map/ppermute | solution.py:26
  10.5 16.8 %collective-permute-done.4 = bf16[2,256,1024]{2,1,0:T(8,128)(2,1)S(1)} collective-permute-done((bf16[2,256,1024]{2,1,0:T(8,128)(2,1)S(1)}, bf16[2,256,1024]{2,1,0:T(8,128)(2,1)S(1)}, u32[]{:S(2)}, u32[]{:S(2)}) %collective-permute-start.4) | collective-permute-done | bytes 1048608 | tf_op jit(solution)/shard_map/ppermute | solution.py:26
  27.2 1.3 %collective-permute-start.6 = (bf16[2,256,1024]{2,1,0:T(8,128)(2,1)S(1)}, bf16[2,256,1024]{2,1,0:T(8,128)(2,1)}, u32[]{:S(2)}, u32[]{:S(2)}) collective-permute-start(bf16[2,256,1024]{2,1,0:T(8,128)(2,1)S(1)} %collective-permute-done.4), channel_id=1, source_target_pairs={{2,0},{3,1},{6,4},{7,5},{10,8},{11,9},{14,12},{15,13},{18,16},{19,... | collective-permute-start | bytes 3145736 | tf_op jit(solution)/shard_map/ppermute | solution.py:26
  28.5 1.1 %broadcast_select_fusion.1 = bf16[2,128,1024]{2,1,0:T(8,128)(2,1)S(1)} fusion(bf16[2,128,1024]{2,1,0:T(8,128)(2,1)S(1)} %collective-permute-done, pred[]{:T(512)S(6)} %and.53, bf16[1,256,1024]{2,1,0:T(8,128)(2,1)} %bitcast.11, bf16[1,256,1024]{2,1,0:T(8,128)(2,1)} %bitcast.7), kind=kLoop, calls=%fused_computation.8 | loop fusion | flops 524288 | bytes 2097153 | tf_op jit(solution)/shard_map/jit(_where)/select_n | solution.py:64
  29.6 1.5 %collective-permute-start.1 = (bf16[2,128,1024]{2,1,0:T(8,128)(2,1)S(1)}, bf16[2,128,1024]{2,1,0:T(8,128)(2,1)}, u32[]{:S(2)}, u32[]{:S(2)}) collective-permute-start(bf16[2,128,1024]{2,1,0:T(8,128)(2,1)S(1)} %broadcast_select_fusion.1), channel_id=1, source_target_pairs={{0,4},{8,12},{16,20},{24,28}} | collective-permute-start | bytes 1572872 | tf_op jit(solution)/shard_map/ppermute | solution.py:61
  31.1 0.0 collective-permute-done.1
  31.1 0.1 broadcast_select_fusion.2
  31.2 1.5 %collective-permute-start.2 = (bf16[2,128,1024]{2,1,0:T(8,128)(2,1)S(1)}, bf16[2,128,1024]{2,1,0:T(8,128)(2,1)}, u32[]{:S(2)}, u32[]{:S(2)}) collective-permute-start(bf16[2,128,1024]{2,1,0:T(8,128)(2,1)S(1)} %broadcast_select_fusion.2), channel_id=1, source_target_pairs={{0,2},{4,6},{8,10},{12,14},{16,18},{20,22},{24,26},{28,30}} | collective-permute-start | bytes 1572872 | tf_op jit(solution)/shard_map/ppermute | solution.py:61
  32.7 1.3 %collective-permute-start.9 = (bf16[2,256,1024]{2,1,0:T(8,128)(2,1)S(1)}, bf16[2,256,1024]{2,1,0:T(8,128)(2,1)}, u32[]{:S(2)}, u32[]{:S(2)}) collective-permute-start(bf16[2,256,1024]{2,1,0:T(8,128)(2,1)S(1)} %pad_maximum_fusion), channel_id=1, source_target_pairs={{0,1},{2,3},{4,5},{6,7},{8,9},{10,11},{12,13},{14,15},{16,17},{18,... | collective-permute-start | bytes 3145736 | tf_op jit(solution)/shard_map/ppermute | solution.py:26
  34.0 0.1 constant_dynamic-slice_fusion
  34.1 0.1 copy.6
  34.2 17.2 %collective-permute-start.5 = (bf16[2,256,1024]{2,1,0:T(8,128)(2,1)S(1)}, bf16[2,256,1024]{2,1,0:T(8,128)(2,1)S(1)}, u32[]{:S(2)}, u32[]{:S(2)}) collective-permute-start(bf16[2,256,1024]{2,1,0:T(8,128)(2,1)S(1)} %collective-permute-done.4), channel_id=1, source_target_pairs={{1,0},{3,2},{5,4},{7,6},{9,8},{11,10},{13,12},{15,14},{17,16},{19,... | collective-permute-start | bytes 3145736 | tf_op jit(solution)/shard_map/ppermute | solution.py:26
  51.4 1.3 %broadcast_select_fusion = bf16[2,256,1024]{2,1,0:T(8,128)(2,1)S(1)} fusion(bf16[2,256,1024]{2,1,0:T(8,128)(2,1)} %collective-permute-done.6, bf16[2,256,1024]{2,1,0:T(8,128)(2,1)} %collective-permute-done.7, pred[]{:T(512)S(6)} %eq.40), kind=kLoop, calls=%fused_computation.5 | loop fusion | flops 524288 | bytes 3145729 | tf_op jit(solution)/shard_map/jit(_where)/select_n | solution.py:37
  52.7 3.5 %collective-permute-start.8 = (bf16[2,256,1024]{2,1,0:T(8,128)(2,1)S(1)}, bf16[2,256,1024]{2,1,0:T(8,128)(2,1)S(1)}, u32[]{:S(2)}, u32[]{:S(2)}) collective-permute-start(bf16[2,256,1024]{2,1,0:T(8,128)(2,1)S(1)} %broadcast_select_fusion), channel_id=1, source_target_pairs={{0,1},{1,0},{2,3},{3,2},{4,5},{5,4},{6,7},{7,6},{8,9},{9,8},{10,11... | collective-permute-start | bytes 3145736 | tf_op jit(solution)/shard_map/ppermute | solution.py:41
  56.2 0.1 broadcast_select_fusion.3
  56.3 1.3 %collective-permute-start.3 = (bf16[2,128,1024]{2,1,0:T(8,128)(2,1)S(1)}, bf16[2,128,1024]{2,1,0:T(8,128)(2,1)S(1)}, u32[]{:S(2)}, u32[]{:S(2)}) collective-permute-start(bf16[2,128,1024]{2,1,0:T(8,128)(2,1)S(1)} %broadcast_select_fusion.3), channel_id=1, source_target_pairs={{0,1},{2,3},{4,5},{6,7},{8,9},{10,11},{12,13},{14,15},{16,17},{18,... | collective-permute-start | bytes 1572872 | tf_op jit(solution)/shard_map/ppermute | solution.py:61
  57.6 0.1 compare_convert_fusion.diag_ref
  57.7 0.0 copy-start.2
  57.7 0.0 copy-start.3
  57.7 2.4 %collective-permute-done.3 = bf16[2,128,1024]{2,1,0:T(8,128)(2,1)S(1)} collective-permute-done((bf16[2,128,1024]{2,1,0:T(8,128)(2,1)S(1)}, bf16[2,128,1024]{2,1,0:T(8,128)(2,1)S(1)}, u32[]{:S(2)}, u32[]{:S(2)}) %collective-permute-start.3) | collective-permute-done | bytes 524320 | tf_op jit(solution)/shard_map/ppermute | solution.py:61
  60.1 0.2 select_dynamic-update-slice_fusion.2
  60.3 0.1 constant_dynamic-update-slice_fusion.2
  60.4 0.0 copy-start.1
  60.4 0.4 select_dynamic-update-slice_fusion.1
  60.8 0.1 constant_dynamic-update-slice_fusion.1
  60.9 1.7 %select_dynamic-update-slice_fusion = bf16[2,1408,1024]{2,1,0:T(8,128)(2,1)S(1)} fusion(bf16[2,1408,1024]{2,1,0:T(8,128)(2,1)S(1)} %constant_dynamic-update-slice_fusion.1, bf16[2,256,1024]{2,1,0:T(8,128)(2,1)S(1)} %collective-permute-done.8, bf16[2,256,1024]{2,1,0:T(8,128)(2,1)} %collective-permute-done.9, pred[]{:T(512)S(6)} %eq.39), kind=kLoop, calls=%fused_computation.3 | loop fusion | flops 524288 | bytes 3145729
  62.6 0.1 constant_dynamic-update-slice_fusion
  62.7 22.0 %shard_map.46 = bf16[256,4096]{1,0:T(8,128)(2,1)} custom-call(s32[2,11]{1,0:T(2,128)S(1)} %fusion.1.slot_ref, s32[2,11]{1,0:T(2,128)S(1)} %compare_convert_fusion.diag_ref, bf16[256,4096]{1,0:T(8,128)(2,1)S(1)} %copy-done.1, bf16[2,11,128,1024]{3,2,1,0:T(8,128)(2,1)S(1)} %bitcast.3, bf16[2,11,128,1024]{3,2,1,0:T(8,128)(2,1)S(1)} %bitcast.4), custom_call_target="tpu_custom_call" | custom-call | flops 5905580032 | bytes 9961472 | tf_op jit(solution)/shard_map/pallas_call | solution.py:127
  (14 shorter events, 0.0 us)
Async XLA Ops:
  0.0 34.0 %copy-start = (s32[32,11]{0,1:T(8,128)S(1)}, s32[32,11]{0,1:T(8,128)}, u32[]{:S(2)}) copy-start(s32[32,11]{0,1:T(8,128)} %param.7) | copy-start | bytes 4228
  1.3 25.9 %collective-permute-start.4 = (bf16[2,256,1024]{2,1,0:T(8,128)(2,1)S(1)}, bf16[2,256,1024]{2,1,0:T(8,128)(2,1)S(1)}, u32[]{:S(2)}, u32[]{:S(2)}) collective-permute-start(bf16[2,256,1024]{2,1,0:T(8,128)(2,1)S(1)} %pad_maximum_fusion), channel_id=1, source_target_pairs={{0,4},{1,5},{2,6},{3,7},{4,8},{5,9},{6,10},{7,11},{8,12},{9,13},{1... | collective-permute-start | bytes 3145736 | tf_op jit(solution)/shard_map/ppermute | solution.py:26
  5.6 22.9 %collective-permute-start = (bf16[2,128,1024]{2,1,0:T(8,128)(2,1)S(1)}, bf16[2,128,1024]{2,1,0:T(8,128)(2,1)S(1)}, u32[]{:S(2)}, u32[]{:S(2)}) collective-permute-start(bf16[2,128,1024]{2,1,0:T(8,128)(2,1)S(1)} %fusion), channel_id=1, source_target_pairs={{0,8},{16,24}} | collective-permute-start | bytes 1572872 | tf_op jit(solution)/shard_map/ppermute | solution.py:61
  6.3 45.1 %collective-permute-start.7 = (bf16[2,256,1024]{2,1,0:T(8,128)(2,1)S(1)}, bf16[2,256,1024]{2,1,0:T(8,128)(2,1)}, u32[]{:S(2)}, u32[]{:S(2)}) collective-permute-start(bf16[2,256,1024]{2,1,0:T(8,128)(2,1)S(1)} %pad_maximum_fusion), channel_id=1, source_target_pairs={{0,2},{1,3},{4,6},{5,7},{8,10},{9,11},{12,14},{13,15},{16,18},{17,... | collective-permute-start | bytes 3145736 | tf_op jit(solution)/shard_map/ppermute | solution.py:26
  27.2 24.2 %collective-permute-start.6 = (bf16[2,256,1024]{2,1,0:T(8,128)(2,1)S(1)}, bf16[2,256,1024]{2,1,0:T(8,128)(2,1)}, u32[]{:S(2)}, u32[]{:S(2)}) collective-permute-start(bf16[2,256,1024]{2,1,0:T(8,128)(2,1)S(1)} %collective-permute-done.4), channel_id=1, source_target_pairs={{2,0},{3,1},{6,4},{7,5},{10,8},{11,9},{14,12},{15,13},{18,16},{19,... | collective-permute-start | bytes 3145736 | tf_op jit(solution)/shard_map/ppermute | solution.py:26
  29.6 1.5 %collective-permute-start.1 = (bf16[2,128,1024]{2,1,0:T(8,128)(2,1)S(1)}, bf16[2,128,1024]{2,1,0:T(8,128)(2,1)}, u32[]{:S(2)}, u32[]{:S(2)}) collective-permute-start(bf16[2,128,1024]{2,1,0:T(8,128)(2,1)S(1)} %broadcast_select_fusion.1), channel_id=1, source_target_pairs={{0,4},{8,12},{16,20},{24,28}} | collective-permute-start | bytes 1572872 | tf_op jit(solution)/shard_map/ppermute | solution.py:61
  31.2 25.0 %collective-permute-start.2 = (bf16[2,128,1024]{2,1,0:T(8,128)(2,1)S(1)}, bf16[2,128,1024]{2,1,0:T(8,128)(2,1)}, u32[]{:S(2)}, u32[]{:S(2)}) collective-permute-start(bf16[2,128,1024]{2,1,0:T(8,128)(2,1)S(1)} %broadcast_select_fusion.2), channel_id=1, source_target_pairs={{0,2},{4,6},{8,10},{12,14},{16,18},{20,22},{24,26},{28,30}} | collective-permute-start | bytes 1572872 | tf_op jit(solution)/shard_map/ppermute | solution.py:61
  32.7 28.2 %collective-permute-start.9 = (bf16[2,256,1024]{2,1,0:T(8,128)(2,1)S(1)}, bf16[2,256,1024]{2,1,0:T(8,128)(2,1)}, u32[]{:S(2)}, u32[]{:S(2)}) collective-permute-start(bf16[2,256,1024]{2,1,0:T(8,128)(2,1)S(1)} %pad_maximum_fusion), channel_id=1, source_target_pairs={{0,1},{2,3},{4,5},{6,7},{8,9},{10,11},{12,13},{14,15},{16,17},{18,... | collective-permute-start | bytes 3145736 | tf_op jit(solution)/shard_map/ppermute | solution.py:26
  34.2 26.2 %collective-permute-start.5 = (bf16[2,256,1024]{2,1,0:T(8,128)(2,1)S(1)}, bf16[2,256,1024]{2,1,0:T(8,128)(2,1)S(1)}, u32[]{:S(2)}, u32[]{:S(2)}) collective-permute-start(bf16[2,256,1024]{2,1,0:T(8,128)(2,1)S(1)} %collective-permute-done.4), channel_id=1, source_target_pairs={{1,0},{3,2},{5,4},{7,6},{9,8},{11,10},{13,12},{15,14},{17,16},{19,... | collective-permute-start | bytes 3145736 | tf_op jit(solution)/shard_map/ppermute | solution.py:26
  52.7 7.6 %collective-permute-start.8 = (bf16[2,256,1024]{2,1,0:T(8,128)(2,1)S(1)}, bf16[2,256,1024]{2,1,0:T(8,128)(2,1)S(1)}, u32[]{:S(2)}, u32[]{:S(2)}) collective-permute-start(bf16[2,256,1024]{2,1,0:T(8,128)(2,1)S(1)} %broadcast_select_fusion), channel_id=1, source_target_pairs={{0,1},{1,0},{2,3},{3,2},{4,5},{5,4},{6,7},{7,6},{8,9},{9,8},{10,11... | collective-permute-start | bytes 3145736 | tf_op jit(solution)/shard_map/ppermute | solution.py:41
  56.3 3.8 %collective-permute-start.3 = (bf16[2,128,1024]{2,1,0:T(8,128)(2,1)S(1)}, bf16[2,128,1024]{2,1,0:T(8,128)(2,1)S(1)}, u32[]{:S(2)}, u32[]{:S(2)}) collective-permute-start(bf16[2,128,1024]{2,1,0:T(8,128)(2,1)S(1)} %broadcast_select_fusion.3), channel_id=1, source_target_pairs={{0,1},{2,3},{4,5},{6,7},{8,9},{10,11},{12,13},{14,15},{16,17},{18,... | collective-permute-start | bytes 1572872 | tf_op jit(solution)/shard_map/ppermute | solution.py:61
  57.7 4.9 %copy-start.2 = (bf16[256,1024]{1,0:T(8,128)(2,1)S(1)}, bf16[256,1024]{1,0:T(8,128)(2,1)}, u32[]{:S(2)}) copy-start(bf16[256,1024]{1,0:T(8,128)(2,1)} %param.5) | copy-start | bytes 1572868
  57.7 4.9 %copy-start.3 = (bf16[256,1024]{1,0:T(8,128)(2,1)S(1)}, bf16[256,1024]{1,0:T(8,128)(2,1)}, u32[]{:S(2)}) copy-start(bf16[256,1024]{1,0:T(8,128)(2,1)} %param.6) | copy-start | bytes 1572868
  60.4 2.4 %copy-start.1 = (bf16[256,4096]{1,0:T(8,128)(2,1)S(1)}, bf16[256,4096]{1,0:T(8,128)(2,1)}, u32[]{:S(2)}) copy-start(bf16[256,4096]{1,0:T(8,128)(2,1)} %q_ref.1) | copy-start | bytes 6291460

commit v16 on v13

--- a/solution.py
+++ b/solution.py
@@ -37,7 +37,11 @@
     partner_back4 = shifted(back4, axis, -1, lambda i: i % 2 == 1)
     size = lax.axis_size(axis)
     swap_pairs = [(i, i ^ 1) for i in range(size)]
-    partner_back2 = lax.ppermute(back2, axis, swap_pairs)
+    partner_back2 = jnp.where(
+        y_low,
+        lax.ppermute(down_y, axis, swap_pairs),
+        lax.ppermute(up_y, axis, swap_pairs),
+    )
     back3 = jnp.where(core0, partner_back4, partner_back2)
     back1 = jnp.where(core0, partner_back2, next_core)
     return [back4, back3, back2, back1]

time: 84.6 us -> 90 us (1.064); the launches traced: 84.2 us -> 88.5 us
  starting transfers between devices: 35.5 us -> 38.5 us
  other arithmetic: 7.44 us -> 9.14 us
  waiting for transfers between devices: 19.2 us -> 17.6 us
  local copies, waits for them, and re-layouts: 0.33 us -> 1.49 us
    ppermute x5, starting transfers between devices: 27.1 us -> 30.4 us  [shifted(): return lax.ppermute(shard, axis, pairs)]
    unnamed x3 -> x4, other arithmetic: 2.31 us -> 4.42 us
    ppermute x5, waiting for transfers between devices: 16.8 us -> 15.3 us  [shifted(): return lax.ppermute(shard, axis, pairs)]
    select_n x1 -> x0, other arithmetic: 1.35 us -> none  [window_blocks(): back2 = jnp.where(y_low, down_y, up_y)]
    unnamed x11 -> x10, local copies, waits for them, and re-layouts: 0.26 us -> 1.41 us
    another operation x2, other arithmetic: 2.38 us -> 3.35 us  [per_device(): kv = jnp.stack([key_rows, value_rows])]
    ppermute x1 -> x2, starting transfers between devices: 3.46 us -> 3.95 us  [the longest x1 3.94 us: window_blocks(): lax.ppermute(down_y, axis, swap_pairs)]
  transfers between devices with their start and end apart: 10 -> 11, of which waited for: 2 -> 2; matrix products, arithmetic and copies ran while one was open for 6% -> 7% of each run, Pallas kernels for 0% -> 0%
where the time goes in v16:
time: 90 us; the launch traced here: 88.5 us
  starting transfers between devices  38.5 us (43%)
  Pallas kernels  21.4 us (24%)
  waiting for transfers between devices  17.6 us (20%)
  other arithmetic  9.14 us (10%)
  local copies, waits for them, and re-layouts  1.49 us (2%)
    ppermute x5, starting transfers between devices, shifted(): return lax.ppermute(shard, axis, pairs)  30.4 us
    pallas_call x1, Pallas kernels, attend(): pl.pallas_call(attend_kernel, out_shape=jax.ShapeDtypeStruct(queries.shap...  21.4 us
    ppermute x5, waiting for transfers between devices, shifted(): return lax.ppermute(shard, axis, pairs)  15.3 us
    unnamed x4, other arithmetic  4.42 us
    ppermute x4, starting transfers between devices, tree_broadcast(): got = lax.ppermute(held, axis, pairs)  4.18 us
    ppermute x1, starting transfers between devices, window_blocks(): lax.ppermute(down_y, axis, swap_pairs)  3.94 us
    another operation x2, other arithmetic, per_device(): kv = jnp.stack([key_rows, value_rows])  3.35 us
    ppermute x4, waiting for transfers between devices, tree_broadcast(): got = lax.ppermute(held, axis, pairs)  2.38 us
  transfers between devices with their start and end apart: 11, of which 2 were waited for; matrix products, arithmetic and copies ran while one was open for 7% of the time, Pallas kernels for 0%

profile of v16, /device:TPU:19, one launch (start us, length us, event | category | flops | bytes accessed | tf_op | source)
XLA Modules:
  0.0 88.5 jit_solution(16987534255811222234)
XLA Ops:
  0.0 2.3 %pad_maximum_fusion = bf16[2,256,1024]{2,1,0:T(8,128)(2,1)} fusion(bf16[1,256,1024]{2,1,0:T(8,128)(2,1)} %bitcast.9, bf16[1,256,1024]{2,1,0:T(8,128)(2,1)} %bitcast.5), kind=kLoop, calls=%fused_computation.1 | loop fusion | flops 524288 | bytes 2097152 | tf_op jit(solution)/shard_map/stack | solution.py:151
  2.3 3.2 %collective-permute-start.4 = (bf16[2,256,1024]{2,1,0:T(8,128)(2,1)}, bf16[2,256,1024]{2,1,0:T(8,128)(2,1)}, u32[]{:S(2)}, u32[]{:S(2)}) collective-permute-start(bf16[2,256,1024]{2,1,0:T(8,128)(2,1)} %pad_maximum_fusion), channel_id=1, source_target_pairs={{0,4},{1,5},{2,6},{3,7},{4,8},{5,9},{6,10},{7,11},{8,12},{9,13},{1... | collective-permute-start | bytes 3145736 | tf_op jit(solution)/shard_map/ppermute | solution.py:25
  5.5 1.1 %fusion = bf16[2,128,1024]{2,1,0:T(8,128)(2,1)S(1)} fusion(bf16[1,256,1024]{2,1,0:T(8,128)(2,1)} %bitcast.6, bf16[1,256,1024]{2,1,0:T(8,128)(2,1)} %bitcast.10), kind=kLoop, calls=%fused_computation.7 | loop fusion | flops 262144 | bytes 1572864 | tf_op jit(solution)/shard_map/stack | solution.py:151
  6.6 0.7 collective-permute-start
  7.3 0.0 collective-permute-done
  7.3 1.1 %broadcast_select_fusion.1 = bf16[2,128,1024]{2,1,0:T(8,128)(2,1)S(1)} fusion(bf16[2,128,1024]{2,1,0:T(8,128)(2,1)S(1)} %collective-permute-done, pred[]{:T(512)S(6)} %and.53, bf16[1,256,1024]{2,1,0:T(8,128)(2,1)} %bitcast.11, bf16[1,256,1024]{2,1,0:T(8,128)(2,1)} %bitcast.7), kind=kLoop, calls=%fused_computation.9 | loop fusion | flops 524288 | bytes 2097153 | tf_op jit(solution)/shard_map/jit(_where)/select_n | solution.py:67
  8.4 0.7 collective-permute-start.1
  9.1 4.2 %collective-permute-start.8 = (bf16[2,256,1024]{2,1,0:T(8,128)(2,1)}, bf16[2,256,1024]{2,1,0:T(8,128)(2,1)}, u32[]{:S(2)}, u32[]{:S(2)}) collective-permute-start(bf16[2,256,1024]{2,1,0:T(8,128)(2,1)} %pad_maximum_fusion), channel_id=1, source_target_pairs={{0,2},{1,3},{4,6},{5,7},{8,10},{9,11},{12,14},{13,15},{16,18},{17,... | collective-permute-start | bytes 3145736 | tf_op jit(solution)/shard_map/ppermute | solution.py:25
  13.2 15.3 %collective-permute-done.4 = bf16[2,256,1024]{2,1,0:T(8,128)(2,1)} collective-permute-done((bf16[2,256,1024]{2,1,0:T(8,128)(2,1)}, bf16[2,256,1024]{2,1,0:T(8,128)(2,1)}, u32[]{:S(2)}, u32[]{:S(2)}) %collective-permute-start.4) | collective-permute-done | bytes 1048608 | tf_op jit(solution)/shard_map/ppermute | solution.py:25
  28.5 1.3 %collective-permute-start.6 = (bf16[2,256,1024]{2,1,0:T(8,128)(2,1)}, bf16[2,256,1024]{2,1,0:T(8,128)(2,1)}, u32[]{:S(2)}, u32[]{:S(2)}) collective-permute-start(bf16[2,256,1024]{2,1,0:T(8,128)(2,1)} %collective-permute-done.4), channel_id=1, source_target_pairs={{2,0},{3,1},{6,4},{7,5},{10,8},{11,9},{14,12},{15,13},{18,16},{19,... | collective-permute-start | bytes 3145736 | tf_op jit(solution)/shard_map/ppermute | solution.py:25
  29.8 0.1 broadcast_select_fusion.2
  29.9 1.5 %collective-permute-start.2 = (bf16[2,128,1024]{2,1,0:T(8,128)(2,1)S(1)}, bf16[2,128,1024]{2,1,0:T(8,128)(2,1)}, u32[]{:S(2)}, u32[]{:S(2)}) collective-permute-start(bf16[2,128,1024]{2,1,0:T(8,128)(2,1)S(1)} %broadcast_select_fusion.2), channel_id=1, source_target_pairs={{0,2},{4,6},{8,10},{12,14},{16,18},{20,22},{24,26},{28,30}} | collective-permute-start | bytes 1572872 | tf_op jit(solution)/shard_map/ppermute | solution.py:64
  31.4 1.3 %collective-permute-start.10 = (bf16[2,256,1024]{2,1,0:T(8,128)(2,1)}, bf16[2,256,1024]{2,1,0:T(8,128)(2,1)}, u32[]{:S(2)}, u32[]{:S(2)}) collective-permute-start(bf16[2,256,1024]{2,1,0:T(8,128)(2,1)} %pad_maximum_fusion), channel_id=1, source_target_pairs={{0,1},{2,3},{4,5},{6,7},{8,9},{10,11},{12,13},{14,15},{16,17},{18,... | collective-permute-start | bytes 3145736 | tf_op jit(solution)/shard_map/ppermute | solution.py:25
  32.7 0.1 constant_dynamic-slice_fusion
  32.8 0.1 copy.6
  32.9 20.5 %collective-permute-start.5 = (bf16[2,256,1024]{2,1,0:T(8,128)(2,1)}, bf16[2,256,1024]{2,1,0:T(8,128)(2,1)}, u32[]{:S(2)}, u32[]{:S(2)}) collective-permute-start(bf16[2,256,1024]{2,1,0:T(8,128)(2,1)} %collective-permute-done.4), channel_id=1, source_target_pairs={{1,0},{3,2},{5,4},{7,6},{9,8},{11,10},{13,12},{15,14},{17,16},{19,... | collective-permute-start | bytes 3145736 | tf_op jit(solution)/shard_map/ppermute | solution.py:25
  53.3 0.0 collective-permute-done.8
  53.3 3.9 %collective-permute-start.7 = (bf16[2,256,1024]{2,1,0:T(8,128)(2,1)}, bf16[2,256,1024]{2,1,0:T(8,128)(2,1)S(1)}, u32[]{:S(2)}, u32[]{:S(2)}) collective-permute-start(bf16[2,256,1024]{2,1,0:T(8,128)(2,1)} %collective-permute-done.6), channel_id=1, source_target_pairs={{0,1},{1,0},{2,3},{3,2},{4,5},{5,4},{6,7},{7,6},{8,9},{9,8},{10,11... | collective-permute-start | bytes 3145736 | tf_op jit(solution)/shard_map/ppermute | solution.py:42
  57.3 0.1 broadcast_select_fusion.3
  57.4 1.3 %collective-permute-start.3 = (bf16[2,128,1024]{2,1,0:T(8,128)(2,1)S(1)}, bf16[2,128,1024]{2,1,0:T(8,128)(2,1)S(1)}, u32[]{:S(2)}, u32[]{:S(2)}) collective-permute-start(bf16[2,128,1024]{2,1,0:T(8,128)(2,1)S(1)} %broadcast_select_fusion.3), channel_id=1, source_target_pairs={{0,1},{2,3},{4,5},{6,7},{8,9},{10,11},{12,13},{14,15},{16,17},{18,... | collective-permute-start | bytes 1572872 | tf_op jit(solution)/shard_map/ppermute | solution.py:64
  58.7 0.1 compare_convert_fusion.diag_ref
  58.8 2.4 %collective-permute-done.3 = bf16[2,128,1024]{2,1,0:T(8,128)(2,1)S(1)} collective-permute-done((bf16[2,128,1024]{2,1,0:T(8,128)(2,1)S(1)}, bf16[2,128,1024]{2,1,0:T(8,128)(2,1)S(1)}, u32[]{:S(2)}, u32[]{:S(2)}) %collective-permute-start.3) | collective-permute-done | bytes 524320 | tf_op jit(solution)/shard_map/ppermute | solution.py:64
  61.2 0.2 select_dynamic-update-slice_fusion.3
  61.4 1.3 %constant_dynamic-update-slice_fusion.1 = bf16[2,1408,1024]{2,1,0:T(8,128)(2,1)S(1)} fusion(bf16[2,1408,1024]{2,1,0:T(8,128)(2,1)S(1)} %select_dynamic-update-slice_fusion.3, bf16[2,256,1024]{2,1,0:T(8,128)(2,1)} %collective-permute-done.4), kind=kLoop, calls=%fused_computation.13 | loop fusion | bytes 2097152
  62.6 0.0 copy-start.2
  62.7 0.0 copy-start.3
  62.7 0.6 select_dynamic-update-slice_fusion.2
  63.3 0.0 copy-start.1
  63.3 1.8 %select_dynamic-update-slice_fusion.1 = bf16[2,1408,1024]{2,1,0:T(8,128)(2,1)S(1)} fusion(bf16[2,1408,1024]{2,1,0:T(8,128)(2,1)S(1)} %select_dynamic-update-slice_fusion.2, bf16[2,256,1024]{2,1,0:T(8,128)(2,1)} %collective-permute-done.6, bf16[2,256,1024]{2,1,0:T(8,128)(2,1)} %collective-permute-done.8, pred[]{:T(512)S(6)} %eq.40), kind=kLoop, calls=%fused_computation.4 | loop fusion | flops 524288 | bytes 3145729
  65.1 1.8 %select_dynamic-update-slice_fusion = bf16[2,1408,1024]{2,1,0:T(8,128)(2,1)S(1)} fusion(bf16[2,1408,1024]{2,1,0:T(8,128)(2,1)S(1)} %select_dynamic-update-slice_fusion.1, bf16[2,256,1024]{2,1,0:T(8,128)(2,1)} %collective-permute-done.10, pred[]{:T(512)S(6)} %eq.39, bf16[2,256,1024]{2,1,0:T(8,128)(2,1)S(1)} %collective-permute-done.7, ...), kind=kLoop, calls=%fused_computation.3 | loop fusion | flops 1048576 | bytes 4194306
  67.0 0.1 constant_dynamic-update-slice_fusion
  67.1 21.4 %shard_map.46 = bf16[256,4096]{1,0:T(8,128)(2,1)} custom-call(s32[2,11]{1,0:T(2,128)S(1)} %fusion.1.slot_ref, s32[2,11]{1,0:T(2,128)S(1)} %compare_convert_fusion.diag_ref, bf16[256,4096]{1,0:T(8,128)(2,1)S(1)} %copy-done.1, bf16[2,11,128,1024]{3,2,1,0:T(8,128)(2,1)S(1)} %bitcast.3, bf16[2,11,128,1024]{3,2,1,0:T(8,128)(2,1)S(1)} %bitcast.4), custom_call_target="tpu_custom_call" | custom-call | flops 5905580032 | bytes 9961472 | tf_op jit(solution)/shard_map/pallas_call | solution.py:130
  (15 shorter events, 0.0 us)
Async XLA Ops:
  0.0 32.7 %copy-start = (s32[32,11]{0,1:T(8,128)S(1)}, s32[32,11]{0,1:T(8,128)}, u32[]{:S(2)}) copy-start(s32[32,11]{0,1:T(8,128)} %param.7) | copy-start | bytes 4228
  2.3 26.2 %collective-permute-start.4 = (bf16[2,256,1024]{2,1,0:T(8,128)(2,1)}, bf16[2,256,1024]{2,1,0:T(8,128)(2,1)}, u32[]{:S(2)}, u32[]{:S(2)}) collective-permute-start(bf16[2,256,1024]{2,1,0:T(8,128)(2,1)} %pad_maximum_fusion), channel_id=1, source_target_pairs={{0,4},{1,5},{2,6},{3,7},{4,8},{5,9},{6,10},{7,11},{8,12},{9,13},{1... | collective-permute-start | bytes 3145736 | tf_op jit(solution)/shard_map/ppermute | solution.py:25
  6.6 0.7 collective-permute-start
  8.4 21.4 %collective-permute-start.1 = (bf16[2,128,1024]{2,1,0:T(8,128)(2,1)S(1)}, bf16[2,128,1024]{2,1,0:T(8,128)(2,1)S(1)}, u32[]{:S(2)}, u32[]{:S(2)}) collective-permute-start(bf16[2,128,1024]{2,1,0:T(8,128)(2,1)S(1)} %broadcast_select_fusion.1), channel_id=1, source_target_pairs={{0,4},{8,12},{16,20},{24,28}} | collective-permute-start | bytes 1572872 | tf_op jit(solution)/shard_map/ppermute | solution.py:64
  9.1 44.2 %collective-permute-start.8 = (bf16[2,256,1024]{2,1,0:T(8,128)(2,1)}, bf16[2,256,1024]{2,1,0:T(8,128)(2,1)}, u32[]{:S(2)}, u32[]{:S(2)}) collective-permute-start(bf16[2,256,1024]{2,1,0:T(8,128)(2,1)} %pad_maximum_fusion), channel_id=1, source_target_pairs={{0,2},{1,3},{4,6},{5,7},{8,10},{9,11},{12,14},{13,15},{16,18},{17,... | collective-permute-start | bytes 3145736 | tf_op jit(solution)/shard_map/ppermute | solution.py:25
  28.5 24.8 %collective-permute-start.6 = (bf16[2,256,1024]{2,1,0:T(8,128)(2,1)}, bf16[2,256,1024]{2,1,0:T(8,128)(2,1)}, u32[]{:S(2)}, u32[]{:S(2)}) collective-permute-start(bf16[2,256,1024]{2,1,0:T(8,128)(2,1)} %collective-permute-done.4), channel_id=1, source_target_pairs={{2,0},{3,1},{6,4},{7,5},{10,8},{11,9},{14,12},{15,13},{18,16},{19,... | collective-permute-start | bytes 3145736 | tf_op jit(solution)/shard_map/ppermute | solution.py:25
  29.9 27.4 %collective-permute-start.2 = (bf16[2,128,1024]{2,1,0:T(8,128)(2,1)S(1)}, bf16[2,128,1024]{2,1,0:T(8,128)(2,1)}, u32[]{:S(2)}, u32[]{:S(2)}) collective-permute-start(bf16[2,128,1024]{2,1,0:T(8,128)(2,1)S(1)} %broadcast_select_fusion.2), channel_id=1, source_target_pairs={{0,2},{4,6},{8,10},{12,14},{16,18},{20,22},{24,26},{28,30}} | collective-permute-start | bytes 1572872 | tf_op jit(solution)/shard_map/ppermute | solution.py:64
  31.4 33.8 %collective-permute-start.10 = (bf16[2,256,1024]{2,1,0:T(8,128)(2,1)}, bf16[2,256,1024]{2,1,0:T(8,128)(2,1)}, u32[]{:S(2)}, u32[]{:S(2)}) collective-permute-start(bf16[2,256,1024]{2,1,0:T(8,128)(2,1)} %pad_maximum_fusion), channel_id=1, source_target_pairs={{0,1},{2,3},{4,5},{6,7},{8,9},{10,11},{12,13},{14,15},{16,17},{18,... | collective-permute-start | bytes 3145736 | tf_op jit(solution)/shard_map/ppermute | solution.py:25
  32.9 29.8 %collective-permute-start.5 = (bf16[2,256,1024]{2,1,0:T(8,128)(2,1)}, bf16[2,256,1024]{2,1,0:T(8,128)(2,1)}, u32[]{:S(2)}, u32[]{:S(2)}) collective-permute-start(bf16[2,256,1024]{2,1,0:T(8,128)(2,1)} %collective-permute-done.4), channel_id=1, source_target_pairs={{1,0},{3,2},{5,4},{7,6},{9,8},{11,10},{13,12},{15,14},{17,16},{19,... | collective-permute-start | bytes 3145736 | tf_op jit(solution)/shard_map/ppermute | solution.py:25
  53.3 9.4 %collective-permute-start.9 = (bf16[2,256,1024]{2,1,0:T(8,128)(2,1)}, bf16[2,256,1024]{2,1,0:T(8,128)(2,1)S(1)}, u32[]{:S(2)}, u32[]{:S(2)}) collective-permute-start(bf16[2,256,1024]{2,1,0:T(8,128)(2,1)} %collective-permute-done.8), channel_id=1, source_target_pairs={{0,1},{1,0},{2,3},{3,2},{4,5},{5,4},{6,7},{7,6},{8,9},{9,8},{10,11... | collective-permute-start | bytes 3145736 | tf_op jit(solution)/shard_map/ppermute | solution.py:43
  53.3 9.4 %collective-permute-start.7 = (bf16[2,256,1024]{2,1,0:T(8,128)(2,1)}, bf16[2,256,1024]{2,1,0:T(8,128)(2,1)S(1)}, u32[]{:S(2)}, u32[]{:S(2)}) collective-permute-start(bf16[2,256,1024]{2,1,0:T(8,128)(2,1)} %collective-permute-done.6), channel_id=1, source_target_pairs={{0,1},{1,0},{2,3},{3,2},{4,5},{5,4},{6,7},{7,6},{8,9},{9,8},{10,11... | collective-permute-start | bytes 3145736 | tf_op jit(solution)/shard_map/ppermute | solution.py:42
  57.4 3.8 %collective-permute-start.3 = (bf16[2,128,1024]{2,1,0:T(8,128)(2,1)S(1)}, bf16[2,128,1024]{2,1,0:T(8,128)(2,1)S(1)}, u32[]{:S(2)}, u32[]{:S(2)}) collective-permute-start(bf16[2,128,1024]{2,1,0:T(8,128)(2,1)S(1)} %broadcast_select_fusion.3), channel_id=1, source_target_pairs={{0,1},{2,3},{4,5},{6,7},{8,9},{10,11},{12,13},{14,15},{16,17},{18,... | collective-permute-start | bytes 1572872 | tf_op jit(solution)/shard_map/ppermute | solution.py:64
  62.6 4.3 %copy-start.2 = (bf16[256,1024]{1,0:T(8,128)(2,1)S(1)}, bf16[256,1024]{1,0:T(8,128)(2,1)}, u32[]{:S(2)}) copy-start(bf16[256,1024]{1,0:T(8,128)(2,1)} %param.5) | copy-start | bytes 1572868
  62.7 4.3 %copy-start.3 = (bf16[256,1024]{1,0:T(8,128)(2,1)S(1)}, bf16[256,1024]{1,0:T(8,128)(2,1)}, u32[]{:S(2)}) copy-start(bf16[256,1024]{1,0:T(8,128)(2,1)} %param.6) | copy-start | bytes 1572868
  63.3 3.7 %copy-start.1 = (bf16[256,4096]{1,0:T(8,128)(2,1)S(1)}, bf16[256,4096]{1,0:T(8,128)(2,1)}, u32[]{:S(2)}) copy-start(bf16[256,4096]{1,0:T(8,128)(2,1)} %q_ref.1) | copy-start | bytes 6291460

commit v17 on v13

--- a/solution.py
+++ b/solution.py
@@ -65,8 +65,9 @@
     return held
 
 
-def attend_kernel(slot_ref, diag_ref, q_ref, k_ref, v_ref, o_ref, score_sc, bias_sc):
+def attend_kernel(slot_ref, diag_ref, q_ref, kv_ref, o_ref, score_sc, bias_sc):
     local = pl.program_id(1)
+    base = pl.program_id(0) * KV_STEP * HD
     exp2_scale = (HD ** (-0.5)) * 1.4426950408889634
     rows = PAIR * BLK
     row = lax.broadcasted_iota(jnp.int32, (rows, BLK), 0) % BLK
@@ -76,13 +77,13 @@
     q = q_ref[...]
     chain = 0
     for kv_head in range(KV_STEP):
-        kv_lanes = slice(kv_head * HD, (kv_head + 1) * HD)
+        kv_lanes = pl.ds(pl.multiple_of(base + kv_head * HD, HD), HD)
         for half in range(GROUP // PAIR):
             heads = [kv_head * GROUP + j for j in range(half * PAIR, (half + 1) * PAIR)]
             stacked = jnp.concatenate([q[:, j * HD:(j + 1) * HD] for j in heads], axis=0)
             run_max = jnp.full((rows, BLK), -jnp.inf, jnp.float32)
             for s in range(LIST):
-                key = k_ref[0, slot_ref[local, s], :, kv_lanes]
+                key = kv_ref[0, slot_ref[local, s], :, kv_lanes]
                 sc = lax.dot_general(
                     stacked, key, (((1,), (1,)), ((), ())), preferred_element_type=jnp.float32
                 ) + bias_sc[diag_ref[local, s]]
@@ -94,7 +95,7 @@
             for s in range(LIST):
                 powers = jnp.exp2((score_sc[chain, s] - row_max) * exp2_scale)
                 total = total + powers
-                value = v_ref[0, slot_ref[local, s], :, kv_lanes]
+                value = kv_ref[1, slot_ref[local, s], :, kv_lanes]
                 acc = acc + jnp.dot(
                     powers.astype(jnp.bfloat16), value, preferred_element_type=jnp.float32
                 )
@@ -114,8 +115,7 @@
         grid=(KVH // KV_STEP, blocks_here),
         in_specs=[
             pl.BlockSpec((BLK, KV_STEP * GROUP * HD), lambda g, b, *_: (b, g)),
-            pl.BlockSpec((1, buffer_blocks, BLK, KV_STEP * HD), lambda g, b, *_: (0, 0, 0, g)),
-            pl.BlockSpec((1, buffer_blocks, BLK, KV_STEP * HD), lambda g, b, *_: (1, 0, 0, g)),
+            pl.BlockSpec(memory_space=pltpu.VMEM),
         ],
         out_specs=pl.BlockSpec((BLK, KV_STEP * GROUP * HD), lambda g, b, *_: (b, g)),
         scratch_shapes=[
@@ -136,7 +136,7 @@
             transcendentals=blocks_here * H * BLK * LIST * BLK,
             bytes_accessed=2 * queries.size * 2 + kv_buffer.size * 2,
         ),
-    )(slots, diag, queries, kv_buffer, kv_buffer)
+    )(slots, diag, queries, kv_buffer)
 
 
 def per_device(queries, key_rows, value_rows, pattern):

time: 84.6 us -> 86.2 us (1.019)
  Pallas kernels: 21.4 us -> 23.1 us
    pallas_call x1, Pallas kernels: 21.4 us -> 23.1 us  [attend(): pl.pallas_call(attend_kernel, out_shape=jax.ShapeDtypeStruct(queries.shap...]
  transfers between devices with their start and end apart: 10 -> 10, of which waited for: 2 -> 2; matrix products, arithmetic and copies ran while one was open for 6% -> 5% of each run, Pallas kernels for 0% -> 0%
where the time goes in v17:
time: 86.2 us; the launch traced here: 85.8 us
  starting transfers between devices  35.5 us (41%)
  Pallas kernels  23.1 us (27%)
  waiting for transfers between devices  19.2 us (22%)
  other arithmetic  7.44 us (9%)
    ppermute x5, starting transfers between devices, shifted(): return lax.ppermute(shard, axis, pairs)  27.1 us
    pallas_call x1, Pallas kernels, attend(): pl.pallas_call(attend_kernel, out_shape=jax.ShapeDtypeStruct(queries.shap...  23.1 us
    ppermute x5, waiting for transfers between devices, shifted(): return lax.ppermute(shard, axis, pairs)  16.8 us
    ppermute x4, starting transfers between devices, tree_broadcast(): got = lax.ppermute(held, axis, pairs)  4.94 us
    ppermute x1, starting transfers between devices, window_blocks(): partner_back2 = lax.ppermute(back2, axis, swap_pairs)  3.46 us
    ppermute x4, waiting for transfers between devices, tree_broadcast(): got = lax.ppermute(held, axis, pairs)  2.39 us
    another operation x2, other arithmetic, per_device(): kv = jnp.stack([key_rows, value_rows])  2.38 us
    unnamed x3, other arithmetic  2.31 us
  transfers between devices with their start and end apart: 10, of which 2 were waited for; matrix products, arithmetic and copies ran while one was open for 5% of the time, Pallas kernels for 0%

profile of v17, /device:TPU:19, one launch (start us, length us, event | category | flops | bytes accessed | tf_op | source)
XLA Modules:
  0.0 85.8 jit_solution(15499978526365000459)
XLA Ops:
  0.0 1.3 %pad_maximum_fusion = bf16[2,256,1024]{2,1,0:T(8,128)(2,1)S(1)} fusion(bf16[1,256,1024]{2,1,0:T(8,128)(2,1)} %bitcast.8, bf16[1,256,1024]{2,1,0:T(8,128)(2,1)} %bitcast.4), kind=kLoop, calls=%fused_computation.1 | loop fusion | flops 524288 | bytes 2097152 | tf_op jit(solution)/shard_map/stack | solution.py:147
  1.3 3.2 %collective-permute-start.4 = (bf16[2,256,1024]{2,1,0:T(8,128)(2,1)S(1)}, bf16[2,256,1024]{2,1,0:T(8,128)(2,1)S(1)}, u32[]{:S(2)}, u32[]{:S(2)}) collective-permute-start(bf16[2,256,1024]{2,1,0:T(8,128)(2,1)S(1)} %pad_maximum_fusion), channel_id=1, source_target_pairs={{0,4},{1,5},{2,6},{3,7},{4,8},{5,9},{6,10},{7,11},{8,12},{9,13},{1... | collective-permute-start | bytes 3145736 | tf_op jit(solution)/shard_map/ppermute | solution.py:25
  4.5 1.1 %fusion = bf16[2,128,1024]{2,1,0:T(8,128)(2,1)S(1)} fusion(bf16[1,256,1024]{2,1,0:T(8,128)(2,1)} %bitcast.5, bf16[1,256,1024]{2,1,0:T(8,128)(2,1)} %bitcast.9), kind=kLoop, calls=%fused_computation.6 | loop fusion | flops 262144 | bytes 1572864 | tf_op jit(solution)/shard_map/stack | solution.py:147
  5.6 0.7 collective-permute-start
  6.3 4.2 %collective-permute-start.7 = (bf16[2,256,1024]{2,1,0:T(8,128)(2,1)S(1)}, bf16[2,256,1024]{2,1,0:T(8,128)(2,1)}, u32[]{:S(2)}, u32[]{:S(2)}) collective-permute-start(bf16[2,256,1024]{2,1,0:T(8,128)(2,1)S(1)} %pad_maximum_fusion), channel_id=1, source_target_pairs={{0,2},{1,3},{4,6},{5,7},{8,10},{9,11},{12,14},{13,15},{16,18},{17,... | collective-permute-start | bytes 3145736 | tf_op jit(solution)/shard_map/ppermute | solution.py:25
  10.5 16.8 %collective-permute-done.4 = bf16[2,256,1024]{2,1,0:T(8,128)(2,1)S(1)} collective-permute-done((bf16[2,256,1024]{2,1,0:T(8,128)(2,1)S(1)}, bf16[2,256,1024]{2,1,0:T(8,128)(2,1)S(1)}, u32[]{:S(2)}, u32[]{:S(2)}) %collective-permute-start.4) | collective-permute-done | bytes 1048608 | tf_op jit(solution)/shard_map/ppermute | solution.py:25
  27.2 1.3 %collective-permute-start.6 = (bf16[2,256,1024]{2,1,0:T(8,128)(2,1)S(1)}, bf16[2,256,1024]{2,1,0:T(8,128)(2,1)}, u32[]{:S(2)}, u32[]{:S(2)}) collective-permute-start(bf16[2,256,1024]{2,1,0:T(8,128)(2,1)S(1)} %collective-permute-done.4), channel_id=1, source_target_pairs={{2,0},{3,1},{6,4},{7,5},{10,8},{11,9},{14,12},{15,13},{18,16},{19,... | collective-permute-start | bytes 3145736 | tf_op jit(solution)/shard_map/ppermute | solution.py:25
  28.5 0.0 collective-permute-done
  28.5 1.1 %broadcast_select_fusion.1 = bf16[2,128,1024]{2,1,0:T(8,128)(2,1)S(1)} fusion(bf16[2,128,1024]{2,1,0:T(8,128)(2,1)S(1)} %collective-permute-done, pred[]{:T(512)S(6)} %and.53, bf16[1,256,1024]{2,1,0:T(8,128)(2,1)} %bitcast.10, bf16[1,256,1024]{2,1,0:T(8,128)(2,1)} %bitcast.6), kind=kLoop, calls=%fused_computation.8 | loop fusion | flops 524288 | bytes 2097153 | tf_op jit(solution)/shard_map/jit(_where)/select_n | solution.py:63
  29.6 1.5 %collective-permute-start.1 = (bf16[2,128,1024]{2,1,0:T(8,128)(2,1)S(1)}, bf16[2,128,1024]{2,1,0:T(8,128)(2,1)}, u32[]{:S(2)}, u32[]{:S(2)}) collective-permute-start(bf16[2,128,1024]{2,1,0:T(8,128)(2,1)S(1)} %broadcast_select_fusion.1), channel_id=1, source_target_pairs={{0,4},{8,12},{16,20},{24,28}} | collective-permute-start | bytes 1572872 | tf_op jit(solution)/shard_map/ppermute | solution.py:60
  31.1 0.1 broadcast_select_fusion.2
  31.2 1.5 %collective-permute-start.2 = (bf16[2,128,1024]{2,1,0:T(8,128)(2,1)S(1)}, bf16[2,128,1024]{2,1,0:T(8,128)(2,1)}, u32[]{:S(2)}, u32[]{:S(2)}) collective-permute-start(bf16[2,128,1024]{2,1,0:T(8,128)(2,1)S(1)} %broadcast_select_fusion.2), channel_id=1, source_target_pairs={{0,2},{4,6},{8,10},{12,14},{16,18},{20,22},{24,26},{28,30}} | collective-permute-start | bytes 1572872 | tf_op jit(solution)/shard_map/ppermute | solution.py:60
  32.7 1.3 %collective-permute-start.9 = (bf16[2,256,1024]{2,1,0:T(8,128)(2,1)S(1)}, bf16[2,256,1024]{2,1,0:T(8,128)(2,1)}, u32[]{:S(2)}, u32[]{:S(2)}) collective-permute-start(bf16[2,256,1024]{2,1,0:T(8,128)(2,1)S(1)} %pad_maximum_fusion), channel_id=1, source_target_pairs={{0,1},{2,3},{4,5},{6,7},{8,9},{10,11},{12,13},{14,15},{16,17},{18,... | collective-permute-start | bytes 3145736 | tf_op jit(solution)/shard_map/ppermute | solution.py:25
  34.0 0.1 constant_dynamic-slice_fusion
  34.1 0.1 copy.6
  34.2 17.2 %collective-permute-start.5 = (bf16[2,256,1024]{2,1,0:T(8,128)(2,1)S(1)}, bf16[2,256,1024]{2,1,0:T(8,128)(2,1)S(1)}, u32[]{:S(2)}, u32[]{:S(2)}) collective-permute-start(bf16[2,256,1024]{2,1,0:T(8,128)(2,1)S(1)} %collective-permute-done.4), channel_id=1, source_target_pairs={{1,0},{3,2},{5,4},{7,6},{9,8},{11,10},{13,12},{15,14},{17,16},{19,... | collective-permute-start | bytes 3145736 | tf_op jit(solution)/shard_map/ppermute | solution.py:25
  51.4 1.3 %broadcast_select_fusion = bf16[2,256,1024]{2,1,0:T(8,128)(2,1)S(1)} fusion(bf16[2,256,1024]{2,1,0:T(8,128)(2,1)} %collective-permute-done.6, bf16[2,256,1024]{2,1,0:T(8,128)(2,1)} %collective-permute-done.7, pred[]{:T(512)S(6)} %eq.40), kind=kLoop, calls=%fused_computation.5 | loop fusion | flops 524288 | bytes 3145729 | tf_op jit(solution)/shard_map/jit(_where)/select_n | solution.py:36
  52.7 3.5 %collective-permute-start.8 = (bf16[2,256,1024]{2,1,0:T(8,128)(2,1)S(1)}, bf16[2,256,1024]{2,1,0:T(8,128)(2,1)S(1)}, u32[]{:S(2)}, u32[]{:S(2)}) collective-permute-start(bf16[2,256,1024]{2,1,0:T(8,128)(2,1)S(1)} %broadcast_select_fusion), channel_id=1, source_target_pairs={{0,1},{1,0},{2,3},{3,2},{4,5},{5,4},{6,7},{7,6},{8,9},{9,8},{10,11... | collective-permute-start | bytes 3145736 | tf_op jit(solution)/shard_map/ppermute | solution.py:40
  56.2 0.1 broadcast_select_fusion.3
  56.3 1.3 %collective-permute-start.3 = (bf16[2,128,1024]{2,1,0:T(8,128)(2,1)S(1)}, bf16[2,128,1024]{2,1,0:T(8,128)(2,1)S(1)}, u32[]{:S(2)}, u32[]{:S(2)}) collective-permute-start(bf16[2,128,1024]{2,1,0:T(8,128)(2,1)S(1)} %broadcast_select_fusion.3), channel_id=1, source_target_pairs={{0,1},{2,3},{4,5},{6,7},{8,9},{10,11},{12,13},{14,15},{16,17},{18,... | collective-permute-start | bytes 1572872 | tf_op jit(solution)/shard_map/ppermute | solution.py:60
  57.6 0.1 compare_convert_fusion.diag_ref
  57.7 0.0 copy-start.2
  57.7 0.0 copy-start.3
  57.7 2.4 %collective-permute-done.3 = bf16[2,128,1024]{2,1,0:T(8,128)(2,1)S(1)} collective-permute-done((bf16[2,128,1024]{2,1,0:T(8,128)(2,1)S(1)}, bf16[2,128,1024]{2,1,0:T(8,128)(2,1)S(1)}, u32[]{:S(2)}, u32[]{:S(2)}) %collective-permute-start.3) | collective-permute-done | bytes 524320 | tf_op jit(solution)/shard_map/ppermute | solution.py:60
  60.1 0.2 select_dynamic-update-slice_fusion.2
  60.3 0.1 constant_dynamic-update-slice_fusion.2
  60.4 0.0 copy-start.1
  60.4 0.4 select_dynamic-update-slice_fusion.1
  60.8 0.1 constant_dynamic-update-slice_fusion.1
  60.9 1.7 %select_dynamic-update-slice_fusion = bf16[2,1408,1024]{2,1,0:T(8,128)(2,1)S(1)} fusion(bf16[2,1408,1024]{2,1,0:T(8,128)(2,1)S(1)} %constant_dynamic-update-slice_fusion.1, bf16[2,256,1024]{2,1,0:T(8,128)(2,1)S(1)} %collective-permute-done.8, bf16[2,256,1024]{2,1,0:T(8,128)(2,1)} %collective-permute-done.9, pred[]{:T(512)S(6)} %eq.39), kind=kLoop, calls=%fused_computation.3 | loop fusion | flops 524288 | bytes 3145729
  62.6 0.1 constant_dynamic-update-slice_fusion
  62.7 23.1 %shard_map.46 = bf16[256,4096]{1,0:T(8,128)(2,1)} custom-call(s32[2,11]{1,0:T(2,128)S(1)} %fusion.1.slot_ref, s32[2,11]{1,0:T(2,128)S(1)} %compare_convert_fusion.diag_ref, bf16[256,4096]{1,0:T(8,128)(2,1)S(1)} %copy-done.1, bf16[2,11,128,1024]{3,2,1,0:T(8,128)(2,1)S(1)} %bitcast.3), custom_call_target="tpu_custom_call" | custom-call | flops 5905580032 | bytes 9961472 | tf_op jit(solution)/shard_map/pallas_call | solution.py:126
  (14 shorter events, 0.0 us)
Async XLA Ops:
  0.0 34.0 %copy-start = (s32[32,11]{0,1:T(8,128)S(1)}, s32[32,11]{0,1:T(8,128)}, u32[]{:S(2)}) copy-start(s32[32,11]{0,1:T(8,128)} %param.7) | copy-start | bytes 4228
  1.3 25.9 %collective-permute-start.4 = (bf16[2,256,1024]{2,1,0:T(8,128)(2,1)S(1)}, bf16[2,256,1024]{2,1,0:T(8,128)(2,1)S(1)}, u32[]{:S(2)}, u32[]{:S(2)}) collective-permute-start(bf16[2,256,1024]{2,1,0:T(8,128)(2,1)S(1)} %pad_maximum_fusion), channel_id=1, source_target_pairs={{0,4},{1,5},{2,6},{3,7},{4,8},{5,9},{6,10},{7,11},{8,12},{9,13},{1... | collective-permute-start | bytes 3145736 | tf_op jit(solution)/shard_map/ppermute | solution.py:25
  5.6 22.9 %collective-permute-start = (bf16[2,128,1024]{2,1,0:T(8,128)(2,1)S(1)}, bf16[2,128,1024]{2,1,0:T(8,128)(2,1)S(1)}, u32[]{:S(2)}, u32[]{:S(2)}) collective-permute-start(bf16[2,128,1024]{2,1,0:T(8,128)(2,1)S(1)} %fusion), channel_id=1, source_target_pairs={{0,8},{16,24}} | collective-permute-start | bytes 1572872 | tf_op jit(solution)/shard_map/ppermute | solution.py:60
  6.3 45.1 %collective-permute-start.7 = (bf16[2,256,1024]{2,1,0:T(8,128)(2,1)S(1)}, bf16[2,256,1024]{2,1,0:T(8,128)(2,1)}, u32[]{:S(2)}, u32[]{:S(2)}) collective-permute-start(bf16[2,256,1024]{2,1,0:T(8,128)(2,1)S(1)} %pad_maximum_fusion), channel_id=1, source_target_pairs={{0,2},{1,3},{4,6},{5,7},{8,10},{9,11},{12,14},{13,15},{16,18},{17,... | collective-permute-start | bytes 3145736 | tf_op jit(solution)/shard_map/ppermute | solution.py:25
  27.2 24.2 %collective-permute-start.6 = (bf16[2,256,1024]{2,1,0:T(8,128)(2,1)S(1)}, bf16[2,256,1024]{2,1,0:T(8,128)(2,1)}, u32[]{:S(2)}, u32[]{:S(2)}) collective-permute-start(bf16[2,256,1024]{2,1,0:T(8,128)(2,1)S(1)} %collective-permute-done.4), channel_id=1, source_target_pairs={{2,0},{3,1},{6,4},{7,5},{10,8},{11,9},{14,12},{15,13},{18,16},{19,... | collective-permute-start | bytes 3145736 | tf_op jit(solution)/shard_map/ppermute | solution.py:25
  29.6 1.5 %collective-permute-start.1 = (bf16[2,128,1024]{2,1,0:T(8,128)(2,1)S(1)}, bf16[2,128,1024]{2,1,0:T(8,128)(2,1)}, u32[]{:S(2)}, u32[]{:S(2)}) collective-permute-start(bf16[2,128,1024]{2,1,0:T(8,128)(2,1)S(1)} %broadcast_select_fusion.1), channel_id=1, source_target_pairs={{0,4},{8,12},{16,20},{24,28}} | collective-permute-start | bytes 1572872 | tf_op jit(solution)/shard_map/ppermute | solution.py:60
  31.2 25.0 %collective-permute-start.2 = (bf16[2,128,1024]{2,1,0:T(8,128)(2,1)S(1)}, bf16[2,128,1024]{2,1,0:T(8,128)(2,1)}, u32[]{:S(2)}, u32[]{:S(2)}) collective-permute-start(bf16[2,128,1024]{2,1,0:T(8,128)(2,1)S(1)} %broadcast_select_fusion.2), channel_id=1, source_target_pairs={{0,2},{4,6},{8,10},{12,14},{16,18},{20,22},{24,26},{28,30}} | collective-permute-start | bytes 1572872 | tf_op jit(solution)/shard_map/ppermute | solution.py:60
  32.7 28.2 %collective-permute-start.9 = (bf16[2,256,1024]{2,1,0:T(8,128)(2,1)S(1)}, bf16[2,256,1024]{2,1,0:T(8,128)(2,1)}, u32[]{:S(2)}, u32[]{:S(2)}) collective-permute-start(bf16[2,256,1024]{2,1,0:T(8,128)(2,1)S(1)} %pad_maximum_fusion), channel_id=1, source_target_pairs={{0,1},{2,3},{4,5},{6,7},{8,9},{10,11},{12,13},{14,15},{16,17},{18,... | collective-permute-start | bytes 3145736 | tf_op jit(solution)/shard_map/ppermute | solution.py:25
  34.2 26.2 %collective-permute-start.5 = (bf16[2,256,1024]{2,1,0:T(8,128)(2,1)S(1)}, bf16[2,256,1024]{2,1,0:T(8,128)(2,1)S(1)}, u32[]{:S(2)}, u32[]{:S(2)}) collective-permute-start(bf16[2,256,1024]{2,1,0:T(8,128)(2,1)S(1)} %collective-permute-done.4), channel_id=1, source_target_pairs={{1,0},{3,2},{5,4},{7,6},{9,8},{11,10},{13,12},{15,14},{17,16},{19,... | collective-permute-start | bytes 3145736 | tf_op jit(solution)/shard_map/ppermute | solution.py:25
  52.7 7.6 %collective-permute-start.8 = (bf16[2,256,1024]{2,1,0:T(8,128)(2,1)S(1)}, bf16[2,256,1024]{2,1,0:T(8,128)(2,1)S(1)}, u32[]{:S(2)}, u32[]{:S(2)}) collective-permute-start(bf16[2,256,1024]{2,1,0:T(8,128)(2,1)S(1)} %broadcast_select_fusion), channel_id=1, source_target_pairs={{0,1},{1,0},{2,3},{3,2},{4,5},{5,4},{6,7},{7,6},{8,9},{9,8},{10,11... | collective-permute-start | bytes 3145736 | tf_op jit(solution)/shard_map/ppermute | solution.py:40
  56.3 3.8 %collective-permute-start.3 = (bf16[2,128,1024]{2,1,0:T(8,128)(2,1)S(1)}, bf16[2,128,1024]{2,1,0:T(8,128)(2,1)S(1)}, u32[]{:S(2)}, u32[]{:S(2)}) collective-permute-start(bf16[2,128,1024]{2,1,0:T(8,128)(2,1)S(1)} %broadcast_select_fusion.3), channel_id=1, source_target_pairs={{0,1},{2,3},{4,5},{6,7},{8,9},{10,11},{12,13},{14,15},{16,17},{18,... | collective-permute-start | bytes 1572872 | tf_op jit(solution)/shard_map/ppermute | solution.py:60
  57.7 4.9 %copy-start.2 = (bf16[256,1024]{1,0:T(8,128)(2,1)S(1)}, bf16[256,1024]{1,0:T(8,128)(2,1)}, u32[]{:S(2)}) copy-start(bf16[256,1024]{1,0:T(8,128)(2,1)} %param.5) | copy-start | bytes 1572868
  57.7 4.9 %copy-start.3 = (bf16[256,1024]{1,0:T(8,128)(2,1)S(1)}, bf16[256,1024]{1,0:T(8,128)(2,1)}, u32[]{:S(2)}) copy-start(bf16[256,1024]{1,0:T(8,128)(2,1)} %param.6) | copy-start | bytes 1572868
  60.4 2.4 %copy-start.1 = (bf16[256,4096]{1,0:T(8,128)(2,1)S(1)}, bf16[256,4096]{1,0:T(8,128)(2,1)}, u32[]{:S(2)}) copy-start(bf16[256,4096]{1,0:T(8,128)(2,1)} %q_ref.1) | copy-start | bytes 6291460
